TPU v7x, 128 devices: a whole 4x4x4 slice. The times are simulated.
128 devices in a mesh: seq: 8 (over x, core), tensor: 16 (over z, y).
Axes of the slice: x: 4, y: 4, z: 4, core: 2. Of those that a mesh axis runs over, the one named last changes fastest.
Arguments:
- tokens: bfloat16 [4096, 2560], P(('seq', 'tensor')), may hold values from -6 to 6
- in_gate: bfloat16 [2560, 5120], P(None, 'tensor')
- in_x: bfloat16 [2560, 5120], P(None, 'tensor'), may hold values from -0.125 to 0.125
- in_dt: bfloat16 [2560, 80], P(None, 'tensor'), may hold values from -0.125 to 0.125
- in_bc: bfloat16 [2560, 256], replicated, may hold values from -0.125 to 0.125
- conv_x_weight: float32 [4, 5120], P(None, 'tensor'), may hold values from -3 to 3
- conv_x_bias: float32 [5120], P('tensor'), may hold values from -0.5 to 0.5
- conv_bc_weight: float32 [4, 256], replicated, may hold values from -3 to 3
- conv_bc_bias: float32 [256], replicated, may hold values from -0.5 to 0.5
- dt_bias: float32 [80], P('tensor'), may hold values from -2 to 1
- head_rate: float32 [80], P('tensor'), may hold values from 2.4414063e-05 to 0.05
- skip_gain: float32 [80], P('tensor'), may hold values from 0.5 to 1.5
- norm_gain: float32 [5120], P('tensor'), may hold values from 0.5 to 1.5
- out_weight: bfloat16 [5120, 2560], P('tensor'), may hold values from -0.078125 to 0.078125
- lengths: int32 [16], replicated, may hold values from 17 to 2048, as said below
- accepted: int32 [16], replicated, may hold values from 0 to 16
- slots: int32 [16], replicated, may hold values from 0 to 15, each once
Outputs:
- mixed: bfloat16 [4096, 2560], P(('seq', 'tensor'))
- accepted_states: float32 [16, 80, 64, 128], P('seq', 'tensor')
Inputs may be any that keep to these rules, and one draw needn't show every extreme that they name: The 16 lengths sum to 4096; requests are packed in order, and the last 16 tokens of each request are its drafts. `slots`: every slot 0 to 15 is named once.
All inputs are finite; a program needn't handle non-finite values.
Results may differ from a plain program's by a relative error of at most 0.02.
Values may be sent and summed in bfloat16 or wider, within the bound.
No kernel may reach another device: no remote copies, remote signals or barrier semaphores. Data moves between devices by JAX's collectives and lax.ppermute only.
A program may use at most 64 MiB of HBM per device.

v0:
```python
import jax
import jax.numpy as jnp
from jax import lax
from jax.sharding import PartitionSpec as P

BLOCK = 256
DRAFTS = 16


HIGHEST_PRECISION = lax.Precision.HIGHEST


def passed_along(block, axis, distance):
    devices = range(lax.axis_size(axis))
    route = [(i - distance, i) for i in devices if i - distance in devices]
    return lax.ppermute(block, axis, route)


def segment_of(positions, starts):
    return jnp.sum((starts[None, :] <= positions[:, None]).astype(jnp.int32), axis=1) - 1


def per_device(
    tokens,
    in_gate,
    in_x,
    in_dt,
    in_bc,
    conv_x_weight,
    conv_x_bias,
    conv_bc_weight,
    conv_bc_bias,
    dt_bias,
    head_rate,
    skip_gain,
    norm_gain,
    out_weight,
    lengths,
    accepted,
    slots,
):
    local_inner = in_x.shape[1]
    local_heads = in_dt.shape[1]
    head_size = local_inner // local_heads
    state_size = in_bc.shape[1] // 2
    tensor_count = lax.axis_size("tensor")
    seq_count = lax.axis_size("seq")
    weight_all = jnp.concatenate([in_gate, in_x, in_dt, in_bc], axis=1)
    projected = jnp.dot(
        lax.all_gather(tokens, "tensor", axis=0, tiled=True),
        weight_all,
        preferred_element_type=jnp.float32,
    )
    bc_inputs = projected[:, 2 * local_inner + local_heads :]
    gate = projected[:, :local_inner]
    raw_step = projected[:, 2 * local_inner : 2 * local_inner + local_heads]
    inputs = jnp.concatenate([projected[:, local_inner : 2 * local_inner], bc_inputs], axis=1)
    row_count = projected.shape[0]
    first = lax.axis_index("seq") * row_count
    starts = jnp.cumsum(lengths) - lengths
    segment = segment_of(first + jnp.arange(row_count, dtype=jnp.int32), starts)
    taps = conv_x_weight.shape[0]
    edge = passed_along(inputs[row_count - taps + 1 :], "seq", 1)
    edge_segment = segment_of(first - taps + 1 + jnp.arange(taps - 1, dtype=jnp.int32), starts)
    extended = jnp.concatenate([edge, inputs], axis=0)
    extended_segment = jnp.concatenate([edge_segment, segment])
    conv_weight = jnp.concatenate([conv_x_weight, conv_bc_weight], axis=1)
    conv_bias = jnp.concatenate([conv_x_bias, conv_bc_bias])
    conv = jnp.zeros_like(inputs) + conv_bias[None, :]
    for offset in range(taps):
        match = (extended_segment[offset : offset + row_count] == segment).astype(jnp.float32)
        conv = (
            conv
            + conv_weight[offset][None, :] * extended[offset : offset + row_count] * match[:, None]
        )
    active = jax.nn.silu(conv)
    block_count = row_count // BLOCK
    values = active[:, :local_inner].reshape(block_count, BLOCK, local_heads, head_size)
    keys = active[:, local_inner : local_inner + state_size].reshape(block_count, BLOCK, state_size)
    queries = active[:, local_inner + state_size :].reshape(block_count, BLOCK, state_size)
    step_size = jax.nn.softplus(raw_step + dt_bias[None, :])
    decay_sum = jnp.cumsum(
        (-head_rate[None, :] * step_size).reshape(block_count, BLOCK, local_heads), axis=1
    )
    steps = step_size.reshape(block_count, BLOCK, local_heads)
    segs = segment.reshape(block_count, BLOCK)
    prior = segment_of(first + jnp.arange(block_count, dtype=jnp.int32) * BLOCK - 1, starts)
    lower = jnp.arange(BLOCK)[:, None] >= jnp.arange(BLOCK)[None, :]
    same = (segs[:, :, None] == segs[:, None, :]) & lower[None]
    spread = decay_sum[:, :, None, :] - decay_sum[:, None, :, :]
    decay = jnp.where(same[..., None], jnp.exp(jnp.minimum(spread, 0.0)), 0.0)
    gram = jnp.einsum("cin,cjn->cij", queries, keys, precision=HIGHEST_PRECISION)
    mixing = gram[..., None] * decay * steps[:, None, :, :]
    inner = jnp.einsum("cijh,cjhp->cihp", mixing, values, precision=HIGHEST_PRECISION)
    last_match = (segs == segs[:, -1:]).astype(jnp.float32)
    weight_last = jnp.exp(decay_sum[:, -1:, :] - decay_sum) * steps * last_match[..., None]
    local = jnp.einsum(
        "cjhp,cjn->chpn", weight_last[..., None] * values, keys, precision=HIGHEST_PRECISION
    )
    passes = jnp.exp(decay_sum[:, -1, :]) * (segs[:, -1] == prior).astype(jnp.float32)[:, None]

    def advance(carry, item):
        zero_start, factor = carry
        local_state, passing = item
        return (
            (passing[:, None, None] * zero_start + local_state, passing * factor),
            (zero_start, factor),
        )

    empty = jnp.zeros((local_heads, head_size, state_size), jnp.float32)
    unit = jnp.ones((local_heads,), jnp.float32)
    (zero_end, factor_end), (zero_starts, factors) = lax.scan(
        advance, (empty, unit), (local, passes)
    )

    def relay(step, incoming):
        return passed_along(
            (factor_end[:, None, None] * incoming + zero_end).astype(jnp.bfloat16), "seq", 1
        ).astype(jnp.float32)

    incoming = lax.fori_loop(0, seq_count - 1, relay, empty)
    block_states = zero_starts + factors[:, :, None, None] * incoming[None]
    keep = jnp.exp(decay_sum) * (segs == prior[:, None]).astype(jnp.float32)[..., None]
    outer = keep[..., None] * jnp.einsum(
        "cin,chpn->cihp", queries, block_states, precision=HIGHEST_PRECISION
    )
    output = (inner + outer + skip_gain[None, None, :, None] * values).reshape(
        row_count, local_inner
    )
    gated = output * jax.nn.silu(gate)
    totals = lax.psum(jnp.sum(gated * gated, axis=1), "tensor")
    scale = lax.rsqrt(totals[:, None] / (local_inner * tensor_count) + 1e-05)
    normed = (gated * scale * norm_gain[None, :]).astype(jnp.bfloat16)
    mixed = lax.psum_scatter(
        jnp.dot(normed, out_weight, preferred_element_type=jnp.float32).astype(jnp.bfloat16),
        "tensor",
        scatter_dimension=0,
        tiled=True,
    )
    request_count = lengths.shape[0]
    request_ids = jnp.arange(request_count, dtype=jnp.int32)
    ends = starts + lengths - 1 - DRAFTS + accepted
    present = (ends >= first) & (ends < first + row_count)
    local_end = jnp.clip(ends - first, 0, row_count - 1)
    which = local_end // BLOCK
    place = local_end % BLOCK
    chosen_values = jnp.take(values, which, axis=0)
    chosen_keys = jnp.take(keys, which, axis=0)
    chosen_sums = jnp.take(decay_sum, which, axis=0)
    chosen_steps = jnp.take(steps, which, axis=0)
    chosen_segs = jnp.take(segs, which, axis=0)
    end_sums = chosen_sums[request_ids, place]
    valid = (jnp.arange(BLOCK, dtype=jnp.int32)[None, :] <= place[:, None]) & (
        chosen_segs == request_ids[:, None]
    )
    weight = jnp.where(
        valid[..., None],
        jnp.exp(jnp.minimum(end_sums[:, None, :] - chosen_sums, 0.0)) * chosen_steps,
        0.0,
    )
    part = jnp.einsum(
        "rjhp,rjn->rhpn",
        weight[..., None] * chosen_values,
        chosen_keys,
        precision=HIGHEST_PRECISION,
    )
    carried = (
        jnp.exp(end_sums) * (jnp.take(prior, which) == request_ids).astype(jnp.float32)[:, None]
    )
    end_states = carried[:, :, None, None] * jnp.take(block_states, which, axis=0) + part
    end_states = jnp.where(present[:, None, None, None], end_states, 0.0)
    inverse = jnp.sum(
        (slots[None, :] == request_ids[:, None]).astype(jnp.int32) * request_ids[None, :], axis=1
    )
    outgoing = jnp.take(end_states, inverse, axis=0)
    received = lax.all_to_all(
        outgoing.astype(jnp.bfloat16), "seq", split_axis=0, concat_axis=0, tiled=True
    ).astype(outgoing.dtype)
    mine = jnp.sum(
        received.reshape(seq_count, request_count // seq_count, local_heads, head_size, state_size),
        axis=0,
    )
    return (mixed, mine)


def solution(mesh):
    return jax.shard_map(
        per_device,
        mesh=mesh,
        in_specs=(
            P(("seq", "tensor"), None),
            P(None, "tensor"),
            P(None, "tensor"),
            P(None, "tensor"),
            P(),
            P(None, "tensor"),
            P("tensor"),
            P(),
            P(),
            P("tensor"),
            P("tensor"),
            P("tensor"),
            P("tensor"),
            P("tensor", None),
            P(),
            P(),
            P(),
        ),
        out_specs=(P(("seq", "tensor"), None), P("seq", "tensor", None, None)),
        check_vma=False,
    )
```

profile of v0, /device:TPU:6, one launch (start us, length us, event | category | flops | bytes accessed | tf_op | source)
XLA Modules:
  0.0 263.1 jit_solution(2475854600190639639)
XLA Ops:
  7.3 0.7 all-gather.2.cloned.1.call-update
  8.1 0.7 neg.17
  8.7 1.6 copy.83
  10.6 0.6 copy-done.8
  11.3 0.2 fusion.79
  12.6 0.8 compare_and_fusion
  13.4 45.3 %all-gather.2.cloned.1.call-done = bf16[512,2560]{1,0:T(8,128)(2,1)} async-done(((bf16[32,2560]{1,0:T(8,128)(2,1)}), bf16[512,2560]{1,0:T(8,128)(2,1)}) %all-gather.2.cloned.1.call-update) | async-done | bytes 2621456 | tf_op jit(solution)/shard_map/all_gather | solution.py:50
  58.8 5.3 %fusion.28 = f32[512,901]{0,1:T(8,128)S(1)} fusion(bf16[512,2560]{1,0:T(8,128)(2,1)} %all-gather.2.cloned.1.call-done, bf16[2560,256]{0,1:T(8,128)(2,1)S(1)} %copy.83, bf16[2560,5]{0,1:T(8,128)(2,1)S(1)} %copy-done.16, bf16[2560,320]{0,1:T(8,128)(2,1)} %param.25, bf16[2560,320]{0,1:T(8,128)(2,1)} %param.24), kind=kOutput, calls=%fused_computation.45 | convolution fusion | flops 2380369920 | bytes 9079808 | tf_op jit(solution)/shard_map/dot_general | solution.py:49
  64.2 1.1 copy-done.3
  65.5 3.0 %reduce-window.20 = f32[2,5,2,128]{3,2,1,0:T(2,128)S(1)} reduce-window(f32[2,5,2,128]{3,2,1,0:T(2,128)S(1)} %copy.87, f32[]{:T(128)} %constant.178.clone.1), window={size=1x1x1x128 pad=0_0x0_0x0_0x127_0}, to_apply=%region_3.4 | reduce-window | flops 325120 | bytes 20484 | tf_op jit(solution)/shard_map/reduce-window.1
  69.1 1.9 collective-permute-start.1
  71.4 5.8 %collective-permute-done.1 = f32[3,576]{0,1:T(8,128)S(1)} collective-permute-done((f32[3,576]{0,1:T(8,128)S(1)}, f32[3,576]{0,1:T(8,128)S(1)}, u32[]{:S(2)}, u32[]{:S(2)}) %collective-permute-start.1) | collective-permute-done | bytes 6944 | tf_op jit(solution)/shard_map/ppermute | solution.py:16
  77.2 0.5 maximum_maximum_fusion
  77.6 1.4 divide_multiply_fusion
  79.0 0.7 fusion.95
  79.8 0.9 slice.125
  81.0 1.5 reshape.284
  82.5 0.7 fusion.56
  83.2 4.2 %while.28 = (s32[]{:T(128)}, f32[5,64,128]{2,1,0:T(8,128)S(1)}, f32[5]{0:T(128)S(1)}, f32[2,5,64,128]{3,2,1,0:T(8,128)}, f32[2,5]{1,0:T(2,128)}, /*index=5*/f32[...) while((s32[]{:T(128)}, f32[5,64,128]{2,1,0:T(8,128)S(1)}, f32[5]{0:T(128)S(1)}, ...), condition=%wide.region_7.8_spmd.clone, body=%wide.region_6.7_spmd.clone.sunk | while | flops 163853 | bytes 819489 | solution.py:112
  83.3 0.7 bitcast_dynamic-update-slice_fusion.2
  84.0 1.3 dynamic_update_slice.14
  85.3 0.7 bitcast_dynamic-update-slice_fusion.2
  86.1 1.3 dynamic_update_slice.14
  87.4 0.9 reshape.285
  88.3 0.6 fusion.62
  88.9 4.9 %fusion.37 = f32[2,256,5,64]{1,3,2,0:T(8,128)} fusion(f32[2,256,5]{1,2,0:T(8,128)S(1)} %bitcast.80, f32[2,256,5]{1,2,0:T(8,128)S(1)} %bitcast.77, f32[2,256,256]{2,1,0:T(8,128)S(1)} %fusion.62, pred[2,256,256]{2,1,0:T(8,128)(4,1)} %compare_and_fusion, f32[2,256,5,64]{1,0,3,2:T(2,128)S(1)} %reshape.284), kind=kOutput, calls=%fused_computation.56 | convolution fusion | flops 506593280 | bytes 1986560 | tf_op jit(solution)/shard_map/cijh,cjhp->cihp/dot_general | solution.py:94
  93.8 41.2 %while.29 = (s32[]{:T(128)}, f32[5,64,128]{2,1,0:T(8,128)S(1)}, f32[5]{0:T(128)S(1)}, f32[5,64,128]{2,1,0:T(8,128)S(1)}, s32[]{:T(128)}, /*index=5*/s32[]{:T(128)}) while((s32[]{:T(128)}, f32[5,64,128]{2,1,0:T(8,128)S(1)}, f32[5]{0:T(128)S(1)}, f32[5,64,128]{2,1,0:T(8,128)S(1)}, s32[]{:T(128)}, /*index=5*/s32[]{:T(128)}) %tuple.66), condition=%wide.region_9.10_spmd.clone, body=%wide.region_8.9_spmd.clone.sunk | while | flops 204803 | bytes 983179 | solution.py:121
  93.9 1.9 collective-permute-start
  95.8 3.8 %collective-permute-done = bf16[5,64,128]{2,1,0:T(8,128)(2,1)S(1)} collective-permute-done((bf16[5,64,128]{2,1,0:T(8,128)(2,1)S(1)}, bf16[5,64,128]{2,1,0:T(8,128)(2,1)S(1)}, u32[]{:S(2)}, u32[]{:S(2)}) %collective-permute-start) | collective-permute-done | bytes 81952 | tf_op jit(solution)/shard_map/while/body/eval_jaxpr/ppermute | solution.py:16
  99.8 1.9 collective-permute-start
  101.7 3.8 %collective-permute-done = bf16[5,64,128]{2,1,0:T(8,128)(2,1)S(1)} collective-permute-done((bf16[5,64,128]{2,1,0:T(8,128)(2,1)S(1)}, bf16[5,64,128]{2,1,0:T(8,128)(2,1)S(1)}, u32[]{:S(2)}, u32[]{:S(2)}) %collective-permute-start) | collective-permute-done | bytes 81952 | tf_op jit(solution)/shard_map/while/body/eval_jaxpr/ppermute | solution.py:16
  105.7 1.9 collective-permute-start
  107.6 3.8 %collective-permute-done = bf16[5,64,128]{2,1,0:T(8,128)(2,1)S(1)} collective-permute-done((bf16[5,64,128]{2,1,0:T(8,128)(2,1)S(1)}, bf16[5,64,128]{2,1,0:T(8,128)(2,1)S(1)}, u32[]{:S(2)}, u32[]{:S(2)}) %collective-permute-start) | collective-permute-done | bytes 81952 | tf_op jit(solution)/shard_map/while/body/eval_jaxpr/ppermute | solution.py:16
  111.6 1.9 collective-permute-start
  113.5 3.8 %collective-permute-done = bf16[5,64,128]{2,1,0:T(8,128)(2,1)S(1)} collective-permute-done((bf16[5,64,128]{2,1,0:T(8,128)(2,1)S(1)}, bf16[5,64,128]{2,1,0:T(8,128)(2,1)S(1)}, u32[]{:S(2)}, u32[]{:S(2)}) %collective-permute-start) | collective-permute-done | bytes 81952 | tf_op jit(solution)/shard_map/while/body/eval_jaxpr/ppermute | solution.py:16
  117.5 1.9 collective-permute-start
  119.4 3.8 %collective-permute-done = bf16[5,64,128]{2,1,0:T(8,128)(2,1)S(1)} collective-permute-done((bf16[5,64,128]{2,1,0:T(8,128)(2,1)S(1)}, bf16[5,64,128]{2,1,0:T(8,128)(2,1)S(1)}, u32[]{:S(2)}, u32[]{:S(2)}) %collective-permute-start) | collective-permute-done | bytes 81952 | tf_op jit(solution)/shard_map/while/body/eval_jaxpr/ppermute | solution.py:16
  123.3 1.9 collective-permute-start
  125.3 3.8 %collective-permute-done = bf16[5,64,128]{2,1,0:T(8,128)(2,1)S(1)} collective-permute-done((bf16[5,64,128]{2,1,0:T(8,128)(2,1)S(1)}, bf16[5,64,128]{2,1,0:T(8,128)(2,1)S(1)}, u32[]{:S(2)}, u32[]{:S(2)}) %collective-permute-start) | collective-permute-done | bytes 81952 | tf_op jit(solution)/shard_map/while/body/eval_jaxpr/ppermute | solution.py:16
  129.2 1.9 collective-permute-start
  131.2 3.8 %collective-permute-done = bf16[5,64,128]{2,1,0:T(8,128)(2,1)S(1)} collective-permute-done((bf16[5,64,128]{2,1,0:T(8,128)(2,1)S(1)}, bf16[5,64,128]{2,1,0:T(8,128)(2,1)S(1)}, u32[]{:S(2)}, u32[]{:S(2)}) %collective-permute-start) | collective-permute-done | bytes 81952 | tf_op jit(solution)/shard_map/while/body/eval_jaxpr/ppermute | solution.py:16
  135.0 1.1 multiply_add_fusion
  136.1 1.9 fusion.41
  138.0 0.5 copy.100
  138.6 0.8 copy-done.1
  139.4 1.3 multiply_reduce_fusion
  140.7 38.4 %psum.7 = f32[512]{0:T(512)S(1)} all-reduce(f32[512]{0:T(512)S(1)} %multiply_reduce_fusion), channel_id=1, replica_groups=mesh['seq'=8,'tensor'=16] {'tensor'}, use_global_device_ids=true, to_apply=%region_11.12 | all-reduce | flops 512 | bytes 4096 | tf_op jit(solution)/shard_map/psum | solution.py:131
  179.1 4.5 %convolution_convert_fusion = bf16[512,2560]{1,0:T(8,128)(2,1)} fusion(bf16[320,2560]{1,0:T(8,128)(2,1)S(1)} %copy-done, f32[320]{0:T(512)S(1)} %copy-done.17, f32[512]{0:T(512)S(1)} %add_rsqrt_fusion, f32[512,320]{0,1:T(8,128)} %bitcast.84, f32[512,901]{0,1:T(8,128)} %copy-done.3), kind=kOutput, calls=%fused_computation.29 | convolution fusion | flops 841482240 | bytes 5573888 | tf_op jit(solution)/shard_map/dot_general | solution.py:135
  183.6 0.6 fusion.96
  184.3 1.2 compare_convert_fusion.2
  185.5 0.6 gather_fusion.2
  186.4 0.6 gather_fusion.6
  186.9 0.6 gather_fusion.7
  187.6 2.0 copy.101
  189.6 1.3 gather_fusion
  191.1 2.3 gather_fusion.1
  193.4 2.0 gather_fusion.4
  195.4 3.2 %gather_fusion.3 = f32[16,256,5,64]{1,3,2,0:T(8,128)} fusion(f32[2,256,5,64]{1,3,2,0:T(8,128)S(1)} %copy.93, s32[1024]{0:T(1024)S(1)} %pad_clamp_fusion.1), kind=kCustom, calls=%fused_computation.5 | custom fusion | bytes 10485824 | tf_op jit(solution)/shard_map/jit(_take)/gather | solution.py:147
  198.6 10.4 %add_select_fusion = bf16[16,5,64,128]{3,2,1,0:T(8,128)(2,1)} fusion(f32[16,5,64,128]{3,2,1,0:T(8,128)} %gather_fusion.1, f32[16,5]{1,0:T(8,128)S(1)} %exponential_multiply_fusion.1, pred[16]{0:T(512)(128)(4,1)S(1)} %compare_and_fusion.1, pred[16]{0:T(512)(128)(4,1)S(1)} %get-tuple-element.154, f32[16,256,128]{2,1,0:T(8,128)} %gather_fusion.4, ...), kind=kOutput, calls=%fused_computation.32 | convolution fusion | flops 2019033088 | bytes 11354464 | tf_op jit(solution)/shard_map/rjhp,rjn->rhpn/dot_general | solution.py:161
  209.0 2.1 gather_fusion.5
  211.1 0.4 select_convert_fusion
  211.6 21.3 %all_to_all.5 = bf16[16,5,64,128]{3,2,1,0:T(8,128)(2,1)S(1)} all-to-all(bf16[16,5,64,128]{3,2,1,0:T(8,128)(2,1)S(1)} %select_convert_fusion), channel_id=1, replica_groups=mesh['seq'=8,'tensor'=16] {'seq'}, dimensions={0} | all-to-all | bytes 2621440 | tf_op jit(solution)/shard_map/all_to_all | solution.py:176
  232.9 1.0 convert_reduce_fusion
  233.8 22.4 %reduce-scatter.2.cloned.1.call-done = bf16[32,2560]{1,0:T(8,128)(2,1)} async-done(((bf16[512,2560]{1,0:T(8,128)(2,1)}), bf16[32,2560]{1,0:T(8,128)(2,1)}) %reduce-scatter.2.cloned.1.call-update) | async-done | bytes 163856 | tf_op jit(solution)/shard_map/reduce_scatter | solution.py:134
  (116 shorter events, 4.6 us)
Async XLA Ops:
  7.2 171.9 %copy-start = (bf16[320,2560]{1,0:T(8,128)(2,1)S(1)}, bf16[320,2560]{1,0:T(8,128)(2,1)}, u32[]{:S(2)}) copy-start(bf16[320,2560]{1,0:T(8,128)(2,1)} %param.36) | copy-start | bytes 4915204
  7.2 3.2 %copy-start.13 = (s32[16]{0:T(128)S(1)}, s32[16]{0:T(128)}, u32[]{:S(2)}) copy-start(s32[16]{0:T(128)} %param.37) | copy-start | bytes 196
  7.2 4.4 %copy-start.6 = (f32[4,256]{1,0:T(4,128)S(1)}, f32[4,256]{1,0:T(4,128)}, u32[]{:S(2)}) copy-start(f32[4,256]{1,0:T(4,128)} %param.30) | copy-start | bytes 12292
  7.2 4.4 %copy-start.5 = (f32[4,320]{1,0:T(4,128)S(1)}, f32[4,320]{1,0:T(4,128)}, u32[]{:S(2)}) copy-start(f32[4,320]{1,0:T(4,128)} %param.28) | copy-start | bytes 15364
  7.2 5.0 %copy-start.11 = (f32[256]{0:T(256)S(1)}, f32[256]{0:T(256)}, u32[]{:S(2)}) copy-start(f32[256]{0:T(256)} %param.31) | copy-start | bytes 3076
  7.2 5.0 %copy-start.7 = (f32[320]{0:T(512)S(1)}, f32[320]{0:T(512)}, u32[]{:S(2)}) copy-start(f32[320]{0:T(512)} %param.29) | copy-start | bytes 3844
  7.2 51.5 %copy-start.16 = (bf16[2560,5]{0,1:T(8,128)(2,1)S(1)}, bf16[2560,5]{0,1:T(8,128)(2,1)}, u32[]{:S(2)}) copy-start(bf16[2560,5]{0,1:T(8,128)(2,1)} %param.26) | copy-start | bytes 76804
  7.2 51.5 %all-gather.2.cloned.1.call-start = ((), (), s32[]{:S(2)}) async-start(), calls=%async_computation.2 | async-start | bytes 2785280 | tf_op jit(solution)/shard_map/all_gather | solution.py:50
  8.0 248.3 %reduce-scatter.2.cloned.1.call-start = ((), (), s32[]{:S(2)}) async-start(), calls=%async_computation.3 | async-start | bytes 2785280 | tf_op jit(solution)/shard_map/reduce_scatter | solution.py:134
  10.6 0.6 copy-start.8
  64.1 1.3 copy-start.3
  64.1 1.3 copy-start.12
  69.1 8.0 %collective-permute-start.1 = (f32[3,576]{0,1:T(8,128)S(1)}, f32[3,576]{0,1:T(8,128)S(1)}, u32[]{:S(2)}, u32[]{:S(2)}) collective-permute-start(f32[3,576]{0,1:T(8,128)S(1)} %fusion.61), channel_id=1, source_target_pairs={{0,16},{16,32},{32,48},{48,64},{64,80},{80,96},{96,112},{1,17},{17... | collective-permute-start | bytes 20744 | tf_op jit(solution)/shard_map/ppermute | solution.py:16
  83.2 4.2 %copy-start.2 = (f32[512,128]{0,1:T(8,128)S(1)}, f32[512,128]{0,1:T(8,128)}, u32[]{:S(2)}) copy-start(f32[512,128]{0,1:T(8,128)} %get-tuple-element.145) | copy-start | bytes 786436
  93.8 41.2 %copy-start.10 = (f32[2,5]{1,0:T(2,128)S(1)}, f32[2,5]{1,0:T(2,128)}, u32[]{:S(2)}) copy-start(f32[2,5]{1,0:T(2,128)} %get-tuple-element.66) | copy-start | bytes 124
  93.8 42.3 %copy-start.4 = (f32[2,256,128]{1,0,2:T(2,128)S(1)}, f32[2,256,128]{1,0,2:T(2,128)}, u32[]{:S(2)}) copy-start(f32[2,256,128]{1,0,2:T(2,128)} %reshape.285) | copy-start | bytes 786436
  93.8 42.3 %copy-start.15 = (f32[5]{0:T(128)S(1)}, f32[5]{0:T(128)}, u32[]{:S(2)}) copy-start(f32[5]{0:T(128)} %param.34) | copy-start | bytes 64
  93.9 5.8 %collective-permute-start = (bf16[5,64,128]{2,1,0:T(8,128)(2,1)S(1)}, bf16[5,64,128]{2,1,0:T(8,128)(2,1)S(1)}, u32[]{:S(2)}, u32[]{:S(2)}) collective-permute-start(bf16[5,64,128]{2,1,0:T(8,128)(2,1)S(1)} %fusion.104), channel_id=1, source_target_pairs={{0,16},{16,32},{32,48},{48,64},{64,80},{80,96},{96,112},{1,17},{17... | collective-permute-start | bytes 245768 | tf_op jit(solution)/shard_map/while/body/eval_jaxpr/ppermute | solution.py:16
  99.8 5.8 %collective-permute-start = (bf16[5,64,128]{2,1,0:T(8,128)(2,1)S(1)}, bf16[5,64,128]{2,1,0:T(8,128)(2,1)S(1)}, u32[]{:S(2)}, u32[]{:S(2)}) collective-permute-start(bf16[5,64,128]{2,1,0:T(8,128)(2,1)S(1)} %fusion.104), channel_id=1, source_target_pairs={{0,16},{16,32},{32,48},{48,64},{64,80},{80,96},{96,112},{1,17},{17... | collective-permute-start | bytes 245768 | tf_op jit(solution)/shard_map/while/body/eval_jaxpr/ppermute | solution.py:16
  105.7 5.8 %collective-permute-start = (bf16[5,64,128]{2,1,0:T(8,128)(2,1)S(1)}, bf16[5,64,128]{2,1,0:T(8,128)(2,1)S(1)}, u32[]{:S(2)}, u32[]{:S(2)}) collective-permute-start(bf16[5,64,128]{2,1,0:T(8,128)(2,1)S(1)} %fusion.104), channel_id=1, source_target_pairs={{0,16},{16,32},{32,48},{48,64},{64,80},{80,96},{96,112},{1,17},{17... | collective-permute-start | bytes 245768 | tf_op jit(solution)/shard_map/while/body/eval_jaxpr/ppermute | solution.py:16
  111.6 5.8 %collective-permute-start = (bf16[5,64,128]{2,1,0:T(8,128)(2,1)S(1)}, bf16[5,64,128]{2,1,0:T(8,128)(2,1)S(1)}, u32[]{:S(2)}, u32[]{:S(2)}) collective-permute-start(bf16[5,64,128]{2,1,0:T(8,128)(2,1)S(1)} %fusion.104), channel_id=1, source_target_pairs={{0,16},{16,32},{32,48},{48,64},{64,80},{80,96},{96,112},{1,17},{17... | collective-permute-start | bytes 245768 | tf_op jit(solution)/shard_map/while/body/eval_jaxpr/ppermute | solution.py:16
  117.5 5.8 %collective-permute-start = (bf16[5,64,128]{2,1,0:T(8,128)(2,1)S(1)}, bf16[5,64,128]{2,1,0:T(8,128)(2,1)S(1)}, u32[]{:S(2)}, u32[]{:S(2)}) collective-permute-start(bf16[5,64,128]{2,1,0:T(8,128)(2,1)S(1)} %fusion.104), channel_id=1, source_target_pairs={{0,16},{16,32},{32,48},{48,64},{64,80},{80,96},{96,112},{1,17},{17... | collective-permute-start | bytes 245768 | tf_op jit(solution)/shard_map/while/body/eval_jaxpr/ppermute | solution.py:16
  123.3 5.8 %collective-permute-start = (bf16[5,64,128]{2,1,0:T(8,128)(2,1)S(1)}, bf16[5,64,128]{2,1,0:T(8,128)(2,1)S(1)}, u32[]{:S(2)}, u32[]{:S(2)}) collective-permute-start(bf16[5,64,128]{2,1,0:T(8,128)(2,1)S(1)} %fusion.104), channel_id=1, source_target_pairs={{0,16},{16,32},{32,48},{48,64},{64,80},{80,96},{96,112},{1,17},{17... | collective-permute-start | bytes 245768 | tf_op jit(solution)/shard_map/while/body/eval_jaxpr/ppermute | solution.py:16
  129.2 5.8 %collective-permute-start = (bf16[5,64,128]{2,1,0:T(8,128)(2,1)S(1)}, bf16[5,64,128]{2,1,0:T(8,128)(2,1)S(1)}, u32[]{:S(2)}, u32[]{:S(2)}) collective-permute-start(bf16[5,64,128]{2,1,0:T(8,128)(2,1)S(1)} %fusion.104), channel_id=1, source_target_pairs={{0,16},{16,32},{32,48},{48,64},{64,80},{80,96},{96,112},{1,17},{17... | collective-permute-start | bytes 245768 | tf_op jit(solution)/shard_map/while/body/eval_jaxpr/ppermute | solution.py:16
  138.0 41.1 %copy-start.17 = (f32[320]{0:T(512)S(1)}, f32[320]{0:T(512)}, u32[]{:S(2)}) copy-start(f32[320]{0:T(512)} %param.35) | copy-start | bytes 3844
  138.6 0.8 copy-start.1
  183.6 0.7 copy-start.9
  183.6 0.7 copy-start.14
  183.6 2.5 copy-start.18
Sparse Core Ops, SparseCore 0:
  10.2 48.5 all-gather.1
  183.7 72.4 reduce-scatter.1
where the time goes:
time: 264 us; the launch traced here: 263 us
  waiting for transfers between devices  101 us (38%)
  blocking collectives  59.7 us (23%)
  matrix products  28.3 us (11%)
  local copies, waits for them, and re-layouts  27.9 us (11%)
  other arithmetic  15.9 us (6%)
  starting transfers between devices  15.4 us (6%)
  between operations  14.5 us (5%)
    all_gather x1, waiting for transfers between devices, per_device(): lax.all_gather(tokens, 'tensor', axis=0, tiled=True)  45.3 us
    psum x1, blocking collectives, per_device(): totals = lax.psum(jnp.sum(gated * gated, axis=1), 'tensor')  38.4 us
    ppermute x8, waiting for transfers between devices, passed_along(): return lax.ppermute(block, axis, route)  32.6 us
    reduce_scatter x1, waiting for transfers between devices, per_device(): lax.psum_scatter(jnp.dot(normed, out_weight, preferred_element_type=jnp.f...  22.4 us
    all_to_all x1, blocking collectives, per_device(): lax.all_to_all(outgoing.astype(jnp.bfloat16), 'seq', split_axis=0, concat...  21.3 us
    ppermute x8, starting transfers between devices, passed_along(): return lax.ppermute(block, axis, route)  15.4 us
    dot_general x1, matrix products, per_device(): jnp.einsum('rjhp,rjn->rhpn', weight[..., None] * chosen_values, chosen_ke...  10.4 us
    dot_general x1, matrix products, per_device(): jnp.dot(lax.all_gather(tokens, 'tensor', axis=0, tiled=True), weight_all,...  5.32 us
  transfers between devices with their start and end apart: 10, of which 10 were waited for; matrix products, arithmetic and copies ran while one was open for 13% of the time, Pallas kernels for 0%

commit v1 on v0

--- a/solution.py
+++ b/solution.py
@@ -113,12 +113,25 @@
         advance, (empty, unit), (local, passes)
     )
 
-    def relay(step, incoming):
-        return passed_along(
-            (factor_end[:, None, None] * incoming + zero_end).astype(jnp.bfloat16), "seq", 1
-        ).astype(jnp.float32)
-
-    incoming = lax.fori_loop(0, seq_count - 1, relay, empty)
+    factor_high = factor_end.astype(jnp.bfloat16)
+    factor_low = (factor_end - factor_high.astype(jnp.float32)).astype(jnp.bfloat16)
+    factor_rows = jnp.zeros((local_heads, 16, state_size), jnp.bfloat16)
+    factor_rows = factor_rows.at[:, 0, :].set(factor_high[:, None])
+    factor_rows = factor_rows.at[:, 1, :].set(factor_low[:, None])
+    sent = lax.all_gather(
+        jnp.concatenate([zero_end.astype(jnp.bfloat16), factor_rows], axis=1), "seq", axis=0
+    )
+    sent_states = sent[:, :, :head_size]
+    sent_factors = sent[:, :, head_size, 0].astype(jnp.float32) + sent[
+        :, :, head_size + 1, 0
+    ].astype(jnp.float32)
+    seq_index = lax.axis_index("seq")
+    incoming = empty
+    for earlier in range(seq_count - 1):
+        advanced = sent_factors[earlier][:, None, None] * incoming + sent_states[earlier].astype(
+            jnp.float32
+        )
+        incoming = jnp.where(earlier < seq_index, advanced, incoming)
     block_states = zero_starts + factors[:, :, None, None] * incoming[None]
     keep = jnp.exp(decay_sum) * (segs == prior[:, None]).astype(jnp.float32)[..., None]
     outer = keep[..., None] * jnp.einsum(
@@ -128,15 +141,17 @@
         row_count, local_inner
     )
     gated = output * jax.nn.silu(gate)
-    totals = lax.psum(jnp.sum(gated * gated, axis=1), "tensor")
-    scale = lax.rsqrt(totals[:, None] / (local_inner * tensor_count) + 1e-05)
-    normed = (gated * scale * norm_gain[None, :]).astype(jnp.bfloat16)
-    mixed = lax.psum_scatter(
-        jnp.dot(normed, out_weight, preferred_element_type=jnp.float32).astype(jnp.bfloat16),
+    squares = jnp.sum(gated * gated, axis=1)
+    totals = lax.psum_scatter(squares, "tensor", scatter_dimension=0, tiled=True)
+    unscaled = (gated * norm_gain[None, :]).astype(jnp.bfloat16)
+    reduced = lax.psum_scatter(
+        jnp.dot(unscaled, out_weight, preferred_element_type=jnp.float32).astype(jnp.bfloat16),
         "tensor",
         scatter_dimension=0,
         tiled=True,
     )
+    scale = lax.rsqrt(totals[:, None] / (local_inner * tensor_count) + 1e-05)
+    mixed = (reduced.astype(jnp.float32) * scale).astype(jnp.bfloat16)
     request_count = lengths.shape[0]
     request_ids = jnp.arange(request_count, dtype=jnp.int32)
     ends = starts + lengths - 1 - DRAFTS + accepted

time: 264 us -> 198 us (0.75)
  waiting for transfers between devices: 101 us -> 51.9 us
  starting transfers between devices: 15.4 us -> 6.64 us
  blocking collectives: 59.7 us -> 51.8 us
  matrix products: 28.3 us -> 25.4 us
    psum x1 -> x0, blocking collectives: 38.4 us -> none  [per_device(): totals = lax.psum(jnp.sum(gated * gated, axis=1), 'tensor')]
    unnamed x0 -> x1, blocking collectives: none -> 38.3 us
    ppermute x8 -> x1, waiting for transfers between devices: 32.6 us -> 5.21 us  [passed_along(): return lax.ppermute(block, axis, route)]
    reduce_scatter x1, waiting for transfers between devices: 22.4 us -> 0.01 us  [per_device(): lax.psum_scatter(jnp.dot(unscaled, out_weight, preferred_element_type=jnp...]
    all_to_all x1 -> x0, blocking collectives: 21.3 us -> none  [per_device(): lax.all_to_all(outgoing.astype(jnp.bfloat16), 'seq', split_axis=0, concat...]
    all_gather x0 -> x1, blocking collectives: none -> 13.5 us  [per_device(): lax.all_gather(jnp.concatenate([zero_end.astype(jnp.bfloat16), factor_row...]
    ppermute x8 -> x1, starting transfers between devices: 15.4 us -> 1.92 us  [passed_along(): return lax.ppermute(block, axis, route)]
    all_to_all x0 -> x1, starting transfers between devices: none -> 4.64 us  [per_device(): lax.all_to_all(outgoing.astype(jnp.bfloat16), 'seq', split_axis=0, concat...]
  transfers between devices with their start and end apart: 10 -> 4, of which waited for: 10 -> 2; matrix products, arithmetic and copies ran while one was open for 13% -> 19% of each run, Pallas kernels for 0% -> 0%
where the time goes in v1:
time: 198 us; the launch traced here: 197 us
  waiting for transfers between devices  51.9 us (26%)
  blocking collectives  51.8 us (26%)
  local copies, waits for them, and re-layouts  28.7 us (14%)
  matrix products  25.4 us (13%)
  other arithmetic  17.7 us (9%)
  between operations  15.3 us (8%)
  starting transfers between devices  6.64 us (3%)
    all_gather x1, waiting for transfers between devices, per_device(): lax.all_gather(tokens, 'tensor', axis=0, tiled=True)  46 us
    unnamed x1, blocking collectives  38.3 us
    all_gather x1, blocking collectives, per_device(): lax.all_gather(jnp.concatenate([zero_end.astype(jnp.bfloat16), factor_row...  13.5 us
    dot_general x1, matrix products, per_device(): jnp.einsum('rjhp,rjn->rhpn', weight[..., None] * chosen_values, chosen_ke...  10.2 us
    unnamed x57, local copies, waits for them, and re-layouts  6.88 us
    dot_general x1, matrix products, per_device(): jnp.dot(lax.all_gather(tokens, 'tensor', axis=0, tiled=True), weight_all,...  5.32 us
    ppermute x1, waiting for transfers between devices, passed_along(): return lax.ppermute(block, axis, route)  5.21 us
    all_to_all x1, starting transfers between devices, per_device(): lax.all_to_all(outgoing.astype(jnp.bfloat16), 'seq', split_axis=0, concat...  4.64 us
  transfers between devices with their start and end apart: 4, of which 2 were waited for; matrix products, arithmetic and copies ran while one was open for 19% of the time, Pallas kernels for 0%

profile of v1, /device:TPU:6, one launch (start us, length us, event | category | flops | bytes accessed | tf_op | source)
XLA Modules:
  0.0 197.4 jit_solution(6653891056701638256)
XLA Ops:
  7.3 0.7 all-gather.3.cloned.1.call-update
  8.1 0.7 neg.17
  8.7 1.6 copy.113
  10.5 0.1 reduce.5
  10.6 0.6 copy-done.14
  11.3 0.2 fusion.76
  11.7 0.2 slice_reduce_fusion.1
  11.9 0.2 convert_reduce_fusion.2
  12.2 0.2 fusion.77
  12.6 0.2 compare_and_fusion
  12.8 46.0 %all-gather.3.cloned.1.call-done = bf16[512,2560]{1,0:T(8,128)(2,1)} async-done(((bf16[32,2560]{1,0:T(8,128)(2,1)}), bf16[512,2560]{1,0:T(8,128)(2,1)}) %all-gather.3.cloned.1.call-update) | async-done | bytes 2621456 | tf_op jit(solution)/shard_map/all_gather | solution.py:50
  58.8 5.3 %fusion.26 = f32[512,901]{0,1:T(8,128)S(1)} fusion(bf16[512,2560]{1,0:T(8,128)(2,1)} %all-gather.3.cloned.1.call-done, bf16[2560,256]{0,1:T(8,128)(2,1)S(1)} %copy.113, bf16[2560,5]{0,1:T(8,128)(2,1)S(1)} %copy-done.22, bf16[2560,320]{0,1:T(8,128)(2,1)} %param.27, bf16[2560,320]{0,1:T(8,128)(2,1)} %param.26), kind=kOutput, calls=%fused_computation.42 | convolution fusion | flops 2380369920 | bytes 9079808 | tf_op jit(solution)/shard_map/dot_general | solution.py:49
  64.2 1.2 copy-done.6
  65.5 3.0 %reduce-window.20 = f32[2,5,2,128]{3,2,1,0:T(2,128)S(1)} reduce-window(f32[2,5,2,128]{3,2,1,0:T(2,128)S(1)} %copy.117, f32[]{:T(128)} %constant.231.clone.1), window={size=1x1x1x128 pad=0_0x0_0x0_0x127_0}, to_apply=%region_3.4 | reduce-window | flops 325120 | bytes 20484 | tf_op jit(solution)/shard_map/reduce-window.1
  69.0 0.2 fusion.58
  69.2 1.9 collective-permute-start
  71.1 0.2 slice_reduce_fusion
  71.2 0.7 exponential_multiply_fusion
  72.0 5.2 %collective-permute-done = f32[3,576]{0,1:T(8,128)S(1)} collective-permute-done((f32[3,576]{0,1:T(8,128)S(1)}, f32[3,576]{0,1:T(8,128)S(1)}, u32[]{:S(2)}, u32[]{:S(2)}) %collective-permute-start) | collective-permute-done | bytes 6944 | tf_op jit(solution)/shard_map/ppermute | solution.py:16
  77.2 0.5 maximum_maximum_fusion
  77.6 1.4 divide_multiply_fusion
  79.1 0.7 fusion.95
  79.8 0.2 reshape.372
  80.0 0.7 copy-done.4
  80.7 0.1 copy.116
  80.9 0.4 reshape.370
  81.3 1.7 fusion.54
  83.0 4.1 %while.19 = (s32[]{:T(128)}, f32[5,64,128]{2,1,0:T(8,128)S(1)}, f32[5]{0:T(128)S(1)}, f32[2,5,64,128]{3,2,1,0:T(8,128)}, f32[2,5]{1,0:T(2,128)}, /*index=5*/f32[...) while((s32[]{:T(128)}, f32[5,64,128]{2,1,0:T(8,128)S(1)}, f32[5]{0:T(128)S(1)}, ...), condition=%wide.region_7.8_spmd.clone, body=%wide.region_6.7_spmd.clone.sunk | while | flops 163853 | bytes 819489 | solution.py:112
  83.0 0.7 bitcast_dynamic-update-slice_fusion.2
  83.8 1.3 dynamic_update_slice.14
  85.1 0.7 bitcast_dynamic-update-slice_fusion.2
  85.9 1.3 dynamic_update_slice.14
  87.3 13.5 %all-gather = bf16[40,80,128]{2,1,0:T(8,128)(2,1)S(1)} all-gather(bf16[5,80,128]{2,1,0:T(8,128)(2,1)S(1)} %pad_maximum_fusion.1), channel_id=2, replica_groups=mesh['seq'=8,'tensor'=16] {'seq'}, dimensions={0}, use_global_device_ids=true | all-gather | bytes 921600 | tf_op jit(solution)/shard_map/all_gather | solution.py:121
  100.8 0.9 copy-done.2
  101.7 0.1 copy.146
  101.9 0.1 copy.145
  102.0 0.9 reshape.371
  102.9 0.6 fusion.59
  103.6 3.5 %fusion.35 = f32[2,256,5,64]{1,3,2,0:T(8,128)S(1)} fusion(f32[2,256,5]{1,2,0:T(8,128)S(1)} %bitcast.98, f32[2,256,5]{1,2,0:T(8,128)S(1)} %bitcast.95, f32[2,256,256]{2,1,0:T(8,128)S(1)} %fusion.59, pred[2,256,256]{2,1,0:T(8,128)(4,1)S(1)} %compare_and_fusion, f32[2,256,5,64]{1,0,3,2:T(2,128)S(1)} %reshape.370), kind=kOutput, calls=%fused_computation.53 | convolution fusion | flops 506593280 | bytes 1986560 | tf_op jit(solution)/shard_map/cijh,cjhp->cihp/dot_general | solution.py:94
  107.2 0.2 select_bitcast_fusion
  107.6 0.8 fusion.39
  108.4 0.5 copy.132
  108.9 0.8 copy-done.1
  109.8 3.2 %convolution_convert_fusion = bf16[512,2560]{1,0:T(8,128)(2,1)} fusion(bf16[320,2560]{1,0:T(8,128)(2,1)S(1)} %copy-done, f32[320]{0:T(512)S(1)} %copy-done.23, f32[512,320]{0,1:T(8,128)S(1)} %bitcast.101, f32[512,901]{0,1:T(8,128)S(1)} %copy-done.7), kind=kOutput, calls=%fused_computation.26 | convolution fusion | flops 841318400 | bytes 5572608 | tf_op jit(solution)/shard_map/dot_general | solution.py:148
  113.1 0.6 fusion.97
  113.7 1.3 compare_convert_fusion.2
  115.1 0.6 gather_fusion.2
  115.9 0.6 gather_fusion.6
  116.5 0.6 gather_fusion.7
  117.2 2.0 %copy.133 = f32[16,256,5]{2,1,0:T(8,128)} copy(f32[16,256,5]{1,2,0:T(8,128)S(1)} %broadcast_select_fusion.1) | data formatting | bytes 163840 | tf_op jit(solution)/shard_map/jit(_take)/select_n | solution.py:164
  119.2 1.3 gather_fusion
  120.5 0.1 fusion.64
  120.7 2.3 %gather_fusion.1 = f32[16,5,64,128]{3,2,1,0:T(8,128)} fusion(f32[2,5,64,128]{3,2,1,0:T(8,128)S(1)} %multiply_add_fusion, s32[1024]{0:T(1024)S(1)} %pad_clamp_fusion.1), kind=kCustom, calls=%fused_computation.3 | custom fusion | bytes 5242944 | tf_op jit(solution)/shard_map/jit(_take)/gather | solution.py:185
  122.9 2.0 %gather_fusion.4 = f32[16,256,128]{2,1,0:T(8,128)} fusion(f32[2,256,128]{2,1,0:T(8,128)S(1)} %copy.116, s32[1024]{0:T(1024)S(1)} %pad_clamp_fusion.1), kind=kCustom, calls=%fused_computation.6 | custom fusion | bytes 4194368 | tf_op jit(solution)/shard_map/jit(_take)/gather | solution.py:163
  125.0 3.2 %gather_fusion.3 = f32[16,256,5,64]{1,3,2,0:T(8,128)} fusion(f32[2,256,5,64]{1,3,2,0:T(8,128)S(1)} %copy.123, s32[1024]{0:T(1024)S(1)} %pad_clamp_fusion.1), kind=kCustom, calls=%fused_computation.5 | custom fusion | bytes 10485824 | tf_op jit(solution)/shard_map/jit(_take)/gather | solution.py:162
  128.2 10.2 %add_select_fusion = bf16[16,5,64,128]{3,2,1,0:T(8,128)(2,1)} fusion(f32[16,5,64,128]{3,2,1,0:T(8,128)} %gather_fusion.1, f32[16,5]{1,0:T(8,128)S(1)} %exponential_multiply_fusion.1, pred[16]{0:T(512)(128)(4,1)S(1)} %compare_and_fusion.1, pred[16]{0:T(512)(128)(4,1)S(1)} %get-tuple-element.141, f32[16,256,128]{2,1,0:T(8,128)} %gather_fusion.4, ...), kind=kOutput, calls=%fused_computation.29 | convolution fusion | flops 2019033088 | bytes 11354464 | tf_op jit(solution)/shard_map/rjhp,rjn->rhpn/dot_general | solution.py:176
  138.4 2.1 %gather_fusion.5 = bf16[16,5,64,128]{3,2,1,0:T(8,128)(2,1)S(1)} fusion(bf16[16,5,64,128]{3,2,1,0:T(8,128)(2,1)} %add_select_fusion, s32[1024]{0:T(1024)S(1)} %pad_clamp_fusion), kind=kCustom, calls=%fused_computation.7 | custom fusion | bytes 2621504 | tf_op jit(solution)/shard_map/jit(_take)/gather | solution.py:190
  140.5 1.6 select_convert_fusion
  142.2 4.6 %all-to-all-start = ((bf16[16,5,64,128]{3,2,1,0:T(8,128)(2,1)}), bf16[16,5,64,128]{3,2,1,0:T(8,128)(2,1)S(1)}, u32[]{:S(2)}, u32[]{:S(2)}) async-start(bf16[16,5,64,128]{3,2,1,0:T(8,128)(2,1)} %select_convert_fusion), calls=%async_computation.1 | async-start | bytes 2621440 | tf_op jit(solution)/shard_map/all_to_all | solution.py:191
  146.8 0.6 dynamic-slice.13
  148.1 1.5 multiply_reduce_fusion
  149.6 38.3 %all-reduce.1 = f32[512]{0:T(512)S(1)} all-reduce(f32[512]{0:T(512)S(1)} %multiply_reduce_fusion), channel_id=4, replica_groups=mesh['seq'=8,'tensor'=16] {'tensor'}, use_global_device_ids=true, to_apply=%region_10.11.clone | all-reduce | flops 512 | bytes 4096
  188.0 1.0 convert_reduce_fusion
  188.9 1.7 multiply_convert_fusion.2
  (117 shorter events, 3.0 us)
Async XLA Ops:
  7.2 102.6 %copy-start = (bf16[320,2560]{1,0:T(8,128)(2,1)S(1)}, bf16[320,2560]{1,0:T(8,128)(2,1)}, u32[]{:S(2)}) copy-start(bf16[320,2560]{1,0:T(8,128)(2,1)} %param.38) | copy-start | bytes 4915204
  7.2 3.2 %copy-start.19 = (s32[16]{0:T(128)S(1)}, s32[16]{0:T(128)}, u32[]{:S(2)}) copy-start(s32[16]{0:T(128)} %param.39) | copy-start | bytes 196
  7.2 4.4 %copy-start.12 = (f32[4,256]{1,0:T(4,128)S(1)}, f32[4,256]{1,0:T(4,128)}, u32[]{:S(2)}) copy-start(f32[4,256]{1,0:T(4,128)} %param.32) | copy-start | bytes 12292
  7.2 4.4 %copy-start.11 = (f32[4,320]{1,0:T(4,128)S(1)}, f32[4,320]{1,0:T(4,128)}, u32[]{:S(2)}) copy-start(f32[4,320]{1,0:T(4,128)} %param.30) | copy-start | bytes 15364
  7.2 5.0 %copy-start.17 = (f32[256]{0:T(256)S(1)}, f32[256]{0:T(256)}, u32[]{:S(2)}) copy-start(f32[256]{0:T(256)} %param.33) | copy-start | bytes 3076
  7.2 4.9 %copy-start.13 = (f32[320]{0:T(512)S(1)}, f32[320]{0:T(512)}, u32[]{:S(2)}) copy-start(f32[320]{0:T(512)} %param.31) | copy-start | bytes 3844
  7.2 51.5 %copy-start.22 = (bf16[2560,5]{0,1:T(8,128)(2,1)S(1)}, bf16[2560,5]{0,1:T(8,128)(2,1)}, u32[]{:S(2)}) copy-start(bf16[2560,5]{0,1:T(8,128)(2,1)} %param.28) | copy-start | bytes 76804
  7.2 51.5 %all-gather.3.cloned.1.call-start = ((), (), s32[]{:S(2)}) async-start(), calls=%async_computation.2 | async-start | bytes 2785280 | tf_op jit(solution)/shard_map/all_gather | solution.py:50
  8.0 180.9 %reduce-scatter.2.cloned.1.call-start = ((), (), s32[]{:S(2)}) async-start(), calls=%async_computation.3 | async-start | bytes 2785280 | tf_op jit(solution)/shard_map/reduce_scatter | solution.py:147
  10.6 0.6 copy-start.14
  64.1 1.3 copy-start.6
  64.1 1.3 copy-start.18
  69.2 8.0 %collective-permute-start = (f32[3,576]{0,1:T(8,128)S(1)}, f32[3,576]{0,1:T(8,128)S(1)}, u32[]{:S(2)}, u32[]{:S(2)}) collective-permute-start(f32[3,576]{0,1:T(8,128)S(1)} %fusion.58), channel_id=1, source_target_pairs={{0,16},{16,32},{32,48},{48,64},{64,80},{80,96},{96,112},{1,17},{17... | collective-permute-start | bytes 20744 | tf_op jit(solution)/shard_map/ppermute | solution.py:16
  80.0 0.7 copy-start.4
  83.0 19.0 %copy-start.5 = (f32[512,128]{0,1:T(8,128)S(1)}, f32[512,128]{0,1:T(8,128)}, u32[]{:S(2)}) copy-start(f32[512,128]{0,1:T(8,128)} %get-tuple-element.123) | copy-start | bytes 786436
  100.8 0.9 copy-start.2
  103.5 3.6 %copy-start.3 = (bf16[40,80,128]{2,1,0:T(8,128)(2,1)S(1)}, bf16[40,80,128]{2,1,0:T(8,128)(2,1)}, u32[]{:S(2)}) copy-start(bf16[40,80,128]{2,1,0:T(8,128)(2,1)} %copy-done.2) | copy-start | bytes 2457604
  103.5 3.9 %copy-start.9 = (f32[2,5,64,128]{3,2,1,0:T(8,128)S(1)}, f32[2,5,64,128]{3,2,1,0:T(8,128)}, u32[]{:S(2)}) copy-start(f32[2,5,64,128]{3,2,1,0:T(8,128)} %get-tuple-element.67) | copy-start | bytes 983044
  103.5 3.9 %copy-start.16 = (f32[2,5]{1,0:T(2,128)S(1)}, f32[2,5]{1,0:T(2,128)}, u32[]{:S(2)}) copy-start(f32[2,5]{1,0:T(2,128)} %get-tuple-element.68) | copy-start | bytes 124
  103.6 4.0 %copy-start.8 = (f32[2,256,128]{1,0,2:T(2,128)S(1)}, f32[2,256,128]{1,0,2:T(2,128)}, u32[]{:S(2)}) copy-start(f32[2,256,128]{1,0,2:T(2,128)} %reshape.371) | copy-start | bytes 786436
  103.6 4.0 %copy-start.10 = (f32[2,256,5]{1,2,0:T(8,128)S(1)}, f32[2,256,5]{1,2,0:T(8,128)}, u32[]{:S(2)}) copy-start(f32[2,256,5]{1,2,0:T(8,128)} %get-tuple-element.127) | copy-start | bytes 30724
  103.6 4.0 %copy-start.21 = (f32[5]{0:T(128)S(1)}, f32[5]{0:T(128)}, u32[]{:S(2)}) copy-start(f32[5]{0:T(128)} %param.36) | copy-start | bytes 64
  108.3 1.5 copy-start.7
  108.3 1.5 copy-start.23
  108.9 0.8 copy-start.1
  113.1 0.7 copy-start.15
  113.1 0.7 copy-start.20
  113.1 2.6 %copy-start.24 = (s32[16]{0:T(128)S(1)}, s32[16]{0:T(128)}, u32[]{:S(2)}) copy-start(s32[16]{0:T(128)} %param.41) | copy-start | bytes 196
  142.2 4.6 %copy-start.25 = (u32[128]{0:T(128)S(1)}, u32[128]{0:T(128)}, u32[]{:S(2)}) copy-start(u32[128]{0:T(128)} %constant.274) | copy-start | bytes 1540
  142.2 45.8 %all-to-all-start = ((bf16[16,5,64,128]{3,2,1,0:T(8,128)(2,1)}), bf16[16,5,64,128]{3,2,1,0:T(8,128)(2,1)S(1)}, u32[]{:S(2)}, u32[]{:S(2)}) async-start(bf16[16,5,64,128]{3,2,1,0:T(8,128)(2,1)} %select_convert_fusion), calls=%async_computation.1 | async-start | bytes 2621440 | tf_op jit(solution)/shard_map/all_to_all | solution.py:191
Sparse Core Ops, SparseCore 0:
  10.2 48.5 all-gather.2
  113.2 75.1 reduce-scatter.1

commit v2 on v1

--- a/solution.py
+++ b/solution.py
@@ -46,8 +46,11 @@
     tensor_count = lax.axis_size("tensor")
     seq_count = lax.axis_size("seq")
     weight_all = jnp.concatenate([in_gate, in_x, in_dt, in_bc], axis=1)
+    gathered = lax.all_to_all(
+        jnp.tile(tokens, (lax.axis_size("tensor"), 1)), "tensor", 0, 0, tiled=True
+    )
     projected = jnp.dot(
-        lax.all_gather(tokens, "tensor", axis=0, tiled=True),
+        gathered,
         weight_all,
         preferred_element_type=jnp.float32,
     )
@@ -142,16 +145,19 @@
     )
     gated = output * jax.nn.silu(gate)
     squares = jnp.sum(gated * gated, axis=1)
-    totals = lax.psum_scatter(squares, "tensor", scatter_dimension=0, tiled=True)
+    totals = jnp.sum(
+        lax.all_to_all(squares, "tensor", 0, 0, tiled=True).reshape(tensor_count, -1), axis=0
+    )
     unscaled = (gated * norm_gain[None, :]).astype(jnp.bfloat16)
-    reduced = lax.psum_scatter(
-        jnp.dot(unscaled, out_weight, preferred_element_type=jnp.float32).astype(jnp.bfloat16),
-        "tensor",
-        scatter_dimension=0,
-        tiled=True,
+    partials = jnp.dot(unscaled, out_weight, preferred_element_type=jnp.float32).astype(
+        jnp.bfloat16
+    )
+    received_partials = lax.all_to_all(partials, "tensor", 0, 0, tiled=True)
+    reduced = jnp.sum(
+        received_partials.reshape(tensor_count, -1, partials.shape[1]).astype(jnp.float32), axis=0
     )
     scale = lax.rsqrt(totals[:, None] / (local_inner * tensor_count) + 1e-05)
-    mixed = (reduced.astype(jnp.float32) * scale).astype(jnp.bfloat16)
+    mixed = (reduced * scale).astype(jnp.bfloat16)
     request_count = lengths.shape[0]
     request_ids = jnp.arange(request_count, dtype=jnp.int32)
     ends = starts + lengths - 1 - DRAFTS + accepted

time: 198 us -> 208 us (1.051); the launches traced: 197 us -> 205 us
  blocking collectives: 51.8 us -> 13.6 us
  waiting for transfers between devices: 51.9 us -> 84.4 us
  starting transfers between devices: 6.64 us -> 25.5 us
  between operations: 15.3 us -> 1.23 us
  other arithmetic: 17.7 us -> 22.5 us
  matrix products: 25.4 us -> 28.7 us
    all_to_all x0 -> x3, waiting for transfers between devices: none -> 70.8 us  [the longest x1 37.9 us: per_device(): received_partials = lax.all_to_all(partials, 'tensor', 0, 0, tiled=True)]
    all_gather x1 -> x0, waiting for transfers between devices: 46 us -> none  [per_device(): lax.all_gather(tokens, 'tensor', axis=0, tiled=True)]
    unnamed x1 -> x0, blocking collectives: 38.3 us -> none
    all_to_all x0 -> x3, starting transfers between devices: none -> 19.1 us  [the longest x1 8.22 us: per_device(): lax.all_to_all(jnp.tile(tokens, (lax.axis_size('tensor'), 1)), 'tensor',...]
    all_to_all x1, waiting for transfers between devices: 0.01 us -> 12.2 us  [per_device(): lax.all_to_all(outgoing.astype(jnp.bfloat16), 'seq', split_axis=0, concat...]
    ppermute x1, waiting for transfers between devices: 5.21 us -> 1.48 us  [passed_along(): return lax.ppermute(block, axis, route)]
    another operation x10 -> x11, local copies, waits for them, and re-layouts: 0.57 us -> 3.39 us  [the longest x1 2.82 us: per_device(): jnp.tile(tokens, (lax.axis_size('tensor'), 1))]
    dynamic_update_slice x2, local copies, waits for them, and re-layouts: 2.53 us -> 0.08 us  [per_device(): lax.scan(advance, (empty, unit), (local, passes))]
  transfers between devices with their start and end apart: 4 -> 5, of which waited for: 2 -> 4; matrix products, arithmetic and copies ran while one was open for 19% -> 17% of each run, Pallas kernels for 0% -> 0%
where the time goes in v2:
time: 208 us; the launch traced here: 205 us
  waiting for transfers between devices  84.4 us (41%)
  local copies, waits for them, and re-layouts  29 us (14%)
  matrix products  28.7 us (14%)
  starting transfers between devices  25.5 us (12%)
  other arithmetic  22.5 us (11%)
  blocking collectives  13.6 us (7%)
    all_to_all x1, waiting for transfers between devices, per_device(): received_partials = lax.all_to_all(partials, 'tensor', 0, 0, tiled=True)  37.9 us
    all_to_all x1, waiting for transfers between devices, per_device(): lax.all_to_all(jnp.tile(tokens, (lax.axis_size('tensor'), 1)), 'tensor',...  32.9 us
    all_gather x1, blocking collectives, per_device(): lax.all_gather(jnp.concatenate([zero_end.astype(jnp.bfloat16), factor_row...  13.6 us
    all_to_all x1, waiting for transfers between devices, per_device(): lax.all_to_all(outgoing.astype(jnp.bfloat16), 'seq', split_axis=0, concat...  12.2 us
    dot_general x1, matrix products, per_device(): jnp.einsum('rjhp,rjn->rhpn', weight[..., None] * chosen_values, chosen_ke...  10.2 us
    all_to_all x1, starting transfers between devices, per_device(): lax.all_to_all(jnp.tile(tokens, (lax.axis_size('tensor'), 1)), 'tensor',...  8.22 us
    all_to_all x1, starting transfers between devices, per_device(): received_partials = lax.all_to_all(partials, 'tensor', 0, 0, tiled=True)  7.26 us
    dot_general x1, matrix products, per_device(): jnp.dot(gathered, weight_all, preferred_element_type=jnp.float32)  5.72 us
  transfers between devices with their start and end apart: 5, of which 4 were waited for; matrix products, arithmetic and copies ran while one was open for 17% of the time, Pallas kernels for 0%

profile of v2, /device:TPU:6, one launch (start us, length us, event | category | flops | bytes accessed | tf_op | source)
XLA Modules:
  0.0 205.0 jit_solution(13422055469096975392)
XLA Ops:
  0.6 2.8 %tile.2 = bf16[16,32,2560]{2,1,0:T(8,128)(2,1)} broadcast(bf16[32,2560]{1,0:T(8,128)(2,1)} %param.25), dimensions={1,2} | broadcast | bytes 2785280 | tf_op jit(solution)/shard_map/tile | solution.py:50
  3.5 8.2 %all-to-all-start = ((bf16[16,32,2560]{2,1,0:T(8,128)(2,1)}), bf16[16,32,2560]{2,1,0:T(8,128)(2,1)}, u32[]{:S(2)}, u32[]{:S(2)}) async-start(bf16[16,32,2560]{2,1,0:T(8,128)(2,1)} %tile.2), calls=%async_computation | async-start | bytes 5242880 | tf_op jit(solution)/shard_map/all_to_all | solution.py:49
  11.9 1.6 copy.114
  13.6 0.1 reduce.6
  13.9 0.2 convert_reduce_fusion.3
  14.1 0.2 fusion.76
  14.4 0.6 fusion.95
  15.1 1.3 compare_convert_fusion.2
  16.5 0.6 gather_fusion.2
  17.1 0.2 slice_reduce_fusion.1
  17.5 0.2 fusion.77
  18.0 0.8 compare_and_fusion
  18.8 32.9 %all-to-all-done = bf16[16,32,2560]{2,1,0:T(8,128)(2,1)} async-done(((bf16[16,32,2560]{2,1,0:T(8,128)(2,1)}), bf16[16,32,2560]{2,1,0:T(8,128)(2,1)}, u32[]{:S(2)}, u32[]{:S(2)}) %all-to-all-start) | async-done | bytes 2621472 | tf_op jit(solution)/shard_map/all_to_all | solution.py:49
  51.6 5.7 %fusion.26 = f32[512,901]{0,1:T(8,128)S(1)} fusion(bf16[512,2560]{1,0:T(8,128)(2,1)} %bitcast, bf16[2560,256]{0,1:T(8,128)(2,1)} %copy.114, bf16[2560,5]{0,1:T(8,128)(2,1)S(1)} %copy-done.17, bf16[2560,320]{0,1:T(8,128)(2,1)} %param.27, bf16[2560,320]{0,1:T(8,128)(2,1)} %param.26), kind=kOutput, calls=%fused_computation.43 | convolution fusion | flops 2380369920 | bytes 9079808 | tf_op jit(solution)/shard_map/dot_general | solution.py:52
  57.5 1.1 copy-done.4
  58.8 3.0 %reduce-window.20 = f32[2,5,2,128]{3,2,1,0:T(2,128)S(1)} reduce-window(f32[2,5,2,128]{3,2,1,0:T(2,128)S(1)} %copy.118, f32[]{:T(128)} %constant.231.clone.1), window={size=1x1x1x128 pad=0_0x0_0x0_0x127_0}, to_apply=%region_3.4 | reduce-window | flops 325120 | bytes 20484 | tf_op jit(solution)/shard_map/reduce-window.1
  62.2 0.2 slice_reduce_fusion
  62.4 0.6 gather_fusion.6
  63.0 0.9 fusion.58
  63.9 1.9 collective-permute-start
  65.9 2.0 copy.135
  67.9 0.6 gather_fusion.7
  68.4 1.3 gather_fusion
  69.8 0.8 fusion.64
  70.7 1.5 collective-permute-done
  72.2 1.4 maximum_maximum_fusion
  73.6 1.4 divide_multiply_fusion
  75.1 0.9 slice.243
  76.0 0.2 reshape.391
  76.2 0.1 copy.117
  76.3 0.9 reshape.390
  77.2 2.1 %gather_fusion.4 = f32[16,256,128]{2,1,0:T(8,128)} fusion(f32[2,256,128]{2,1,0:T(8,128)S(1)} %copy.117, s32[1024]{0:T(1024)S(1)} %pad_clamp_fusion.1), kind=kCustom, calls=%fused_computation.6 | custom fusion | bytes 4194368 | tf_op jit(solution)/shard_map/jit(_take)/gather | solution.py:169
  79.3 1.4 fusion.59
  80.7 1.5 reshape.389
  82.3 1.7 fusion.54
  84.0 1.7 while.19
  84.0 0.7 bitcast_dynamic-update-slice_fusion.2
  84.8 0.7 bitcast_dynamic-update-slice_fusion.2
  85.9 13.6 %all-gather = bf16[40,80,128]{2,1,0:T(8,128)(2,1)S(1)} all-gather(bf16[5,80,128]{2,1,0:T(8,128)(2,1)S(1)} %pad_maximum_fusion.1), channel_id=2, replica_groups=mesh['seq'=8,'tensor'=16] {'seq'}, dimensions={0}, use_global_device_ids=true | all-gather | bytes 921600 | tf_op jit(solution)/shard_map/all_gather | solution.py:124
  99.5 0.9 copy-done.2
  100.4 0.1 copy.148
  100.6 0.1 copy.147
  100.7 1.4 select_bitcast_fusion
  102.1 1.1 multiply_add_fusion
  103.2 2.2 %gather_fusion.1 = f32[16,5,64,128]{3,2,1,0:T(8,128)} fusion(f32[2,5,64,128]{3,2,1,0:T(8,128)S(1)} %multiply_add_fusion, s32[1024]{0:T(1024)S(1)} %pad_clamp_fusion.1), kind=kCustom, calls=%fused_computation.3 | custom fusion | bytes 5242944 | tf_op jit(solution)/shard_map/jit(_take)/gather | solution.py:191
  105.4 4.4 %fusion.35 = f32[2,256,5,64]{1,3,2,0:T(8,128)S(1)} fusion(f32[2,256,5]{1,2,0:T(8,128)S(1)} %bitcast.101, f32[2,256,5]{1,2,0:T(8,128)S(1)} %bitcast.98, f32[2,256,256]{2,1,0:T(8,128)} %fusion.59, pred[2,256,256]{2,1,0:T(8,128)(4,1)S(1)} %copy-done.8, f32[2,256,5,64]{1,0,3,2:T(2,128)S(1)} %reshape.389), kind=kOutput, calls=%fused_computation.54 | convolution fusion | flops 506593280 | bytes 1986560 | tf_op jit(solution)/shard_map/cijh,cjhp->cihp/dot_general | solution.py:97
  109.8 0.8 fusion.39
  110.6 0.5 copy.133
  111.2 0.9 copy-done.1
  112.0 1.3 multiply_reduce_fusion
  113.3 0.7 all_to_all.25
  114.0 3.6 %all-to-all-start.2 = ((f32[16,32,1]{1,2,0:T(1,128)}), f32[16,32,1]{1,2,0:T(1,128)S(1)}, u32[]{:S(2)}, u32[]{:S(2)}) async-start(f32[16,32,1]{1,2,0:T(1,128)} %bitcast.22), calls=%async_computation.2 | async-start | bytes 16384 | tf_op jit(solution)/shard_map/all_to_all | solution.py:149
  117.6 3.2 %gather_fusion.3 = f32[16,256,5,64]{1,3,2,0:T(8,128)} fusion(f32[2,256,5,64]{1,3,2,0:T(8,128)S(1)} %copy.124, s32[1024]{0:T(1024)S(1)} %pad_clamp_fusion.1), kind=kCustom, calls=%fused_computation.5 | custom fusion | bytes 10485824 | tf_op jit(solution)/shard_map/jit(_take)/gather | solution.py:168
  120.8 10.2 %add_select_fusion = bf16[16,5,64,128]{3,2,1,0:T(8,128)(2,1)} fusion(f32[16,5,64,128]{3,2,1,0:T(8,128)} %gather_fusion.1, f32[16,5]{1,0:T(8,128)S(1)} %exponential_multiply_fusion.1, pred[16]{0:T(512)(128)(4,1)S(1)} %compare_and_fusion.1, pred[16]{0:T(512)(128)(4,1)S(1)} %get-tuple-element.141, f32[16,256,128]{2,1,0:T(8,128)} %gather_fusion.4, ...), kind=kOutput, calls=%fused_computation.30 | convolution fusion | flops 2019033088 | bytes 11354464 | tf_op jit(solution)/shard_map/rjhp,rjn->rhpn/dot_general | solution.py:182
  131.1 2.1 %gather_fusion.5 = bf16[16,5,64,128]{3,2,1,0:T(8,128)(2,1)S(1)} fusion(bf16[16,5,64,128]{3,2,1,0:T(8,128)(2,1)} %add_select_fusion, s32[1024]{0:T(1024)S(1)} %pad_clamp_fusion), kind=kCustom, calls=%fused_computation.7 | custom fusion | bytes 2621504 | tf_op jit(solution)/shard_map/jit(_take)/gather | solution.py:196
  133.2 1.6 select_convert_fusion
  134.8 4.5 %all-to-all-start.3 = ((bf16[16,5,64,128]{3,2,1,0:T(8,128)(2,1)}), bf16[16,5,64,128]{3,2,1,0:T(8,128)(2,1)S(1)}, u32[]{:S(2)}, u32[]{:S(2)}) async-start(bf16[16,5,64,128]{3,2,1,0:T(8,128)(2,1)} %select_convert_fusion), calls=%async_computation.3 | async-start | bytes 2621440 | tf_op jit(solution)/shard_map/all_to_all | solution.py:197
  139.3 4.5 %convolution_convert_fusion = bf16[512,2560]{1,0:T(8,128)(2,1)} fusion(bf16[320,2560]{1,0:T(8,128)(2,1)S(1)} %copy-done, f32[320]{0:T(512)S(1)} %copy-done.18, f32[512,320]{0,1:T(8,128)} %bitcast.105, f32[512,901]{0,1:T(8,128)} %copy-done.4), kind=kOutput, calls=%fused_computation.27 | convolution fusion | flops 841318400 | bytes 5571840 | tf_op jit(solution)/shard_map/dot_general | solution.py:152
  143.8 12.2 %all-to-all-done.3 = bf16[16,5,64,128]{3,2,1,0:T(8,128)(2,1)S(1)} async-done(((bf16[16,5,64,128]{3,2,1,0:T(8,128)(2,1)}), bf16[16,5,64,128]{3,2,1,0:T(8,128)(2,1)S(1)}, u32[]{:S(2)}, u32[]{:S(2)}) %all-to-all-start.3) | async-done | bytes 1310752 | tf_op jit(solution)/shard_map/all_to_all | solution.py:197
  156.0 7.3 %all-to-all-start.1 = ((bf16[16,32,2560]{2,1,0:T(8,128)(2,1)}), bf16[16,32,2560]{2,1,0:T(8,128)(2,1)}, u32[]{:S(2)}, u32[]{:S(2)}) async-start(bf16[16,32,2560]{2,1,0:T(8,128)(2,1)} %bitcast.103), calls=%async_computation.1 | async-start | bytes 5242880 | tf_op jit(solution)/shard_map/all_to_all | solution.py:155
  163.3 1.0 convert_reduce_fusion.1
  164.2 37.9 %all-to-all-done.1 = bf16[16,32,2560]{2,1,0:T(8,128)(2,1)} async-done(((bf16[16,32,2560]{2,1,0:T(8,128)(2,1)}), bf16[16,32,2560]{2,1,0:T(8,128)(2,1)}, u32[]{:S(2)}, u32[]{:S(2)}) %all-to-all-start.1) | async-done | bytes 2621472 | tf_op jit(solution)/shard_map/all_to_all | solution.py:155
  202.1 2.2 %convert_reduce_fusion = f32[32,2560]{1,0:T(8,128)S(1)} fusion(bf16[16,32,2560]{2,1,0:T(8,128)(2,1)} %all-to-all-done.1), kind=kLoop, calls=%fused_computation.18 | loop fusion | flops 2539520 | bytes 2949120 | tf_op jit(solution)/shard_map/reduce_sum | solution.py:156
  204.3 0.8 multiply_convert_fusion.2
  (109 shorter events, 2.8 us)
Async XLA Ops:
  0.6 138.7 %copy-start = (bf16[320,2560]{1,0:T(8,128)(2,1)S(1)}, bf16[320,2560]{1,0:T(8,128)(2,1)}, u32[]{:S(2)}) copy-start(bf16[320,2560]{1,0:T(8,128)(2,1)} %param.38) | copy-start | bytes 4915204
  3.5 8.4 %copy-start.19 = (f32[5]{0:T(128)S(1)}, f32[5]{0:T(128)}, u32[]{:S(2)}) copy-start(f32[5]{0:T(128)} %param.35) | copy-start | bytes 64
  3.5 8.4 %copy-start.5 = (bf16[2560,256]{1,0:T(8,128)(2,1)S(1)}, bf16[2560,256]{1,0:T(8,128)(2,1)}, u32[]{:S(2)}) copy-start(bf16[2560,256]{1,0:T(8,128)(2,1)} %param.29) | copy-start | bytes 3932164
  3.5 48.2 %all-to-all-start = ((bf16[16,32,2560]{2,1,0:T(8,128)(2,1)}), bf16[16,32,2560]{2,1,0:T(8,128)(2,1)}, u32[]{:S(2)}, u32[]{:S(2)}) async-start(bf16[16,32,2560]{2,1,0:T(8,128)(2,1)} %tile.2), calls=%async_computation | async-start | bytes 5242880 | tf_op jit(solution)/shard_map/all_to_all | solution.py:49
  11.7 1.8 copy-start.14
  11.7 3.4 %copy-start.15 = (s32[16]{0:T(128)S(1)}, s32[16]{0:T(128)}, u32[]{:S(2)}) copy-start(s32[16]{0:T(128)} %param.40) | copy-start | bytes 196
  11.7 4.6 %copy-start.9 = (f32[4,320]{1,0:T(4,128)S(1)}, f32[4,320]{1,0:T(4,128)}, u32[]{:S(2)}) copy-start(f32[4,320]{1,0:T(4,128)} %param.30) | copy-start | bytes 15364
  11.7 4.6 %copy-start.10 = (f32[4,256]{1,0:T(4,128)S(1)}, f32[4,256]{1,0:T(4,128)}, u32[]{:S(2)}) copy-start(f32[4,256]{1,0:T(4,128)} %param.32) | copy-start | bytes 12292
  11.8 5.5 %copy-start.20 = (s32[16]{0:T(128)S(1)}, s32[16]{0:T(128)}, u32[]{:S(2)}) copy-start(s32[16]{0:T(128)} %param.41) | copy-start | bytes 196
  11.8 5.6 %copy-start.11 = (f32[320]{0:T(512)S(1)}, f32[320]{0:T(512)}, u32[]{:S(2)}) copy-start(f32[320]{0:T(512)} %param.31) | copy-start | bytes 3844
  11.8 5.6 %copy-start.12 = (f32[256]{0:T(256)S(1)}, f32[256]{0:T(256)}, u32[]{:S(2)}) copy-start(f32[256]{0:T(256)} %param.33) | copy-start | bytes 3076
  11.8 39.9 %copy-start.17 = (bf16[2560,5]{0,1:T(8,128)(2,1)S(1)}, bf16[2560,5]{0,1:T(8,128)(2,1)}, u32[]{:S(2)}) copy-start(bf16[2560,5]{0,1:T(8,128)(2,1)} %param.28) | copy-start | bytes 76804
  57.4 1.2 copy-start.4
  57.4 1.2 copy-start.13
  63.9 8.3 %collective-permute-start = (f32[3,576]{0,1:T(8,128)}, f32[3,576]{0,1:T(8,128)}, u32[]{:S(2)}, u32[]{:S(2)}) collective-permute-start(f32[3,576]{0,1:T(8,128)} %fusion.58), channel_id=1, source_target_pairs={{0,16},{16,32},{32,48},{48,64},{64,80},{80,96},{96,112},{1,17},{17... | collective-permute-start | bytes 20744 | tf_op jit(solution)/shard_map/ppermute | solution.py:16
  76.1 3.1 %copy-start.3 = (f32[2,256,128]{1,0,2:T(2,128)}, f32[2,256,128]{1,0,2:T(2,128)S(1)}, u32[]{:S(2)}) copy-start(f32[2,256,128]{1,0,2:T(2,128)S(1)} %reshape.391) | copy-start | bytes 786436
  99.5 0.9 copy-start.2
  103.2 2.2 %copy-start.8 = (pred[2,256,256]{2,1,0:T(8,128)(4,1)S(1)}, pred[2,256,256]{2,1,0:T(8,128)(4,1)}, u32[]{:S(2)}) copy-start(pred[2,256,256]{2,1,0:T(8,128)(4,1)} %compare_and_fusion) | copy-start | bytes 393220
  105.4 4.4 %copy-start.6 = (f32[2,256,128]{1,0,2:T(2,128)S(1)}, f32[2,256,128]{1,0,2:T(2,128)}, u32[]{:S(2)}) copy-start(f32[2,256,128]{1,0,2:T(2,128)} %reshape.390) | copy-start | bytes 786436
  105.4 4.4 %copy-start.16 = (f32[5]{0:T(128)S(1)}, f32[5]{0:T(128)}, u32[]{:S(2)}) copy-start(f32[5]{0:T(128)} %param.36) | copy-start | bytes 64
  111.2 0.9 copy-start.1
  114.0 20.7 %all-to-all-start.2 = ((f32[16,32,1]{1,2,0:T(1,128)}), f32[16,32,1]{1,2,0:T(1,128)S(1)}, u32[]{:S(2)}, u32[]{:S(2)}) async-start(f32[16,32,1]{1,2,0:T(1,128)} %bitcast.22), calls=%async_computation.2 | async-start | bytes 16384 | tf_op jit(solution)/shard_map/all_to_all | solution.py:149
  117.6 3.2 %copy-start.7 = (f32[16,256,5]{1,2,0:T(8,128)S(1)}, f32[16,256,5]{1,2,0:T(8,128)}, u32[]{:S(2)}) copy-start(f32[16,256,5]{1,2,0:T(8,128)} %fusion.64) | copy-start | bytes 245764
  133.2 6.1 %copy-start.18 = (f32[320]{0:T(512)S(1)}, f32[320]{0:T(512)}, u32[]{:S(2)}) copy-start(f32[320]{0:T(512)} %param.37) | copy-start | bytes 3844
  134.8 21.2 %all-to-all-start.3 = ((bf16[16,5,64,128]{3,2,1,0:T(8,128)(2,1)}), bf16[16,5,64,128]{3,2,1,0:T(8,128)(2,1)S(1)}, u32[]{:S(2)}, u32[]{:S(2)}) async-start(bf16[16,5,64,128]{3,2,1,0:T(8,128)(2,1)} %select_convert_fusion), calls=%async_computation.3 | async-start | bytes 2621440 | tf_op jit(solution)/shard_map/all_to_all | solution.py:197
  156.0 46.2 %all-to-all-start.1 = ((bf16[16,32,2560]{2,1,0:T(8,128)(2,1)}), bf16[16,32,2560]{2,1,0:T(8,128)(2,1)}, u32[]{:S(2)}, u32[]{:S(2)}) async-start(bf16[16,32,2560]{2,1,0:T(8,128)(2,1)} %bitcast.103), calls=%async_computation.1 | async-start | bytes 5242880 | tf_op jit(solution)/shard_map/all_to_all | solution.py:155

commit v3 on v2

--- a/solution.py
+++ b/solution.py
@@ -121,9 +121,8 @@
     factor_rows = jnp.zeros((local_heads, 16, state_size), jnp.bfloat16)
     factor_rows = factor_rows.at[:, 0, :].set(factor_high[:, None])
     factor_rows = factor_rows.at[:, 1, :].set(factor_low[:, None])
-    sent = lax.all_gather(
-        jnp.concatenate([zero_end.astype(jnp.bfloat16), factor_rows], axis=1), "seq", axis=0
-    )
+    packed = jnp.concatenate([zero_end.astype(jnp.bfloat16), factor_rows], axis=1)
+    sent = lax.all_to_all(jnp.tile(packed[None], (seq_count, 1, 1, 1)), "seq", 0, 0, tiled=True)
     sent_states = sent[:, :, :head_size]
     sent_factors = sent[:, :, head_size, 0].astype(jnp.float32) + sent[
         :, :, head_size + 1, 0
@@ -145,16 +144,23 @@
     )
     gated = output * jax.nn.silu(gate)
     squares = jnp.sum(gated * gated, axis=1)
-    totals = jnp.sum(
-        lax.all_to_all(squares, "tensor", 0, 0, tiled=True).reshape(tensor_count, -1), axis=0
-    )
     unscaled = (gated * norm_gain[None, :]).astype(jnp.bfloat16)
     partials = jnp.dot(unscaled, out_weight, preferred_element_type=jnp.float32).astype(
         jnp.bfloat16
     )
-    received_partials = lax.all_to_all(partials, "tensor", 0, 0, tiled=True)
-    reduced = jnp.sum(
-        received_partials.reshape(tensor_count, -1, partials.shape[1]).astype(jnp.float32), axis=0
+    squares_high = squares.astype(jnp.bfloat16)
+    squares_low = (squares - squares_high.astype(jnp.float32)).astype(jnp.bfloat16)
+    square_columns = jnp.zeros((row_count, 128), jnp.bfloat16)
+    square_columns = square_columns.at[:, 0].set(squares_high).at[:, 1].set(squares_low)
+    width = partials.shape[1]
+    received_partials = lax.all_to_all(
+        jnp.concatenate([partials, square_columns], axis=1), "tensor", 0, 0, tiled=True
+    ).reshape(tensor_count, -1, width + 128)
+    reduced = jnp.sum(received_partials[:, :, :width].astype(jnp.float32), axis=0)
+    totals = jnp.sum(
+        received_partials[:, :, width].astype(jnp.float32)
+        + received_partials[:, :, width + 1].astype(jnp.float32),
+        axis=0,
     )
     scale = lax.rsqrt(totals[:, None] / (local_inner * tensor_count) + 1e-05)
     mixed = (reduced * scale).astype(jnp.bfloat16)
@@ -188,7 +194,9 @@
     carried = (
         jnp.exp(end_sums) * (jnp.take(prior, which) == request_ids).astype(jnp.float32)[:, None]
     )
-    end_states = carried[:, :, None, None] * jnp.take(block_states, which, axis=0) + part
+    bracket = carried[:, :, None, None] * jnp.take(zero_starts, which, axis=0) + part
+    coefficient = carried * jnp.take(factors, which, axis=0)
+    end_states = bracket + coefficient[:, :, None, None] * incoming[None]
     end_states = jnp.where(present[:, None, None, None], end_states, 0.0)
     inverse = jnp.sum(
         (slots[None, :] == request_ids[:, None]).astype(jnp.int32) * request_ids[None, :], axis=1

time: 208 us -> 196 us (0.942)
  blocking collectives: 13.6 us -> 0 us
  other arithmetic: 22.5 us -> 30.4 us
  waiting for transfers between devices: 84.4 us -> 78.7 us
  local copies, waits for them, and re-layouts: 29 us -> 31.3 us
    all_gather x1 -> x0, blocking collectives: 13.6 us -> none  [per_device(): lax.all_gather(jnp.concatenate([zero_end.astype(jnp.bfloat16), factor_row...]
    all_to_all x1, waiting for transfers between devices: 32.9 us -> 28.2 us  [per_device(): lax.all_to_all(jnp.tile(tokens, (lax.axis_size('tensor'), 1)), 'tensor',...]
    all_to_all x1, waiting for transfers between devices: 12.2 us -> 8.26 us  [per_device(): lax.all_to_all(outgoing.astype(jnp.bfloat16), 'seq', split_axis=0, concat...]
    all_to_all x2, waiting for transfers between devices: 37.9 us -> 40.8 us  [the longest x1 40.8 us: per_device(): lax.all_to_all(jnp.concatenate([partials, square_columns], axis=1), 'tens...]
    another operation x6 -> x9, other arithmetic: 3.31 us -> 6.04 us
    unnamed x46 -> x60, local copies, waits for them, and re-layouts: 4.86 us -> 3.7 us
  transfers between devices with their start and end apart: 5 -> 5, of which waited for: 4 -> 4; matrix products, arithmetic and copies ran while one was open for 17% -> 20% of each run, Pallas kernels for 0% -> 0%
where the time goes in v3:
time: 196 us; the launch traced here: 193 us
  waiting for transfers between devices  78.7 us (40%)
  local copies, waits for them, and re-layouts  31.3 us (16%)
  other arithmetic  30.4 us (16%)
  matrix products  27.3 us (14%)
  starting transfers between devices  24.3 us (12%)
    all_to_all x1, waiting for transfers between devices, per_device(): lax.all_to_all(jnp.concatenate([partials, square_columns], axis=1), 'tens...  40.8 us
    all_to_all x1, waiting for transfers between devices, per_device(): lax.all_to_all(jnp.tile(tokens, (lax.axis_size('tensor'), 1)), 'tensor',...  28.2 us
    dot_general x1, matrix products, per_device(): jnp.einsum('rjhp,rjn->rhpn', weight[..., None] * chosen_values, chosen_ke...  8.83 us
    all_to_all x1, waiting for transfers between devices, per_device(): lax.all_to_all(outgoing.astype(jnp.bfloat16), 'seq', split_axis=0, concat...  8.26 us
    all_to_all x1, starting transfers between devices, per_device(): lax.all_to_all(jnp.tile(tokens, (lax.axis_size('tensor'), 1)), 'tensor',...  8.22 us
    another operation x9, other arithmetic  6.04 us
    dot_general x1, matrix products, per_device(): jnp.dot(gathered, weight_all, preferred_element_type=jnp.float32)  5.73 us
    dot_general x1, matrix products, per_device(): jnp.einsum('cijh,cjhp->cihp', mixing, values, precision=HIGHEST_PRECISION)  5.16 us
  transfers between devices with their start and end apart: 5, of which 4 were waited for; matrix products, arithmetic and copies ran while one was open for 20% of the time, Pallas kernels for 0%

profile of v3, /device:TPU:6, one launch (start us, length us, event | category | flops | bytes accessed | tf_op | source)
XLA Modules:
  0.0 193.3 jit_solution(8114657980153804007)
XLA Ops:
  0.6 2.8 %tile.4 = bf16[16,32,2560]{2,1,0:T(8,128)(2,1)} broadcast(bf16[32,2560]{1,0:T(8,128)(2,1)} %param.29), dimensions={1,2} | broadcast | bytes 2785280 | tf_op jit(solution)/shard_map/tile | solution.py:50
  3.5 8.2 %all-to-all-start = ((bf16[16,32,2560]{2,1,0:T(8,128)(2,1)}), bf16[16,32,2560]{2,1,0:T(8,128)(2,1)}, u32[]{:S(2)}, u32[]{:S(2)}) async-start(bf16[16,32,2560]{2,1,0:T(8,128)(2,1)} %tile.4), calls=%async_computation | async-start | bytes 5242880 | tf_op jit(solution)/shard_map/all_to_all | solution.py:49
  11.9 0.7 compare_reduce_fusion
  12.6 0.7 compare_reduce_fusion.1
  13.3 1.6 copy.144
  15.8 0.6 fusion.100
  16.4 1.9 compare_convert_fusion.2
  18.4 0.6 gather_fusion.2
  18.9 0.2 slice_reduce_fusion.7
  19.2 0.6 pad_clamp_fusion
  19.9 0.7 fusion.84
  20.6 0.6 compare_and_fusion.3
  21.2 0.6 compare_convert_fusion.1
  21.8 0.7 fusion.80
  22.6 0.8 compare_and_fusion
  23.4 28.2 %all-to-all-done = bf16[16,32,2560]{2,1,0:T(8,128)(2,1)} async-done(((bf16[16,32,2560]{2,1,0:T(8,128)(2,1)}), bf16[16,32,2560]{2,1,0:T(8,128)(2,1)}, u32[]{:S(2)}, u32[]{:S(2)}) %all-to-all-start) | async-done | bytes 2621472 | tf_op jit(solution)/shard_map/all_to_all | solution.py:49
  51.6 5.7 %fusion.26 = f32[512,901]{0,1:T(8,128)S(1)} fusion(bf16[512,2560]{1,0:T(8,128)(2,1)} %bitcast, bf16[2560,256]{0,1:T(8,128)(2,1)} %copy.144, bf16[2560,5]{0,1:T(8,128)(2,1)} %param.32, bf16[2560,320]{0,1:T(8,128)(2,1)} %param.31, bf16[2560,320]{0,1:T(8,128)(2,1)} %param.30), kind=kOutput, calls=%fused_computation.45 | convolution fusion | flops 2380369920 | bytes 9079808 | tf_op jit(solution)/shard_map/dot_general | solution.py:52
  57.5 1.1 copy-done.7
  58.8 3.0 %reduce-window.20 = f32[2,5,2,128]{3,2,1,0:T(2,128)S(1)} reduce-window(f32[2,5,2,128]{3,2,1,0:T(2,128)S(1)} %copy.148, f32[]{:T(128)} %constant.292.clone.1), window={size=1x1x1x128 pad=0_0x0_0x0_0x127_0}, to_apply=%region_3.4 | reduce-window | flops 325120 | bytes 20484 | tf_op jit(solution)/shard_map/reduce-window.1
  62.4 0.6 gather_fusion.7
  63.0 0.9 fusion.60
  63.8 1.9 collective-permute-start
  65.9 2.0 %copy.164 = f32[16,256,5]{2,1,0:T(8,128)} copy(f32[16,256,5]{1,2,0:T(8,128)S(1)} %broadcast_select_fusion.2) | data formatting | bytes 163840 | tf_op jit(solution)/shard_map/jit(_take)/select_n | solution.py:176
  67.8 0.6 gather_fusion.8
  68.4 1.3 gather_fusion
  69.8 0.8 fusion.69
  70.7 1.4 collective-permute-done
  72.1 1.5 maximum_maximum_fusion
  73.6 1.4 divide_multiply_fusion
  75.0 0.7 fusion.99
  76.1 1.3 reshape.488
  77.4 1.1 copy.154
  78.5 1.9 fusion.54
  80.4 0.4 while.21
  80.8 1.8 reshape.489
  82.9 1.0 tile.5
  83.9 4.8 %all-to-all-start.1 = ((bf16[8,5,80,128]{3,2,1,0:T(8,128)(2,1)}), bf16[8,5,80,128]{3,2,1,0:T(8,128)(2,1)}, u32[]{:S(2)}, u32[]{:S(2)}) async-start(bf16[8,5,80,128]{3,2,1,0:T(8,128)(2,1)} %tile.5), calls=%async_computation.1 | async-start | bytes 1638400 | tf_op jit(solution)/shard_map/all_to_all | solution.py:125
  88.7 2.2 %gather_fusion.1 = f32[16,5,64,128]{3,2,1,0:T(8,128)} fusion(f32[2,5,64,128]{3,2,1,0:T(8,128)S(1)} %get-tuple-element.91, s32[1024]{0:T(1024)S(1)} %pad_clamp_fusion.1), kind=kCustom, calls=%fused_computation.3 | custom fusion | bytes 5242944 | tf_op jit(solution)/shard_map/jit(_take)/gather | solution.py:197
  90.9 0.6 gather_fusion.5
  91.5 2.1 %gather_fusion.4 = f32[16,256,128]{2,1,0:T(8,128)} fusion(f32[2,256,128]{2,1,0:T(8,128)S(1)} %copy.147, s32[1024]{0:T(1024)S(1)} %pad_clamp_fusion.1), kind=kCustom, calls=%fused_computation.6 | custom fusion | bytes 4194368 | tf_op jit(solution)/shard_map/jit(_take)/gather | solution.py:175
  93.6 3.2 %gather_fusion.3 = f32[16,256,5,64]{1,3,2,0:T(8,128)} fusion(f32[2,256,5,64]{1,3,2,0:T(8,128)S(1)} %copy.154, s32[1024]{0:T(1024)S(1)} %pad_clamp_fusion.1), kind=kCustom, calls=%fused_computation.5 | custom fusion | bytes 10485824 | tf_op jit(solution)/shard_map/jit(_take)/gather | solution.py:174
  96.8 0.6 fusion.61
  97.5 5.2 %fusion.39 = f32[2,256,5,64]{1,3,2,0:T(8,128)} fusion(f32[2,256,5]{1,2,0:T(8,128)S(1)} %bitcast.85, f32[2,256,5]{1,2,0:T(8,128)S(1)} %bitcast.82, f32[2,256,256]{2,1,0:T(8,128)S(1)} %fusion.61, pred[2,256,256]{2,1,0:T(8,128)(4,1)S(1)} %copy-done.9, f32[2,256,5,64]{1,0,3,2:T(2,128)} %reshape.488), kind=kOutput, calls=%fused_computation.56 | convolution fusion | flops 506593280 | bytes 1986560 | tf_op jit(solution)/shard_map/cijh,cjhp->cihp/dot_general | solution.py:97
  102.7 1.0 fusion.70
  103.8 1.4 select_bitcast_fusion
  105.3 2.1 %fusion.43 = f32[2,256,5,64]{1,3,2,0:T(8,128)S(1)} fusion(f32[2,256,5,64]{1,3,2,0:T(8,128)} %fusion.39, f32[5]{0:T(128)S(1)} %copy-done.24, f32[2,5,64,128]{3,2,1,0:T(8,128)S(1)} %get-tuple-element.91, f32[2,256,5]{1,2,0:T(8,128)S(1)} %get-tuple-element.160, f32[2,256,128,1]{1,0,2,3:T(2,128)} %bitcast.93, f32[5,64,128]{2,1,0:T(8,128)S(1)} %select_bitcast_fusion, ...), kind=kOutput, calls=%fused_computation.59 | convolution fusion | flops 252477440 | bytes 2730044 | tf_op jit(solution)/shard_map/cin,chpn->cihp/dot_general | solution.py:139
  107.4 0.5 copy.161
  107.9 0.9 copy.177
  108.8 8.8 %add_select_fusion = bf16[16,5,64,128]{3,2,1,0:T(8,128)(2,1)} fusion(f32[16,5,64,128]{3,2,1,0:T(8,128)} %gather_fusion.1, f32[5,64,128]{2,1,0:T(8,128)S(1)} %select_bitcast_fusion, f32[16,5]{1,0:T(8,128)S(1)} %get-tuple-element.146, f32[16,5]{1,0:T(8,128)S(1)} %get-tuple-element.147, pred[16]{0:T(512)(128)(4,1)S(1)} %compare_and_fusion.1, ...), kind=kOutput, calls=%fused_computation.32 | convolution fusion | flops 2020343808 | bytes 11518624 | tf_op jit(solution)/shard_map/rjhp,rjn->rhpn/dot_general | solution.py:188
  117.6 2.2 %gather_fusion.6 = bf16[16,5,64,128]{3,2,1,0:T(8,128)(2,1)S(1)} fusion(bf16[16,5,64,128]{3,2,1,0:T(8,128)(2,1)} %add_select_fusion, s32[1024]{0:T(1024)} %pad_clamp_fusion), kind=kCustom, calls=%fused_computation.8 | custom fusion | bytes 2621504 | tf_op jit(solution)/shard_map/jit(_take)/gather | solution.py:204
  119.9 1.5 select_convert_fusion
  121.4 4.9 %all-to-all-start.3 = ((bf16[16,5,64,128]{3,2,1,0:T(8,128)(2,1)}), bf16[16,5,64,128]{3,2,1,0:T(8,128)(2,1)S(1)}, u32[]{:S(2)}, u32[]{:S(2)}) async-start(bf16[16,5,64,128]{3,2,1,0:T(8,128)(2,1)} %select_convert_fusion), calls=%async_computation.3 | async-start | bytes 2621440 | tf_op jit(solution)/shard_map/all_to_all | solution.py:205
  126.3 1.5 multiply_reduce_fusion
  128.0 1.3 fusion.68
  129.4 0.6 scatter.19
  130.0 3.0 %convolution_convert_fusion = bf16[512,2560]{1,0:T(8,128)(2,1)S(1)} fusion(bf16[320,2560]{1,0:T(8,128)(2,1)S(1)} %copy-done, f32[320]{0:T(512)S(1)} %copy-done.26, f32[512,320]{0,1:T(8,128)} %bitcast.89, f32[512,901]{0,1:T(8,128)} %copy-done.7), kind=kOutput, calls=%fused_computation.28 | convolution fusion | flops 841318400 | bytes 5571840 | tf_op jit(solution)/shard_map/dot_general | solution.py:148
  133.0 1.8 pad_maximum_fusion
  134.7 8.3 %all-to-all-done.3 = bf16[16,5,64,128]{3,2,1,0:T(8,128)(2,1)S(1)} async-done(((bf16[16,5,64,128]{3,2,1,0:T(8,128)(2,1)}), bf16[16,5,64,128]{3,2,1,0:T(8,128)(2,1)S(1)}, u32[]{:S(2)}, u32[]{:S(2)}) %all-to-all-start.3) | async-done | bytes 1310752 | tf_op jit(solution)/shard_map/all_to_all | solution.py:205
  143.0 4.5 %all-to-all-start.2 = ((bf16[16,32,2688]{2,1,0:T(8,128)(2,1)}), bf16[16,32,2688]{2,1,0:T(8,128)(2,1)}, u32[]{:S(2)}, u32[]{:S(2)}) async-start(bf16[16,32,2688]{2,1,0:T(8,128)(2,1)} %bitcast.86), calls=%async_computation.2 | async-start | bytes 5505024 | tf_op jit(solution)/shard_map/all_to_all | solution.py:156
  147.5 0.9 convert_reduce_fusion.1
  148.4 40.8 %all-to-all-done.2 = bf16[16,32,2688]{2,1,0:T(8,128)(2,1)} async-done(((bf16[16,32,2688]{2,1,0:T(8,128)(2,1)}), bf16[16,32,2688]{2,1,0:T(8,128)(2,1)}, u32[]{:S(2)}, u32[]{:S(2)}) %all-to-all-start.2) | async-done | bytes 2752544 | tf_op jit(solution)/shard_map/all_to_all | solution.py:156
  189.2 1.2 add_reduce_fusion
  190.4 2.2 %convert_reduce_fusion = f32[32,2560]{1,0:T(8,128)S(1)} fusion(bf16[16,32,2688]{2,1,0:T(8,128)(2,1)} %all-to-all-done.2), kind=kLoop, calls=%fused_computation.19 | loop fusion | flops 2539520 | bytes 2949120 | tf_op jit(solution)/shard_map/reduce_sum | solution.py:159
  192.6 0.8 multiply_convert_fusion.2
  (128 shorter events, 3.8 us)
Async XLA Ops:
  0.6 129.4 %copy-start = (bf16[320,2560]{1,0:T(8,128)(2,1)S(1)}, bf16[320,2560]{1,0:T(8,128)(2,1)}, u32[]{:S(2)}) copy-start(bf16[320,2560]{1,0:T(8,128)(2,1)} %param.42) | copy-start | bytes 4915204
  3.5 9.8 %copy-start.27 = (f32[5]{0:T(128)S(1)}, f32[5]{0:T(128)}, u32[]{:S(2)}) copy-start(f32[5]{0:T(128)} %param.39) | copy-start | bytes 64
  3.5 9.8 %copy-start.8 = (bf16[2560,256]{1,0:T(8,128)(2,1)S(1)}, bf16[2560,256]{1,0:T(8,128)(2,1)}, u32[]{:S(2)}) copy-start(bf16[2560,256]{1,0:T(8,128)(2,1)} %param.33) | copy-start | bytes 3932164
  3.5 48.2 %all-to-all-start = ((bf16[16,32,2560]{2,1,0:T(8,128)(2,1)}), bf16[16,32,2560]{2,1,0:T(8,128)(2,1)}, u32[]{:S(2)}, u32[]{:S(2)}) async-start(bf16[16,32,2560]{2,1,0:T(8,128)(2,1)} %tile.4), calls=%async_computation | async-start | bytes 5242880 | tf_op jit(solution)/shard_map/all_to_all | solution.py:49
  11.7 3.1 %copy-start.21 = (s32[16]{0:T(128)S(1)}, s32[16]{0:T(128)}, u32[]{:S(2)}) copy-start(s32[16]{0:T(128)} %param.43) | copy-start | bytes 196
  11.7 4.6 %copy-start.22 = (s32[16]{0:T(128)S(1)}, s32[16]{0:T(128)}, u32[]{:S(2)}) copy-start(s32[16]{0:T(128)} %param.44) | copy-start | bytes 196
  11.7 6.5 %copy-start.14 = (f32[4,320]{1,0:T(4,128)S(1)}, f32[4,320]{1,0:T(4,128)}, u32[]{:S(2)}) copy-start(f32[4,320]{1,0:T(4,128)} %param.34) | copy-start | bytes 15364
  11.7 6.5 %copy-start.15 = (f32[4,256]{1,0:T(4,128)S(1)}, f32[4,256]{1,0:T(4,128)}, u32[]{:S(2)}) copy-start(f32[4,256]{1,0:T(4,128)} %param.36) | copy-start | bytes 12292
  11.8 7.4 %copy-start.28 = (s32[16]{0:T(128)S(1)}, s32[16]{0:T(128)}, u32[]{:S(2)}) copy-start(s32[16]{0:T(128)} %param.45) | copy-start | bytes 196
  11.8 8.1 %copy-start.17 = (f32[320]{0:T(512)S(1)}, f32[320]{0:T(512)}, u32[]{:S(2)}) copy-start(f32[320]{0:T(512)} %param.35) | copy-start | bytes 3844
  11.8 8.1 %copy-start.19 = (f32[256]{0:T(256)S(1)}, f32[256]{0:T(256)}, u32[]{:S(2)}) copy-start(f32[256]{0:T(256)} %param.37) | copy-start | bytes 3076
  57.4 1.2 copy-start.7
  57.4 1.2 copy-start.20
  57.5 5.5 %copy-start.3 = (f32[512,256]{0,1:T(8,128)}, f32[512,256]{0,1:T(8,128)S(1)}, u32[]{:S(2)}) copy-start(f32[512,256]{0,1:T(8,128)S(1)} %slice.276) | copy-start | bytes 1572868
  63.8 8.2 %collective-permute-start = (f32[3,576]{0,1:T(8,128)}, f32[3,576]{0,1:T(8,128)S(1)}, u32[]{:S(2)}, u32[]{:S(2)}) collective-permute-start(f32[3,576]{0,1:T(8,128)} %fusion.60), channel_id=1, source_target_pairs={{0,16},{16,32},{32,48},{48,64},{64,80},{80,96},{96,112},{1,17},{17... | collective-permute-start | bytes 20744 | tf_op jit(solution)/shard_map/ppermute | solution.py:16
  67.8 1.9 copy-start.12
  67.8 1.9 copy-start.13
  67.8 2.8 %copy-start.18 = (f32[2]{0:T(128)S(1)}, f32[2]{0:T(128)}, u32[]{:S(2)}) copy-start(f32[2]{0:T(128)} %fusion.84) | copy-start | bytes 28
  68.4 5.2 %copy-start.11 = (f32[512]{0:T(512)S(1)}, f32[512]{0:T(512)}, u32[]{:S(2)}) copy-start(f32[512]{0:T(512)} %get-tuple-element.164) | copy-start | bytes 6148
  69.7 3.9 %copy-start.4 = (f32[512,256]{0,1:T(8,128)S(1)}, f32[512,256]{0,1:T(8,128)}, u32[]{:S(2)}) copy-start(f32[512,256]{0,1:T(8,128)} %copy-done.3) | copy-start | bytes 1572868
  76.0 2.6 %copy-start.5 = (f32[2,256,128]{1,0,2:T(2,128)}, f32[2,256,128]{1,0,2:T(2,128)S(1)}, u32[]{:S(2)}) copy-start(f32[2,256,128]{1,0,2:T(2,128)S(1)} %reshape.490) | copy-start | bytes 786436
  83.9 18.7 %all-to-all-start.1 = ((bf16[8,5,80,128]{3,2,1,0:T(8,128)(2,1)}), bf16[8,5,80,128]{3,2,1,0:T(8,128)(2,1)}, u32[]{:S(2)}, u32[]{:S(2)}) async-start(bf16[8,5,80,128]{3,2,1,0:T(8,128)(2,1)} %tile.5), calls=%async_computation.1 | async-start | bytes 1638400 | tf_op jit(solution)/shard_map/all_to_all | solution.py:125
  93.6 3.2 %copy-start.16 = (f32[16]{0:T(128)S(1)}, f32[16]{0:T(128)}, u32[]{:S(2)}) copy-start(f32[16]{0:T(128)} %get-tuple-element.148) | copy-start | bytes 196
  93.6 3.3 %copy-start.6 = (f32[512,128]{0,1:T(8,128)S(1)}, f32[512,128]{0,1:T(8,128)}, u32[]{:S(2)}) copy-start(f32[512,128]{0,1:T(8,128)} %get-tuple-element.156) | copy-start | bytes 786436
  93.6 3.9 %copy-start.9 = (pred[2,256,256]{2,1,0:T(8,128)(4,1)S(1)}, pred[2,256,256]{2,1,0:T(8,128)(4,1)}, u32[]{:S(2)}) copy-start(pred[2,256,256]{2,1,0:T(8,128)(4,1)} %compare_and_fusion) | copy-start | bytes 393220
  97.5 7.7 %copy-start.2 = (f32[2,256,5,64]{1,0,3,2:T(2,128)S(1)}, f32[2,256,5,64]{1,0,3,2:T(2,128)}, u32[]{:S(2)}) copy-start(f32[2,256,5,64]{1,0,3,2:T(2,128)} %reshape.488) | copy-start | bytes 1966084
  97.5 7.7 %copy-start.24 = (f32[5]{0:T(128)S(1)}, f32[5]{0:T(128)}, u32[]{:S(2)}) copy-start(f32[5]{0:T(128)} %param.40) | copy-start | bytes 64
  102.7 6.1 %copy-start.10 = (f32[16,256,5]{1,2,0:T(8,128)S(1)}, f32[16,256,5]{1,2,0:T(8,128)}, u32[]{:S(2)}) copy-start(f32[16,256,5]{1,2,0:T(8,128)} %fusion.69) | copy-start | bytes 245764
  105.2 3.5 %copy-start.1 = (f32[16,256,5,64]{1,3,2,0:T(8,128)S(1)}, f32[16,256,5,64]{1,3,2,0:T(8,128)}, u32[]{:S(2)}) copy-start(f32[16,256,5,64]{1,3,2,0:T(8,128)} %gather_fusion.3) | copy-start | bytes 15728644
  105.3 3.5 %copy-start.23 = (pred[16]{0:T(512)(128)(4,1)S(1)}, pred[16]{0:T(512)(128)(4,1)}, u32[]{:S(2)}) copy-start(pred[16]{0:T(512)(128)(4,1)} %get-tuple-element.167) | copy-start | bytes 52
  117.6 2.2 %copy-start.25 = (pred[16]{0:T(512)(128)(4,1)S(1)}, pred[16]{0:T(512)(128)(4,1)}, u32[]{:S(2)}) copy-start(pred[16]{0:T(512)(128)(4,1)} %compare_and_fusion.3) | copy-start | bytes 52
  121.4 8.6 %copy-start.26 = (f32[320]{0:T(512)S(1)}, f32[320]{0:T(512)}, u32[]{:S(2)}) copy-start(f32[320]{0:T(512)} %param.41) | copy-start | bytes 3844
  121.4 21.6 %all-to-all-start.3 = ((bf16[16,5,64,128]{3,2,1,0:T(8,128)(2,1)}), bf16[16,5,64,128]{3,2,1,0:T(8,128)(2,1)S(1)}, u32[]{:S(2)}, u32[]{:S(2)}) async-start(bf16[16,5,64,128]{3,2,1,0:T(8,128)(2,1)} %select_convert_fusion), calls=%async_computation.3 | async-start | bytes 2621440 | tf_op jit(solution)/shard_map/all_to_all | solution.py:205
  143.0 46.2 %all-to-all-start.2 = ((bf16[16,32,2688]{2,1,0:T(8,128)(2,1)}), bf16[16,32,2688]{2,1,0:T(8,128)(2,1)}, u32[]{:S(2)}, u32[]{:S(2)}) async-start(bf16[16,32,2688]{2,1,0:T(8,128)(2,1)} %bitcast.86), calls=%async_computation.2 | async-start | bytes 5505024 | tf_op jit(solution)/shard_map/all_to_all | solution.py:156

commit v4 on v3

--- a/solution.py
+++ b/solution.py
@@ -202,13 +202,17 @@
         (slots[None, :] == request_ids[:, None]).astype(jnp.int32) * request_ids[None, :], axis=1
     )
     outgoing = jnp.take(end_states, inverse, axis=0)
-    received = lax.all_to_all(
-        outgoing.astype(jnp.bfloat16), "seq", split_axis=0, concat_axis=0, tiled=True
-    ).astype(outgoing.dtype)
-    mine = jnp.sum(
-        received.reshape(seq_count, request_count // seq_count, local_heads, head_size, state_size),
-        axis=0,
-    )
+    chunks = outgoing.astype(jnp.bfloat16).reshape(
+        seq_count, request_count // seq_count, local_heads, head_size, state_size
+    )
+    pieces = [jnp.take(chunks, seq_index, axis=0).astype(jnp.float32)]
+    for distance in range(1, seq_count):
+        target = (seq_index + distance) % seq_count
+        route = [(i, (i + distance) % seq_count) for i in range(seq_count)]
+        pieces.append(
+            lax.ppermute(jnp.take(chunks, target, axis=0), "seq", route).astype(jnp.float32)
+        )
+    mine = sum(pieces[1:], pieces[0])
     return (mixed, mine)
 
 

time: 196 us -> 172 us (0.88)
  waiting for transfers between devices: 78.7 us -> 47.9 us
  other arithmetic: 30.4 us -> 33.3 us
  starting transfers between devices: 24.3 us -> 26.4 us
    all_to_all x1, waiting for transfers between devices: 40.8 us -> 0.01 us  [per_device(): lax.all_to_all(jnp.concatenate([partials, square_columns], axis=1), 'tens...]
    ppermute x0 -> x7, waiting for transfers between devices: none -> 12.5 us  [per_device(): lax.ppermute(jnp.take(chunks, target, axis=0), 'seq', route)]
    all_to_all x1 -> x0, waiting for transfers between devices: 8.26 us -> none  [per_device(): lax.all_to_all(outgoing.astype(jnp.bfloat16), 'seq', split_axis=0, concat...]
    ppermute x0 -> x7, starting transfers between devices: none -> 6.68 us  [per_device(): lax.ppermute(jnp.take(chunks, target, axis=0), 'seq', route)]
    all_to_all x1 -> x0, starting transfers between devices: 4.94 us -> none  [per_device(): lax.all_to_all(outgoing.astype(jnp.bfloat16), 'seq', split_axis=0, concat...]
    all_to_all x1, waiting for transfers between devices: 0.01 us -> 4.54 us  [per_device(): lax.all_to_all(jnp.tile(packed[None], (seq_count, 1, 1, 1)), 'seq', 0, 0,...]
    ppermute x1, waiting for transfers between devices: 1.38 us -> 3.88 us  [passed_along(): return lax.ppermute(block, axis, route)]
    add x0 -> x1, other arithmetic: none -> 2.27 us  [per_device(): mine = sum(pieces[1:], pieces[0])]
  transfers between devices with their start and end apart: 5 -> 11, of which waited for: 4 -> 9; matrix products, arithmetic and copies ran while one was open for 20% -> 31% of each run, Pallas kernels for 0% -> 0%
where the time goes in v4:
time: 172 us; the launch traced here: 168 us
  waiting for transfers between devices  47.9 us (28%)
  other arithmetic  33.3 us (19%)
  local copies, waits for them, and re-layouts  32.3 us (19%)
  matrix products  27.1 us (16%)
  starting transfers between devices  26.4 us (15%)
    all_to_all x1, waiting for transfers between devices, per_device(): lax.all_to_all(jnp.tile(tokens, (lax.axis_size('tensor'), 1)), 'tensor',...  26.9 us
    ppermute x7, waiting for transfers between devices, per_device(): lax.ppermute(jnp.take(chunks, target, axis=0), 'seq', route)  12.5 us
    dot_general x1, matrix products, per_device(): jnp.einsum('rjhp,rjn->rhpn', weight[..., None] * chosen_values, chosen_ke...  9.22 us
    all_to_all x1, starting transfers between devices, per_device(): lax.all_to_all(jnp.tile(tokens, (lax.axis_size('tensor'), 1)), 'tensor',...  8.22 us
    ppermute x7, starting transfers between devices, per_device(): lax.ppermute(jnp.take(chunks, target, axis=0), 'seq', route)  6.68 us
    another operation x9, other arithmetic  5.93 us
    dot_general x1, matrix products, per_device(): jnp.dot(gathered, weight_all, preferred_element_type=jnp.float32)  5.72 us
    unnamed x68, local copies, waits for them, and re-layouts  5.26 us
  transfers between devices with their start and end apart: 11, of which 9 were waited for; matrix products, arithmetic and copies ran while one was open for 31% of the time, Pallas kernels for 0%

profile of v4, /device:TPU:6, one launch (start us, length us, event | category | flops | bytes accessed | tf_op | source)
XLA Modules:
  0.0 168.5 jit_solution(14317205304277893679)
XLA Ops:
  0.6 2.8 %tile.4 = bf16[16,32,2560]{2,1,0:T(8,128)(2,1)} broadcast(bf16[32,2560]{1,0:T(8,128)(2,1)} %param.31), dimensions={1,2} | broadcast | bytes 2785280 | tf_op jit(solution)/shard_map/tile | solution.py:50
  3.5 8.2 %all-to-all-start = ((bf16[16,32,2560]{2,1,0:T(8,128)(2,1)}), bf16[16,32,2560]{2,1,0:T(8,128)(2,1)}, u32[]{:S(2)}, u32[]{:S(2)}) async-start(bf16[16,32,2560]{2,1,0:T(8,128)(2,1)} %tile.4), calls=%async_computation | async-start | bytes 5242880 | tf_op jit(solution)/shard_map/all_to_all | solution.py:49
  11.9 0.7 compare_reduce_fusion
  12.5 0.7 compare_reduce_fusion.1
  13.7 2.4 %copy.144 = bf16[2560,256]{0,1:T(8,128)(2,1)} copy(bf16[2560,256]{1,0:T(8,128)(2,1)} %param.35) | data formatting | bytes 2621440 | tf_op args[4]
  16.8 0.6 fusion.100
  17.4 1.9 %compare_convert_fusion.2 = (f32[16]{0:T(128)}, s32[16]{0:T(128)S(1)}, s32[16]{0:T(128)S(1)}, pred[16]{0:T(512)(128)(4,1)}) fusion(s32[]{:T(128)} %bitcast.17, s32[]{:T(128)} %bitcast.18, s32[]{:T(128)S(6)} %mul.358, s32[16]{0:T(128)S(1)} %copy-done.25, s32[16]{0:T(128)S(1)} %reduce.20, s32[]{:T(128)S(6)} %add.342), kind=kLoop, calls=%fused_computation.171 | loop fusion | flops 528 | bytes 352 | tf_op jit(solution)/shard_map/convert_element_type | solution.py:195
  19.6 0.6 gather_fusion.2
  20.7 0.6 pad_clamp_fusion
  21.4 0.7 fusion.84
  22.6 0.6 fusion.91
  23.2 0.7 compare_convert_fusion.1
  23.9 0.7 fusion.80
  24.7 26.9 %all-to-all-done = bf16[16,32,2560]{2,1,0:T(8,128)(2,1)} async-done(((bf16[16,32,2560]{2,1,0:T(8,128)(2,1)}), bf16[16,32,2560]{2,1,0:T(8,128)(2,1)}, u32[]{:S(2)}, u32[]{:S(2)}) %all-to-all-start) | async-done | bytes 2621472 | tf_op jit(solution)/shard_map/all_to_all | solution.py:49
  51.6 5.7 %fusion.26 = f32[512,901]{0,1:T(8,128)S(1)} fusion(bf16[512,2560]{1,0:T(8,128)(2,1)} %bitcast, bf16[2560,256]{0,1:T(8,128)(2,1)} %copy.144, bf16[2560,5]{0,1:T(8,128)(2,1)S(1)} %copy-done.29, bf16[2560,320]{0,1:T(8,128)(2,1)} %param.33, bf16[2560,320]{0,1:T(8,128)(2,1)} %param.32), kind=kOutput, calls=%fused_computation.44 | convolution fusion | flops 2380369920 | bytes 9079808 | tf_op jit(solution)/shard_map/dot_general | solution.py:52
  57.5 1.1 copy-done.3
  58.8 3.0 %reduce-window.20 = f32[2,5,2,128]{3,2,1,0:T(2,128)S(1)} reduce-window(f32[2,5,2,128]{3,2,1,0:T(2,128)S(1)} %copy.148, f32[]{:T(128)} %constant.338.clone.1), window={size=1x1x1x128 pad=0_0x0_0x0_0x127_0}, to_apply=%region_3.4 | reduce-window | flops 325120 | bytes 20484 | tf_op jit(solution)/shard_map/reduce-window.1
  62.5 1.9 %collective-permute-start = (f32[3,576]{0,1:T(8,128)S(1)}, f32[3,576]{0,1:T(8,128)S(1)}, u32[]{:S(2)}, u32[]{:S(2)}) collective-permute-start(f32[3,576]{0,1:T(8,128)S(1)} %fusion.60), channel_id=1, source_target_pairs={{0,16},{16,32},{32,48},{48,64},{64,80},{80,96},{96,112},{1,17},{17... | collective-permute-start | bytes 20744 | tf_op jit(solution)/shard_map/ppermute | solution.py:16
  64.5 0.8 exponential_multiply_fusion
  65.3 1.3 exponential_multiply_fusion.2
  66.6 3.9 %collective-permute-done = f32[3,576]{0,1:T(8,128)S(1)} collective-permute-done((f32[3,576]{0,1:T(8,128)S(1)}, f32[3,576]{0,1:T(8,128)S(1)}, u32[]{:S(2)}, u32[]{:S(2)}) %collective-permute-start) | collective-permute-done | bytes 6944 | tf_op jit(solution)/shard_map/ppermute | solution.py:16
  71.0 1.4 divide_multiply_fusion
  72.4 0.7 fusion.99
  73.2 0.9 slice.299
  74.1 0.9 reshape.489
  74.9 1.5 reshape.487
  76.4 1.7 %fusion.54 = f32[2,5,64,128]{3,2,1,0:T(8,128)S(1)} fusion(f32[2,256,5]{1,2,0:T(8,128)S(1)} %get-tuple-element.180, f32[2,256,128,1]{1,0,2,3:T(2,128)} %bitcast.106, f32[2,256,5,64]{1,0,3,2:T(2,128)S(1)} %reshape.487), kind=kOutput, calls=%fused_computation.76 | convolution fusion | flops 251822080 | bytes 1255424 | tf_op jit(solution)/shard_map/cjhp,cjn->chpn/dot_general | solution.py:100
  78.8 1.0 tile.5
  79.8 4.8 %all-to-all-start.1 = ((bf16[8,5,80,128]{3,2,1,0:T(8,128)(2,1)}), bf16[8,5,80,128]{3,2,1,0:T(8,128)(2,1)}, u32[]{:S(2)}, u32[]{:S(2)}) async-start(bf16[8,5,80,128]{3,2,1,0:T(8,128)(2,1)} %tile.5), calls=%async_computation.1 | async-start | bytes 1638400 | tf_op jit(solution)/shard_map/all_to_all | solution.py:125
  84.8 1.1 reshape.488
  85.9 1.6 fusion.61
  87.5 4.0 %fusion.39 = f32[2,256,5,64]{1,3,2,0:T(8,128)} fusion(f32[2,256,5]{1,2,0:T(8,128)S(1)} %bitcast.99, f32[2,256,5]{1,2,0:T(8,128)S(1)} %bitcast.96, f32[2,256,256]{2,1,0:T(8,128)S(1)} %fusion.61, pred[2,256,256]{2,1,0:T(8,128)(4,1)S(1)} %compare_and_fusion, f32[2,256,5,64]{1,0,3,2:T(2,128)S(1)} %reshape.487), kind=kOutput, calls=%fused_computation.55 | convolution fusion | flops 506593280 | bytes 1986560 | tf_op jit(solution)/shard_map/cijh,cjhp->cihp/dot_general | solution.py:97
  91.5 4.5 %all-to-all-done.1 = bf16[8,5,80,128]{3,2,1,0:T(8,128)(2,1)} async-done(((bf16[8,5,80,128]{3,2,1,0:T(8,128)(2,1)}), bf16[8,5,80,128]{3,2,1,0:T(8,128)(2,1)}, u32[]{:S(2)}, u32[]{:S(2)}) %all-to-all-start.1) | async-done | bytes 819232 | tf_op jit(solution)/shard_map/all_to_all | solution.py:125
  96.1 1.0 fusion.70
  97.2 1.4 select_bitcast_fusion.7
  98.6 1.9 %fusion.43 = f32[2,256,5,64]{1,3,2,0:T(8,128)S(1)} fusion(f32[2,256,5,64]{1,3,2,0:T(8,128)} %fusion.39, f32[5]{0:T(128)S(1)} %copy-done.28, f32[2,5,64,128]{3,2,1,0:T(8,128)S(1)} %get-tuple-element.92, f32[2,256,5]{1,2,0:T(8,128)S(1)} %get-tuple-element.179, f32[2,256,128,1]{1,0,2,3:T(2,128)S(1)} %bitcast.108, f32[5,64,128]{2,1,0:T(8,128)S(1)} %select_bitcast_fusion.7, ...), kind=kOutput, calls=%fused_computation.58 | convolution fusion | flops 252477440 | bytes 2730044 | tf_op jit(solution)/shard_map/cin,chpn->cihp/dot_general | solution.py:139
  101.2 0.8 copy-done.1
  102.0 1.3 multiply_reduce_fusion
  103.5 1.3 fusion.68
  105.3 3.0 %convolution_convert_fusion = bf16[512,2560]{1,0:T(8,128)(2,1)S(1)} fusion(bf16[320,2560]{1,0:T(8,128)(2,1)S(1)} %copy-done, f32[320]{0:T(512)S(1)} %copy-done.30, f32[512,320]{0,1:T(8,128)} %bitcast.104, f32[512,901]{0,1:T(8,128)} %copy-done.3), kind=kOutput, calls=%fused_computation.28 | convolution fusion | flops 841318400 | bytes 5571840 | tf_op jit(solution)/shard_map/dot_general | solution.py:148
  108.2 1.8 %pad_maximum_fusion = bf16[512,2688]{1,0:T(8,128)(2,1)} fusion(bf16[512,128]{1,0:T(8,128)(2,1)S(1)} %scatter.19, bf16[512,2560]{1,0:T(8,128)(2,1)S(1)} %convolution_convert_fusion), kind=kLoop, calls=%fused_computation.29 | loop fusion | flops 5505024 | bytes 5505024 | tf_op jit(solution)/shard_map/concatenate | solution.py:157
  110.0 4.8 %all-to-all-start.2 = ((bf16[16,32,2688]{2,1,0:T(8,128)(2,1)}), bf16[16,32,2688]{2,1,0:T(8,128)(2,1)}, u32[]{:S(2)}, u32[]{:S(2)}) async-start(bf16[16,32,2688]{2,1,0:T(8,128)(2,1)} %bitcast.101), calls=%async_computation.2 | async-start | bytes 5505024 | tf_op jit(solution)/shard_map/all_to_all | solution.py:156
  116.1 2.0 %copy.164 = f32[16,256,5]{2,1,0:T(8,128)} copy(f32[16,256,5]{1,2,0:T(8,128)S(1)} %broadcast_select_fusion.2) | data formatting | bytes 163840 | tf_op jit(solution)/shard_map/jit(_take)/select_n | solution.py:176
  118.1 1.3 gather_fusion
  119.4 0.8 fusion.69
  120.2 2.3 %gather_fusion.1 = f32[16,5,64,128]{3,2,1,0:T(8,128)} fusion(f32[2,5,64,128]{3,2,1,0:T(8,128)S(1)} %get-tuple-element.92, s32[1024]{0:T(1024)S(1)} %copy-done.10), kind=kCustom, calls=%fused_computation.3 | custom fusion | bytes 5242944 | tf_op jit(solution)/shard_map/jit(_take)/gather | solution.py:197
  123.0 2.0 %gather_fusion.4 = f32[16,256,128]{2,1,0:T(8,128)} fusion(f32[2,256,128]{2,1,0:T(8,128)S(1)} %copy.147, s32[1024]{0:T(1024)S(1)} %copy-done.10), kind=kCustom, calls=%fused_computation.6 | custom fusion | bytes 4194368 | tf_op jit(solution)/shard_map/jit(_take)/gather | solution.py:175
  125.1 3.2 %gather_fusion.3 = f32[16,256,5,64]{1,3,2,0:T(8,128)} fusion(f32[2,256,5,64]{1,3,2,0:T(8,128)S(1)} %copy.154, s32[1024]{0:T(1024)S(1)} %copy-done.10), kind=kCustom, calls=%fused_computation.5 | custom fusion | bytes 10485824 | tf_op jit(solution)/shard_map/jit(_take)/gather | solution.py:174
  128.4 9.2 %add_select_fusion = bf16[16,5,64,128]{3,2,1,0:T(8,128)(2,1)S(1)} fusion(f32[16,5,64,128]{3,2,1,0:T(8,128)} %gather_fusion.1, f32[5,64,128]{2,1,0:T(8,128)S(1)} %copy-done.5, f32[16,5]{1,0:T(8,128)S(1)} %get-tuple-element.158, f32[16,5]{1,0:T(8,128)S(1)} %get-tuple-element.159, pred[16]{0:T(512)(128)(4,1)S(1)} %copy-done.13, ...), kind=kOutput, calls=%fused_computation.31 | convolution fusion | flops 2020343808 | bytes 11518624 | tf_op jit(solution)/shard_map/rjhp,rjn->rhpn/dot_general | solution.py:188
  137.6 1.9 %gather_fusion.6 = bf16[16,5,64,128]{3,2,1,0:T(8,128)(2,1)} fusion(bf16[16,5,64,128]{3,2,1,0:T(8,128)(2,1)S(1)} %add_select_fusion, s32[1024]{0:T(1024)} %pad_clamp_fusion), kind=kCustom, calls=%fused_computation.8 | custom fusion | bytes 2621504 | tf_op jit(solution)/shard_map/jit(_take)/gather | solution.py:204
  139.5 1.9 %select_convert_fusion = bf16[8,2,5,64,128]{4,3,2,1,0:T(8,128)(2,1)S(1)} fusion(bf16[8,2,5,64,128]{4,3,2,1,0:T(8,128)(2,1)} %bitcast.102, pred[8,2]{1,0:T(8,128)(4,1)S(1)} %compare_and_fusion.1), kind=kLoop, calls=%fused_computation.30 | loop fusion | flops 655360 | bytes 2621456 | tf_op jit(solution)/shard_map/convert_element_type | solution.py:205
  141.4 0.8 select_bitcast_fusion.6
  142.2 1.2 collective-permute-start.6
  143.4 2.2 %collective-permute-start.5 = (bf16[2,5,64,128]{3,2,1,0:T(8,128)(2,1)}, bf16[2,5,64,128]{3,2,1,0:T(8,128)(2,1)}, u32[]{:S(2)}, u32[]{:S(2)}) collective-permute-start(bf16[2,5,64,128]{3,2,1,0:T(8,128)(2,1)} %get-tuple-element.171), channel_id=1, source_target_pairs={{0,80},{16,96},{32,112},{48,0},{64,16},{80,32},{96,48},{112,64},{1... | collective-permute-start | bytes 491528 | tf_op jit(solution)/shard_map/ppermute | solution.py:213
  146.1 2.1 %collective-permute-start.3 = (bf16[2,5,64,128]{3,2,1,0:T(8,128)(2,1)S(1)}, bf16[2,5,64,128]{3,2,1,0:T(8,128)(2,1)}, u32[]{:S(2)}, u32[]{:S(2)}) collective-permute-start(bf16[2,5,64,128]{3,2,1,0:T(8,128)(2,1)S(1)} %get-tuple-element.173), channel_id=1, source_target_pairs={{0,48},{16,64},{32,80},{48,96},{64,112},{80,0},{96,16},{112,32},{1... | collective-permute-start | bytes 491528 | tf_op jit(solution)/shard_map/ppermute | solution.py:213
  148.1 0.8 collective-permute-start.2
  148.9 3.8 %collective-permute-done.6 = bf16[2,5,64,128]{3,2,1,0:T(8,128)(2,1)S(1)} collective-permute-done((bf16[2,5,64,128]{3,2,1,0:T(8,128)(2,1)S(1)}, bf16[2,5,64,128]{3,2,1,0:T(8,128)(2,1)S(1)}, u32[]{:S(2)}, u32[]{:S(2)}) %collective-permute-start.6) | collective-permute-done | bytes 163872 | tf_op jit(solution)/shard_map/ppermute | solution.py:213
  152.7 0.7 copy-done.7
  153.9 6.2 %collective-permute-done.4 = bf16[2,5,64,128]{3,2,1,0:T(8,128)(2,1)} collective-permute-done((bf16[2,5,64,128]{3,2,1,0:T(8,128)(2,1)}, bf16[2,5,64,128]{3,2,1,0:T(8,128)(2,1)}, u32[]{:S(2)}, u32[]{:S(2)}) %collective-permute-start.4) | collective-permute-done | bytes 163872 | tf_op jit(solution)/shard_map/ppermute | solution.py:213
  160.6 1.0 collective-permute-done.2
  162.1 2.3 %convert_add_fusion = f32[2,5,64,128]{3,2,1,0:T(8,128)} fusion(bf16[2,5,64,128]{3,2,1,0:T(8,128)(2,1)} %copy-done.6, bf16[2,5,64,128]{3,2,1,0:T(8,128)(2,1)} %copy-done.7, bf16[2,5,64,128]{3,2,1,0:T(8,128)(2,1)} %collective-permute-done.5, bf16[2,5,64,128]{3,2,1,0:T(8,128)(2,1)} %collective-permute-done.4, ...), kind=kLoop, calls=%fused_computation.79 | loop fusion | flops 1310720 | bytes 1638405 | tf_op jit(solution)/shard_map/add | solution.py:215
  164.4 1.2 add_reduce_fusion
  165.6 2.2 %convert_reduce_fusion = f32[32,2560]{1,0:T(8,128)S(1)} fusion(bf16[16,32,2688]{2,1,0:T(8,128)(2,1)} %all-to-all-done.2), kind=kLoop, calls=%fused_computation.19 | loop fusion | flops 2539520 | bytes 2949120 | tf_op jit(solution)/shard_map/reduce_sum | solution.py:159
  167.7 0.8 multiply_convert_fusion.2
  (150 shorter events, 10.5 us)
Async XLA Ops:
  0.6 104.6 %copy-start = (bf16[320,2560]{1,0:T(8,128)(2,1)S(1)}, bf16[320,2560]{1,0:T(8,128)(2,1)}, u32[]{:S(2)}) copy-start(bf16[320,2560]{1,0:T(8,128)(2,1)} %param.44) | copy-start | bytes 4915204
  3.5 9.7 %copy-start.31 = (f32[5]{0:T(128)S(1)}, f32[5]{0:T(128)}, u32[]{:S(2)}) copy-start(f32[5]{0:T(128)} %param.41) | copy-start | bytes 64
  3.5 48.2 %all-to-all-start = ((bf16[16,32,2560]{2,1,0:T(8,128)(2,1)}), bf16[16,32,2560]{2,1,0:T(8,128)(2,1)}, u32[]{:S(2)}, u32[]{:S(2)}) async-start(bf16[16,32,2560]{2,1,0:T(8,128)(2,1)} %tile.4), calls=%async_computation | async-start | bytes 5242880 | tf_op jit(solution)/shard_map/all_to_all | solution.py:49
  11.7 4.5 %copy-start.24 = (s32[16]{0:T(128)S(1)}, s32[16]{0:T(128)}, u32[]{:S(2)}) copy-start(s32[16]{0:T(128)} %param.45) | copy-start | bytes 196
  11.7 5.7 %copy-start.25 = (s32[16]{0:T(128)S(1)}, s32[16]{0:T(128)}, u32[]{:S(2)}) copy-start(s32[16]{0:T(128)} %param.46) | copy-start | bytes 196
  11.7 7.6 %copy-start.32 = (s32[16]{0:T(128)S(1)}, s32[16]{0:T(128)}, u32[]{:S(2)}) copy-start(s32[16]{0:T(128)} %param.47) | copy-start | bytes 196
  11.7 7.8 %copy-start.17 = (f32[4,320]{1,0:T(4,128)S(1)}, f32[4,320]{1,0:T(4,128)}, u32[]{:S(2)}) copy-start(f32[4,320]{1,0:T(4,128)} %param.36) | copy-start | bytes 15364
  11.7 7.7 %copy-start.18 = (f32[4,256]{1,0:T(4,128)S(1)}, f32[4,256]{1,0:T(4,128)}, u32[]{:S(2)}) copy-start(f32[4,256]{1,0:T(4,128)} %param.38) | copy-start | bytes 12292
  11.8 9.5 %copy-start.20 = (f32[320]{0:T(512)S(1)}, f32[320]{0:T(512)}, u32[]{:S(2)}) copy-start(f32[320]{0:T(512)} %param.37) | copy-start | bytes 3844
  11.8 9.5 %copy-start.21 = (f32[256]{0:T(256)S(1)}, f32[256]{0:T(256)}, u32[]{:S(2)}) copy-start(f32[256]{0:T(256)} %param.39) | copy-start | bytes 3076
  11.8 39.9 %copy-start.29 = (bf16[2560,5]{0,1:T(8,128)(2,1)S(1)}, bf16[2560,5]{0,1:T(8,128)(2,1)}, u32[]{:S(2)}) copy-start(bf16[2560,5]{0,1:T(8,128)(2,1)} %param.34) | copy-start | bytes 76804
  19.3 1.4 copy-start.9
  57.4 1.3 copy-start.3
  57.4 1.3 copy-start.22
  57.4 1.3 copy-start.23
  62.3 8.7 %copy-start.14 = (f32[512]{0:T(512)S(1)}, f32[512]{0:T(512)}, u32[]{:S(2)}) copy-start(f32[512]{0:T(512)} %get-tuple-element.181) | copy-start | bytes 6148
  62.3 8.7 %copy-start.15 = (f32[512]{0:T(512)S(1)}, f32[512]{0:T(512)}, u32[]{:S(2)}) copy-start(f32[512]{0:T(512)} %get-tuple-element.182) | copy-start | bytes 6148
  62.3 8.7 %copy-start.16 = (f32[512]{0:T(512)S(1)}, f32[512]{0:T(512)}, u32[]{:S(2)}) copy-start(f32[512]{0:T(512)} %get-tuple-element.183) | copy-start | bytes 6148
  62.5 8.0 %collective-permute-start = (f32[3,576]{0,1:T(8,128)S(1)}, f32[3,576]{0,1:T(8,128)S(1)}, u32[]{:S(2)}, u32[]{:S(2)}) collective-permute-start(f32[3,576]{0,1:T(8,128)S(1)} %fusion.60), channel_id=1, source_target_pairs={{0,16},{16,32},{32,48},{48,64},{64,80},{80,96},{96,112},{1,17},{17... | collective-permute-start | bytes 20744 | tf_op jit(solution)/shard_map/ppermute | solution.py:16
  73.2 5.0 %copy-start.11 = (f32[5]{0:T(128)S(1)}, f32[5]{0:T(128)}, u32[]{:S(2)}) copy-start(f32[5]{0:T(128)} %custom-call.3) | copy-start | bytes 64
  73.2 5.0 %copy-start.12 = (f32[2,5]{1,0:T(2,128)S(1)}, f32[2,5]{1,0:T(2,128)}, u32[]{:S(2)}) copy-start(f32[2,5]{1,0:T(2,128)} %exponential_multiply_fusion.2) | copy-start | bytes 124
  78.5 6.0 %copy-start.13 = (pred[16]{0:T(512)(128)(4,1)S(1)}, pred[16]{0:T(512)(128)(4,1)}, u32[]{:S(2)}) copy-start(pred[16]{0:T(512)(128)(4,1)} %compare_and_fusion.2) | copy-start | bytes 52
  78.5 6.0 %copy-start.27 = (s32[16]{0:T(128)S(1)}, s32[16]{0:T(128)}, u32[]{:S(2)}) copy-start(s32[16]{0:T(128)} %get-tuple-element.164) | copy-start | bytes 196
  78.5 6.1 %copy-start.2 = (f32[2,256,128]{1,0,2:T(2,128)S(1)}, f32[2,256,128]{1,0,2:T(2,128)}, u32[]{:S(2)}) copy-start(f32[2,256,128]{1,0,2:T(2,128)} %reshape.489) | copy-start | bytes 786436
  79.8 16.3 %all-to-all-start.1 = ((bf16[8,5,80,128]{3,2,1,0:T(8,128)(2,1)}), bf16[8,5,80,128]{3,2,1,0:T(8,128)(2,1)}, u32[]{:S(2)}, u32[]{:S(2)}) async-start(bf16[8,5,80,128]{3,2,1,0:T(8,128)(2,1)} %tile.5), calls=%async_computation.1 | async-start | bytes 1638400 | tf_op jit(solution)/shard_map/all_to_all | solution.py:125
  87.5 11.1 %copy-start.28 = (f32[5]{0:T(128)S(1)}, f32[5]{0:T(128)}, u32[]{:S(2)}) copy-start(f32[5]{0:T(128)} %param.42) | copy-start | bytes 64
  98.6 2.5 %copy-start.4 = (f32[5,64,128]{2,1,0:T(8,128)}, f32[5,64,128]{2,1,0:T(8,128)S(1)}, u32[]{:S(2)}) copy-start(f32[5,64,128]{2,1,0:T(8,128)S(1)} %select_bitcast_fusion.7) | copy-start | bytes 491524
  101.1 4.2 %copy-start.30 = (f32[320]{0:T(512)S(1)}, f32[320]{0:T(512)}, u32[]{:S(2)}) copy-start(f32[320]{0:T(512)} %param.43) | copy-start | bytes 3844
  101.2 0.8 copy-start.1
  110.0 4.8 %copy-start.10 = (s32[1024]{0:T(1024)S(1)}, s32[1024]{0:T(1024)}, u32[]{:S(2)}) copy-start(s32[1024]{0:T(1024)} %copy-done.9) | copy-start | bytes 12292
  110.0 54.3 %all-to-all-start.2 = ((bf16[16,32,2688]{2,1,0:T(8,128)(2,1)}), bf16[16,32,2688]{2,1,0:T(8,128)(2,1)}, u32[]{:S(2)}, u32[]{:S(2)}) async-start(bf16[16,32,2688]{2,1,0:T(8,128)(2,1)} %bitcast.101), calls=%async_computation.2 | async-start | bytes 5505024 | tf_op jit(solution)/shard_map/all_to_all | solution.py:156
  125.1 3.2 %copy-start.19 = (f32[16]{0:T(128)S(1)}, f32[16]{0:T(128)}, u32[]{:S(2)}) copy-start(f32[16]{0:T(128)} %get-tuple-element.160) | copy-start | bytes 196
  125.1 3.3 %copy-start.5 = (f32[5,64,128]{2,1,0:T(8,128)S(1)}, f32[5,64,128]{2,1,0:T(8,128)}, u32[]{:S(2)}) copy-start(f32[5,64,128]{2,1,0:T(8,128)} %copy-done.4) | copy-start | bytes 491524
  125.1 3.3 %copy-start.8 = (f32[16,256,5]{1,2,0:T(8,128)S(1)}, f32[16,256,5]{1,2,0:T(8,128)}, u32[]{:S(2)}) copy-start(f32[16,256,5]{1,2,0:T(8,128)} %fusion.69) | copy-start | bytes 245764
  125.1 3.3 %copy-start.26 = (pred[16]{0:T(512)(128)(4,1)S(1)}, pred[16]{0:T(512)(128)(4,1)}, u32[]{:S(2)}) copy-start(pred[16]{0:T(512)(128)(4,1)} %get-tuple-element.186) | copy-start | bytes 52
  142.2 5.9 %collective-permute-start.7 = (bf16[2,5,64,128]{3,2,1,0:T(8,128)(2,1)S(1)}, bf16[2,5,64,128]{3,2,1,0:T(8,128)(2,1)S(1)}, u32[]{:S(2)}, u32[]{:S(2)}) collective-permute-start(bf16[2,5,64,128]{3,2,1,0:T(8,128)(2,1)S(1)} %get-tuple-element.169), channel_id=1, source_target_pairs={{0,112},{16,0},{32,16},{48,32},{64,48},{80,64},{96,80},{112,96},{1... | collective-permute-start | bytes 491528 | tf_op jit(solution)/shard_map/ppermute | solution.py:213
  142.2 10.5 %collective-permute-start.6 = (bf16[2,5,64,128]{3,2,1,0:T(8,128)(2,1)S(1)}, bf16[2,5,64,128]{3,2,1,0:T(8,128)(2,1)S(1)}, u32[]{:S(2)}, u32[]{:S(2)}) collective-permute-start(bf16[2,5,64,128]{3,2,1,0:T(8,128)(2,1)S(1)} %get-tuple-element.170), channel_id=1, source_target_pairs={{0,96},{16,112},{32,0},{48,16},{64,32},{80,48},{96,64},{112,80},{1... | collective-permute-start | bytes 491528 | tf_op jit(solution)/shard_map/ppermute | solution.py:213
  143.4 10.5 %collective-permute-start.5 = (bf16[2,5,64,128]{3,2,1,0:T(8,128)(2,1)}, bf16[2,5,64,128]{3,2,1,0:T(8,128)(2,1)}, u32[]{:S(2)}, u32[]{:S(2)}) collective-permute-start(bf16[2,5,64,128]{3,2,1,0:T(8,128)(2,1)} %get-tuple-element.171), channel_id=1, source_target_pairs={{0,80},{16,96},{32,112},{48,0},{64,16},{80,32},{96,48},{112,64},{1... | collective-permute-start | bytes 491528 | tf_op jit(solution)/shard_map/ppermute | solution.py:213
  145.6 14.6 %collective-permute-start.4 = (bf16[2,5,64,128]{3,2,1,0:T(8,128)(2,1)}, bf16[2,5,64,128]{3,2,1,0:T(8,128)(2,1)}, u32[]{:S(2)}, u32[]{:S(2)}) collective-permute-start(bf16[2,5,64,128]{3,2,1,0:T(8,128)(2,1)} %get-tuple-element.172), channel_id=1, source_target_pairs={{0,64},{16,80},{32,96},{48,112},{64,0},{80,16},{96,32},{112,48},{1... | collective-permute-start | bytes 491528 | tf_op jit(solution)/shard_map/ppermute | solution.py:213
  146.1 14.5 %collective-permute-start.3 = (bf16[2,5,64,128]{3,2,1,0:T(8,128)(2,1)S(1)}, bf16[2,5,64,128]{3,2,1,0:T(8,128)(2,1)}, u32[]{:S(2)}, u32[]{:S(2)}) collective-permute-start(bf16[2,5,64,128]{3,2,1,0:T(8,128)(2,1)S(1)} %get-tuple-element.173), channel_id=1, source_target_pairs={{0,48},{16,64},{32,80},{48,96},{64,112},{80,0},{96,16},{112,32},{1... | collective-permute-start | bytes 491528 | tf_op jit(solution)/shard_map/ppermute | solution.py:213
  148.1 4.6 %copy-start.6 = (bf16[2,5,64,128]{3,2,1,0:T(8,128)(2,1)}, bf16[2,5,64,128]{3,2,1,0:T(8,128)(2,1)S(1)}, u32[]{:S(2)}) copy-start(bf16[2,5,64,128]{3,2,1,0:T(8,128)(2,1)S(1)} %collective-permute-done.7) | copy-start | bytes 491524
  148.1 13.5 %collective-permute-start.2 = (bf16[2,5,64,128]{3,2,1,0:T(8,128)(2,1)S(1)}, bf16[2,5,64,128]{3,2,1,0:T(8,128)(2,1)}, u32[]{:S(2)}, u32[]{:S(2)}) collective-permute-start(bf16[2,5,64,128]{3,2,1,0:T(8,128)(2,1)S(1)} %get-tuple-element.174), channel_id=1, source_target_pairs={{0,32},{16,48},{32,64},{48,80},{64,96},{80,112},{96,0},{112,16},{1... | collective-permute-start | bytes 491528 | tf_op jit(solution)/shard_map/ppermute | solution.py:213
  152.7 0.7 copy-start.7
  153.4 8.7 %collective-permute-start.1 = (bf16[2,5,64,128]{3,2,1,0:T(8,128)(2,1)S(1)}, bf16[2,5,64,128]{3,2,1,0:T(8,128)(2,1)}, u32[]{:S(2)}, u32[]{:S(2)}) collective-permute-start(bf16[2,5,64,128]{3,2,1,0:T(8,128)(2,1)S(1)} %get-tuple-element.168), channel_id=1, source_target_pairs={{0,16},{16,32},{32,48},{48,64},{64,80},{80,96},{96,112},{112,0},{1... | collective-permute-start | bytes 491528 | tf_op jit(solution)/shard_map/ppermute | solution.py:213

commit v5 on v4

--- a/solution.py
+++ b/solution.py
@@ -166,42 +166,43 @@
     mixed = (reduced * scale).astype(jnp.bfloat16)
     request_count = lengths.shape[0]
     request_ids = jnp.arange(request_count, dtype=jnp.int32)
-    ends = starts + lengths - 1 - DRAFTS + accepted
+    slot_request = jnp.sum(
+        (slots[None, :] == request_ids[:, None]).astype(jnp.int32) * request_ids[None, :], axis=1
+    )
+    ends = jnp.take(starts + lengths - 1 - DRAFTS + accepted, slot_request)
     present = (ends >= first) & (ends < first + row_count)
     local_end = jnp.clip(ends - first, 0, row_count - 1)
     which = local_end // BLOCK
     place = local_end % BLOCK
-    chosen_values = jnp.take(values, which, axis=0)
-    chosen_keys = jnp.take(keys, which, axis=0)
-    chosen_sums = jnp.take(decay_sum, which, axis=0)
-    chosen_steps = jnp.take(steps, which, axis=0)
-    chosen_segs = jnp.take(segs, which, axis=0)
-    end_sums = chosen_sums[request_ids, place]
-    valid = (jnp.arange(BLOCK, dtype=jnp.int32)[None, :] <= place[:, None]) & (
-        chosen_segs == request_ids[:, None]
-    )
-    weight = jnp.where(
-        valid[..., None],
-        jnp.exp(jnp.minimum(end_sums[:, None, :] - chosen_sums, 0.0)) * chosen_steps,
-        0.0,
-    )
-    part = jnp.einsum(
-        "rjhp,rjn->rhpn",
-        weight[..., None] * chosen_values,
-        chosen_keys,
-        precision=HIGHEST_PRECISION,
-    )
-    carried = (
-        jnp.exp(end_sums) * (jnp.take(prior, which) == request_ids).astype(jnp.float32)[:, None]
-    )
-    bracket = carried[:, :, None, None] * jnp.take(zero_starts, which, axis=0) + part
-    coefficient = carried * jnp.take(factors, which, axis=0)
-    end_states = bracket + coefficient[:, :, None, None] * incoming[None]
-    end_states = jnp.where(present[:, None, None, None], end_states, 0.0)
-    inverse = jnp.sum(
-        (slots[None, :] == request_ids[:, None]).astype(jnp.int32) * request_ids[None, :], axis=1
-    )
-    outgoing = jnp.take(end_states, inverse, axis=0)
+    positions = jnp.arange(BLOCK, dtype=jnp.int32)
+    bracket = jnp.zeros((request_count, local_heads, head_size, state_size), jnp.float32)
+    coefficient = jnp.zeros((request_count, local_heads), jnp.float32)
+    for block in range(block_count):
+        in_block = (which == block) & present
+        end_sums = jnp.take(decay_sum[block], place, axis=0)
+        valid = (
+            in_block[:, None]
+            & (positions[None, :] <= place[:, None])
+            & (segs[block][None, :] == slot_request[:, None])
+        )
+        weight = jnp.where(
+            valid[..., None],
+            jnp.exp(jnp.minimum(end_sums[:, None, :] - decay_sum[block][None], 0.0))
+            * steps[block][None],
+            0.0,
+        )
+        bracket = bracket + jnp.einsum(
+            "rjhp,jn->rhpn",
+            weight[..., None] * values[block][None],
+            keys[block],
+            preferred_element_type=jnp.float32,
+        )
+        carried = jnp.where(
+            (in_block & (prior[block] == slot_request))[:, None], jnp.exp(end_sums), 0.0
+        )
+        bracket = bracket + carried[:, :, None, None] * zero_starts[block][None]
+        coefficient = coefficient + carried * factors[block][None]
+    outgoing = bracket + coefficient[:, :, None, None] * incoming[None]
     chunks = outgoing.astype(jnp.bfloat16).reshape(
         seq_count, request_count // seq_count, local_heads, head_size, state_size
     )

time: 172 us -> 168 us (0.977)
  waiting for transfers between devices: 47.9 us -> 59.8 us
  matrix products: 27.1 us -> 19.9 us
  local copies, waits for them, and re-layouts: 32.3 us -> 27.4 us
  other arithmetic: 33.3 us -> 29.5 us
    all_to_all x1, waiting for transfers between devices: 0.01 us -> 16.4 us  [per_device(): lax.all_to_all(jnp.concatenate([partials, square_columns], axis=1), 'tens...]
    gather x10 -> x3, local copies, waits for them, and re-layouts: 13.5 us -> 3.19 us  [the longest x2 2.54 us: per_device(): end_sums = jnp.take(decay_sum[block], place, axis=0)]
    dot_general x1 -> x2, matrix products: 9.22 us -> 2.08 us  [per_device(): jnp.einsum('rjhp,jn->rhpn', weight[..., None] * values[block][None], keys...]
    ppermute x1, waiting for transfers between devices: 3.88 us -> 0.01 us  [passed_along(): return lax.ppermute(block, axis, route)]
    convert_element_type x2 -> x0, other arithmetic: 3.73 us -> none  [the longest x1 1.88 us: per_device(): (jnp.take(prior, which) == request_ids).astype(jnp.float32)[:, None]]
    and x3 -> x4, other arithmetic: 0.59 us -> 3.56 us  [the longest x2 2.35 us: per_device(): in_block & (prior[block] == slot_request)]
    mul x0 -> x5, local copies, waits for them, and re-layouts: none -> 2.65 us  [the longest x1 1.3 us: per_device(): jnp.exp(decay_sum) * (segs == prior[:, None]).astype(jnp.float32)[..., None]]
    dynamic_update_slice x2, local copies, waits for them, and re-layouts: 0.08 us -> 2.52 us  [per_device(): lax.scan(advance, (empty, unit), (local, passes))]
  transfers between devices with their start and end apart: 11 -> 11, of which waited for: 9 -> 9; matrix products, arithmetic and copies ran while one was open for 31% -> 21% of each run, Pallas kernels for 0% -> 0%
where the time goes in v5:
time: 168 us; the launch traced here: 165 us
  waiting for transfers between devices  59.8 us (36%)
  other arithmetic  29.5 us (18%)
  local copies, waits for them, and re-layouts  27.4 us (16%)
  starting transfers between devices  27 us (16%)
  matrix products  19.9 us (12%)
    all_to_all x1, waiting for transfers between devices, per_device(): lax.all_to_all(jnp.tile(tokens, (lax.axis_size('tensor'), 1)), 'tensor',...  27 us
    all_to_all x1, waiting for transfers between devices, per_device(): lax.all_to_all(jnp.concatenate([partials, square_columns], axis=1), 'tens...  16.4 us
    ppermute x7, waiting for transfers between devices, per_device(): lax.ppermute(jnp.take(chunks, target, axis=0), 'seq', route)  13 us
    all_to_all x1, starting transfers between devices, per_device(): lax.all_to_all(jnp.tile(tokens, (lax.axis_size('tensor'), 1)), 'tensor',...  8.22 us
    unnamed x90, local copies, waits for them, and re-layouts  7.23 us
    ppermute x7, starting transfers between devices, per_device(): lax.ppermute(jnp.take(chunks, target, axis=0), 'seq', route)  6.61 us
    another operation x9, other arithmetic  5.93 us
    dot_general x1, matrix products, per_device(): jnp.dot(gathered, weight_all, preferred_element_type=jnp.float32)  5.73 us
  transfers between devices with their start and end apart: 11, of which 9 were waited for; matrix products, arithmetic and copies ran while one was open for 21% of the time, Pallas kernels for 0%

profile of v5, /device:TPU:6, one launch (start us, length us, event | category | flops | bytes accessed | tf_op | source)
XLA Modules:
  0.0 165.2 jit_solution(11690294164509474351)
XLA Ops:
  0.6 2.8 %tile.4 = bf16[16,32,2560]{2,1,0:T(8,128)(2,1)} broadcast(bf16[32,2560]{1,0:T(8,128)(2,1)} %param.31), dimensions={1,2} | broadcast | bytes 2785280 | tf_op jit(solution)/shard_map/tile | solution.py:50
  3.4 8.2 %all-to-all-start = ((bf16[16,32,2560]{2,1,0:T(8,128)(2,1)}), bf16[16,32,2560]{2,1,0:T(8,128)(2,1)}, u32[]{:S(2)}, u32[]{:S(2)}) async-start(bf16[16,32,2560]{2,1,0:T(8,128)(2,1)} %tile.4), calls=%async_computation | async-start | bytes 5242880 | tf_op jit(solution)/shard_map/all_to_all | solution.py:49
  11.8 0.7 compare_reduce_fusion
  12.5 0.7 compare_reduce_fusion.1
  13.2 1.6 copy.192
  16.6 0.7 fusion.79
  17.3 0.7 gather_fusion
  18.0 1.1 compare_and_fusion.4
  20.2 0.7 pad_maximum_fusion.3
  21.1 1.2 compare_and_fusion.2
  22.4 0.7 fusion.82
  23.1 0.7 fusion.72
  23.8 0.8 compare_and_fusion
  24.6 27.0 %all-to-all-done = bf16[16,32,2560]{2,1,0:T(8,128)(2,1)} async-done(((bf16[16,32,2560]{2,1,0:T(8,128)(2,1)}), bf16[16,32,2560]{2,1,0:T(8,128)(2,1)}, u32[]{:S(2)}, u32[]{:S(2)}) %all-to-all-start) | async-done | bytes 2621472 | tf_op jit(solution)/shard_map/all_to_all | solution.py:49
  51.6 5.7 %fusion.28 = f32[512,901]{0,1:T(8,128)S(1)} fusion(bf16[512,2560]{1,0:T(8,128)(2,1)} %bitcast, bf16[2560,256]{0,1:T(8,128)(2,1)} %copy.192, bf16[2560,5]{0,1:T(8,128)(2,1)S(1)} %copy-done.38, bf16[2560,320]{0,1:T(8,128)(2,1)} %param.33, bf16[2560,320]{0,1:T(8,128)(2,1)} %param.32), kind=kOutput, calls=%fused_computation.37 | convolution fusion | flops 2380369920 | bytes 9079808 | tf_op jit(solution)/shard_map/dot_general | solution.py:52
  57.5 1.1 copy-done.3
  58.8 3.0 %reduce-window.20 = f32[2,5,2,128]{3,2,1,0:T(2,128)S(1)} reduce-window(f32[2,5,2,128]{3,2,1,0:T(2,128)S(1)} %copy.196, f32[]{:T(128)} %constant.266.clone.1), window={size=1x1x1x128 pad=0_0x0_0x0_0x127_0}, to_apply=%region_3.4 | reduce-window | flops 325120 | bytes 20484 | tf_op jit(solution)/shard_map/reduce-window.1
  62.9 0.9 fusion.58
  63.8 1.9 %collective-permute-start = (f32[3,576]{0,1:T(8,128)}, f32[3,576]{0,1:T(8,128)S(1)}, u32[]{:S(2)}, u32[]{:S(2)}) collective-permute-start(f32[3,576]{0,1:T(8,128)} %fusion.58), channel_id=1, source_target_pairs={{0,16},{16,32},{32,48},{48,64},{64,80},{80,96},{96,112},{1,17},{17... | collective-permute-start | bytes 20744 | tf_op jit(solution)/shard_map/ppermute | solution.py:16
  65.9 0.7 exponential_multiply_fusion
  66.6 0.6 exponential_multiply_fusion.1
  68.6 0.8 copy.232
  69.4 1.3 copy.259
  70.7 1.3 copy.208
  72.0 1.3 copy.204
  73.3 1.3 gather_fusion.1
  74.6 1.3 gather_fusion.2
  76.4 1.4 divide_multiply_fusion
  77.9 0.7 fusion.93
  79.5 1.1 reshape.590
  80.6 0.7 fusion.50
  81.4 4.1 %while.22 = (s32[]{:T(128)}, f32[5,64,128]{2,1,0:T(8,128)S(1)}, f32[5]{0:T(128)S(1)}, f32[2,5,64,128]{3,2,1,0:T(8,128)}, f32[2,5]{1,0:T(2,128)}, /*index=5*/f32[...) while((s32[]{:T(128)}, f32[5,64,128]{2,1,0:T(8,128)S(1)}, f32[5]{0:T(128)S(1)}, ...), condition=%wide.region_7.8_spmd.clone, body=%wide.region_6.7_spmd.clone.sunk | while | flops 163853 | bytes 819489 | solution.py:115
  81.4 0.7 bitcast_dynamic-update-slice_fusion.2
  82.2 1.3 dynamic_update_slice.14
  83.4 0.7 bitcast_dynamic-update-slice_fusion.2
  84.2 1.3 dynamic_update_slice.14
  85.7 1.0 tile.5
  86.7 5.7 %all-to-all-start.1 = ((bf16[8,5,80,128]{3,2,1,0:T(8,128)(2,1)}), bf16[8,5,80,128]{3,2,1,0:T(8,128)(2,1)S(1)}, u32[]{:S(2)}, u32[]{:S(2)}) async-start(bf16[8,5,80,128]{3,2,1,0:T(8,128)(2,1)} %tile.5), calls=%async_computation.1 | async-start | bytes 1638400 | tf_op jit(solution)/shard_map/all_to_all | solution.py:125
  93.0 0.9 reshape.589
  93.9 1.6 fusion.59
  95.5 5.0 %fusion.37 = f32[2,256,5,64]{1,3,2,0:T(8,128)} fusion(f32[2,256,5]{1,2,0:T(8,128)S(1)} %bitcast.128, f32[2,256,5]{1,2,0:T(8,128)} %copy.200, f32[2,256,256]{2,1,0:T(8,128)S(1)} %fusion.59, pred[2,256,256]{2,1,0:T(8,128)(4,1)} %compare_and_fusion, f32[2,256,5,64]{1,0,3,2:T(2,128)S(1)} %reshape.588), kind=kOutput, calls=%fused_computation.48 | convolution fusion | flops 506593280 | bytes 1986560 | tf_op jit(solution)/shard_map/cijh,cjhp->cihp/dot_general | solution.py:97
  100.5 3.3 %all-to-all-done.1 = bf16[8,5,80,128]{3,2,1,0:T(8,128)(2,1)S(1)} async-done(((bf16[8,5,80,128]{3,2,1,0:T(8,128)(2,1)}), bf16[8,5,80,128]{3,2,1,0:T(8,128)(2,1)S(1)}, u32[]{:S(2)}, u32[]{:S(2)}) %all-to-all-start.1) | async-done | bytes 819232 | tf_op jit(solution)/shard_map/all_to_all | solution.py:125
  104.2 2.0 %fusion.41 = f32[2,256,5,64]{1,3,2,0:T(8,128)S(1)} fusion(f32[2,256,5,64]{1,3,2,0:T(8,128)} %fusion.37, f32[2,256,5,64]{1,0,3,2:T(2,128)S(1)} %reshape.588, f32[5]{0:T(128)} %param.42, f32[2,5,64,128]{3,2,1,0:T(8,128)} %get-tuple-element.92, f32[2,256,5]{1,2,0:T(8,128)} %copy.204, f32[2,256,128,1]{1,0,2,3:T(2,128)S(1)} %bitcast.121, ...), kind=kOutput, calls=%fused_computation.51 | convolution fusion | flops 252477440 | bytes 2730044 | tf_op jit(solution)/shard_map/cin,chpn->cihp/dot_general | solution.py:139
  106.8 1.3 multiply_reduce_fusion
  108.3 1.3 fusion.68
  110.1 2.8 %convolution_convert_fusion = bf16[512,2560]{1,0:T(8,128)(2,1)S(1)} fusion(bf16[320,2560]{1,0:T(8,128)(2,1)S(1)} %copy-done, f32[320]{0:T(512)S(1)} %copy-done.39, f32[512,320]{0,1:T(8,128)S(1)} %bitcast.113, f32[512,901]{0,1:T(8,128)} %copy-done.3), kind=kOutput, calls=%fused_computation.23 | convolution fusion | flops 841318400 | bytes 5571840 | tf_op jit(solution)/shard_map/dot_general | solution.py:148
  112.8 1.8 %pad_maximum_fusion = bf16[512,2688]{1,0:T(8,128)(2,1)} fusion(bf16[512,128]{1,0:T(8,128)(2,1)S(1)} %scatter.19, bf16[512,2560]{1,0:T(8,128)(2,1)S(1)} %convolution_convert_fusion), kind=kLoop, calls=%fused_computation.24 | loop fusion | flops 5505024 | bytes 5505024 | tf_op jit(solution)/shard_map/concatenate | solution.py:157
  114.7 4.6 %all-to-all-start.2 = ((bf16[16,32,2688]{2,1,0:T(8,128)(2,1)}), bf16[16,32,2688]{2,1,0:T(8,128)(2,1)}, u32[]{:S(2)}, u32[]{:S(2)}) async-start(bf16[16,32,2688]{2,1,0:T(8,128)(2,1)} %bitcast.111), calls=%async_computation.2 | async-start | bytes 5505024 | tf_op jit(solution)/shard_map/all_to_all | solution.py:156
  119.8 0.8 fusion.3
  120.6 1.2 add_convert_fusion
  121.9 1.1 copy-done.5
  123.1 1.2 collective-permute-start.6
  124.3 2.2 %collective-permute-start.5 = (bf16[2,5,64,128]{3,2,1,0:T(8,128)(2,1)S(1)}, bf16[2,5,64,128]{3,2,1,0:T(8,128)(2,1)S(1)}, u32[]{:S(2)}, u32[]{:S(2)}) collective-permute-start(bf16[2,5,64,128]{3,2,1,0:T(8,128)(2,1)S(1)} %get-tuple-element.178), channel_id=1, source_target_pairs={{0,80},{16,96},{32,112},{48,0},{64,16},{80,32},{96,48},{112,64},{1... | collective-permute-start | bytes 491528 | tf_op jit(solution)/shard_map/ppermute | solution.py:214
  126.9 2.1 %collective-permute-start.3 = (bf16[2,5,64,128]{3,2,1,0:T(8,128)(2,1)S(1)}, bf16[2,5,64,128]{3,2,1,0:T(8,128)(2,1)S(1)}, u32[]{:S(2)}, u32[]{:S(2)}) collective-permute-start(bf16[2,5,64,128]{3,2,1,0:T(8,128)(2,1)S(1)} %get-tuple-element.180), channel_id=1, source_target_pairs={{0,48},{16,64},{32,80},{48,96},{64,112},{80,0},{96,16},{112,32},{1... | collective-permute-start | bytes 491528 | tf_op jit(solution)/shard_map/ppermute | solution.py:214
  129.0 0.7 collective-permute-start.2
  129.7 3.9 %collective-permute-done.6 = bf16[2,5,64,128]{3,2,1,0:T(8,128)(2,1)S(1)} collective-permute-done((bf16[2,5,64,128]{3,2,1,0:T(8,128)(2,1)S(1)}, bf16[2,5,64,128]{3,2,1,0:T(8,128)(2,1)S(1)}, u32[]{:S(2)}, u32[]{:S(2)}) %collective-permute-start.6) | collective-permute-done | bytes 163872 | tf_op jit(solution)/shard_map/ppermute | solution.py:214
  133.6 1.1 collective-permute-done.5
  134.7 6.2 %collective-permute-done.4 = bf16[2,5,64,128]{3,2,1,0:T(8,128)(2,1)S(1)} collective-permute-done((bf16[2,5,64,128]{3,2,1,0:T(8,128)(2,1)S(1)}, bf16[2,5,64,128]{3,2,1,0:T(8,128)(2,1)S(1)}, u32[]{:S(2)}, u32[]{:S(2)}) %collective-permute-start.4) | collective-permute-done | bytes 163872 | tf_op jit(solution)/shard_map/ppermute | solution.py:214
  141.4 0.8 collective-permute-done.2
  142.8 1.9 %convert_add_fusion = f32[2,5,64,128]{3,2,1,0:T(8,128)} fusion(bf16[2,5,64,128]{3,2,1,0:T(8,128)(2,1)S(1)} %collective-permute-done.7, bf16[2,5,64,128]{3,2,1,0:T(8,128)(2,1)S(1)} %collective-permute-done.6, bf16[2,5,64,128]{3,2,1,0:T(8,128)(2,1)S(1)} %collective-permute-done.5, bf16[2,5,64,128]{3,2,1,0:T(8,128)(2,1)S(1)} %collective-permute-done.4, ...), kind=kLoop, calls=%fused_computation.72 | loop fusion | flops 1310720 | bytes 1638405 | tf_op jit(solution)/shard_map/add | solution.py:216
  144.7 16.4 %all-to-all-done.2 = bf16[16,32,2688]{2,1,0:T(8,128)(2,1)} async-done(((bf16[16,32,2688]{2,1,0:T(8,128)(2,1)}), bf16[16,32,2688]{2,1,0:T(8,128)(2,1)}, u32[]{:S(2)}, u32[]{:S(2)}) %all-to-all-start.2) | async-done | bytes 2752544 | tf_op jit(solution)/shard_map/all_to_all | solution.py:156
  161.0 1.2 add_reduce_fusion
  162.2 2.2 %convert_reduce_fusion = f32[32,2560]{1,0:T(8,128)S(1)} fusion(bf16[16,32,2688]{2,1,0:T(8,128)(2,1)} %all-to-all-done.2), kind=kLoop, calls=%fused_computation.14 | loop fusion | flops 2539520 | bytes 2949120 | tf_op jit(solution)/shard_map/reduce_sum | solution.py:159
  164.4 0.8 multiply_convert_fusion.2
  (174 shorter events, 12.0 us)
Async XLA Ops:
  0.6 109.4 %copy-start = (bf16[320,2560]{1,0:T(8,128)(2,1)S(1)}, bf16[320,2560]{1,0:T(8,128)(2,1)}, u32[]{:S(2)}) copy-start(bf16[320,2560]{1,0:T(8,128)(2,1)} %param.44) | copy-start | bytes 4915204
  3.4 9.7 %copy-start.40 = (f32[5]{0:T(128)S(1)}, f32[5]{0:T(128)}, u32[]{:S(2)}) copy-start(f32[5]{0:T(128)} %param.41) | copy-start | bytes 64
  3.4 9.7 %copy-start.4 = (bf16[2560,256]{1,0:T(8,128)(2,1)S(1)}, bf16[2560,256]{1,0:T(8,128)(2,1)}, u32[]{:S(2)}) copy-start(bf16[2560,256]{1,0:T(8,128)(2,1)} %param.35) | copy-start | bytes 3932164
  3.4 48.2 %all-to-all-start = ((bf16[16,32,2560]{2,1,0:T(8,128)(2,1)}), bf16[16,32,2560]{2,1,0:T(8,128)(2,1)}, u32[]{:S(2)}, u32[]{:S(2)}) async-start(bf16[16,32,2560]{2,1,0:T(8,128)(2,1)} %tile.4), calls=%async_computation | async-start | bytes 5242880 | tf_op jit(solution)/shard_map/all_to_all | solution.py:49
  11.7 3.1 %copy-start.33 = (s32[16]{0:T(128)S(1)}, s32[16]{0:T(128)}, u32[]{:S(2)}) copy-start(s32[16]{0:T(128)} %param.45) | copy-start | bytes 196
  11.7 3.3 %copy-start.37 = (s32[16]{0:T(128)S(1)}, s32[16]{0:T(128)}, u32[]{:S(2)}) copy-start(s32[16]{0:T(128)} %param.46) | copy-start | bytes 196
  11.7 4.2 %copy-start.41 = (s32[16]{0:T(128)S(1)}, s32[16]{0:T(128)}, u32[]{:S(2)}) copy-start(s32[16]{0:T(128)} %param.47) | copy-start | bytes 196
  11.7 4.9 %copy-start.27 = (f32[4,320]{1,0:T(4,128)S(1)}, f32[4,320]{1,0:T(4,128)}, u32[]{:S(2)}) copy-start(f32[4,320]{1,0:T(4,128)} %param.36) | copy-start | bytes 15364
  11.7 4.9 %copy-start.29 = (f32[4,256]{1,0:T(4,128)S(1)}, f32[4,256]{1,0:T(4,128)}, u32[]{:S(2)}) copy-start(f32[4,256]{1,0:T(4,128)} %param.38) | copy-start | bytes 12292
  11.7 8.5 %copy-start.32 = (f32[320]{0:T(512)S(1)}, f32[320]{0:T(512)}, u32[]{:S(2)}) copy-start(f32[320]{0:T(512)} %param.37) | copy-start | bytes 3844
  11.7 8.5 %copy-start.34 = (f32[256]{0:T(256)S(1)}, f32[256]{0:T(256)}, u32[]{:S(2)}) copy-start(f32[256]{0:T(256)} %param.39) | copy-start | bytes 3076
  11.8 39.9 %copy-start.38 = (bf16[2560,5]{0,1:T(8,128)(2,1)S(1)}, bf16[2560,5]{0,1:T(8,128)(2,1)}, u32[]{:S(2)}) copy-start(bf16[2560,5]{0,1:T(8,128)(2,1)} %param.34) | copy-start | bytes 76804
  51.6 7.0 %copy-start.35 = (f32[5]{0:T(128)S(1)}, f32[5]{0:T(128)}, u32[]{:S(2)}) copy-start(f32[5]{0:T(128)} %param.40) | copy-start | bytes 64
  57.4 1.2 copy-start.3
  63.8 12.1 %collective-permute-start = (f32[3,576]{0,1:T(8,128)}, f32[3,576]{0,1:T(8,128)S(1)}, u32[]{:S(2)}, u32[]{:S(2)}) collective-permute-start(f32[3,576]{0,1:T(8,128)} %fusion.58), channel_id=1, source_target_pairs={{0,16},{16,32},{32,48},{48,64},{64,80},{80,96},{96,112},{1,17},{17... | collective-permute-start | bytes 20744 | tf_op jit(solution)/shard_map/ppermute | solution.py:16
  74.6 1.8 %copy-start.17 = (f32[576]{0:T(1024)S(1)}, f32[576]{0:T(1024)}, u32[]{:S(2)}) copy-start(f32[576]{0:T(1024)} %pad_maximum_fusion.3) | copy-start | bytes 6916
  74.6 1.8 %copy-start.18 = (f32[576]{0:T(1024)S(1)}, f32[576]{0:T(1024)}, u32[]{:S(2)}) copy-start(f32[576]{0:T(1024)} %get-tuple-element.138) | copy-start | bytes 6916
  74.6 1.8 %copy-start.19 = (f32[576]{0:T(1024)S(1)}, f32[576]{0:T(1024)}, u32[]{:S(2)}) copy-start(f32[576]{0:T(1024)} %get-tuple-element.139) | copy-start | bytes 6916
  74.6 1.8 %copy-start.20 = (f32[576]{0:T(1024)S(1)}, f32[576]{0:T(1024)}, u32[]{:S(2)}) copy-start(f32[576]{0:T(1024)} %get-tuple-element.140) | copy-start | bytes 6916
  74.6 1.8 %copy-start.21 = (f32[576]{0:T(1024)S(1)}, f32[576]{0:T(1024)}, u32[]{:S(2)}) copy-start(f32[576]{0:T(1024)} %get-tuple-element.141) | copy-start | bytes 6916
  74.6 1.8 %copy-start.24 = (f32[512]{0:T(512)S(1)}, f32[512]{0:T(512)}, u32[]{:S(2)}) copy-start(f32[512]{0:T(512)} %get-tuple-element.196) | copy-start | bytes 6148
  74.6 1.8 %copy-start.25 = (f32[512]{0:T(512)S(1)}, f32[512]{0:T(512)}, u32[]{:S(2)}) copy-start(f32[512]{0:T(512)} %get-tuple-element.197) | copy-start | bytes 6148
  74.6 1.8 %copy-start.26 = (f32[512]{0:T(512)S(1)}, f32[512]{0:T(512)}, u32[]{:S(2)}) copy-start(f32[512]{0:T(512)} %get-tuple-element.198) | copy-start | bytes 6148
  77.9 1.1 copy-start.1
  77.9 2.7 %copy-start.8 = (f32[2,256,5]{1,2,0:T(8,128)S(1)}, f32[2,256,5]{1,2,0:T(8,128)}, u32[]{:S(2)}) copy-start(f32[2,256,5]{1,2,0:T(8,128)} %copy.208) | copy-start | bytes 30724
  77.9 3.5 %copy-start.22 = (f32[5]{0:T(128)S(1)}, f32[5]{0:T(128)}, u32[]{:S(2)}) copy-start(f32[5]{0:T(128)} %custom-call.1) | copy-start | bytes 64
  77.9 3.5 %copy-start.23 = (f32[2,5]{1,0:T(2,128)S(1)}, f32[2,5]{1,0:T(2,128)}, u32[]{:S(2)}) copy-start(f32[2,5]{1,0:T(2,128)} %exponential_multiply_fusion.1) | copy-start | bytes 124
  86.7 17.1 %all-to-all-start.1 = ((bf16[8,5,80,128]{3,2,1,0:T(8,128)(2,1)}), bf16[8,5,80,128]{3,2,1,0:T(8,128)(2,1)S(1)}, u32[]{:S(2)}, u32[]{:S(2)}) async-start(bf16[8,5,80,128]{3,2,1,0:T(8,128)(2,1)} %tile.5), calls=%async_computation.1 | async-start | bytes 1638400 | tf_op jit(solution)/shard_map/all_to_all | solution.py:125
  95.4 8.8 %copy-start.7 = (f32[2,256,128]{1,0,2:T(2,128)S(1)}, f32[2,256,128]{1,0,2:T(2,128)}, u32[]{:S(2)}) copy-start(f32[2,256,128]{1,0,2:T(2,128)} %reshape.589) | copy-start | bytes 786436
  106.2 3.8 %copy-start.39 = (f32[320]{0:T(512)S(1)}, f32[320]{0:T(512)}, u32[]{:S(2)}) copy-start(f32[320]{0:T(512)} %param.43) | copy-start | bytes 3844
  114.6 4.7 %copy-start.28 = (f32[2,5]{1,0:T(2,128)S(1)}, f32[2,5]{1,0:T(2,128)}, u32[]{:S(2)}) copy-start(f32[2,5]{1,0:T(2,128)} %get-tuple-element.93) | copy-start | bytes 124
  114.6 4.8 %copy-start.13 = (f32[16,5]{1,0:T(8,128)S(1)}, f32[16,5]{1,0:T(8,128)}, u32[]{:S(2)}) copy-start(f32[16,5]{1,0:T(8,128)} %gather_fusion.1) | copy-start | bytes 964
  114.6 4.8 %copy-start.14 = (f32[16,5]{1,0:T(8,128)S(1)}, f32[16,5]{1,0:T(8,128)}, u32[]{:S(2)}) copy-start(f32[16,5]{1,0:T(8,128)} %gather_fusion.2) | copy-start | bytes 964
  114.6 4.8 %copy-start.30 = (pred[16]{0:T(512)(128)(4,1)S(1)}, pred[16]{0:T(512)(128)(4,1)}, u32[]{:S(2)}) copy-start(pred[16]{0:T(512)(128)(4,1)} %get-tuple-element.163) | copy-start | bytes 52
  114.6 4.8 %copy-start.31 = (pred[16]{0:T(512)(128)(4,1)S(1)}, pred[16]{0:T(512)(128)(4,1)}, u32[]{:S(2)}) copy-start(pred[16]{0:T(512)(128)(4,1)} %get-tuple-element.168) | copy-start | bytes 52
  114.6 4.8 %copy-start.36 = (pred[16]{0:T(512)(128)(4,1)S(1)}, pred[16]{0:T(512)(128)(4,1)}, u32[]{:S(2)}) copy-start(pred[16]{0:T(512)(128)(4,1)} %get-tuple-element.170) | copy-start | bytes 52
  114.6 4.9 %copy-start.9 = (f32[1,256,5]{1,2,0:T(8,128)S(1)}, f32[1,256,5]{1,2,0:T(8,128)}, u32[]{:S(2)}) copy-start(f32[1,256,5]{1,2,0:T(8,128)} %copy.258) | copy-start | bytes 15364
  114.6 4.9 %copy-start.10 = (f32[1,256,5]{1,2,0:T(8,128)S(1)}, f32[1,256,5]{1,2,0:T(8,128)}, u32[]{:S(2)}) copy-start(f32[1,256,5]{1,2,0:T(8,128)} %copy.259) | copy-start | bytes 15364
  114.7 4.9 %copy-start.11 = (f32[256,5]{0,1:T(8,128)S(1)}, f32[256,5]{0,1:T(8,128)}, u32[]{:S(2)}) copy-start(f32[256,5]{0,1:T(8,128)} %get-tuple-element.190) | copy-start | bytes 15364
  114.7 4.9 %copy-start.12 = (f32[256,5]{0,1:T(8,128)S(1)}, f32[256,5]{0,1:T(8,128)}, u32[]{:S(2)}) copy-start(f32[256,5]{0,1:T(8,128)} %get-tuple-element.191) | copy-start | bytes 15364
  114.7 4.9 %copy-start.15 = (pred[16,256]{1,0:T(8,128)(4,1)S(1)}, pred[16,256]{1,0:T(8,128)(4,1)}, u32[]{:S(2)}) copy-start(pred[16,256]{1,0:T(8,128)(4,1)} %get-tuple-element.203) | copy-start | bytes 12292
  114.7 4.9 %copy-start.16 = (pred[16,256]{1,0:T(8,128)(4,1)S(1)}, pred[16,256]{1,0:T(8,128)(4,1)}, u32[]{:S(2)}) copy-start(pred[16,256]{1,0:T(8,128)(4,1)} %get-tuple-element.204) | copy-start | bytes 12292
  114.7 5.0 %copy-start.6 = (f32[2,5,64,128]{3,2,1,0:T(8,128)S(1)}, f32[2,5,64,128]{3,2,1,0:T(8,128)}, u32[]{:S(2)}) copy-start(f32[2,5,64,128]{3,2,1,0:T(8,128)} %get-tuple-element.92) | copy-start | bytes 983044
  114.7 5.0 %copy-start.2 = (f32[512,576]{0,1:T(8,128)S(1)}, f32[512,576]{0,1:T(8,128)}, u32[]{:S(2)}) copy-start(f32[512,576]{0,1:T(8,128)} %copy-done.1) | copy-start | bytes 3538948
  114.7 46.3 %all-to-all-start.2 = ((bf16[16,32,2688]{2,1,0:T(8,128)(2,1)}), bf16[16,32,2688]{2,1,0:T(8,128)(2,1)}, u32[]{:S(2)}, u32[]{:S(2)}) async-start(bf16[16,32,2688]{2,1,0:T(8,128)(2,1)} %bitcast.111), calls=%async_computation.2 | async-start | bytes 5505024 | tf_op jit(solution)/shard_map/all_to_all | solution.py:156
  121.9 1.1 copy-start.5
  123.1 5.9 %collective-permute-start.7 = (bf16[2,5,64,128]{3,2,1,0:T(8,128)(2,1)S(1)}, bf16[2,5,64,128]{3,2,1,0:T(8,128)(2,1)S(1)}, u32[]{:S(2)}, u32[]{:S(2)}) collective-permute-start(bf16[2,5,64,128]{3,2,1,0:T(8,128)(2,1)S(1)} %get-tuple-element.176), channel_id=1, source_target_pairs={{0,112},{16,0},{32,16},{48,32},{64,48},{80,64},{96,80},{112,96},{1... | collective-permute-start | bytes 491528 | tf_op jit(solution)/shard_map/ppermute | solution.py:214
  123.1 10.5 %collective-permute-start.6 = (bf16[2,5,64,128]{3,2,1,0:T(8,128)(2,1)S(1)}, bf16[2,5,64,128]{3,2,1,0:T(8,128)(2,1)S(1)}, u32[]{:S(2)}, u32[]{:S(2)}) collective-permute-start(bf16[2,5,64,128]{3,2,1,0:T(8,128)(2,1)S(1)} %get-tuple-element.177), channel_id=1, source_target_pairs={{0,96},{16,112},{32,0},{48,16},{64,32},{80,48},{96,64},{112,80},{1... | collective-permute-start | bytes 491528 | tf_op jit(solution)/shard_map/ppermute | solution.py:214
  124.3 10.4 %collective-permute-start.5 = (bf16[2,5,64,128]{3,2,1,0:T(8,128)(2,1)S(1)}, bf16[2,5,64,128]{3,2,1,0:T(8,128)(2,1)S(1)}, u32[]{:S(2)}, u32[]{:S(2)}) collective-permute-start(bf16[2,5,64,128]{3,2,1,0:T(8,128)(2,1)S(1)} %get-tuple-element.178), channel_id=1, source_target_pairs={{0,80},{16,96},{32,112},{48,0},{64,16},{80,32},{96,48},{112,64},{1... | collective-permute-start | bytes 491528 | tf_op jit(solution)/shard_map/ppermute | solution.py:214
  126.5 14.5 %collective-permute-start.4 = (bf16[2,5,64,128]{3,2,1,0:T(8,128)(2,1)S(1)}, bf16[2,5,64,128]{3,2,1,0:T(8,128)(2,1)S(1)}, u32[]{:S(2)}, u32[]{:S(2)}) collective-permute-start(bf16[2,5,64,128]{3,2,1,0:T(8,128)(2,1)S(1)} %get-tuple-element.179), channel_id=1, source_target_pairs={{0,64},{16,80},{32,96},{48,112},{64,0},{80,16},{96,32},{112,48},{1... | collective-permute-start | bytes 491528 | tf_op jit(solution)/shard_map/ppermute | solution.py:214
  126.9 14.4 %collective-permute-start.3 = (bf16[2,5,64,128]{3,2,1,0:T(8,128)(2,1)S(1)}, bf16[2,5,64,128]{3,2,1,0:T(8,128)(2,1)S(1)}, u32[]{:S(2)}, u32[]{:S(2)}) collective-permute-start(bf16[2,5,64,128]{3,2,1,0:T(8,128)(2,1)S(1)} %get-tuple-element.180), channel_id=1, source_target_pairs={{0,48},{16,64},{32,80},{48,96},{64,112},{80,0},{96,16},{112,32},{1... | collective-permute-start | bytes 491528 | tf_op jit(solution)/shard_map/ppermute | solution.py:214
  129.0 13.2 %collective-permute-start.2 = (bf16[2,5,64,128]{3,2,1,0:T(8,128)(2,1)S(1)}, bf16[2,5,64,128]{3,2,1,0:T(8,128)(2,1)S(1)}, u32[]{:S(2)}, u32[]{:S(2)}) collective-permute-start(bf16[2,5,64,128]{3,2,1,0:T(8,128)(2,1)S(1)} %get-tuple-element.181), channel_id=1, source_target_pairs={{0,32},{16,48},{32,64},{48,80},{64,96},{80,112},{96,0},{112,16},{1... | collective-permute-start | bytes 491528 | tf_op jit(solution)/shard_map/ppermute | solution.py:214
  133.6 9.1 %collective-permute-start.1 = (bf16[2,5,64,128]{3,2,1,0:T(8,128)(2,1)S(1)}, bf16[2,5,64,128]{3,2,1,0:T(8,128)(2,1)}, u32[]{:S(2)}, u32[]{:S(2)}) collective-permute-start(bf16[2,5,64,128]{3,2,1,0:T(8,128)(2,1)S(1)} %get-tuple-element.175), channel_id=1, source_target_pairs={{0,16},{16,32},{32,48},{48,64},{64,80},{80,96},{96,112},{112,0},{1... | collective-permute-start | bytes 491528 | tf_op jit(solution)/shard_map/ppermute | solution.py:214

commit v6 on v5

--- a/solution.py
+++ b/solution.py
@@ -82,8 +82,14 @@
     keys = active[:, local_inner : local_inner + state_size].reshape(block_count, BLOCK, state_size)
     queries = active[:, local_inner + state_size :].reshape(block_count, BLOCK, state_size)
     step_size = jax.nn.softplus(raw_step + dt_bias[None, :])
-    decay_sum = jnp.cumsum(
-        (-head_rate[None, :] * step_size).reshape(block_count, BLOCK, local_heads), axis=1
+    lower_ones = (
+        jnp.arange(BLOCK)[:, None] >= jnp.arange(BLOCK)[None, :]
+    ).astype(jnp.float32)
+    decay_sum = jnp.einsum(
+        "ij,cjh->cih",
+        lower_ones,
+        (-head_rate[None, :] * step_size).reshape(block_count, BLOCK, local_heads),
+        precision=HIGHEST_PRECISION,
     )
     steps = step_size.reshape(block_count, BLOCK, local_heads)
     segs = segment.reshape(block_count, BLOCK)
@@ -102,19 +108,18 @@
     )
     passes = jnp.exp(decay_sum[:, -1, :]) * (segs[:, -1] == prior).astype(jnp.float32)[:, None]
 
-    def advance(carry, item):
-        zero_start, factor = carry
-        local_state, passing = item
-        return (
-            (passing[:, None, None] * zero_start + local_state, passing * factor),
-            (zero_start, factor),
-        )
-
     empty = jnp.zeros((local_heads, head_size, state_size), jnp.float32)
-    unit = jnp.ones((local_heads,), jnp.float32)
-    (zero_end, factor_end), (zero_starts, factors) = lax.scan(
-        advance, (empty, unit), (local, passes)
-    )
+    zero_start_list = []
+    factor_list = []
+    zero_end = empty
+    factor_end = jnp.ones((local_heads,), jnp.float32)
+    for block in range(block_count):
+        zero_start_list.append(zero_end)
+        factor_list.append(factor_end)
+        zero_end = passes[block][:, None, None] * zero_end + local[block]
+        factor_end = passes[block] * factor_end
+    zero_starts = jnp.stack(zero_start_list)
+    factors = jnp.stack(factor_list)
 
     factor_high = factor_end.astype(jnp.bfloat16)
     factor_low = (factor_end - factor_high.astype(jnp.float32)).astype(jnp.bfloat16)

time: 168 us -> 168 us (level)
  local copies, waits for them, and re-layouts: 27.4 us -> 25.1 us
    ppermute x1, waiting for transfers between devices: 0.01 us -> 2.7 us  [passed_along(): return lax.ppermute(block, axis, route)]
    dynamic_update_slice x2 -> x0, local copies, waits for them, and re-layouts: 2.52 us -> none  [per_device(): lax.scan(advance, (empty, unit), (local, passes))]
    unnamed x90 -> x62, local copies, waits for them, and re-layouts: 7.23 us -> 4.94 us
    scatter x2, local copies, waits for them, and re-layouts: 0.43 us -> 2.58 us  [per_device(): square_columns.at[:, 0].set(squares_high).at[:, 1].set(squares_low)]
    mul x5 -> x1, local copies, waits for them, and re-layouts: 2.65 us -> 0.58 us  [per_device(): zero_end = passes[block][:, None, None] * zero_end + local[block]]
    another operation x9 -> x5, other arithmetic: 5.93 us -> 4.34 us
  transfers between devices with their start and end apart: 11 -> 11, of which waited for: 9 -> 10; matrix products, arithmetic and copies ran while one was open for 21% -> 18% of each run, Pallas kernels for 0% -> 0%
where the time goes in v6:
time: 168 us; the launch traced here: 165 us
  waiting for transfers between devices  60.8 us (36%)
  other arithmetic  31 us (18%)
  starting transfers between devices  26.1 us (16%)
  local copies, waits for them, and re-layouts  25.1 us (15%)
  matrix products  21 us (12%)
    all_to_all x1, waiting for transfers between devices, per_device(): lax.all_to_all(jnp.tile(tokens, (lax.axis_size('tensor'), 1)), 'tensor',...  27.1 us
    all_to_all x1, waiting for transfers between devices, per_device(): lax.all_to_all(jnp.concatenate([partials, square_columns], axis=1), 'tens...  14.7 us
    ppermute x7, waiting for transfers between devices, per_device(): lax.ppermute(jnp.take(chunks, target, axis=0), 'seq', route)  13 us
    all_to_all x1, starting transfers between devices, per_device(): lax.all_to_all(jnp.tile(tokens, (lax.axis_size('tensor'), 1)), 'tensor',...  8.22 us
    ppermute x7, starting transfers between devices, per_device(): lax.ppermute(jnp.take(chunks, target, axis=0), 'seq', route)  6.61 us
    dot_general x1, matrix products, per_device(): jnp.dot(gathered, weight_all, preferred_element_type=jnp.float32)  5.72 us
    dot_general x1, matrix products, per_device(): jnp.einsum('cijh,cjhp->cihp', mixing, values, precision=HIGHEST_PRECISION)  4.94 us
    unnamed x62, local copies, waits for them, and re-layouts  4.94 us
  transfers between devices with their start and end apart: 11, of which 10 were waited for; matrix products, arithmetic and copies ran while one was open for 18% of the time, Pallas kernels for 0%

profile of v6, /device:TPU:6, one launch (start us, length us, event | category | flops | bytes accessed | tf_op | source)
XLA Modules:
  0.0 165.2 jit_solution(13972790463462763518)
XLA Ops:
  0.6 2.8 %tile.4 = bf16[16,32,2560]{2,1,0:T(8,128)(2,1)} broadcast(bf16[32,2560]{1,0:T(8,128)(2,1)} %param.29), dimensions={1,2} | broadcast | bytes 2785280 | tf_op jit(solution)/shard_map/tile | solution.py:50
  3.5 8.2 %all-to-all-start = ((bf16[16,32,2560]{2,1,0:T(8,128)(2,1)}), bf16[16,32,2560]{2,1,0:T(8,128)(2,1)}, u32[]{:S(2)}, u32[]{:S(2)}) async-start(bf16[16,32,2560]{2,1,0:T(8,128)(2,1)} %tile.4), calls=%async_computation | async-start | bytes 5242880 | tf_op jit(solution)/shard_map/all_to_all | solution.py:49
  11.8 0.6 compare_reduce_fusion
  12.4 0.6 compare_reduce_fusion.1
  13.1 1.6 copy.125
  16.5 0.7 fusion.82
  17.2 0.7 gather_fusion
  17.9 1.1 compare_and_fusion.4
  20.3 0.7 pad_maximum_fusion.3
  21.1 1.2 compare_and_fusion.2
  22.4 0.7 fusion.85
  23.1 0.7 fusion.74
  23.7 0.8 compare_and_fusion
  24.5 27.1 %all-to-all-done = bf16[16,32,2560]{2,1,0:T(8,128)(2,1)} async-done(((bf16[16,32,2560]{2,1,0:T(8,128)(2,1)}), bf16[16,32,2560]{2,1,0:T(8,128)(2,1)}, u32[]{:S(2)}, u32[]{:S(2)}) %all-to-all-start) | async-done | bytes 2621472 | tf_op jit(solution)/shard_map/all_to_all | solution.py:49
  51.6 5.7 %fusion.25 = f32[512,901]{0,1:T(8,128)S(1)} fusion(bf16[512,2560]{1,0:T(8,128)(2,1)} %bitcast, bf16[2560,256]{0,1:T(8,128)(2,1)} %copy.125, bf16[2560,5]{0,1:T(8,128)(2,1)S(1)} %copy-done.26, bf16[2560,320]{0,1:T(8,128)(2,1)} %param.31, bf16[2560,320]{0,1:T(8,128)(2,1)} %param.30), kind=kOutput, calls=%fused_computation.30 | convolution fusion | flops 2380369920 | bytes 9079808 | tf_op jit(solution)/shard_map/dot_general | solution.py:52
  58.6 1.9 %collective-permute-start = (f32[3,576]{0,1:T(8,128)S(1)}, f32[3,576]{0,1:T(8,128)S(1)}, u32[]{:S(2)}, u32[]{:S(2)}) collective-permute-start(f32[3,576]{0,1:T(8,128)S(1)} %fusion.56), channel_id=1, source_target_pairs={{0,16},{16,32},{32,48},{48,64},{64,80},{80,96},{96,112},{1,17},{17... | collective-permute-start | bytes 20744 | tf_op jit(solution)/shard_map/ppermute | solution.py:16
  61.9 0.7 exponential_multiply_fusion
  63.4 0.6 stack.8
  64.0 2.7 %collective-permute-done = f32[3,576]{0,1:T(8,128)S(1)} collective-permute-done((f32[3,576]{0,1:T(8,128)S(1)}, f32[3,576]{0,1:T(8,128)S(1)}, u32[]{:S(2)}, u32[]{:S(2)}) %collective-permute-start) | collective-permute-done | bytes 6944 | tf_op jit(solution)/shard_map/ppermute | solution.py:16
  67.1 2.1 %divide_multiply_fusion = f32[512,576]{0,1:T(8,128)S(1)} fusion(f32[512,256]{0,1:T(8,128)} %copy-done.1, f32[512,320]{0,1:T(8,128)S(1)} %slice.345, f32[515,576]{0,1:T(8,128)S(1)} %maximum_maximum_fusion, f32[576]{0:T(1024)} %get-tuple-element.72, f32[512]{0:T(512)} %get-tuple-element.110, f32[576]{0:T(1024)} %get-tuple-element.73, ...), kind=kLoop, calls=%fused_computation.56 | loop fusion | flops 4718592 | bytes 5915904 | tf_op jit(solution)/shard_map/jit(silu)/mul | solution.py:79
  69.3 0.8 fusion.96
  70.1 0.9 slice.356
  71.0 1.5 reshape.597
  72.5 1.8 %reshape.599 = f32[2,256,128]{1,0,2:T(2,128)} reshape(f32[512,128]{0,1:T(8,128)} %get-tuple-element.100) | data formatting | bytes 524288 | tf_op jit(solution)/shard_map/reshape | solution.py:82
  74.3 1.8 %reshape.598 = f32[2,256,128]{1,0,2:T(2,128)} reshape(f32[512,128]{0,1:T(8,128)} %get-tuple-element.99) | data formatting | bytes 524288 | tf_op jit(solution)/shard_map/reshape | solution.py:83
  76.1 1.7 %fusion.47 = f32[2,5,64,128]{3,2,1,0:T(8,128)S(1)} fusion(f32[2,256,5,64]{1,0,3,2:T(2,128)S(1)} %reshape.597, f32[2,256,5]{1,2,0:T(8,128)} %get-tuple-element.108, f32[2,256,128,1]{1,0,2,3:T(2,128)} %bitcast.113), kind=kOutput, calls=%fused_computation.61 | convolution fusion | flops 251822080 | bytes 1255424 | tf_op jit(solution)/shard_map/cjhp,cjn->chpn/dot_general | solution.py:106
  77.8 0.7 copy-done.2
  78.5 0.8 fusion.66
  79.3 1.0 tile.5
  80.3 4.8 %all-to-all-start.1 = ((bf16[8,5,80,128]{3,2,1,0:T(8,128)(2,1)}), bf16[8,5,80,128]{3,2,1,0:T(8,128)(2,1)}, u32[]{:S(2)}, u32[]{:S(2)}) async-start(bf16[8,5,80,128]{3,2,1,0:T(8,128)(2,1)} %tile.5), calls=%async_computation.1 | async-start | bytes 1638400 | tf_op jit(solution)/shard_map/all_to_all | solution.py:130
  85.1 1.7 %slice_add_fusion = f32[1,5,64,128]{3,2,1,0:T(8,128)} fusion(f32[2,5,64,128]{3,2,1,0:T(8,128)} %copy-done.2, f32[5]{0:T(128)} %get-tuple-element.122), kind=kLoop, calls=%fused_computation.100 | loop fusion | flops 40960 | bytes 327700 | tf_op jit(solution)/shard_map/add | solution.py:119
  86.8 1.7 fusion.57
  88.4 4.9 %fusion.34 = f32[2,256,5,64]{1,3,2,0:T(8,128)} fusion(f32[2,256,5]{1,2,0:T(8,128)S(1)} %bitcast.117, f32[2,256,5]{1,2,0:T(8,128)S(1)} %convolution_bitcast_fusion, f32[2,256,256]{2,1,0:T(8,128)S(1)} %fusion.57, pred[2,256,256]{2,1,0:T(8,128)(4,1)} %compare_and_fusion, f32[2,256,5,64]{1,0,3,2:T(2,128)S(1)} %reshape.597), kind=kOutput, calls=%fused_computation.41 | convolution fusion | flops 506593280 | bytes 1986560 | tf_op jit(solution)/shard_map/cijh,cjhp->cihp/dot_general | solution.py:103
  93.4 3.2 %all-to-all-done.1 = bf16[8,5,80,128]{3,2,1,0:T(8,128)(2,1)} async-done(((bf16[8,5,80,128]{3,2,1,0:T(8,128)(2,1)}), bf16[8,5,80,128]{3,2,1,0:T(8,128)(2,1)}, u32[]{:S(2)}, u32[]{:S(2)}) %all-to-all-start.1) | async-done | bytes 819232 | tf_op jit(solution)/shard_map/all_to_all | solution.py:130
  96.6 1.0 fusion.71
  97.7 1.4 select_bitcast_fusion.7
  99.2 0.7 copy-done.7
  99.8 2.0 %fusion.38 = f32[2,256,5,64]{1,3,2,0:T(8,128)S(1)} fusion(f32[2,256,5,64]{1,3,2,0:T(8,128)} %fusion.34, f32[2,256,5,64]{1,0,3,2:T(2,128)S(1)} %reshape.597, f32[5]{0:T(128)S(1)} %copy-done.25, f32[1,5,64,128]{3,2,1,0:T(8,128)} %slice_add_fusion, f32[2,256,5]{1,2,0:T(8,128)S(1)} %get-tuple-element.107, f32[2,256,128,1]{1,0,2,3:T(2,128)} %bitcast.114, ...), kind=kOutput, calls=%fused_computation.44 | convolution fusion | flops 252477440 | bytes 2566204 | tf_op jit(solution)/shard_map/cin,chpn->cihp/dot_general | solution.py:144
  102.5 1.3 multiply_reduce_fusion
  103.8 0.9 copy.139
  104.6 2.9 %fusion.70 = (bf16[512,1]{1,0:T(8,128)(2,1)}, bf16[512,1]{1,0:T(8,128)(2,1)S(1)}) fusion(f32[512,1]{1,0:T(8,128)} %copy.139, pred[]{:T(512)} %compare_reduce_fusion, pred[]{:T(512)} %compare_reduce_fusion.1), kind=kLoop, calls=%fused_computation.101 | loop fusion | flops 3072 | bytes 4098 | tf_op jit(solution)/shard_map/select.92
  107.5 0.7 scatter.16
  108.2 1.9 %scatter.19 = bf16[512,128]{1,0:T(8,128)(2,1)} dynamic-update-slice(bf16[512,128]{1,0:T(8,128)(2,1)} %scatter.16, bf16[512,1]{1,0:T(8,128)(2,1)} %get-tuple-element.101, s32[]{:T(128)} %constant.243.clone.1, s32[]{:T(128)} %constant.254.clone.1) | dynamic-update-slice | bytes 2052 | tf_op jit(solution)/shard_map/scatter | solution.py:159
  110.1 2.8 %convolution_convert_fusion = bf16[512,2560]{1,0:T(8,128)(2,1)S(1)} fusion(bf16[320,2560]{1,0:T(8,128)(2,1)S(1)} %copy-done, f32[320]{0:T(512)S(1)} %copy-done.27, f32[512,320]{0,1:T(8,128)S(1)} %bitcast.106, f32[512,901]{0,1:T(8,128)} %copy-done.4), kind=kOutput, calls=%fused_computation.16 | convolution fusion | flops 841318400 | bytes 5571840 | tf_op jit(solution)/shard_map/dot_general | solution.py:153
  112.9 1.8 %pad_maximum_fusion = bf16[512,2688]{1,0:T(8,128)(2,1)} fusion(bf16[512,128]{1,0:T(8,128)(2,1)S(1)} %copy-done.9, bf16[512,2560]{1,0:T(8,128)(2,1)S(1)} %convolution_convert_fusion), kind=kLoop, calls=%fused_computation.17 | loop fusion | flops 5505024 | bytes 5505024 | tf_op jit(solution)/shard_map/concatenate | solution.py:162
  114.8 4.6 %all-to-all-start.2 = ((bf16[16,32,2688]{2,1,0:T(8,128)(2,1)}), bf16[16,32,2688]{2,1,0:T(8,128)(2,1)}, u32[]{:S(2)}, u32[]{:S(2)}) async-start(bf16[16,32,2688]{2,1,0:T(8,128)(2,1)} %bitcast.104), calls=%async_computation.2 | async-start | bytes 5505024 | tf_op jit(solution)/shard_map/all_to_all | solution.py:161
  119.7 0.7 gather_fusion.1
  120.4 0.7 gather_fusion.2
  121.6 0.8 fusion
  122.5 1.1 add_convert_fusion
  123.6 1.1 copy-done.6
  124.8 1.2 collective-permute-start.6
  126.0 2.2 %collective-permute-start.5 = (bf16[2,5,64,128]{3,2,1,0:T(8,128)(2,1)S(1)}, bf16[2,5,64,128]{3,2,1,0:T(8,128)(2,1)S(1)}, u32[]{:S(2)}, u32[]{:S(2)}) collective-permute-start(bf16[2,5,64,128]{3,2,1,0:T(8,128)(2,1)S(1)} %get-tuple-element.93), channel_id=1, source_target_pairs={{0,80},{16,96},{32,112},{48,0},{64,16},{80,32},{96,48},{112,64},{1... | collective-permute-start | bytes 491528 | tf_op jit(solution)/shard_map/ppermute | solution.py:219
  128.7 2.1 %collective-permute-start.3 = (bf16[2,5,64,128]{3,2,1,0:T(8,128)(2,1)S(1)}, bf16[2,5,64,128]{3,2,1,0:T(8,128)(2,1)S(1)}, u32[]{:S(2)}, u32[]{:S(2)}) collective-permute-start(bf16[2,5,64,128]{3,2,1,0:T(8,128)(2,1)S(1)} %get-tuple-element.95), channel_id=1, source_target_pairs={{0,48},{16,64},{32,80},{48,96},{64,112},{80,0},{96,16},{112,32},{1... | collective-permute-start | bytes 491528 | tf_op jit(solution)/shard_map/ppermute | solution.py:219
  130.8 0.7 collective-permute-start.2
  131.4 3.9 %collective-permute-done.6 = bf16[2,5,64,128]{3,2,1,0:T(8,128)(2,1)S(1)} collective-permute-done((bf16[2,5,64,128]{3,2,1,0:T(8,128)(2,1)S(1)}, bf16[2,5,64,128]{3,2,1,0:T(8,128)(2,1)S(1)}, u32[]{:S(2)}, u32[]{:S(2)}) %collective-permute-start.6) | collective-permute-done | bytes 163872 | tf_op jit(solution)/shard_map/ppermute | solution.py:219
  135.4 1.1 collective-permute-done.5
  136.5 6.3 %collective-permute-done.4 = bf16[2,5,64,128]{3,2,1,0:T(8,128)(2,1)S(1)} collective-permute-done((bf16[2,5,64,128]{3,2,1,0:T(8,128)(2,1)S(1)}, bf16[2,5,64,128]{3,2,1,0:T(8,128)(2,1)S(1)}, u32[]{:S(2)}, u32[]{:S(2)}) %collective-permute-start.4) | collective-permute-done | bytes 163872 | tf_op jit(solution)/shard_map/ppermute | solution.py:219
  143.1 0.8 collective-permute-done.2
  144.5 1.9 %convert_add_fusion = f32[2,5,64,128]{3,2,1,0:T(8,128)} fusion(bf16[2,5,64,128]{3,2,1,0:T(8,128)(2,1)S(1)} %collective-permute-done.7, bf16[2,5,64,128]{3,2,1,0:T(8,128)(2,1)S(1)} %collective-permute-done.6, bf16[2,5,64,128]{3,2,1,0:T(8,128)(2,1)S(1)} %collective-permute-done.5, bf16[2,5,64,128]{3,2,1,0:T(8,128)(2,1)S(1)} %collective-permute-done.4, ...), kind=kLoop, calls=%fused_computation.66 | loop fusion | flops 1310720 | bytes 1638405 | tf_op jit(solution)/shard_map/add | solution.py:221
  146.4 14.7 %all-to-all-done.2 = bf16[16,32,2688]{2,1,0:T(8,128)(2,1)} async-done(((bf16[16,32,2688]{2,1,0:T(8,128)(2,1)}), bf16[16,32,2688]{2,1,0:T(8,128)(2,1)}, u32[]{:S(2)}, u32[]{:S(2)}) %all-to-all-start.2) | async-done | bytes 2752544 | tf_op jit(solution)/shard_map/all_to_all | solution.py:161
  161.1 1.2 add_reduce_fusion
  162.3 2.2 %convert_reduce_fusion = f32[32,2560]{1,0:T(8,128)S(1)} fusion(bf16[16,32,2688]{2,1,0:T(8,128)(2,1)} %all-to-all-done.2), kind=kLoop, calls=%fused_computation.7 | loop fusion | flops 2539520 | bytes 2949120 | tf_op jit(solution)/shard_map/reduce_sum | solution.py:164
  164.5 0.8 multiply_convert_fusion.2
  (121 shorter events, 10.2 us)
Async XLA Ops:
  0.6 109.5 %copy-start = (bf16[320,2560]{1,0:T(8,128)(2,1)S(1)}, bf16[320,2560]{1,0:T(8,128)(2,1)}, u32[]{:S(2)}) copy-start(bf16[320,2560]{1,0:T(8,128)(2,1)} %param.42) | copy-start | bytes 4915204
  3.5 9.6 %copy-start.28 = (f32[5]{0:T(128)S(1)}, f32[5]{0:T(128)}, u32[]{:S(2)}) copy-start(f32[5]{0:T(128)} %param.39) | copy-start | bytes 64
  3.5 9.6 %copy-start.5 = (bf16[2560,256]{1,0:T(8,128)(2,1)S(1)}, bf16[2560,256]{1,0:T(8,128)(2,1)}, u32[]{:S(2)}) copy-start(bf16[2560,256]{1,0:T(8,128)(2,1)} %param.33) | copy-start | bytes 3932164
  3.5 48.2 %all-to-all-start = ((bf16[16,32,2560]{2,1,0:T(8,128)(2,1)}), bf16[16,32,2560]{2,1,0:T(8,128)(2,1)}, u32[]{:S(2)}, u32[]{:S(2)}) async-start(bf16[16,32,2560]{2,1,0:T(8,128)(2,1)} %tile.4), calls=%async_computation | async-start | bytes 5242880 | tf_op jit(solution)/shard_map/all_to_all | solution.py:49
  11.7 3.0 %copy-start.21 = (s32[16]{0:T(128)S(1)}, s32[16]{0:T(128)}, u32[]{:S(2)}) copy-start(s32[16]{0:T(128)} %param.43) | copy-start | bytes 196
  11.7 3.2 %copy-start.24 = (s32[16]{0:T(128)S(1)}, s32[16]{0:T(128)}, u32[]{:S(2)}) copy-start(s32[16]{0:T(128)} %param.44) | copy-start | bytes 196
  11.7 4.1 %copy-start.29 = (s32[16]{0:T(128)S(1)}, s32[16]{0:T(128)}, u32[]{:S(2)}) copy-start(s32[16]{0:T(128)} %param.45) | copy-start | bytes 196
  11.7 4.8 %copy-start.13 = (f32[4,320]{1,0:T(4,128)S(1)}, f32[4,320]{1,0:T(4,128)}, u32[]{:S(2)}) copy-start(f32[4,320]{1,0:T(4,128)} %param.34) | copy-start | bytes 15364
  11.8 4.8 %copy-start.16 = (f32[4,256]{1,0:T(4,128)S(1)}, f32[4,256]{1,0:T(4,128)}, u32[]{:S(2)}) copy-start(f32[4,256]{1,0:T(4,128)} %param.36) | copy-start | bytes 12292
  11.8 8.5 %copy-start.20 = (f32[320]{0:T(512)S(1)}, f32[320]{0:T(512)}, u32[]{:S(2)}) copy-start(f32[320]{0:T(512)} %param.35) | copy-start | bytes 3844
  11.8 8.5 %copy-start.22 = (f32[256]{0:T(256)S(1)}, f32[256]{0:T(256)}, u32[]{:S(2)}) copy-start(f32[256]{0:T(256)} %param.37) | copy-start | bytes 3076
  13.1 38.6 %copy-start.26 = (bf16[2560,5]{0,1:T(8,128)(2,1)S(1)}, bf16[2560,5]{0,1:T(8,128)(2,1)}, u32[]{:S(2)}) copy-start(bf16[2560,5]{0,1:T(8,128)(2,1)} %param.32) | copy-start | bytes 76804
  57.4 1.3 copy-start.4
  57.4 0.7 copy-start.23
  57.4 9.7 %copy-start.1 = (f32[512,256]{0,1:T(8,128)}, f32[512,256]{0,1:T(8,128)S(1)}, u32[]{:S(2)}) copy-start(f32[512,256]{0,1:T(8,128)S(1)} %slice.346) | copy-start | bytes 1572868
  58.6 8.0 %collective-permute-start = (f32[3,576]{0,1:T(8,128)S(1)}, f32[3,576]{0,1:T(8,128)S(1)}, u32[]{:S(2)}, u32[]{:S(2)}) collective-permute-start(f32[3,576]{0,1:T(8,128)S(1)} %fusion.56), channel_id=1, source_target_pairs={{0,16},{16,32},{32,48},{48,64},{64,80},{80,96},{96,112},{1,17},{17... | collective-permute-start | bytes 20744 | tf_op jit(solution)/shard_map/ppermute | solution.py:16
  77.8 0.7 copy-start.2
  80.3 16.3 %all-to-all-start.1 = ((bf16[8,5,80,128]{3,2,1,0:T(8,128)(2,1)}), bf16[8,5,80,128]{3,2,1,0:T(8,128)(2,1)}, u32[]{:S(2)}, u32[]{:S(2)}) async-start(bf16[8,5,80,128]{3,2,1,0:T(8,128)(2,1)} %tile.5), calls=%async_computation.1 | async-start | bytes 1638400 | tf_op jit(solution)/shard_map/all_to_all | solution.py:130
  88.4 11.4 %copy-start.15 = (f32[2,5]{1,0:T(2,128)S(1)}, f32[2,5]{1,0:T(2,128)}, u32[]{:S(2)}) copy-start(f32[2,5]{1,0:T(2,128)} %stack.8) | copy-start | bytes 124
  88.4 11.4 %copy-start.25 = (f32[5]{0:T(128)S(1)}, f32[5]{0:T(128)}, u32[]{:S(2)}) copy-start(f32[5]{0:T(128)} %param.40) | copy-start | bytes 64
  99.2 0.7 copy-start.7
  102.4 7.7 %copy-start.27 = (f32[320]{0:T(512)S(1)}, f32[320]{0:T(512)}, u32[]{:S(2)}) copy-start(f32[320]{0:T(512)} %param.41) | copy-start | bytes 3844
  110.1 2.8 %copy-start.9 = (bf16[512,128]{1,0:T(8,128)(2,1)S(1)}, bf16[512,128]{1,0:T(8,128)(2,1)}, u32[]{:S(2)}) copy-start(bf16[512,128]{1,0:T(8,128)(2,1)} %scatter.19) | copy-start | bytes 393220
  114.7 6.3 %copy-start.14 = (pred[16]{0:T(512)(128)(4,1)S(1)}, pred[16]{0:T(512)(128)(4,1)}, u32[]{:S(2)}) copy-start(pred[16]{0:T(512)(128)(4,1)} %get-tuple-element.79) | copy-start | bytes 52
  114.7 6.3 %copy-start.17 = (pred[16]{0:T(512)(128)(4,1)S(1)}, pred[16]{0:T(512)(128)(4,1)}, u32[]{:S(2)}) copy-start(pred[16]{0:T(512)(128)(4,1)} %get-tuple-element.86) | copy-start | bytes 52
  114.7 6.4 %copy-start.18 = (f32[5]{0:T(128)S(1)}, f32[5]{0:T(128)}, u32[]{:S(2)}) copy-start(f32[5]{0:T(128)} %get-tuple-element.118) | copy-start | bytes 64
  114.7 6.4 %copy-start.19 = (pred[16]{0:T(512)(128)(4,1)S(1)}, pred[16]{0:T(512)(128)(4,1)}, u32[]{:S(2)}) copy-start(pred[16]{0:T(512)(128)(4,1)} %get-tuple-element.84) | copy-start | bytes 52
  114.7 6.5 %copy-start.10 = (f32[256,5]{0,1:T(8,128)S(1)}, f32[256,5]{0,1:T(8,128)}, u32[]{:S(2)}) copy-start(f32[256,5]{0,1:T(8,128)} %get-tuple-element.104) | copy-start | bytes 15364
  114.7 6.5 %copy-start.11 = (pred[16,256]{1,0:T(8,128)(4,1)S(1)}, pred[16,256]{1,0:T(8,128)(4,1)}, u32[]{:S(2)}) copy-start(pred[16,256]{1,0:T(8,128)(4,1)} %get-tuple-element.117) | copy-start | bytes 12292
  114.7 6.7 %copy-start.3 = (f32[2,5,64,128]{3,2,1,0:T(8,128)S(1)}, f32[2,5,64,128]{3,2,1,0:T(8,128)}, u32[]{:S(2)}) copy-start(f32[2,5,64,128]{3,2,1,0:T(8,128)} %copy-done.2) | copy-start | bytes 983044
  114.7 6.7 %copy-start.12 = (f32[5]{0:T(128)S(1)}, f32[5]{0:T(128)}, u32[]{:S(2)}) copy-start(f32[5]{0:T(128)} %get-tuple-element.122) | copy-start | bytes 64
  114.8 46.3 %all-to-all-start.2 = ((bf16[16,32,2688]{2,1,0:T(8,128)(2,1)}), bf16[16,32,2688]{2,1,0:T(8,128)(2,1)}, u32[]{:S(2)}, u32[]{:S(2)}) async-start(bf16[16,32,2688]{2,1,0:T(8,128)(2,1)} %bitcast.104), calls=%async_computation.2 | async-start | bytes 5505024 | tf_op jit(solution)/shard_map/all_to_all | solution.py:161
  121.6 0.9 copy-start.8
  123.6 1.1 copy-start.6
  124.8 5.9 %collective-permute-start.7 = (bf16[2,5,64,128]{3,2,1,0:T(8,128)(2,1)S(1)}, bf16[2,5,64,128]{3,2,1,0:T(8,128)(2,1)S(1)}, u32[]{:S(2)}, u32[]{:S(2)}) collective-permute-start(bf16[2,5,64,128]{3,2,1,0:T(8,128)(2,1)S(1)} %get-tuple-element.91), channel_id=1, source_target_pairs={{0,112},{16,0},{32,16},{48,32},{64,48},{80,64},{96,80},{112,96},{1... | collective-permute-start | bytes 491528 | tf_op jit(solution)/shard_map/ppermute | solution.py:219
  124.8 10.5 %collective-permute-start.6 = (bf16[2,5,64,128]{3,2,1,0:T(8,128)(2,1)S(1)}, bf16[2,5,64,128]{3,2,1,0:T(8,128)(2,1)S(1)}, u32[]{:S(2)}, u32[]{:S(2)}) collective-permute-start(bf16[2,5,64,128]{3,2,1,0:T(8,128)(2,1)S(1)} %get-tuple-element.92), channel_id=1, source_target_pairs={{0,96},{16,112},{32,0},{48,16},{64,32},{80,48},{96,64},{112,80},{1... | collective-permute-start | bytes 491528 | tf_op jit(solution)/shard_map/ppermute | solution.py:219
  126.0 10.4 %collective-permute-start.5 = (bf16[2,5,64,128]{3,2,1,0:T(8,128)(2,1)S(1)}, bf16[2,5,64,128]{3,2,1,0:T(8,128)(2,1)S(1)}, u32[]{:S(2)}, u32[]{:S(2)}) collective-permute-start(bf16[2,5,64,128]{3,2,1,0:T(8,128)(2,1)S(1)} %get-tuple-element.93), channel_id=1, source_target_pairs={{0,80},{16,96},{32,112},{48,0},{64,16},{80,32},{96,48},{112,64},{1... | collective-permute-start | bytes 491528 | tf_op jit(solution)/shard_map/ppermute | solution.py:219
  128.2 14.5 %collective-permute-start.4 = (bf16[2,5,64,128]{3,2,1,0:T(8,128)(2,1)S(1)}, bf16[2,5,64,128]{3,2,1,0:T(8,128)(2,1)S(1)}, u32[]{:S(2)}, u32[]{:S(2)}) collective-permute-start(bf16[2,5,64,128]{3,2,1,0:T(8,128)(2,1)S(1)} %get-tuple-element.94), channel_id=1, source_target_pairs={{0,64},{16,80},{32,96},{48,112},{64,0},{80,16},{96,32},{112,48},{1... | collective-permute-start | bytes 491528 | tf_op jit(solution)/shard_map/ppermute | solution.py:219
  128.7 14.4 %collective-permute-start.3 = (bf16[2,5,64,128]{3,2,1,0:T(8,128)(2,1)S(1)}, bf16[2,5,64,128]{3,2,1,0:T(8,128)(2,1)S(1)}, u32[]{:S(2)}, u32[]{:S(2)}) collective-permute-start(bf16[2,5,64,128]{3,2,1,0:T(8,128)(2,1)S(1)} %get-tuple-element.95), channel_id=1, source_target_pairs={{0,48},{16,64},{32,80},{48,96},{64,112},{80,0},{96,16},{112,32},{1... | collective-permute-start | bytes 491528 | tf_op jit(solution)/shard_map/ppermute | solution.py:219
  130.8 13.1 %collective-permute-start.2 = (bf16[2,5,64,128]{3,2,1,0:T(8,128)(2,1)S(1)}, bf16[2,5,64,128]{3,2,1,0:T(8,128)(2,1)S(1)}, u32[]{:S(2)}, u32[]{:S(2)}) collective-permute-start(bf16[2,5,64,128]{3,2,1,0:T(8,128)(2,1)S(1)} %get-tuple-element.96), channel_id=1, source_target_pairs={{0,32},{16,48},{32,64},{48,80},{64,96},{80,112},{96,0},{112,16},{1... | collective-permute-start | bytes 491528 | tf_op jit(solution)/shard_map/ppermute | solution.py:219
  135.4 9.1 %collective-permute-start.1 = (bf16[2,5,64,128]{3,2,1,0:T(8,128)(2,1)S(1)}, bf16[2,5,64,128]{3,2,1,0:T(8,128)(2,1)}, u32[]{:S(2)}, u32[]{:S(2)}) collective-permute-start(bf16[2,5,64,128]{3,2,1,0:T(8,128)(2,1)S(1)} %get-tuple-element.90), channel_id=1, source_target_pairs={{0,16},{16,32},{32,48},{48,64},{64,80},{80,96},{96,112},{112,0},{1... | collective-permute-start | bytes 491528 | tf_op jit(solution)/shard_map/ppermute | solution.py:219

commit v7 on v6

--- a/solution.py
+++ b/solution.py
@@ -123,9 +123,13 @@
 
     factor_high = factor_end.astype(jnp.bfloat16)
     factor_low = (factor_end - factor_high.astype(jnp.float32)).astype(jnp.bfloat16)
-    factor_rows = jnp.zeros((local_heads, 16, state_size), jnp.bfloat16)
-    factor_rows = factor_rows.at[:, 0, :].set(factor_high[:, None])
-    factor_rows = factor_rows.at[:, 1, :].set(factor_low[:, None])
+    row_slot = jnp.arange(16)[None, :, None]
+    factor_rows = jnp.where(
+        row_slot == 0,
+        factor_high[:, None, None],
+        jnp.where(row_slot == 1, factor_low[:, None, None], jnp.zeros((), jnp.bfloat16)),
+    )
+    factor_rows = jnp.broadcast_to(factor_rows, (local_heads, 16, state_size))
     packed = jnp.concatenate([zero_end.astype(jnp.bfloat16), factor_rows], axis=1)
     sent = lax.all_to_all(jnp.tile(packed[None], (seq_count, 1, 1, 1)), "seq", 0, 0, tiled=True)
     sent_states = sent[:, :, :head_size]
@@ -155,8 +159,12 @@
     )
     squares_high = squares.astype(jnp.bfloat16)
     squares_low = (squares - squares_high.astype(jnp.float32)).astype(jnp.bfloat16)
-    square_columns = jnp.zeros((row_count, 128), jnp.bfloat16)
-    square_columns = square_columns.at[:, 0].set(squares_high).at[:, 1].set(squares_low)
+    column_slot = jnp.arange(128)[None, :]
+    square_columns = jnp.where(
+        column_slot == 0,
+        squares_high[:, None],
+        jnp.where(column_slot == 1, squares_low[:, None], jnp.zeros((), jnp.bfloat16)),
+    )
     width = partials.shape[1]
     received_partials = lax.all_to_all(
         jnp.concatenate([partials, square_columns], axis=1), "tensor", 0, 0, tiled=True

time: 168 us -> 162 us (0.964)
  other arithmetic: 31 us -> 27 us
  local copies, waits for them, and re-layouts: 25.1 us -> 22.2 us
  waiting for transfers between devices: 60.8 us -> 63.1 us
    another operation x5 -> x2, other arithmetic: 4.34 us -> 0.16 us
    scatter x4 -> x0, local copies, waits for them, and re-layouts: 2.62 us -> none  [the longest x2 2.58 us: per_device(): square_columns.at[:, 0].set(squares_high).at[:, 1].set(squares_low)]
    all_to_all x1, waiting for transfers between devices: 27.1 us -> 29.4 us  [per_device(): lax.all_to_all(jnp.tile(tokens, (lax.axis_size('tensor'), 1)), 'tensor',...]
    unnamed x62 -> x68, local copies, waits for them, and re-layouts: 4.94 us -> 5.75 us
where the time goes in v7:
time: 162 us; the launch traced here: 160 us
  waiting for transfers between devices  63.1 us (39%)
  other arithmetic  27 us (17%)
  starting transfers between devices  26.1 us (16%)
  local copies, waits for them, and re-layouts  22.2 us (14%)
  matrix products  19.9 us (12%)
    all_to_all x1, waiting for transfers between devices, per_device(): lax.all_to_all(jnp.tile(tokens, (lax.axis_size('tensor'), 1)), 'tensor',...  29.4 us
    all_to_all x1, waiting for transfers between devices, per_device(): lax.all_to_all(jnp.concatenate([partials, square_columns], axis=1), 'tens...  15.5 us
    ppermute x7, waiting for transfers between devices, per_device(): lax.ppermute(jnp.take(chunks, target, axis=0), 'seq', route)  13 us
    all_to_all x1, starting transfers between devices, per_device(): lax.all_to_all(jnp.tile(tokens, (lax.axis_size('tensor'), 1)), 'tensor',...  8.22 us
    ppermute x7, starting transfers between devices, per_device(): lax.ppermute(jnp.take(chunks, target, axis=0), 'seq', route)  6.61 us
    unnamed x68, local copies, waits for them, and re-layouts  5.75 us
    dot_general x1, matrix products, per_device(): jnp.dot(gathered, weight_all, preferred_element_type=jnp.float32)  5.72 us
    dot_general x1, matrix products, per_device(): jnp.einsum('cijh,cjhp->cihp', mixing, values, precision=HIGHEST_PRECISION)  4.93 us
  transfers between devices with their start and end apart: 11, of which 10 were waited for; matrix products, arithmetic and copies ran while one was open for 18% of the time, Pallas kernels for 0%

profile of v7, /device:TPU:6, one launch (start us, length us, event | category | flops | bytes accessed | tf_op | source)
XLA Modules:
  0.0 159.5 jit_solution(16035125729579750069)
XLA Ops:
  0.6 2.8 %tile.4 = bf16[16,32,2560]{2,1,0:T(8,128)(2,1)} broadcast(bf16[32,2560]{1,0:T(8,128)(2,1)} %param.21), dimensions={1,2} | broadcast | bytes 2785280 | tf_op jit(solution)/shard_map/tile | solution.py:50
  3.4 8.2 %all-to-all-start = ((bf16[16,32,2560]{2,1,0:T(8,128)(2,1)}), bf16[16,32,2560]{2,1,0:T(8,128)(2,1)}, u32[]{:S(2)}, u32[]{:S(2)}) async-start(bf16[16,32,2560]{2,1,0:T(8,128)(2,1)} %tile.4), calls=%async_computation | async-start | bytes 5242880 | tf_op jit(solution)/shard_map/all_to_all | solution.py:49
  11.8 0.6 iota_compare_fusion.4
  12.9 1.6 %copy.117 = bf16[2560,256]{0,1:T(8,128)(2,1)} copy(bf16[2560,256]{1,0:T(8,128)(2,1)S(1)} %copy-done.6) | data formatting | bytes 2621440 | tf_op args[4]
  15.7 0.6 fusion.98
  16.4 0.7 fusion.81
  17.0 0.7 gather_fusion
  17.7 0.7 compare_and_fusion.4
  18.5 0.7 pad_maximum_fusion.3
  19.4 1.2 compare_and_fusion.2
  20.6 0.7 fusion.84
  21.4 0.8 compare_and_fusion
  22.2 29.4 %all-to-all-done = bf16[16,32,2560]{2,1,0:T(8,128)(2,1)} async-done(((bf16[16,32,2560]{2,1,0:T(8,128)(2,1)}), bf16[16,32,2560]{2,1,0:T(8,128)(2,1)}, u32[]{:S(2)}, u32[]{:S(2)}) %all-to-all-start) | async-done | bytes 2621472 | tf_op jit(solution)/shard_map/all_to_all | solution.py:49
  51.6 5.7 %fusion.25 = f32[512,901]{0,1:T(8,128)S(1)} fusion(bf16[512,2560]{1,0:T(8,128)(2,1)} %bitcast, bf16[2560,256]{0,1:T(8,128)(2,1)} %copy.117, bf16[2560,5]{0,1:T(8,128)(2,1)S(1)} %copy-done.29, bf16[2560,320]{0,1:T(8,128)(2,1)} %param.23, bf16[2560,320]{0,1:T(8,128)(2,1)} %param.22), kind=kOutput, calls=%fused_computation.30 | convolution fusion | flops 2380369920 | bytes 9079808 | tf_op jit(solution)/shard_map/dot_general | solution.py:52
  58.5 0.9 fusion.56
  59.4 1.9 %collective-permute-start = (f32[3,576]{0,1:T(8,128)}, f32[3,576]{0,1:T(8,128)S(1)}, u32[]{:S(2)}, u32[]{:S(2)}) collective-permute-start(f32[3,576]{0,1:T(8,128)} %fusion.56), channel_id=1, source_target_pairs={{0,16},{16,32},{32,48},{48,64},{64,80},{80,96},{96,112},{1,17},{17... | collective-permute-start | bytes 20744 | tf_op jit(solution)/shard_map/ppermute | solution.py:16
  61.4 0.6 multiply_convert_fusion.3
  62.7 0.7 exponential_multiply_fusion
  63.4 0.7 fusion.75
  64.1 0.6 select_select_fusion.1
  65.3 0.6 stack.8
  65.8 1.8 %collective-permute-done = f32[3,576]{0,1:T(8,128)S(1)} collective-permute-done((f32[3,576]{0,1:T(8,128)}, f32[3,576]{0,1:T(8,128)S(1)}, u32[]{:S(2)}, u32[]{:S(2)}) %collective-permute-start) | collective-permute-done | bytes 6944 | tf_op jit(solution)/shard_map/ppermute | solution.py:16
  68.1 2.1 %divide_multiply_fusion = f32[512,576]{0,1:T(8,128)S(1)} fusion(f32[512,256]{0,1:T(8,128)} %copy-done.1, f32[512,320]{0,1:T(8,128)S(1)} %slice.277, f32[515,576]{0,1:T(8,128)S(1)} %maximum_maximum_fusion, f32[576]{0:T(1024)} %get-tuple-element.24, f32[512]{0:T(512)} %get-tuple-element.62, f32[576]{0:T(1024)} %get-tuple-element.25, f32[512]{0:T(512)} %get-tuple-element.63, ...), kind=kLoop, calls=%fused_computation.56 | loop fusion | flops 4718592 | bytes 5915904 | tf_op jit(solution)/shard_map/jit(silu)/mul | solution.py:79
  70.3 0.8 fusion.95
  71.1 0.9 slice.288
  72.0 1.5 reshape.565
  73.5 1.8 %reshape.567 = f32[2,256,128]{1,0,2:T(2,128)} reshape(f32[512,128]{0,1:T(8,128)} %get-tuple-element.54) | data formatting | bytes 524288 | tf_op jit(solution)/shard_map/reshape | solution.py:82
  75.3 1.8 %reshape.566 = f32[2,256,128]{1,0,2:T(2,128)} reshape(f32[512,128]{0,1:T(8,128)} %get-tuple-element.53) | data formatting | bytes 524288 | tf_op jit(solution)/shard_map/reshape | solution.py:83
  77.1 1.7 %fusion.47 = f32[2,5,64,128]{3,2,1,0:T(8,128)S(1)} fusion(f32[2,256,5,64]{1,0,3,2:T(2,128)S(1)} %reshape.565, f32[2,256,5]{1,2,0:T(8,128)} %get-tuple-element.60, f32[2,256,128,1]{1,0,2,3:T(2,128)} %bitcast.112), kind=kOutput, calls=%fused_computation.61 | convolution fusion | flops 251822080 | bytes 1255424 | tf_op jit(solution)/shard_map/cjhp,cjn->chpn/dot_general | solution.py:106
  78.8 0.7 copy-done.2
  79.5 0.8 fusion.66
  80.3 0.7 broadcast_in_dim.148
  81.1 1.0 tile.5
  82.1 4.8 %all-to-all-start.1 = ((bf16[8,5,80,128]{3,2,1,0:T(8,128)(2,1)}), bf16[8,5,80,128]{3,2,1,0:T(8,128)(2,1)}, u32[]{:S(2)}, u32[]{:S(2)}) async-start(bf16[8,5,80,128]{3,2,1,0:T(8,128)(2,1)} %tile.5), calls=%async_computation.1 | async-start | bytes 1638400 | tf_op jit(solution)/shard_map/all_to_all | solution.py:134
  86.9 1.7 %slice_add_fusion = f32[1,5,64,128]{3,2,1,0:T(8,128)} fusion(f32[2,5,64,128]{3,2,1,0:T(8,128)} %copy-done.2, f32[5]{0:T(128)} %get-tuple-element.74), kind=kLoop, calls=%fused_computation.99 | loop fusion | flops 40960 | bytes 327700 | tf_op jit(solution)/shard_map/add | solution.py:119
  88.5 1.7 %fusion.57 = f32[2,256,256]{2,1,0:T(8,128)S(1)} fusion(f32[16,2,8,256]{3,2,1,0:T(8,128)} %bitcast.108, f32[16,2,8,256]{3,2,1,0:T(8,128)} %bitcast.107), kind=kOutput, calls=%fused_computation.74 | convolution fusion | flops 201326592 | bytes 1048576 | tf_op jit(solution)/shard_map/cin,cjn->cij/dot_general | solution.py:101
  90.2 4.9 %fusion.34 = f32[2,256,5,64]{1,3,2,0:T(8,128)} fusion(f32[2,256,5]{1,2,0:T(8,128)S(1)} %bitcast.116, f32[2,256,5]{1,2,0:T(8,128)S(1)} %convolution_bitcast_fusion, f32[2,256,256]{2,1,0:T(8,128)S(1)} %fusion.57, pred[2,256,256]{2,1,0:T(8,128)(4,1)} %compare_and_fusion, f32[2,256,5,64]{1,0,3,2:T(2,128)S(1)} %reshape.565), kind=kOutput, calls=%fused_computation.41 | convolution fusion | flops 506593280 | bytes 1986560 | tf_op jit(solution)/shard_map/cijh,cjhp->cihp/dot_general | solution.py:103
  95.1 3.3 %all-to-all-done.1 = bf16[8,5,80,128]{3,2,1,0:T(8,128)(2,1)} async-done(((bf16[8,5,80,128]{3,2,1,0:T(8,128)(2,1)}), bf16[8,5,80,128]{3,2,1,0:T(8,128)(2,1)}, u32[]{:S(2)}, u32[]{:S(2)}) %all-to-all-start.1) | async-done | bytes 819232 | tf_op jit(solution)/shard_map/all_to_all | solution.py:134
  98.4 1.0 fusion.70
  99.5 1.4 select_bitcast_fusion.7
  100.9 0.7 copy-done.8
  101.6 2.0 %fusion.38 = f32[2,256,5,64]{1,3,2,0:T(8,128)S(1)} fusion(f32[2,256,5,64]{1,3,2,0:T(8,128)} %fusion.34, f32[2,256,5,64]{1,0,3,2:T(2,128)S(1)} %reshape.565, f32[5]{0:T(128)} %param.32, f32[1,5,64,128]{3,2,1,0:T(8,128)} %slice_add_fusion, f32[2,256,5]{1,2,0:T(8,128)S(1)} %get-tuple-element.59, f32[2,256,128,1]{1,0,2,3:T(2,128)} %bitcast.113, ...), kind=kOutput, calls=%fused_computation.44 | convolution fusion | flops 252477440 | bytes 2566204 | tf_op jit(solution)/shard_map/cin,chpn->cihp/dot_general | solution.py:148
  104.2 0.9 copy-done.5
  105.4 1.7 %convolution_convert_fusion = bf16[512,2560]{1,0:T(8,128)(2,1)S(1)} fusion(bf16[320,2560]{1,0:T(8,128)(2,1)S(1)} %copy-done, f32[320]{0:T(512)S(1)} %copy-done.30, f32[512,320]{0,1:T(8,128)S(1)} %bitcast.105, f32[512,901]{0,1:T(8,128)S(1)} %copy-done.5), kind=kOutput, calls=%fused_computation.16 | convolution fusion | flops 841318400 | bytes 5572608 | tf_op jit(solution)/shard_map/dot_general | solution.py:157
  107.3 1.8 %pad_maximum_fusion = bf16[512,2688]{1,0:T(8,128)(2,1)} fusion(bf16[512,128]{1,0:T(8,128)(2,1)S(1)} %select_select_fusion, bf16[512,2560]{1,0:T(8,128)(2,1)S(1)} %convolution_convert_fusion), kind=kLoop, calls=%fused_computation.17 | loop fusion | flops 5505024 | bytes 5505024 | tf_op jit(solution)/shard_map/concatenate | solution.py:170
  109.1 4.6 %all-to-all-start.2 = ((bf16[16,32,2688]{2,1,0:T(8,128)(2,1)}), bf16[16,32,2688]{2,1,0:T(8,128)(2,1)}, u32[]{:S(2)}, u32[]{:S(2)}) async-start(bf16[16,32,2688]{2,1,0:T(8,128)(2,1)} %bitcast.103), calls=%async_computation.2 | async-start | bytes 5505024 | tf_op jit(solution)/shard_map/all_to_all | solution.py:169
  113.9 0.7 gather_fusion.2
  115.1 0.9 fusion
  116.0 1.1 add_convert_fusion
  117.1 1.1 copy-done.7
  118.3 1.2 collective-permute-start.6
  119.5 2.2 %collective-permute-start.5 = (bf16[2,5,64,128]{3,2,1,0:T(8,128)(2,1)S(1)}, bf16[2,5,64,128]{3,2,1,0:T(8,128)(2,1)S(1)}, u32[]{:S(2)}, u32[]{:S(2)}) collective-permute-start(bf16[2,5,64,128]{3,2,1,0:T(8,128)(2,1)S(1)} %get-tuple-element.47), channel_id=1, source_target_pairs={{0,80},{16,96},{32,112},{48,0},{64,16},{80,32},{96,48},{112,64},{1... | collective-permute-start | bytes 491528 | tf_op jit(solution)/shard_map/ppermute | solution.py:227
  122.2 2.1 %collective-permute-start.3 = (bf16[2,5,64,128]{3,2,1,0:T(8,128)(2,1)S(1)}, bf16[2,5,64,128]{3,2,1,0:T(8,128)(2,1)S(1)}, u32[]{:S(2)}, u32[]{:S(2)}) collective-permute-start(bf16[2,5,64,128]{3,2,1,0:T(8,128)(2,1)S(1)} %get-tuple-element.49), channel_id=1, source_target_pairs={{0,48},{16,64},{32,80},{48,96},{64,112},{80,0},{96,16},{112,32},{1... | collective-permute-start | bytes 491528 | tf_op jit(solution)/shard_map/ppermute | solution.py:227
  124.2 0.7 collective-permute-start.2
  124.9 3.9 %collective-permute-done.6 = bf16[2,5,64,128]{3,2,1,0:T(8,128)(2,1)S(1)} collective-permute-done((bf16[2,5,64,128]{3,2,1,0:T(8,128)(2,1)S(1)}, bf16[2,5,64,128]{3,2,1,0:T(8,128)(2,1)S(1)}, u32[]{:S(2)}, u32[]{:S(2)}) %collective-permute-start.6) | collective-permute-done | bytes 163872 | tf_op jit(solution)/shard_map/ppermute | solution.py:227
  128.9 1.1 collective-permute-done.5
  129.9 6.2 %collective-permute-done.4 = bf16[2,5,64,128]{3,2,1,0:T(8,128)(2,1)S(1)} collective-permute-done((bf16[2,5,64,128]{3,2,1,0:T(8,128)(2,1)S(1)}, bf16[2,5,64,128]{3,2,1,0:T(8,128)(2,1)S(1)}, u32[]{:S(2)}, u32[]{:S(2)}) %collective-permute-start.4) | collective-permute-done | bytes 163872 | tf_op jit(solution)/shard_map/ppermute | solution.py:227
  136.6 0.8 collective-permute-done.2
  137.4 0.6 collective-permute-done.1
  138.0 1.9 %convert_add_fusion = f32[2,5,64,128]{3,2,1,0:T(8,128)} fusion(bf16[2,5,64,128]{3,2,1,0:T(8,128)(2,1)S(1)} %collective-permute-done.7, bf16[2,5,64,128]{3,2,1,0:T(8,128)(2,1)S(1)} %collective-permute-done.6, bf16[2,5,64,128]{3,2,1,0:T(8,128)(2,1)S(1)} %collective-permute-done.5, bf16[2,5,64,128]{3,2,1,0:T(8,128)(2,1)S(1)} %collective-permute-done.4, ...), kind=kLoop, calls=%fused_computation.66 | loop fusion | flops 1310720 | bytes 1638405 | tf_op jit(solution)/shard_map/add | solution.py:229
  139.9 15.5 %all-to-all-done.2 = bf16[16,32,2688]{2,1,0:T(8,128)(2,1)} async-done(((bf16[16,32,2688]{2,1,0:T(8,128)(2,1)}), bf16[16,32,2688]{2,1,0:T(8,128)(2,1)}, u32[]{:S(2)}, u32[]{:S(2)}) %all-to-all-start.2) | async-done | bytes 2752544 | tf_op jit(solution)/shard_map/all_to_all | solution.py:169
  155.4 1.2 add_reduce_fusion
  156.6 2.2 %convert_reduce_fusion = f32[32,2560]{1,0:T(8,128)S(1)} fusion(bf16[16,32,2688]{2,1,0:T(8,128)(2,1)} %all-to-all-done.2), kind=kLoop, calls=%fused_computation.7 | loop fusion | flops 2539520 | bytes 2949120 | tf_op jit(solution)/shard_map/reduce_sum | solution.py:172
  158.8 0.8 multiply_convert_fusion.2
  (124 shorter events, 7.8 us)
Async XLA Ops:
  0.6 104.7 %copy-start = (bf16[320,2560]{1,0:T(8,128)(2,1)S(1)}, bf16[320,2560]{1,0:T(8,128)(2,1)}, u32[]{:S(2)}) copy-start(bf16[320,2560]{1,0:T(8,128)(2,1)} %param.34) | copy-start | bytes 4915204
  3.4 9.5 %copy-start.31 = (f32[5]{0:T(128)S(1)}, f32[5]{0:T(128)}, u32[]{:S(2)}) copy-start(f32[5]{0:T(128)} %param.31) | copy-start | bytes 64
  3.4 9.5 %copy-start.6 = (bf16[2560,256]{1,0:T(8,128)(2,1)S(1)}, bf16[2560,256]{1,0:T(8,128)(2,1)}, u32[]{:S(2)}) copy-start(bf16[2560,256]{1,0:T(8,128)(2,1)} %param.25) | copy-start | bytes 3932164
  3.4 48.2 %all-to-all-start = ((bf16[16,32,2560]{2,1,0:T(8,128)(2,1)}), bf16[16,32,2560]{2,1,0:T(8,128)(2,1)}, u32[]{:S(2)}, u32[]{:S(2)}) async-start(bf16[16,32,2560]{2,1,0:T(8,128)(2,1)} %tile.4), calls=%async_computation | async-start | bytes 5242880 | tf_op jit(solution)/shard_map/all_to_all | solution.py:49
  11.7 2.8 %copy-start.22 = (s32[16]{0:T(128)S(1)}, s32[16]{0:T(128)}, u32[]{:S(2)}) copy-start(s32[16]{0:T(128)} %param.35) | copy-start | bytes 196
  11.7 3.1 %copy-start.27 = (s32[16]{0:T(128)S(1)}, s32[16]{0:T(128)}, u32[]{:S(2)}) copy-start(s32[16]{0:T(128)} %param.36) | copy-start | bytes 196
  11.7 3.9 %copy-start.32 = (s32[16]{0:T(128)S(1)}, s32[16]{0:T(128)}, u32[]{:S(2)}) copy-start(s32[16]{0:T(128)} %param.37) | copy-start | bytes 196
  11.7 4.6 %copy-start.13 = (f32[4,320]{1,0:T(4,128)S(1)}, f32[4,320]{1,0:T(4,128)}, u32[]{:S(2)}) copy-start(f32[4,320]{1,0:T(4,128)} %param.26) | copy-start | bytes 15364
  11.7 4.6 %copy-start.18 = (f32[4,256]{1,0:T(4,128)S(1)}, f32[4,256]{1,0:T(4,128)}, u32[]{:S(2)}) copy-start(f32[4,256]{1,0:T(4,128)} %param.28) | copy-start | bytes 12292
  11.7 6.7 %copy-start.21 = (f32[320]{0:T(512)S(1)}, f32[320]{0:T(512)}, u32[]{:S(2)}) copy-start(f32[320]{0:T(512)} %param.27) | copy-start | bytes 3844
  11.8 6.7 %copy-start.23 = (f32[256]{0:T(256)S(1)}, f32[256]{0:T(256)}, u32[]{:S(2)}) copy-start(f32[256]{0:T(256)} %param.29) | copy-start | bytes 3076
  12.9 38.7 %copy-start.29 = (bf16[2560,5]{0,1:T(8,128)(2,1)S(1)}, bf16[2560,5]{0,1:T(8,128)(2,1)}, u32[]{:S(2)}) copy-start(bf16[2560,5]{0,1:T(8,128)(2,1)} %param.24) | copy-start | bytes 76804
  18.4 45.0 %copy-start.14 = (pred[16]{0:T(512)(128)(4,1)}, pred[16]{0:T(512)(128)(4,1)S(1)}, u32[]{:S(2)}) copy-start(pred[16]{0:T(512)(128)(4,1)S(1)} %get-tuple-element.31) | copy-start | bytes 52
  18.4 45.0 %copy-start.16 = (pred[16]{0:T(512)(128)(4,1)}, pred[16]{0:T(512)(128)(4,1)S(1)}, u32[]{:S(2)}) copy-start(pred[16]{0:T(512)(128)(4,1)S(1)} %get-tuple-element.38) | copy-start | bytes 52
  18.5 43.7 %copy-start.12 = (s32[1024]{0:T(1024)}, s32[1024]{0:T(1024)S(1)}, u32[]{:S(2)}) copy-start(s32[1024]{0:T(1024)S(1)} %pad_clamp_fusion) | copy-start | bytes 12292
  57.4 2.1 %copy-start.4 = (f32[512,901]{0,1:T(8,128)}, f32[512,901]{0,1:T(8,128)S(1)}, u32[]{:S(2)}) copy-start(f32[512,901]{0,1:T(8,128)S(1)} %fusion.25) | copy-start | bytes 5535748
  57.4 0.7 copy-start.24
  57.4 10.7 %copy-start.1 = (f32[512,256]{0,1:T(8,128)}, f32[512,256]{0,1:T(8,128)S(1)}, u32[]{:S(2)}) copy-start(f32[512,256]{0,1:T(8,128)S(1)} %slice.278) | copy-start | bytes 1572868
  57.4 6.6 %copy-start.28 = (pred[16]{0:T(512)(128)(4,1)S(1)}, pred[16]{0:T(512)(128)(4,1)}, u32[]{:S(2)}) copy-start(pred[16]{0:T(512)(128)(4,1)} %iota_compare_fusion.6) | copy-start | bytes 52
  59.4 8.2 %collective-permute-start = (f32[3,576]{0,1:T(8,128)}, f32[3,576]{0,1:T(8,128)S(1)}, u32[]{:S(2)}, u32[]{:S(2)}) collective-permute-start(f32[3,576]{0,1:T(8,128)} %fusion.56), channel_id=1, source_target_pairs={{0,16},{16,32},{32,48},{48,64},{64,80},{80,96},{96,112},{1,17},{17... | collective-permute-start | bytes 20744 | tf_op jit(solution)/shard_map/ppermute | solution.py:16
  78.8 0.7 copy-start.2
  82.1 16.3 %all-to-all-start.1 = ((bf16[8,5,80,128]{3,2,1,0:T(8,128)(2,1)}), bf16[8,5,80,128]{3,2,1,0:T(8,128)(2,1)}, u32[]{:S(2)}, u32[]{:S(2)}) async-start(bf16[8,5,80,128]{3,2,1,0:T(8,128)(2,1)} %tile.5), calls=%async_computation.1 | async-start | bytes 1638400 | tf_op jit(solution)/shard_map/all_to_all | solution.py:134
  100.9 0.7 copy-start.8
  103.6 1.5 copy-start.5
  103.6 1.7 %copy-start.30 = (f32[320]{0:T(512)S(1)}, f32[320]{0:T(512)}, u32[]{:S(2)}) copy-start(f32[320]{0:T(512)} %param.33) | copy-start | bytes 3844
  105.4 1.7 %copy-start.25 = (pred[128]{0:T(512)(128)(4,1)S(1)}, pred[128]{0:T(512)(128)(4,1)}, u32[]{:S(2)}) copy-start(pred[128]{0:T(512)(128)(4,1)} %get-tuple-element.83) | copy-start | bytes 388
  105.4 1.7 %copy-start.26 = (pred[128]{0:T(512)(128)(4,1)S(1)}, pred[128]{0:T(512)(128)(4,1)}, u32[]{:S(2)}) copy-start(pred[128]{0:T(512)(128)(4,1)} %get-tuple-element.84) | copy-start | bytes 388
  109.1 5.5 %copy-start.15 = (pred[16]{0:T(512)(128)(4,1)S(1)}, pred[16]{0:T(512)(128)(4,1)}, u32[]{:S(2)}) copy-start(pred[16]{0:T(512)(128)(4,1)} %copy-done.14) | copy-start | bytes 52
  109.1 5.5 %copy-start.17 = (pred[16]{0:T(512)(128)(4,1)S(1)}, pred[16]{0:T(512)(128)(4,1)}, u32[]{:S(2)}) copy-start(pred[16]{0:T(512)(128)(4,1)} %copy-done.16) | copy-start | bytes 52
  109.1 5.5 %copy-start.19 = (f32[5]{0:T(128)S(1)}, f32[5]{0:T(128)}, u32[]{:S(2)}) copy-start(f32[5]{0:T(128)} %get-tuple-element.70) | copy-start | bytes 64
  109.1 5.5 %copy-start.20 = (pred[16]{0:T(512)(128)(4,1)S(1)}, pred[16]{0:T(512)(128)(4,1)}, u32[]{:S(2)}) copy-start(pred[16]{0:T(512)(128)(4,1)} %get-tuple-element.36) | copy-start | bytes 52
  109.1 5.8 %copy-start.3 = (f32[2,5,64,128]{3,2,1,0:T(8,128)S(1)}, f32[2,5,64,128]{3,2,1,0:T(8,128)}, u32[]{:S(2)}) copy-start(f32[2,5,64,128]{3,2,1,0:T(8,128)} %copy-done.2) | copy-start | bytes 983044
  109.1 5.8 %copy-start.10 = (f32[5]{0:T(128)S(1)}, f32[5]{0:T(128)}, u32[]{:S(2)}) copy-start(f32[5]{0:T(128)} %get-tuple-element.74) | copy-start | bytes 64
  109.1 46.3 %all-to-all-start.2 = ((bf16[16,32,2688]{2,1,0:T(8,128)(2,1)}), bf16[16,32,2688]{2,1,0:T(8,128)(2,1)}, u32[]{:S(2)}, u32[]{:S(2)}) async-start(bf16[16,32,2688]{2,1,0:T(8,128)(2,1)} %bitcast.103), calls=%async_computation.2 | async-start | bytes 5505024 | tf_op jit(solution)/shard_map/all_to_all | solution.py:169
  115.1 0.9 copy-start.9
  115.1 0.9 copy-start.11
  117.1 1.1 copy-start.7
  118.3 5.9 %collective-permute-start.7 = (bf16[2,5,64,128]{3,2,1,0:T(8,128)(2,1)S(1)}, bf16[2,5,64,128]{3,2,1,0:T(8,128)(2,1)S(1)}, u32[]{:S(2)}, u32[]{:S(2)}) collective-permute-start(bf16[2,5,64,128]{3,2,1,0:T(8,128)(2,1)S(1)} %get-tuple-element.45), channel_id=1, source_target_pairs={{0,112},{16,0},{32,16},{48,32},{64,48},{80,64},{96,80},{112,96},{1... | collective-permute-start | bytes 491528 | tf_op jit(solution)/shard_map/ppermute | solution.py:227
  118.3 10.5 %collective-permute-start.6 = (bf16[2,5,64,128]{3,2,1,0:T(8,128)(2,1)S(1)}, bf16[2,5,64,128]{3,2,1,0:T(8,128)(2,1)S(1)}, u32[]{:S(2)}, u32[]{:S(2)}) collective-permute-start(bf16[2,5,64,128]{3,2,1,0:T(8,128)(2,1)S(1)} %get-tuple-element.46), channel_id=1, source_target_pairs={{0,96},{16,112},{32,0},{48,16},{64,32},{80,48},{96,64},{112,80},{1... | collective-permute-start | bytes 491528 | tf_op jit(solution)/shard_map/ppermute | solution.py:227
  119.5 10.4 %collective-permute-start.5 = (bf16[2,5,64,128]{3,2,1,0:T(8,128)(2,1)S(1)}, bf16[2,5,64,128]{3,2,1,0:T(8,128)(2,1)S(1)}, u32[]{:S(2)}, u32[]{:S(2)}) collective-permute-start(bf16[2,5,64,128]{3,2,1,0:T(8,128)(2,1)S(1)} %get-tuple-element.47), channel_id=1, source_target_pairs={{0,80},{16,96},{32,112},{48,0},{64,16},{80,32},{96,48},{112,64},{1... | collective-permute-start | bytes 491528 | tf_op jit(solution)/shard_map/ppermute | solution.py:227
  121.7 14.5 %collective-permute-start.4 = (bf16[2,5,64,128]{3,2,1,0:T(8,128)(2,1)S(1)}, bf16[2,5,64,128]{3,2,1,0:T(8,128)(2,1)S(1)}, u32[]{:S(2)}, u32[]{:S(2)}) collective-permute-start(bf16[2,5,64,128]{3,2,1,0:T(8,128)(2,1)S(1)} %get-tuple-element.48), channel_id=1, source_target_pairs={{0,64},{16,80},{32,96},{48,112},{64,0},{80,16},{96,32},{112,48},{1... | collective-permute-start | bytes 491528 | tf_op jit(solution)/shard_map/ppermute | solution.py:227
  122.2 14.4 %collective-permute-start.3 = (bf16[2,5,64,128]{3,2,1,0:T(8,128)(2,1)S(1)}, bf16[2,5,64,128]{3,2,1,0:T(8,128)(2,1)S(1)}, u32[]{:S(2)}, u32[]{:S(2)}) collective-permute-start(bf16[2,5,64,128]{3,2,1,0:T(8,128)(2,1)S(1)} %get-tuple-element.49), channel_id=1, source_target_pairs={{0,48},{16,64},{32,80},{48,96},{64,112},{80,0},{96,16},{112,32},{1... | collective-permute-start | bytes 491528 | tf_op jit(solution)/shard_map/ppermute | solution.py:227
  124.2 13.2 %collective-permute-start.2 = (bf16[2,5,64,128]{3,2,1,0:T(8,128)(2,1)S(1)}, bf16[2,5,64,128]{3,2,1,0:T(8,128)(2,1)S(1)}, u32[]{:S(2)}, u32[]{:S(2)}) collective-permute-start(bf16[2,5,64,128]{3,2,1,0:T(8,128)(2,1)S(1)} %get-tuple-element.50), channel_id=1, source_target_pairs={{0,32},{16,48},{32,64},{48,80},{64,96},{80,112},{96,0},{112,16},{1... | collective-permute-start | bytes 491528 | tf_op jit(solution)/shard_map/ppermute | solution.py:227
  128.9 9.1 %collective-permute-start.1 = (bf16[2,5,64,128]{3,2,1,0:T(8,128)(2,1)S(1)}, bf16[2,5,64,128]{3,2,1,0:T(8,128)(2,1)}, u32[]{:S(2)}, u32[]{:S(2)}) collective-permute-start(bf16[2,5,64,128]{3,2,1,0:T(8,128)(2,1)S(1)} %get-tuple-element.44), channel_id=1, source_target_pairs={{0,16},{16,32},{32,48},{48,64},{64,80},{80,96},{96,112},{112,0},{1... | collective-permute-start | bytes 491528 | tf_op jit(solution)/shard_map/ppermute | solution.py:227

commit v8 on v7

--- a/solution.py
+++ b/solution.py
@@ -8,6 +8,7 @@
 
 
 HIGHEST_PRECISION = lax.Precision.HIGHEST
+HIGH_PRECISION = lax.Precision.HIGH
 
 
 def passed_along(block, axis, distance):
@@ -98,13 +99,13 @@
     same = (segs[:, :, None] == segs[:, None, :]) & lower[None]
     spread = decay_sum[:, :, None, :] - decay_sum[:, None, :, :]
     decay = jnp.where(same[..., None], jnp.exp(jnp.minimum(spread, 0.0)), 0.0)
-    gram = jnp.einsum("cin,cjn->cij", queries, keys, precision=HIGHEST_PRECISION)
+    gram = jnp.einsum("cin,cjn->cij", queries, keys, precision=HIGH_PRECISION)
     mixing = gram[..., None] * decay * steps[:, None, :, :]
-    inner = jnp.einsum("cijh,cjhp->cihp", mixing, values, precision=HIGHEST_PRECISION)
+    inner = jnp.einsum("cijh,cjhp->cihp", mixing, values, precision=HIGH_PRECISION)
     last_match = (segs == segs[:, -1:]).astype(jnp.float32)
     weight_last = jnp.exp(decay_sum[:, -1:, :] - decay_sum) * steps * last_match[..., None]
     local = jnp.einsum(
-        "cjhp,cjn->chpn", weight_last[..., None] * values, keys, precision=HIGHEST_PRECISION
+        "cjhp,cjn->chpn", weight_last[..., None] * values, keys, precision=HIGH_PRECISION
     )
     passes = jnp.exp(decay_sum[:, -1, :]) * (segs[:, -1] == prior).astype(jnp.float32)[:, None]
 
@@ -146,7 +147,7 @@
     block_states = zero_starts + factors[:, :, None, None] * incoming[None]
     keep = jnp.exp(decay_sum) * (segs == prior[:, None]).astype(jnp.float32)[..., None]
     outer = keep[..., None] * jnp.einsum(
-        "cin,chpn->cihp", queries, block_states, precision=HIGHEST_PRECISION
+        "cin,chpn->cihp", queries, block_states, precision=HIGH_PRECISION
     )
     output = (inner + outer + skip_gain[None, None, :, None] * values).reshape(
         row_count, local_inner
@@ -169,14 +170,15 @@
     received_partials = lax.all_to_all(
         jnp.concatenate([partials, square_columns], axis=1), "tensor", 0, 0, tiled=True
     ).reshape(tensor_count, -1, width + 128)
-    reduced = jnp.sum(received_partials[:, :, :width].astype(jnp.float32), axis=0)
     totals = jnp.sum(
         received_partials[:, :, width].astype(jnp.float32)
         + received_partials[:, :, width + 1].astype(jnp.float32),
         axis=0,
     )
     scale = lax.rsqrt(totals[:, None] / (local_inner * tensor_count) + 1e-05)
-    mixed = (reduced * scale).astype(jnp.bfloat16)
+    mixed = jnp.sum(
+        received_partials[:, :, :width].astype(jnp.float32) * scale[None], axis=0
+    ).astype(jnp.bfloat16)
     request_count = lengths.shape[0]
     request_ids = jnp.arange(request_count, dtype=jnp.int32)
     slot_request = jnp.sum(

time: 162 us -> 161 us (level)
  matrix products: 19.9 us -> 17.8 us
    dot_general x3, matrix products: 8.6 us -> 6.82 us  [the longest x1 3.63 us: per_device(): jnp.einsum('cijh,cjhp->cihp', mixing, values, precision=HIGH_PRECISION)]
  transfers between devices with their start and end apart: 11 -> 11, of which waited for: 10 -> 10; matrix products, arithmetic and copies ran while one was open for 18% -> 17% of each run, Pallas kernels for 0% -> 0%
where the time goes in v8:
time: 161 us; the launch traced here: 159 us
  waiting for transfers between devices  64.6 us (40%)
  other arithmetic  27.1 us (17%)
  starting transfers between devices  26.1 us (16%)
  local copies, waits for them, and re-layouts  21.8 us (14%)
  matrix products  17.8 us (11%)
    all_to_all x1, waiting for transfers between devices, per_device(): lax.all_to_all(jnp.tile(tokens, (lax.axis_size('tensor'), 1)), 'tensor',...  29.4 us
    all_to_all x1, waiting for transfers between devices, per_device(): lax.all_to_all(jnp.concatenate([partials, square_columns], axis=1), 'tens...  15.5 us
    ppermute x7, waiting for transfers between devices, per_device(): lax.ppermute(jnp.take(chunks, target, axis=0), 'seq', route)  13 us
    all_to_all x1, starting transfers between devices, per_device(): lax.all_to_all(jnp.tile(tokens, (lax.axis_size('tensor'), 1)), 'tensor',...  8.22 us
    ppermute x7, starting transfers between devices, per_device(): lax.ppermute(jnp.take(chunks, target, axis=0), 'seq', route)  6.61 us
    dot_general x1, matrix products, per_device(): jnp.dot(gathered, weight_all, preferred_element_type=jnp.float32)  5.73 us
    unnamed x68, local copies, waits for them, and re-layouts  5.37 us
    all_to_all x1, waiting for transfers between devices, per_device(): lax.all_to_all(jnp.tile(packed[None], (seq_count, 1, 1, 1)), 'seq', 0, 0,...  4.78 us
  transfers between devices with their start and end apart: 11, of which 10 were waited for; matrix products, arithmetic and copies ran while one was open for 17% of the time, Pallas kernels for 0%

profile of v8, /device:TPU:6, one launch (start us, length us, event | category | flops | bytes accessed | tf_op | source)
XLA Modules:
  0.0 158.8 jit_solution(12867065564850639382)
XLA Ops:
  0.6 2.8 %tile.4 = bf16[16,32,2560]{2,1,0:T(8,128)(2,1)} broadcast(bf16[32,2560]{1,0:T(8,128)(2,1)} %param.21), dimensions={1,2} | broadcast | bytes 2785280 | tf_op jit(solution)/shard_map/tile | solution.py:51
  3.4 8.2 %all-to-all-start = ((bf16[16,32,2560]{2,1,0:T(8,128)(2,1)}), bf16[16,32,2560]{2,1,0:T(8,128)(2,1)}, u32[]{:S(2)}, u32[]{:S(2)}) async-start(bf16[16,32,2560]{2,1,0:T(8,128)(2,1)} %tile.4), calls=%async_computation | async-start | bytes 5242880 | tf_op jit(solution)/shard_map/all_to_all | solution.py:50
  11.8 0.6 iota_compare_fusion.4
  12.9 1.6 %copy.117 = bf16[2560,256]{0,1:T(8,128)(2,1)} copy(bf16[2560,256]{1,0:T(8,128)(2,1)S(1)} %copy-done.6) | data formatting | bytes 2621440 | tf_op args[4]
  15.7 0.6 fusion.98
  16.4 0.7 fusion.81
  17.0 0.7 gather_fusion
  17.7 0.7 compare_and_fusion.4
  18.5 0.7 pad_maximum_fusion.3
  19.4 1.2 compare_and_fusion.2
  20.6 0.7 fusion.84
  21.4 0.8 compare_and_fusion
  22.2 29.4 %all-to-all-done = bf16[16,32,2560]{2,1,0:T(8,128)(2,1)} async-done(((bf16[16,32,2560]{2,1,0:T(8,128)(2,1)}), bf16[16,32,2560]{2,1,0:T(8,128)(2,1)}, u32[]{:S(2)}, u32[]{:S(2)}) %all-to-all-start) | async-done | bytes 2621472 | tf_op jit(solution)/shard_map/all_to_all | solution.py:50
  51.6 5.7 %fusion.25 = f32[512,901]{0,1:T(8,128)S(1)} fusion(bf16[512,2560]{1,0:T(8,128)(2,1)} %bitcast, bf16[2560,256]{0,1:T(8,128)(2,1)} %copy.117, bf16[2560,5]{0,1:T(8,128)(2,1)S(1)} %copy-done.29, bf16[2560,320]{0,1:T(8,128)(2,1)} %param.23, bf16[2560,320]{0,1:T(8,128)(2,1)} %param.22), kind=kOutput, calls=%fused_computation.30 | convolution fusion | flops 2380369920 | bytes 9079808 | tf_op jit(solution)/shard_map/dot_general | solution.py:53
  57.5 1.1 copy-done.4
  59.1 0.9 fusion.56
  60.0 1.9 %collective-permute-start = (f32[3,576]{0,1:T(8,128)}, f32[3,576]{0,1:T(8,128)S(1)}, u32[]{:S(2)}, u32[]{:S(2)}) collective-permute-start(f32[3,576]{0,1:T(8,128)} %fusion.56), channel_id=1, source_target_pairs={{0,16},{16,32},{32,48},{48,64},{64,80},{80,96},{96,112},{1,17},{17... | collective-permute-start | bytes 20744 | tf_op jit(solution)/shard_map/ppermute | solution.py:17
  62.0 0.6 multiply_convert_fusion.2
  62.7 0.6 gather_fusion.1
  63.3 0.7 exponential_multiply_fusion
  64.0 0.7 fusion.75
  64.7 0.6 select_select_fusion.1
  65.8 0.6 stack.8
  66.4 1.8 %collective-permute-done = f32[3,576]{0,1:T(8,128)S(1)} collective-permute-done((f32[3,576]{0,1:T(8,128)}, f32[3,576]{0,1:T(8,128)S(1)}, u32[]{:S(2)}, u32[]{:S(2)}) %collective-permute-start) | collective-permute-done | bytes 6944 | tf_op jit(solution)/shard_map/ppermute | solution.py:17
  68.7 2.1 %divide_multiply_fusion = f32[512,576]{0,1:T(8,128)S(1)} fusion(f32[512,256]{0,1:T(8,128)} %copy-done.1, f32[512,320]{0,1:T(8,128)S(1)} %slice.277, f32[515,576]{0,1:T(8,128)S(1)} %maximum_maximum_fusion, f32[576]{0:T(1024)} %get-tuple-element.24, f32[512]{0:T(512)} %get-tuple-element.62, f32[576]{0:T(1024)} %get-tuple-element.25, f32[512]{0:T(512)} %get-tuple-element.63, ...), kind=kLoop, calls=%fused_computation.56 | loop fusion | flops 4718592 | bytes 5915904 | tf_op jit(solution)/shard_map/jit(silu)/mul | solution.py:80
  70.8 0.8 fusion.95
  71.7 0.9 slice.288
  72.6 1.5 reshape.566
  74.0 1.8 %reshape.568 = f32[2,256,128]{1,0,2:T(2,128)} reshape(f32[512,128]{0,1:T(8,128)} %get-tuple-element.54) | data formatting | bytes 524288 | tf_op jit(solution)/shard_map/reshape | solution.py:83
  75.9 1.8 %reshape.567 = f32[2,256,128]{1,0,2:T(2,128)} reshape(f32[512,128]{0,1:T(8,128)} %get-tuple-element.53) | data formatting | bytes 524288 | tf_op jit(solution)/shard_map/reshape | solution.py:84
  77.7 1.4 fusion.47
  79.1 0.7 copy-done.2
  79.8 0.8 fusion.66
  80.6 0.7 broadcast_in_dim.148
  81.3 1.0 tile.5
  82.4 4.8 %all-to-all-start.1 = ((bf16[8,5,80,128]{3,2,1,0:T(8,128)(2,1)}), bf16[8,5,80,128]{3,2,1,0:T(8,128)(2,1)}, u32[]{:S(2)}, u32[]{:S(2)}) async-start(bf16[8,5,80,128]{3,2,1,0:T(8,128)(2,1)} %tile.5), calls=%async_computation.1 | async-start | bytes 1638400 | tf_op jit(solution)/shard_map/all_to_all | solution.py:135
  87.1 1.7 %slice_add_fusion = f32[1,5,64,128]{3,2,1,0:T(8,128)} fusion(f32[2,5,64,128]{3,2,1,0:T(8,128)} %copy-done.2, f32[5]{0:T(128)} %get-tuple-element.74), kind=kLoop, calls=%fused_computation.98 | loop fusion | flops 40960 | bytes 327700 | tf_op jit(solution)/shard_map/add | solution.py:120
  88.8 1.4 fusion.57
  90.2 3.6 %fusion.34 = f32[2,256,5,64]{1,3,2,0:T(8,128)} fusion(f32[2,256,5]{1,2,0:T(8,128)S(1)} %bitcast.116, f32[2,256,5]{1,2,0:T(8,128)S(1)} %convolution_bitcast_fusion, f32[2,256,256]{2,1,0:T(8,128)S(1)} %fusion.57, pred[2,256,256]{2,1,0:T(8,128)(4,1)} %compare_and_fusion, f32[2,256,5,64]{1,0,3,2:T(2,128)S(1)} %reshape.566), kind=kOutput, calls=%fused_computation.41 | convolution fusion | flops 254935040 | bytes 1986560 | tf_op jit(solution)/shard_map/cijh,cjhp->cihp/dot_general | solution.py:104
  93.9 4.8 %all-to-all-done.1 = bf16[8,5,80,128]{3,2,1,0:T(8,128)(2,1)} async-done(((bf16[8,5,80,128]{3,2,1,0:T(8,128)(2,1)}), bf16[8,5,80,128]{3,2,1,0:T(8,128)(2,1)}, u32[]{:S(2)}, u32[]{:S(2)}) %all-to-all-start.1) | async-done | bytes 819232 | tf_op jit(solution)/shard_map/all_to_all | solution.py:135
  98.6 1.0 fusion.70
  99.8 1.4 select_bitcast_fusion.7
  101.2 0.7 copy-done.8
  101.9 1.8 %fusion.38 = f32[2,256,5,64]{1,3,2,0:T(8,128)S(1)} fusion(f32[2,256,5,64]{1,3,2,0:T(8,128)} %fusion.34, f32[2,256,5,64]{1,0,3,2:T(2,128)S(1)} %reshape.566, f32[5]{0:T(128)} %param.32, f32[1,5,64,128]{3,2,1,0:T(8,128)} %slice_add_fusion, f32[2,256,5]{1,2,0:T(8,128)S(1)} %get-tuple-element.59, f32[2,256,128,1]{1,0,2,3:T(2,128)} %bitcast.113, ...), kind=kOutput, calls=%fused_computation.44 | convolution fusion | flops 126648320 | bytes 2566204 | tf_op jit(solution)/shard_map/cin,chpn->cihp/dot_general | solution.py:149
  104.5 1.7 %convolution_convert_fusion = bf16[512,2560]{1,0:T(8,128)(2,1)S(1)} fusion(bf16[320,2560]{1,0:T(8,128)(2,1)S(1)} %copy-done, f32[320]{0:T(512)S(1)} %copy-done.30, f32[512,320]{0,1:T(8,128)S(1)} %bitcast.105, f32[512,901]{0,1:T(8,128)S(1)} %copy-done.5), kind=kOutput, calls=%fused_computation.16 | convolution fusion | flops 841318400 | bytes 5572608 | tf_op jit(solution)/shard_map/dot_general | solution.py:158
  106.4 1.8 %pad_maximum_fusion = bf16[512,2688]{1,0:T(8,128)(2,1)} fusion(bf16[512,128]{1,0:T(8,128)(2,1)S(1)} %select_select_fusion, bf16[512,2560]{1,0:T(8,128)(2,1)S(1)} %convolution_convert_fusion), kind=kLoop, calls=%fused_computation.17 | loop fusion | flops 5505024 | bytes 5505024 | tf_op jit(solution)/shard_map/concatenate | solution.py:171
  108.2 4.6 %all-to-all-start.2 = ((bf16[16,32,2688]{2,1,0:T(8,128)(2,1)}), bf16[16,32,2688]{2,1,0:T(8,128)(2,1)}, u32[]{:S(2)}, u32[]{:S(2)}) async-start(bf16[16,32,2688]{2,1,0:T(8,128)(2,1)} %bitcast.103), calls=%async_computation.2 | async-start | bytes 5505024 | tf_op jit(solution)/shard_map/all_to_all | solution.py:170
  113.0 0.7 gather_fusion.2
  114.2 0.8 fusion
  115.0 1.1 add_convert_fusion
  116.2 1.1 copy-done.7
  117.4 1.2 collective-permute-start.6
  118.6 2.2 %collective-permute-start.5 = (bf16[2,5,64,128]{3,2,1,0:T(8,128)(2,1)S(1)}, bf16[2,5,64,128]{3,2,1,0:T(8,128)(2,1)S(1)}, u32[]{:S(2)}, u32[]{:S(2)}) collective-permute-start(bf16[2,5,64,128]{3,2,1,0:T(8,128)(2,1)S(1)} %get-tuple-element.47), channel_id=1, source_target_pairs={{0,80},{16,96},{32,112},{48,0},{64,16},{80,32},{96,48},{112,64},{1... | collective-permute-start | bytes 491528 | tf_op jit(solution)/shard_map/ppermute | solution.py:229
  121.2 2.1 %collective-permute-start.3 = (bf16[2,5,64,128]{3,2,1,0:T(8,128)(2,1)S(1)}, bf16[2,5,64,128]{3,2,1,0:T(8,128)(2,1)S(1)}, u32[]{:S(2)}, u32[]{:S(2)}) collective-permute-start(bf16[2,5,64,128]{3,2,1,0:T(8,128)(2,1)S(1)} %get-tuple-element.49), channel_id=1, source_target_pairs={{0,48},{16,64},{32,80},{48,96},{64,112},{80,0},{96,16},{112,32},{1... | collective-permute-start | bytes 491528 | tf_op jit(solution)/shard_map/ppermute | solution.py:229
  123.3 0.7 collective-permute-start.2
  124.0 3.9 %collective-permute-done.6 = bf16[2,5,64,128]{3,2,1,0:T(8,128)(2,1)S(1)} collective-permute-done((bf16[2,5,64,128]{3,2,1,0:T(8,128)(2,1)S(1)}, bf16[2,5,64,128]{3,2,1,0:T(8,128)(2,1)S(1)}, u32[]{:S(2)}, u32[]{:S(2)}) %collective-permute-start.6) | collective-permute-done | bytes 163872 | tf_op jit(solution)/shard_map/ppermute | solution.py:229
  127.9 1.1 collective-permute-done.5
  129.0 6.2 %collective-permute-done.4 = bf16[2,5,64,128]{3,2,1,0:T(8,128)(2,1)S(1)} collective-permute-done((bf16[2,5,64,128]{3,2,1,0:T(8,128)(2,1)S(1)}, bf16[2,5,64,128]{3,2,1,0:T(8,128)(2,1)S(1)}, u32[]{:S(2)}, u32[]{:S(2)}) %collective-permute-start.4) | collective-permute-done | bytes 163872 | tf_op jit(solution)/shard_map/ppermute | solution.py:229
  135.6 0.8 collective-permute-done.2
  136.5 0.6 collective-permute-done.1
  137.0 1.9 %convert_add_fusion = f32[2,5,64,128]{3,2,1,0:T(8,128)} fusion(bf16[2,5,64,128]{3,2,1,0:T(8,128)(2,1)S(1)} %collective-permute-done.7, bf16[2,5,64,128]{3,2,1,0:T(8,128)(2,1)S(1)} %collective-permute-done.6, bf16[2,5,64,128]{3,2,1,0:T(8,128)(2,1)S(1)} %collective-permute-done.5, bf16[2,5,64,128]{3,2,1,0:T(8,128)(2,1)S(1)} %collective-permute-done.4, ...), kind=kLoop, calls=%fused_computation.66 | loop fusion | flops 1310720 | bytes 1638405 | tf_op jit(solution)/shard_map/add | solution.py:231
  139.0 15.5 %all-to-all-done.2 = bf16[16,32,2688]{2,1,0:T(8,128)(2,1)} async-done(((bf16[16,32,2688]{2,1,0:T(8,128)(2,1)}), bf16[16,32,2688]{2,1,0:T(8,128)(2,1)}, u32[]{:S(2)}, u32[]{:S(2)}) %all-to-all-start.2) | async-done | bytes 2752544 | tf_op jit(solution)/shard_map/all_to_all | solution.py:170
  154.5 1.2 add_reduce_fusion
  155.7 3.0 %multiply_reduce_fusion = bf16[32,2560]{1,0:T(8,128)(2,1)} fusion(bf16[16,32,2688]{2,1,0:T(8,128)(2,1)} %all-to-all-done.2, f32[32]{0:T(128)S(1)} %add_rsqrt_fusion), kind=kLoop, calls=%fused_computation.7 | loop fusion | flops 3850240 | bytes 2785408 | tf_op jit(solution)/shard_map/reduce_sum | solution.py:179
  (123 shorter events, 6.7 us)
Async XLA Ops:
  0.6 103.8 %copy-start = (bf16[320,2560]{1,0:T(8,128)(2,1)S(1)}, bf16[320,2560]{1,0:T(8,128)(2,1)}, u32[]{:S(2)}) copy-start(bf16[320,2560]{1,0:T(8,128)(2,1)} %param.34) | copy-start | bytes 4915204
  3.4 9.5 %copy-start.31 = (f32[5]{0:T(128)S(1)}, f32[5]{0:T(128)}, u32[]{:S(2)}) copy-start(f32[5]{0:T(128)} %param.31) | copy-start | bytes 64
  3.4 9.5 %copy-start.6 = (bf16[2560,256]{1,0:T(8,128)(2,1)S(1)}, bf16[2560,256]{1,0:T(8,128)(2,1)}, u32[]{:S(2)}) copy-start(bf16[2560,256]{1,0:T(8,128)(2,1)} %param.25) | copy-start | bytes 3932164
  3.4 48.2 %all-to-all-start = ((bf16[16,32,2560]{2,1,0:T(8,128)(2,1)}), bf16[16,32,2560]{2,1,0:T(8,128)(2,1)}, u32[]{:S(2)}, u32[]{:S(2)}) async-start(bf16[16,32,2560]{2,1,0:T(8,128)(2,1)} %tile.4), calls=%async_computation | async-start | bytes 5242880 | tf_op jit(solution)/shard_map/all_to_all | solution.py:50
  11.7 2.8 %copy-start.22 = (s32[16]{0:T(128)S(1)}, s32[16]{0:T(128)}, u32[]{:S(2)}) copy-start(s32[16]{0:T(128)} %param.35) | copy-start | bytes 196
  11.7 3.1 %copy-start.27 = (s32[16]{0:T(128)S(1)}, s32[16]{0:T(128)}, u32[]{:S(2)}) copy-start(s32[16]{0:T(128)} %param.36) | copy-start | bytes 196
  11.7 3.9 %copy-start.32 = (s32[16]{0:T(128)S(1)}, s32[16]{0:T(128)}, u32[]{:S(2)}) copy-start(s32[16]{0:T(128)} %param.37) | copy-start | bytes 196
  11.7 4.6 %copy-start.13 = (f32[4,320]{1,0:T(4,128)S(1)}, f32[4,320]{1,0:T(4,128)}, u32[]{:S(2)}) copy-start(f32[4,320]{1,0:T(4,128)} %param.26) | copy-start | bytes 15364
  11.7 4.6 %copy-start.18 = (f32[4,256]{1,0:T(4,128)S(1)}, f32[4,256]{1,0:T(4,128)}, u32[]{:S(2)}) copy-start(f32[4,256]{1,0:T(4,128)} %param.28) | copy-start | bytes 12292
  11.7 6.7 %copy-start.21 = (f32[320]{0:T(512)S(1)}, f32[320]{0:T(512)}, u32[]{:S(2)}) copy-start(f32[320]{0:T(512)} %param.27) | copy-start | bytes 3844
  11.8 6.7 %copy-start.23 = (f32[256]{0:T(256)S(1)}, f32[256]{0:T(256)}, u32[]{:S(2)}) copy-start(f32[256]{0:T(256)} %param.29) | copy-start | bytes 3076
  11.8 39.9 %copy-start.29 = (bf16[2560,5]{0,1:T(8,128)(2,1)S(1)}, bf16[2560,5]{0,1:T(8,128)(2,1)}, u32[]{:S(2)}) copy-start(bf16[2560,5]{0,1:T(8,128)(2,1)} %param.24) | copy-start | bytes 76804
  18.4 45.6 %copy-start.14 = (pred[16]{0:T(512)(128)(4,1)}, pred[16]{0:T(512)(128)(4,1)S(1)}, u32[]{:S(2)}) copy-start(pred[16]{0:T(512)(128)(4,1)S(1)} %get-tuple-element.31) | copy-start | bytes 52
  18.4 45.6 %copy-start.16 = (pred[16]{0:T(512)(128)(4,1)}, pred[16]{0:T(512)(128)(4,1)S(1)}, u32[]{:S(2)}) copy-start(pred[16]{0:T(512)(128)(4,1)S(1)} %get-tuple-element.38) | copy-start | bytes 52
  18.5 44.2 %copy-start.12 = (s32[1024]{0:T(1024)}, s32[1024]{0:T(1024)S(1)}, u32[]{:S(2)}) copy-start(s32[1024]{0:T(1024)S(1)} %pad_clamp_fusion) | copy-start | bytes 12292
  51.6 7.0 %copy-start.24 = (f32[5]{0:T(128)S(1)}, f32[5]{0:T(128)}, u32[]{:S(2)}) copy-start(f32[5]{0:T(128)} %param.30) | copy-start | bytes 64
  57.4 1.3 copy-start.4
  57.4 7.3 %copy-start.28 = (pred[16]{0:T(512)(128)(4,1)S(1)}, pred[16]{0:T(512)(128)(4,1)}, u32[]{:S(2)}) copy-start(pred[16]{0:T(512)(128)(4,1)} %iota_compare_fusion.6) | copy-start | bytes 52
  57.4 11.2 %copy-start.1 = (f32[512,256]{0,1:T(8,128)}, f32[512,256]{0,1:T(8,128)S(1)}, u32[]{:S(2)}) copy-start(f32[512,256]{0,1:T(8,128)S(1)} %slice.278) | copy-start | bytes 1572868
  60.0 8.2 %collective-permute-start = (f32[3,576]{0,1:T(8,128)}, f32[3,576]{0,1:T(8,128)S(1)}, u32[]{:S(2)}, u32[]{:S(2)}) collective-permute-start(f32[3,576]{0,1:T(8,128)} %fusion.56), channel_id=1, source_target_pairs={{0,16},{16,32},{32,48},{48,64},{64,80},{80,96},{96,112},{1,17},{17... | collective-permute-start | bytes 20744 | tf_op jit(solution)/shard_map/ppermute | solution.py:17
  79.1 0.7 copy-start.2
  82.4 16.3 %all-to-all-start.1 = ((bf16[8,5,80,128]{3,2,1,0:T(8,128)(2,1)}), bf16[8,5,80,128]{3,2,1,0:T(8,128)(2,1)}, u32[]{:S(2)}, u32[]{:S(2)}) async-start(bf16[8,5,80,128]{3,2,1,0:T(8,128)(2,1)} %tile.5), calls=%async_computation.1 | async-start | bytes 1638400 | tf_op jit(solution)/shard_map/all_to_all | solution.py:135
  101.2 0.7 copy-start.8
  101.2 3.0 %copy-start.5 = (f32[512,901]{0,1:T(8,128)S(1)}, f32[512,901]{0,1:T(8,128)}, u32[]{:S(2)}) copy-start(f32[512,901]{0,1:T(8,128)} %copy-done.4) | copy-start | bytes 5535748
  101.9 2.6 %copy-start.30 = (f32[320]{0:T(512)S(1)}, f32[320]{0:T(512)}, u32[]{:S(2)}) copy-start(f32[320]{0:T(512)} %param.33) | copy-start | bytes 3844
  104.5 1.7 %copy-start.25 = (pred[128]{0:T(512)(128)(4,1)S(1)}, pred[128]{0:T(512)(128)(4,1)}, u32[]{:S(2)}) copy-start(pred[128]{0:T(512)(128)(4,1)} %get-tuple-element.83) | copy-start | bytes 388
  104.5 1.7 %copy-start.26 = (pred[128]{0:T(512)(128)(4,1)S(1)}, pred[128]{0:T(512)(128)(4,1)}, u32[]{:S(2)}) copy-start(pred[128]{0:T(512)(128)(4,1)} %get-tuple-element.84) | copy-start | bytes 388
  108.2 5.5 %copy-start.15 = (pred[16]{0:T(512)(128)(4,1)S(1)}, pred[16]{0:T(512)(128)(4,1)}, u32[]{:S(2)}) copy-start(pred[16]{0:T(512)(128)(4,1)} %copy-done.14) | copy-start | bytes 52
  108.2 5.5 %copy-start.17 = (pred[16]{0:T(512)(128)(4,1)S(1)}, pred[16]{0:T(512)(128)(4,1)}, u32[]{:S(2)}) copy-start(pred[16]{0:T(512)(128)(4,1)} %copy-done.16) | copy-start | bytes 52
  108.2 5.5 %copy-start.19 = (f32[5]{0:T(128)S(1)}, f32[5]{0:T(128)}, u32[]{:S(2)}) copy-start(f32[5]{0:T(128)} %get-tuple-element.70) | copy-start | bytes 64
  108.2 5.5 %copy-start.20 = (pred[16]{0:T(512)(128)(4,1)S(1)}, pred[16]{0:T(512)(128)(4,1)}, u32[]{:S(2)}) copy-start(pred[16]{0:T(512)(128)(4,1)} %get-tuple-element.36) | copy-start | bytes 52
  108.2 5.8 %copy-start.3 = (f32[2,5,64,128]{3,2,1,0:T(8,128)S(1)}, f32[2,5,64,128]{3,2,1,0:T(8,128)}, u32[]{:S(2)}) copy-start(f32[2,5,64,128]{3,2,1,0:T(8,128)} %copy-done.2) | copy-start | bytes 983044
  108.2 5.8 %copy-start.10 = (f32[5]{0:T(128)S(1)}, f32[5]{0:T(128)}, u32[]{:S(2)}) copy-start(f32[5]{0:T(128)} %get-tuple-element.74) | copy-start | bytes 64
  108.2 46.3 %all-to-all-start.2 = ((bf16[16,32,2688]{2,1,0:T(8,128)(2,1)}), bf16[16,32,2688]{2,1,0:T(8,128)(2,1)}, u32[]{:S(2)}, u32[]{:S(2)}) async-start(bf16[16,32,2688]{2,1,0:T(8,128)(2,1)} %bitcast.103), calls=%async_computation.2 | async-start | bytes 5505024 | tf_op jit(solution)/shard_map/all_to_all | solution.py:170
  113.6 1.4 copy-start.9
  113.7 1.4 copy-start.11
  116.2 1.1 copy-start.7
  117.4 5.9 %collective-permute-start.7 = (bf16[2,5,64,128]{3,2,1,0:T(8,128)(2,1)S(1)}, bf16[2,5,64,128]{3,2,1,0:T(8,128)(2,1)S(1)}, u32[]{:S(2)}, u32[]{:S(2)}) collective-permute-start(bf16[2,5,64,128]{3,2,1,0:T(8,128)(2,1)S(1)} %get-tuple-element.45), channel_id=1, source_target_pairs={{0,112},{16,0},{32,16},{48,32},{64,48},{80,64},{96,80},{112,96},{1... | collective-permute-start | bytes 491528 | tf_op jit(solution)/shard_map/ppermute | solution.py:229
  117.4 10.5 %collective-permute-start.6 = (bf16[2,5,64,128]{3,2,1,0:T(8,128)(2,1)S(1)}, bf16[2,5,64,128]{3,2,1,0:T(8,128)(2,1)S(1)}, u32[]{:S(2)}, u32[]{:S(2)}) collective-permute-start(bf16[2,5,64,128]{3,2,1,0:T(8,128)(2,1)S(1)} %get-tuple-element.46), channel_id=1, source_target_pairs={{0,96},{16,112},{32,0},{48,16},{64,32},{80,48},{96,64},{112,80},{1... | collective-permute-start | bytes 491528 | tf_op jit(solution)/shard_map/ppermute | solution.py:229
  118.6 10.4 %collective-permute-start.5 = (bf16[2,5,64,128]{3,2,1,0:T(8,128)(2,1)S(1)}, bf16[2,5,64,128]{3,2,1,0:T(8,128)(2,1)S(1)}, u32[]{:S(2)}, u32[]{:S(2)}) collective-permute-start(bf16[2,5,64,128]{3,2,1,0:T(8,128)(2,1)S(1)} %get-tuple-element.47), channel_id=1, source_target_pairs={{0,80},{16,96},{32,112},{48,0},{64,16},{80,32},{96,48},{112,64},{1... | collective-permute-start | bytes 491528 | tf_op jit(solution)/shard_map/ppermute | solution.py:229
  120.7 14.5 %collective-permute-start.4 = (bf16[2,5,64,128]{3,2,1,0:T(8,128)(2,1)S(1)}, bf16[2,5,64,128]{3,2,1,0:T(8,128)(2,1)S(1)}, u32[]{:S(2)}, u32[]{:S(2)}) collective-permute-start(bf16[2,5,64,128]{3,2,1,0:T(8,128)(2,1)S(1)} %get-tuple-element.48), channel_id=1, source_target_pairs={{0,64},{16,80},{32,96},{48,112},{64,0},{80,16},{96,32},{112,48},{1... | collective-permute-start | bytes 491528 | tf_op jit(solution)/shard_map/ppermute | solution.py:229
  121.2 14.4 %collective-permute-start.3 = (bf16[2,5,64,128]{3,2,1,0:T(8,128)(2,1)S(1)}, bf16[2,5,64,128]{3,2,1,0:T(8,128)(2,1)S(1)}, u32[]{:S(2)}, u32[]{:S(2)}) collective-permute-start(bf16[2,5,64,128]{3,2,1,0:T(8,128)(2,1)S(1)} %get-tuple-element.49), channel_id=1, source_target_pairs={{0,48},{16,64},{32,80},{48,96},{64,112},{80,0},{96,16},{112,32},{1... | collective-permute-start | bytes 491528 | tf_op jit(solution)/shard_map/ppermute | solution.py:229
  123.3 13.2 %collective-permute-start.2 = (bf16[2,5,64,128]{3,2,1,0:T(8,128)(2,1)S(1)}, bf16[2,5,64,128]{3,2,1,0:T(8,128)(2,1)S(1)}, u32[]{:S(2)}, u32[]{:S(2)}) collective-permute-start(bf16[2,5,64,128]{3,2,1,0:T(8,128)(2,1)S(1)} %get-tuple-element.50), channel_id=1, source_target_pairs={{0,32},{16,48},{32,64},{48,80},{64,96},{80,112},{96,0},{112,16},{1... | collective-permute-start | bytes 491528 | tf_op jit(solution)/shard_map/ppermute | solution.py:229
  127.9 9.1 %collective-permute-start.1 = (bf16[2,5,64,128]{3,2,1,0:T(8,128)(2,1)S(1)}, bf16[2,5,64,128]{3,2,1,0:T(8,128)(2,1)}, u32[]{:S(2)}, u32[]{:S(2)}) collective-permute-start(bf16[2,5,64,128]{3,2,1,0:T(8,128)(2,1)S(1)} %get-tuple-element.44), channel_id=1, source_target_pairs={{0,16},{16,32},{32,48},{48,64},{64,80},{80,96},{96,112},{112,0},{1... | collective-permute-start | bytes 491528 | tf_op jit(solution)/shard_map/ppermute | solution.py:229

commit v9 on v8

--- a/solution.py
+++ b/solution.py
@@ -46,42 +46,46 @@
     state_size = in_bc.shape[1] // 2
     tensor_count = lax.axis_size("tensor")
     seq_count = lax.axis_size("seq")
-    weight_all = jnp.concatenate([in_gate, in_x, in_dt, in_bc], axis=1)
     gathered = lax.all_to_all(
         jnp.tile(tokens, (lax.axis_size("tensor"), 1)), "tensor", 0, 0, tiled=True
     )
-    projected = jnp.dot(
-        gathered,
-        weight_all,
-        preferred_element_type=jnp.float32,
-    )
-    bc_inputs = projected[:, 2 * local_inner + local_heads :]
-    gate = projected[:, :local_inner]
-    raw_step = projected[:, 2 * local_inner : 2 * local_inner + local_heads]
-    inputs = jnp.concatenate([projected[:, local_inner : 2 * local_inner], bc_inputs], axis=1)
-    row_count = projected.shape[0]
+    weight_state = jnp.concatenate([in_x, in_dt, in_bc[:, :state_size]], axis=1)
+    weight_read = jnp.concatenate([in_gate, in_bc[:, state_size:]], axis=1)
+    projected_state = jnp.dot(gathered, weight_state, preferred_element_type=jnp.float32)
+    raw_step = projected_state[:, local_inner : local_inner + local_heads]
+    state_inputs = jnp.concatenate(
+        [projected_state[:, :local_inner], projected_state[:, local_inner + local_heads :]], axis=1
+    )
+    row_count = gathered.shape[0]
     first = lax.axis_index("seq") * row_count
     starts = jnp.cumsum(lengths) - lengths
     segment = segment_of(first + jnp.arange(row_count, dtype=jnp.int32), starts)
     taps = conv_x_weight.shape[0]
-    edge = passed_along(inputs[row_count - taps + 1 :], "seq", 1)
     edge_segment = segment_of(first - taps + 1 + jnp.arange(taps - 1, dtype=jnp.int32), starts)
-    extended = jnp.concatenate([edge, inputs], axis=0)
     extended_segment = jnp.concatenate([edge_segment, segment])
-    conv_weight = jnp.concatenate([conv_x_weight, conv_bc_weight], axis=1)
-    conv_bias = jnp.concatenate([conv_x_bias, conv_bc_bias])
-    conv = jnp.zeros_like(inputs) + conv_bias[None, :]
-    for offset in range(taps):
-        match = (extended_segment[offset : offset + row_count] == segment).astype(jnp.float32)
-        conv = (
-            conv
-            + conv_weight[offset][None, :] * extended[offset : offset + row_count] * match[:, None]
-        )
-    active = jax.nn.silu(conv)
+
+    def convolved(inputs, conv_weight, conv_bias):
+        edge = passed_along(inputs[row_count - taps + 1 :], "seq", 1)
+        extended = jnp.concatenate([edge, inputs], axis=0)
+        conv = jnp.zeros_like(inputs) + conv_bias[None, :]
+        for offset in range(taps):
+            match = (extended_segment[offset : offset + row_count] == segment).astype(jnp.float32)
+            conv = (
+                conv
+                + conv_weight[offset][None, :]
+                * extended[offset : offset + row_count]
+                * match[:, None]
+            )
+        return jax.nn.silu(conv)
+
+    active = convolved(
+        state_inputs,
+        jnp.concatenate([conv_x_weight, conv_bc_weight[:, :state_size]], axis=1),
+        jnp.concatenate([conv_x_bias, conv_bc_bias[:state_size]]),
+    )
     block_count = row_count // BLOCK
     values = active[:, :local_inner].reshape(block_count, BLOCK, local_heads, head_size)
-    keys = active[:, local_inner : local_inner + state_size].reshape(block_count, BLOCK, state_size)
-    queries = active[:, local_inner + state_size :].reshape(block_count, BLOCK, state_size)
+    keys = active[:, local_inner:].reshape(block_count, BLOCK, state_size)
     step_size = jax.nn.softplus(raw_step + dt_bias[None, :])
     lower_ones = (
         jnp.arange(BLOCK)[:, None] >= jnp.arange(BLOCK)[None, :]
@@ -99,9 +103,6 @@
     same = (segs[:, :, None] == segs[:, None, :]) & lower[None]
     spread = decay_sum[:, :, None, :] - decay_sum[:, None, :, :]
     decay = jnp.where(same[..., None], jnp.exp(jnp.minimum(spread, 0.0)), 0.0)
-    gram = jnp.einsum("cin,cjn->cij", queries, keys, precision=HIGH_PRECISION)
-    mixing = gram[..., None] * decay * steps[:, None, :, :]
-    inner = jnp.einsum("cijh,cjhp->cihp", mixing, values, precision=HIGH_PRECISION)
     last_match = (segs == segs[:, -1:]).astype(jnp.float32)
     weight_last = jnp.exp(decay_sum[:, -1:, :] - decay_sum) * steps * last_match[..., None]
     local = jnp.einsum(
@@ -132,7 +133,18 @@
     )
     factor_rows = jnp.broadcast_to(factor_rows, (local_heads, 16, state_size))
     packed = jnp.concatenate([zero_end.astype(jnp.bfloat16), factor_rows], axis=1)
-    sent = lax.all_to_all(jnp.tile(packed[None], (seq_count, 1, 1, 1)), "seq", 0, 0, tiled=True)
+    relay_message, gathered_late = lax.optimization_barrier(
+        (jnp.tile(packed[None], (seq_count, 1, 1, 1)), gathered)
+    )
+    sent = lax.all_to_all(relay_message, "seq", 0, 0, tiled=True)
+    projected_read = jnp.dot(gathered_late, weight_read, preferred_element_type=jnp.float32)
+    gate = projected_read[:, :local_inner]
+    read_inputs = projected_read[:, local_inner:]
+    read_active = convolved(read_inputs, conv_bc_weight[:, state_size:], conv_bc_bias[state_size:])
+    queries = read_active.reshape(block_count, BLOCK, state_size)
+    gram = jnp.einsum("cin,cjn->cij", queries, keys, precision=HIGH_PRECISION)
+    mixing = gram[..., None] * decay * steps[:, None, :, :]
+    inner = jnp.einsum("cijh,cjhp->cihp", mixing, values, precision=HIGH_PRECISION)
     sent_states = sent[:, :, :head_size]
     sent_factors = sent[:, :, head_size, 0].astype(jnp.float32) + sent[
         :, :, head_size + 1, 0

time: 161 us -> 161 us (level)
  waiting for transfers between devices: 64.6 us -> 58.4 us
  starting transfers between devices: 26.1 us -> 29 us
  local copies, waits for them, and re-layouts: 21.8 us -> 23.7 us
    slice x3 -> x11, local copies, waits for them, and re-layouts: 0.93 us -> 5.78 us  [the longest x2 2.49 us: per_device(): weight_read = jnp.concatenate([in_gate, in_bc[:, state_size:]], axis=1)]
    unnamed x68 -> x87, local copies, waits for them, and re-layouts: 5.37 us -> 1.98 us
    all_to_all x1, waiting for transfers between devices: 4.78 us -> 2.13 us  [per_device(): sent = lax.all_to_all(relay_message, 'seq', 0, 0, tiled=True)]
    all_to_all x1, waiting for transfers between devices: 29.4 us -> 26.8 us  [per_device(): lax.all_to_all(jnp.tile(tokens, (lax.axis_size('tensor'), 1)), 'tensor',...]
    mul x1 -> x3, other arithmetic: 2.15 us -> 4.55 us  [the longest x2 4.04 us: convolved(): return jax.nn.silu(conv)]
    ppermute x1 -> x2, starting transfers between devices: 1.91 us -> 3.83 us  [passed_along(): return lax.ppermute(block, axis, route)]
    dot_general x1 -> x2, matrix products: 5.73 us -> 6.96 us  [the longest x1 3.85 us: per_device(): jnp.dot(gathered, weight_state, preferred_element_type=jnp.float32)]
  transfers between devices with their start and end apart: 11 -> 12, of which waited for: 10 -> 10; matrix products, arithmetic and copies ran while one was open for 17% -> 21% of each run, Pallas kernels for 0% -> 0%
where the time goes in v9:
time: 161 us; the launch traced here: 158 us
  waiting for transfers between devices  58.4 us (36%)
  starting transfers between devices  29 us (18%)
  other arithmetic  26.6 us (17%)
  local copies, waits for them, and re-layouts  23.7 us (15%)
  matrix products  19.3 us (12%)
    all_to_all x1, waiting for transfers between devices, per_device(): lax.all_to_all(jnp.tile(tokens, (lax.axis_size('tensor'), 1)), 'tensor',...  26.8 us
    all_to_all x1, waiting for transfers between devices, per_device(): lax.all_to_all(jnp.concatenate([partials, square_columns], axis=1), 'tens...  15.5 us
    ppermute x7, waiting for transfers between devices, per_device(): lax.ppermute(jnp.take(chunks, target, axis=0), 'seq', route)  13 us
    all_to_all x1, starting transfers between devices, per_device(): lax.all_to_all(jnp.tile(tokens, (lax.axis_size('tensor'), 1)), 'tensor',...  8.22 us
    ppermute x7, starting transfers between devices, per_device(): lax.ppermute(jnp.take(chunks, target, axis=0), 'seq', route)  6.61 us
    all_to_all x1, starting transfers between devices, per_device(): sent = lax.all_to_all(relay_message, 'seq', 0, 0, tiled=True)  5.88 us
    all_to_all x1, starting transfers between devices, per_device(): lax.all_to_all(jnp.concatenate([partials, square_columns], axis=1), 'tens...  4.48 us
    mul x2, other arithmetic, convolved(): return jax.nn.silu(conv)  4.04 us
  transfers between devices with their start and end apart: 12, of which 10 were waited for; matrix products, arithmetic and copies ran while one was open for 21% of the time, Pallas kernels for 0%

profile of v9, /device:TPU:6, one launch (start us, length us, event | category | flops | bytes accessed | tf_op | source)
XLA Modules:
  0.0 158.4 jit_solution(6976407166140580740)
XLA Ops:
  0.6 2.8 %tile.4 = bf16[16,32,2560]{2,1,0:T(8,128)(2,1)} broadcast(bf16[32,2560]{1,0:T(8,128)(2,1)} %param.21), dimensions={1,2} | broadcast | bytes 2785280 | tf_op jit(solution)/shard_map/tile | solution.py:50
  3.5 8.2 %all-to-all-start = ((bf16[16,32,2560]{2,1,0:T(8,128)(2,1)}), bf16[16,32,2560]{2,1,0:T(8,128)(2,1)}, u32[]{:S(2)}, u32[]{:S(2)}) async-start(bf16[16,32,2560]{2,1,0:T(8,128)(2,1)} %tile.4), calls=%async_computation | async-start | bytes 5242880 | tf_op jit(solution)/shard_map/all_to_all | solution.py:49
  11.8 0.6 iota_compare_fusion.4
  13.0 1.4 fusion.105
  14.4 1.1 copy.122
  17.9 1.1 copy.129
  19.1 0.7 gather_fusion
  19.8 0.7 compare_and_fusion.4
  20.7 0.7 fusion.92
  21.4 1.2 compare_and_fusion.2
  23.4 0.7 fusion.87
  24.0 0.8 compare_and_fusion
  24.8 26.8 %all-to-all-done = bf16[16,32,2560]{2,1,0:T(8,128)(2,1)} async-done(((bf16[16,32,2560]{2,1,0:T(8,128)(2,1)}), bf16[16,32,2560]{2,1,0:T(8,128)(2,1)}, u32[]{:S(2)}, u32[]{:S(2)}) %all-to-all-start) | async-done | bytes 2621472 | tf_op jit(solution)/shard_map/all_to_all | solution.py:49
  51.7 3.9 %fusion.27 = f32[512,453]{0,1:T(8,128)S(1)} fusion(bf16[512,2560]{1,0:T(8,128)(2,1)} %bitcast.1, bf16[2560,128]{0,1:T(8,128)(2,1)} %copy.122, bf16[2560,5]{0,1:T(8,128)(2,1)S(1)} %copy-done.39, bf16[2560,320]{0,1:T(8,128)(2,1)} %param.23), kind=kOutput, calls=%fused_computation.32 | convolution fusion | flops 1194470400 | bytes 5868544 | tf_op jit(solution)/shard_map/dot_general | solution.py:54
  56.1 0.6 slice_bitcast_fusion.6
  56.9 1.9 %collective-permute-start = (f32[3,448]{0,1:T(8,128)S(1)}, f32[3,448]{0,1:T(8,128)S(1)}, u32[]{:S(2)}, u32[]{:S(2)}) collective-permute-start(f32[3,448]{0,1:T(8,128)S(1)} %fusion.78), channel_id=1, source_target_pairs={{0,16},{16,32},{32,48},{48,64},{64,80},{80,96},{96,112},{1,17},{17... | collective-permute-start | bytes 16136 | tf_op jit(solution)/shard_map/ppermute | solution.py:17
  60.1 0.7 exponential_multiply_fusion
  60.8 0.7 fusion.89
  61.5 0.7 select_select_fusion.1
  62.7 0.6 stack.8
  63.3 0.9 collective-permute-done
  64.6 1.6 %divide_multiply_fusion = f32[512,448]{0,1:T(8,128)S(1)} fusion(f32[512,128]{0,1:T(8,128)S(1)} %slice.339, f32[512,320]{0,1:T(8,128)S(1)} %slice.338, f32[515,448]{0,1:T(8,128)S(1)} %maximum_maximum_fusion, f32[448]{0:T(512)} %bitcast.133, f32[512]{0:T(512)S(1)} %get-tuple-element.66, f32[448]{0:T(512)} %bitcast.134, f32[512]{0:T(512)S(1)} %get-tuple-element.67, ...), kind=kLoop, calls=%fused_computation.59 | loop fusion | flops 3670016 | bytes 4602624 | tf_op jit(solution)/shard_map/jit(silu)/mul | solution.py:79
  66.3 0.9 slice.349
  67.2 1.5 reshape.569
  68.7 0.9 reshape.572
  69.6 1.5 fusion.49
  71.2 0.8 fusion.80
  71.9 0.7 broadcast_in_dim.147
  72.7 1.0 tile.5
  73.7 3.1 %fusion.21 = f32[512,448]{0,1:T(8,128)S(1)} fusion(bf16[512,2560]{1,0:T(8,128)(2,1)} %bitcast.1, bf16[2560,128]{0,1:T(8,128)(2,1)S(1)} %copy-done.5, bf16[2560,320]{0,1:T(8,128)(2,1)S(1)} %copy-done.38), kind=kOutput, calls=%fused_computation.28 | convolution fusion | flops 1178992640 | bytes 5832704 | tf_op jit(solution)/shard_map/dot_general | solution.py:140
  76.8 0.8 slice.356
  77.6 1.9 %collective-permute-start.1 = (f32[3,128]{0,1:T(8,128)}, f32[3,128]{0,1:T(8,128)}, u32[]{:S(2)}, u32[]{:S(2)}) collective-permute-start(f32[3,128]{0,1:T(8,128)} %slice.356), channel_id=1, source_target_pairs={{0,16},{16,32},{32,48},{48,64},{64,80},{80,96},{96,112},{1,17},{17... | collective-permute-start | bytes 4616 | tf_op jit(solution)/shard_map/ppermute | solution.py:17
  79.6 0.7 slice_add_fusion
  80.3 0.7 slice.357
  81.0 5.9 %all-to-all-start.1 = ((bf16[8,5,80,128]{3,2,1,0:T(8,128)(2,1)}), bf16[8,5,80,128]{3,2,1,0:T(8,128)(2,1)}, u32[]{:S(2)}, u32[]{:S(2)}) async-start(bf16[8,5,80,128]{3,2,1,0:T(8,128)(2,1)} %tile.5), calls=%async_computation.1 | async-start | bytes 1638400 | tf_op jit(solution)/shard_map/all_to_all | solution.py:139
  86.9 2.4 %divide_multiply_fusion.1 = f32[512,128]{0,1:T(8,128)} fusion(f32[512,128]{0,1:T(8,128)} %slice.357, f32[3,128]{0,1:T(8,128)} %collective-permute-done.1, f32[128]{0:T(128)} %get-tuple-element.70, f32[512]{0:T(512)} %copy-done.14, f32[128]{0:T(128)} %get-tuple-element.71, f32[512]{0:T(512)} %copy-done.15, f32[128]{0:T(128)} %get-tuple-element.69, ...), kind=kLoop, calls=%fused_computation.99 | loop fusion | flops 1179648 | bytes 534528 | tf_op jit(solution)/shard_map/jit(silu)/mul | solution.py:79
  89.3 1.8 %reshape.573 = f32[2,256,128]{1,0,2:T(2,128)} reshape(f32[512,128]{0,1:T(8,128)} %divide_multiply_fusion.1) | data formatting | bytes 524288 | tf_op jit(solution)/shard_map/reshape | solution.py:144
  91.1 1.4 fusion.68
  92.6 3.7 %fusion.36 = f32[2,256,5,64]{1,3,2,0:T(8,128)} fusion(f32[2,256,5]{1,2,0:T(8,128)S(1)} %bitcast.129, f32[2,256,5]{1,2,0:T(8,128)} %copy-done.8, f32[2,256,256]{2,1,0:T(8,128)S(1)} %fusion.68, pred[2,256,256]{2,1,0:T(8,128)(4,1)} %compare_and_fusion, f32[2,256,5,64]{1,0,3,2:T(2,128)S(1)} %reshape.569), kind=kOutput, calls=%fused_computation.39 | convolution fusion | flops 254935040 | bytes 1986560 | tf_op jit(solution)/shard_map/cijh,cjhp->cihp/dot_general | solution.py:147
  96.3 2.1 %all-to-all-done.1 = bf16[8,5,80,128]{3,2,1,0:T(8,128)(2,1)} async-done(((bf16[8,5,80,128]{3,2,1,0:T(8,128)(2,1)}), bf16[8,5,80,128]{3,2,1,0:T(8,128)(2,1)}, u32[]{:S(2)}, u32[]{:S(2)}) %all-to-all-start.1) | async-done | bytes 819232 | tf_op jit(solution)/shard_map/all_to_all | solution.py:139
  98.4 1.0 fusion.84
  99.6 1.4 select_bitcast_fusion.7
  101.0 0.6 copy-done.6
  101.6 1.8 %fusion.40 = f32[2,256,5,64]{1,3,2,0:T(8,128)S(1)} fusion(f32[2,256,5,64]{1,3,2,0:T(8,128)} %fusion.36, f32[2,256,5,64]{1,0,3,2:T(2,128)S(1)} %reshape.569, f32[5]{0:T(128)} %param.32, f32[1,5,64,128]{3,2,1,0:T(8,128)} %slice_add_fusion, f32[2,256,5]{1,2,0:T(8,128)} %get-tuple-element.59, f32[2,256,128,1]{1,0,2,3:T(2,128)} %bitcast.126, ...), kind=kOutput, calls=%fused_computation.42 | convolution fusion | flops 126648320 | bytes 2566204 | tf_op jit(solution)/shard_map/cin,chpn->cihp/dot_general | solution.py:161
  104.3 1.7 %convolution_convert_fusion = bf16[512,2560]{1,0:T(8,128)(2,1)S(1)} fusion(bf16[320,2560]{1,0:T(8,128)(2,1)S(1)} %copy-done, f32[320]{0:T(512)S(1)} %copy-done.40, f32[512,320]{0,1:T(8,128)S(1)} %bitcast.118, f32[512,448]{0,1:T(8,128)S(1)} %copy-done.4), kind=kOutput, calls=%fused_computation.8 | convolution fusion | flops 841318400 | bytes 5572608 | tf_op jit(solution)/shard_map/dot_general | solution.py:170
  106.2 1.7 %pad_maximum_fusion = bf16[512,2688]{1,0:T(8,128)(2,1)} fusion(bf16[512,128]{1,0:T(8,128)(2,1)S(1)} %select_select_fusion, bf16[512,2560]{1,0:T(8,128)(2,1)S(1)} %convolution_convert_fusion), kind=kLoop, calls=%fused_computation.9 | loop fusion | flops 5505024 | bytes 5505024 | tf_op jit(solution)/shard_map/concatenate | solution.py:183
  108.0 4.5 %all-to-all-start.2 = ((bf16[16,32,2688]{2,1,0:T(8,128)(2,1)}), bf16[16,32,2688]{2,1,0:T(8,128)(2,1)}, u32[]{:S(2)}, u32[]{:S(2)}) async-start(bf16[16,32,2688]{2,1,0:T(8,128)(2,1)} %bitcast.116), calls=%async_computation.2 | async-start | bytes 5505024 | tf_op jit(solution)/shard_map/all_to_all | solution.py:182
  112.6 0.7 gather_fusion.2
  113.9 0.8 fusion
  114.8 1.1 add_convert_fusion
  115.9 1.1 copy-done.2
  117.1 1.2 collective-permute-start.7
  118.3 2.2 %collective-permute-start.6 = (bf16[2,5,64,128]{3,2,1,0:T(8,128)(2,1)S(1)}, bf16[2,5,64,128]{3,2,1,0:T(8,128)(2,1)S(1)}, u32[]{:S(2)}, u32[]{:S(2)}) collective-permute-start(bf16[2,5,64,128]{3,2,1,0:T(8,128)(2,1)S(1)} %get-tuple-element.47), channel_id=1, source_target_pairs={{0,80},{16,96},{32,112},{48,0},{64,16},{80,32},{96,48},{112,64},{1... | collective-permute-start | bytes 491528 | tf_op jit(solution)/shard_map/ppermute | solution.py:241
  121.0 2.1 %collective-permute-start.4 = (bf16[2,5,64,128]{3,2,1,0:T(8,128)(2,1)S(1)}, bf16[2,5,64,128]{3,2,1,0:T(8,128)(2,1)S(1)}, u32[]{:S(2)}, u32[]{:S(2)}) collective-permute-start(bf16[2,5,64,128]{3,2,1,0:T(8,128)(2,1)S(1)} %get-tuple-element.49), channel_id=1, source_target_pairs={{0,48},{16,64},{32,80},{48,96},{64,112},{80,0},{96,16},{112,32},{1... | collective-permute-start | bytes 491528 | tf_op jit(solution)/shard_map/ppermute | solution.py:241
  123.0 0.7 collective-permute-start.3
  123.7 3.9 %collective-permute-done.7 = bf16[2,5,64,128]{3,2,1,0:T(8,128)(2,1)S(1)} collective-permute-done((bf16[2,5,64,128]{3,2,1,0:T(8,128)(2,1)S(1)}, bf16[2,5,64,128]{3,2,1,0:T(8,128)(2,1)S(1)}, u32[]{:S(2)}, u32[]{:S(2)}) %collective-permute-start.7) | collective-permute-done | bytes 163872 | tf_op jit(solution)/shard_map/ppermute | solution.py:241
  127.7 1.1 collective-permute-done.6
  128.7 6.3 %collective-permute-done.5 = bf16[2,5,64,128]{3,2,1,0:T(8,128)(2,1)S(1)} collective-permute-done((bf16[2,5,64,128]{3,2,1,0:T(8,128)(2,1)S(1)}, bf16[2,5,64,128]{3,2,1,0:T(8,128)(2,1)S(1)}, u32[]{:S(2)}, u32[]{:S(2)}) %collective-permute-start.5) | collective-permute-done | bytes 163872 | tf_op jit(solution)/shard_map/ppermute | solution.py:241
  135.4 0.8 collective-permute-done.3
  136.2 0.6 collective-permute-done.2
  136.8 1.9 %convert_add_fusion = f32[2,5,64,128]{3,2,1,0:T(8,128)} fusion(bf16[2,5,64,128]{3,2,1,0:T(8,128)(2,1)S(1)} %collective-permute-done.8, bf16[2,5,64,128]{3,2,1,0:T(8,128)(2,1)S(1)} %collective-permute-done.7, bf16[2,5,64,128]{3,2,1,0:T(8,128)(2,1)S(1)} %collective-permute-done.6, bf16[2,5,64,128]{3,2,1,0:T(8,128)(2,1)S(1)} %collective-permute-done.5, ...), kind=kLoop, calls=%fused_computation.72 | loop fusion | flops 1310720 | bytes 1638405 | tf_op jit(solution)/shard_map/add | solution.py:243
  138.7 15.5 %all-to-all-done.2 = bf16[16,32,2688]{2,1,0:T(8,128)(2,1)} async-done(((bf16[16,32,2688]{2,1,0:T(8,128)(2,1)}), bf16[16,32,2688]{2,1,0:T(8,128)(2,1)}, u32[]{:S(2)}, u32[]{:S(2)}) %all-to-all-start.2) | async-done | bytes 2752544 | tf_op jit(solution)/shard_map/all_to_all | solution.py:182
  154.2 1.2 add_reduce_fusion
  155.4 3.0 %multiply_reduce_fusion = bf16[32,2560]{1,0:T(8,128)(2,1)} fusion(bf16[16,32,2688]{2,1,0:T(8,128)(2,1)} %all-to-all-done.2, f32[32]{0:T(128)S(1)} %add_rsqrt_fusion), kind=kLoop, calls=%fused_computation.7 | loop fusion | flops 3850240 | bytes 2785408 | tf_op jit(solution)/shard_map/reduce_sum | solution.py:191
  (155 shorter events, 9.8 us)
Async XLA Ops:
  0.6 103.6 %copy-start = (bf16[320,2560]{1,0:T(8,128)(2,1)S(1)}, bf16[320,2560]{1,0:T(8,128)(2,1)}, u32[]{:S(2)}) copy-start(bf16[320,2560]{1,0:T(8,128)(2,1)} %param.34) | copy-start | bytes 4915204
  3.5 9.5 %copy-start.41 = (f32[5]{0:T(128)S(1)}, f32[5]{0:T(128)}, u32[]{:S(2)}) copy-start(f32[5]{0:T(128)} %param.31) | copy-start | bytes 64
  3.5 48.2 %all-to-all-start = ((bf16[16,32,2560]{2,1,0:T(8,128)(2,1)}), bf16[16,32,2560]{2,1,0:T(8,128)(2,1)}, u32[]{:S(2)}, u32[]{:S(2)}) async-start(bf16[16,32,2560]{2,1,0:T(8,128)(2,1)} %tile.4), calls=%async_computation | async-start | bytes 5242880 | tf_op jit(solution)/shard_map/all_to_all | solution.py:49
  11.7 3.8 %copy-start.30 = (s32[16]{0:T(128)S(1)}, s32[16]{0:T(128)}, u32[]{:S(2)}) copy-start(s32[16]{0:T(128)} %param.35) | copy-start | bytes 196
  11.7 4.0 %copy-start.36 = (s32[16]{0:T(128)S(1)}, s32[16]{0:T(128)}, u32[]{:S(2)}) copy-start(s32[16]{0:T(128)} %param.36) | copy-start | bytes 196
  11.7 4.4 %copy-start.32 = (f32[256]{0:T(256)S(1)}, f32[256]{0:T(256)}, u32[]{:S(2)}) copy-start(f32[256]{0:T(256)} %param.29) | copy-start | bytes 3076
  11.7 5.0 %copy-start.42 = (s32[16]{0:T(128)S(1)}, s32[16]{0:T(128)}, u32[]{:S(2)}) copy-start(s32[16]{0:T(128)} %param.37) | copy-start | bytes 196
  13.0 6.0 %copy-start.31 = (f32[320]{0:T(512)S(1)}, f32[320]{0:T(512)}, u32[]{:S(2)}) copy-start(f32[320]{0:T(512)} %param.27) | copy-start | bytes 3844
  13.0 7.7 %slice-start = ((f32[4,256]{1,0:T(4,128)}), f32[4,128]{1,0:T(4,128)S(1)}, s32[]{:S(2)}) async-start(f32[4,256]{1,0:T(4,128)} %param.28), calls=%async_computation.3 | async-start | bytes 4096 | tf_op jit(solution)/shard_map/slice | solution.py:83
  13.0 7.7 %copy-start.23 = (f32[4,320]{1,0:T(4,128)S(1)}, f32[4,320]{1,0:T(4,128)}, u32[]{:S(2)}) copy-start(f32[4,320]{1,0:T(4,128)} %param.26) | copy-start | bytes 15364
  13.0 9.6 %copy-start.21 = (f32[4,256]{1,0:T(4,128)S(1)}, f32[4,256]{1,0:T(4,128)}, u32[]{:S(2)}) copy-start(f32[4,256]{1,0:T(4,128)} %param.28) | copy-start | bytes 12292
  13.0 38.6 %copy-start.39 = (bf16[2560,5]{0,1:T(8,128)(2,1)S(1)}, bf16[2560,5]{0,1:T(8,128)(2,1)}, u32[]{:S(2)}) copy-start(bf16[2560,5]{0,1:T(8,128)(2,1)} %param.24) | copy-start | bytes 76804
  20.4 40.3 %copy-start.24 = (pred[16]{0:T(512)(128)(4,1)}, pred[16]{0:T(512)(128)(4,1)S(1)}, u32[]{:S(2)}) copy-start(pred[16]{0:T(512)(128)(4,1)S(1)} %get-tuple-element.31) | copy-start | bytes 52
  20.5 40.3 %copy-start.26 = (pred[16]{0:T(512)(128)(4,1)}, pred[16]{0:T(512)(128)(4,1)S(1)}, u32[]{:S(2)}) copy-start(pred[16]{0:T(512)(128)(4,1)S(1)} %get-tuple-element.38) | copy-start | bytes 52
  20.5 39.0 %copy-start.22 = (s32[1024]{0:T(1024)}, s32[1024]{0:T(1024)S(1)}, u32[]{:S(2)}) copy-start(s32[1024]{0:T(1024)S(1)} %pad_clamp_fusion) | copy-start | bytes 12292
  23.3 41.2 %copy-start.13 = (f32[512]{0:T(512)}, f32[512]{0:T(512)S(1)}, u32[]{:S(2)}) copy-start(f32[512]{0:T(512)S(1)} %get-tuple-element.65) | copy-start | bytes 6148
  23.3 41.2 %copy-start.14 = (f32[512]{0:T(512)}, f32[512]{0:T(512)S(1)}, u32[]{:S(2)}) copy-start(f32[512]{0:T(512)S(1)} %get-tuple-element.66) | copy-start | bytes 6148
  23.4 41.2 %copy-start.15 = (f32[512]{0:T(512)}, f32[512]{0:T(512)S(1)}, u32[]{:S(2)}) copy-start(f32[512]{0:T(512)S(1)} %get-tuple-element.67) | copy-start | bytes 6148
  51.7 4.0 %copy-start.33 = (f32[5]{0:T(128)S(1)}, f32[5]{0:T(128)}, u32[]{:S(2)}) copy-start(f32[5]{0:T(128)} %param.30) | copy-start | bytes 64
  55.5 5.9 %copy-start.37 = (pred[16]{0:T(512)(128)(4,1)S(1)}, pred[16]{0:T(512)(128)(4,1)}, u32[]{:S(2)}) copy-start(pred[16]{0:T(512)(128)(4,1)} %iota_compare_fusion.6) | copy-start | bytes 52
  55.9 10.3 %copy-start.8 = (f32[2,256,5]{1,2,0:T(8,128)}, f32[2,256,5]{1,2,0:T(8,128)S(1)}, u32[]{:S(2)}) copy-start(f32[2,256,5]{1,2,0:T(8,128)S(1)} %convolution_bitcast_fusion) | copy-start | bytes 30724
  56.7 9.5 %copy-start.10 = (f32[256,5]{0,1:T(8,128)}, f32[256,5]{0,1:T(8,128)S(1)}, u32[]{:S(2)}) copy-start(f32[256,5]{0,1:T(8,128)S(1)} %get-tuple-element.57) | copy-start | bytes 15364
  56.9 7.3 %collective-permute-start = (f32[3,448]{0,1:T(8,128)S(1)}, f32[3,448]{0,1:T(8,128)S(1)}, u32[]{:S(2)}, u32[]{:S(2)}) collective-permute-start(f32[3,448]{0,1:T(8,128)S(1)} %fusion.78), channel_id=1, source_target_pairs={{0,16},{16,32},{32,48},{48,64},{64,80},{80,96},{96,112},{1,17},{17... | collective-permute-start | bytes 16136 | tf_op jit(solution)/shard_map/ppermute | solution.py:17
  66.3 3.3 %copy-start.1 = (f32[512,128]{0,1:T(8,128)}, f32[512,128]{0,1:T(8,128)S(1)}, u32[]{:S(2)}) copy-start(f32[512,128]{0,1:T(8,128)S(1)} %slice.353) | copy-start | bytes 786436
  69.6 4.1 %copy-start.5 = (bf16[2560,128]{0,1:T(8,128)(2,1)S(1)}, bf16[2560,128]{0,1:T(8,128)(2,1)}, u32[]{:S(2)}) copy-start(bf16[2560,128]{0,1:T(8,128)(2,1)} %copy.129) | copy-start | bytes 1966084
  69.6 4.1 %copy-start.38 = (bf16[2560,320]{0,1:T(8,128)(2,1)S(1)}, bf16[2560,320]{0,1:T(8,128)(2,1)}, u32[]{:S(2)}) copy-start(bf16[2560,320]{0,1:T(8,128)(2,1)} %param.22) | copy-start | bytes 4915204
  73.7 5.9 %copy-start.18 = (f32[5]{0:T(128)S(1)}, f32[5]{0:T(128)}, u32[]{:S(2)}) copy-start(f32[5]{0:T(128)} %get-tuple-element.83) | copy-start | bytes 64
  76.8 3.5 %copy-start.3 = (f32[512,448]{0,1:T(8,128)}, f32[512,448]{0,1:T(8,128)S(1)}, u32[]{:S(2)}) copy-start(f32[512,448]{0,1:T(8,128)S(1)} %fusion.21) | copy-start | bytes 2752516
  77.6 9.3 %collective-permute-start.1 = (f32[3,128]{0,1:T(8,128)}, f32[3,128]{0,1:T(8,128)}, u32[]{:S(2)}, u32[]{:S(2)}) collective-permute-start(f32[3,128]{0,1:T(8,128)} %slice.356), channel_id=1, source_target_pairs={{0,16},{16,32},{32,48},{48,64},{64,80},{80,96},{96,112},{1,17},{17... | collective-permute-start | bytes 4616 | tf_op jit(solution)/shard_map/ppermute | solution.py:17
  81.0 17.4 %all-to-all-start.1 = ((bf16[8,5,80,128]{3,2,1,0:T(8,128)(2,1)}), bf16[8,5,80,128]{3,2,1,0:T(8,128)(2,1)}, u32[]{:S(2)}, u32[]{:S(2)}) async-start(bf16[8,5,80,128]{3,2,1,0:T(8,128)(2,1)} %tile.5), calls=%async_computation.1 | async-start | bytes 1638400 | tf_op jit(solution)/shard_map/all_to_all | solution.py:139
  101.0 0.7 copy-start.6
  101.0 3.0 %copy-start.4 = (f32[512,448]{0,1:T(8,128)S(1)}, f32[512,448]{0,1:T(8,128)}, u32[]{:S(2)}) copy-start(f32[512,448]{0,1:T(8,128)} %copy-done.3) | copy-start | bytes 2752516
  101.6 2.6 %copy-start.40 = (f32[320]{0:T(512)S(1)}, f32[320]{0:T(512)}, u32[]{:S(2)}) copy-start(f32[320]{0:T(512)} %param.33) | copy-start | bytes 3844
  104.2 1.7 %copy-start.34 = (pred[128]{0:T(512)(128)(4,1)S(1)}, pred[128]{0:T(512)(128)(4,1)}, u32[]{:S(2)}) copy-start(pred[128]{0:T(512)(128)(4,1)} %get-tuple-element.93) | copy-start | bytes 388
  104.2 1.7 %copy-start.35 = (pred[128]{0:T(512)(128)(4,1)S(1)}, pred[128]{0:T(512)(128)(4,1)}, u32[]{:S(2)}) copy-start(pred[128]{0:T(512)(128)(4,1)} %get-tuple-element.94) | copy-start | bytes 388
  107.9 4.6 %copy-start.9 = (f32[256,5]{0,1:T(8,128)S(1)}, f32[256,5]{0,1:T(8,128)}, u32[]{:S(2)}) copy-start(f32[256,5]{0,1:T(8,128)} %get-tuple-element.58) | copy-start | bytes 15364
  107.9 5.4 %copy-start.12 = (f32[16,5]{1,0:T(8,128)S(1)}, f32[16,5]{1,0:T(8,128)}, u32[]{:S(2)}) copy-start(f32[16,5]{1,0:T(8,128)} %get-tuple-element.27) | copy-start | bytes 964
  107.9 5.4 %copy-start.25 = (pred[16]{0:T(512)(128)(4,1)S(1)}, pred[16]{0:T(512)(128)(4,1)}, u32[]{:S(2)}) copy-start(pred[16]{0:T(512)(128)(4,1)} %copy-done.24) | copy-start | bytes 52
  107.9 5.5 %copy-start.27 = (pred[16]{0:T(512)(128)(4,1)S(1)}, pred[16]{0:T(512)(128)(4,1)}, u32[]{:S(2)}) copy-start(pred[16]{0:T(512)(128)(4,1)} %copy-done.26) | copy-start | bytes 52
  107.9 5.5 %copy-start.28 = (f32[5]{0:T(128)S(1)}, f32[5]{0:T(128)}, u32[]{:S(2)}) copy-start(f32[5]{0:T(128)} %get-tuple-element.78) | copy-start | bytes 64
  107.9 5.5 %copy-start.29 = (pred[16]{0:T(512)(128)(4,1)S(1)}, pred[16]{0:T(512)(128)(4,1)}, u32[]{:S(2)}) copy-start(pred[16]{0:T(512)(128)(4,1)} %get-tuple-element.36) | copy-start | bytes 52
  108.0 5.5 %copy-start.11 = (f32[256,5]{0,1:T(8,128)S(1)}, f32[256,5]{0,1:T(8,128)}, u32[]{:S(2)}) copy-start(f32[256,5]{0,1:T(8,128)} %copy-done.10) | copy-start | bytes 15364
  108.0 5.5 %copy-start.17 = (pred[16,256]{1,0:T(8,128)(4,1)S(1)}, pred[16,256]{1,0:T(8,128)(4,1)}, u32[]{:S(2)}) copy-start(pred[16,256]{1,0:T(8,128)(4,1)} %get-tuple-element.76) | copy-start | bytes 12292
  108.0 5.7 %copy-start.16 = (pred[16,256]{1,0:T(8,128)(4,1)S(1)}, pred[16,256]{1,0:T(8,128)(4,1)}, u32[]{:S(2)}) copy-start(pred[16,256]{1,0:T(8,128)(4,1)} %get-tuple-element.77) | copy-start | bytes 12292
  108.0 5.8 %copy-start.19 = (f32[5]{0:T(128)S(1)}, f32[5]{0:T(128)}, u32[]{:S(2)}) copy-start(f32[5]{0:T(128)} %get-tuple-element.83) | copy-start | bytes 64
  108.0 46.2 %all-to-all-start.2 = ((bf16[16,32,2688]{2,1,0:T(8,128)(2,1)}), bf16[16,32,2688]{2,1,0:T(8,128)(2,1)}, u32[]{:S(2)}, u32[]{:S(2)}) async-start(bf16[16,32,2688]{2,1,0:T(8,128)(2,1)} %bitcast.116), calls=%async_computation.2 | async-start | bytes 5505024 | tf_op jit(solution)/shard_map/all_to_all | solution.py:182
  113.3 1.4 copy-start.7
  113.3 1.4 copy-start.20
  115.9 1.1 copy-start.2
  117.1 5.9 %collective-permute-start.8 = (bf16[2,5,64,128]{3,2,1,0:T(8,128)(2,1)S(1)}, bf16[2,5,64,128]{3,2,1,0:T(8,128)(2,1)S(1)}, u32[]{:S(2)}, u32[]{:S(2)}) collective-permute-start(bf16[2,5,64,128]{3,2,1,0:T(8,128)(2,1)S(1)} %get-tuple-element.45), channel_id=1, source_target_pairs={{0,112},{16,0},{32,16},{48,32},{64,48},{80,64},{96,80},{112,96},{1... | collective-permute-start | bytes 491528 | tf_op jit(solution)/shard_map/ppermute | solution.py:241
  117.1 10.5 %collective-permute-start.7 = (bf16[2,5,64,128]{3,2,1,0:T(8,128)(2,1)S(1)}, bf16[2,5,64,128]{3,2,1,0:T(8,128)(2,1)S(1)}, u32[]{:S(2)}, u32[]{:S(2)}) collective-permute-start(bf16[2,5,64,128]{3,2,1,0:T(8,128)(2,1)S(1)} %get-tuple-element.46), channel_id=1, source_target_pairs={{0,96},{16,112},{32,0},{48,16},{64,32},{80,48},{96,64},{112,80},{1... | collective-permute-start | bytes 491528 | tf_op jit(solution)/shard_map/ppermute | solution.py:241
  118.3 10.4 %collective-permute-start.6 = (bf16[2,5,64,128]{3,2,1,0:T(8,128)(2,1)S(1)}, bf16[2,5,64,128]{3,2,1,0:T(8,128)(2,1)S(1)}, u32[]{:S(2)}, u32[]{:S(2)}) collective-permute-start(bf16[2,5,64,128]{3,2,1,0:T(8,128)(2,1)S(1)} %get-tuple-element.47), channel_id=1, source_target_pairs={{0,80},{16,96},{32,112},{48,0},{64,16},{80,32},{96,48},{112,64},{1... | collective-permute-start | bytes 491528 | tf_op jit(solution)/shard_map/ppermute | solution.py:241
  120.5 14.5 %collective-permute-start.5 = (bf16[2,5,64,128]{3,2,1,0:T(8,128)(2,1)S(1)}, bf16[2,5,64,128]{3,2,1,0:T(8,128)(2,1)S(1)}, u32[]{:S(2)}, u32[]{:S(2)}) collective-permute-start(bf16[2,5,64,128]{3,2,1,0:T(8,128)(2,1)S(1)} %get-tuple-element.48), channel_id=1, source_target_pairs={{0,64},{16,80},{32,96},{48,112},{64,0},{80,16},{96,32},{112,48},{1... | collective-permute-start | bytes 491528 | tf_op jit(solution)/shard_map/ppermute | solution.py:241
  121.0 14.4 %collective-permute-start.4 = (bf16[2,5,64,128]{3,2,1,0:T(8,128)(2,1)S(1)}, bf16[2,5,64,128]{3,2,1,0:T(8,128)(2,1)S(1)}, u32[]{:S(2)}, u32[]{:S(2)}) collective-permute-start(bf16[2,5,64,128]{3,2,1,0:T(8,128)(2,1)S(1)} %get-tuple-element.49), channel_id=1, source_target_pairs={{0,48},{16,64},{32,80},{48,96},{64,112},{80,0},{96,16},{112,32},{1... | collective-permute-start | bytes 491528 | tf_op jit(solution)/shard_map/ppermute | solution.py:241
  123.0 13.1 %collective-permute-start.3 = (bf16[2,5,64,128]{3,2,1,0:T(8,128)(2,1)S(1)}, bf16[2,5,64,128]{3,2,1,0:T(8,128)(2,1)S(1)}, u32[]{:S(2)}, u32[]{:S(2)}) collective-permute-start(bf16[2,5,64,128]{3,2,1,0:T(8,128)(2,1)S(1)} %get-tuple-element.50), channel_id=1, source_target_pairs={{0,32},{16,48},{32,64},{48,80},{64,96},{80,112},{96,0},{112,16},{1... | collective-permute-start | bytes 491528 | tf_op jit(solution)/shard_map/ppermute | solution.py:241
  127.7 9.1 %collective-permute-start.2 = (bf16[2,5,64,128]{3,2,1,0:T(8,128)(2,1)S(1)}, bf16[2,5,64,128]{3,2,1,0:T(8,128)(2,1)}, u32[]{:S(2)}, u32[]{:S(2)}) collective-permute-start(bf16[2,5,64,128]{3,2,1,0:T(8,128)(2,1)S(1)} %get-tuple-element.44), channel_id=1, source_target_pairs={{0,16},{16,32},{32,48},{48,64},{64,80},{80,96},{96,112},{112,0},{1... | collective-permute-start | bytes 491528 | tf_op jit(solution)/shard_map/ppermute | solution.py:241

commit v10 on v8

--- a/solution.py
+++ b/solution.py
@@ -155,9 +155,6 @@
     gated = output * jax.nn.silu(gate)
     squares = jnp.sum(gated * gated, axis=1)
     unscaled = (gated * norm_gain[None, :]).astype(jnp.bfloat16)
-    partials = jnp.dot(unscaled, out_weight, preferred_element_type=jnp.float32).astype(
-        jnp.bfloat16
-    )
     squares_high = squares.astype(jnp.bfloat16)
     squares_low = (squares - squares_high.astype(jnp.float32)).astype(jnp.bfloat16)
     column_slot = jnp.arange(128)[None, :]
@@ -166,10 +163,25 @@
         squares_high[:, None],
         jnp.where(column_slot == 1, squares_low[:, None], jnp.zeros((), jnp.bfloat16)),
     )
-    width = partials.shape[1]
-    received_partials = lax.all_to_all(
-        jnp.concatenate([partials, square_columns], axis=1), "tensor", 0, 0, tiled=True
-    ).reshape(tensor_count, -1, width + 128)
+    width = out_weight.shape[1]
+    widened_weight = jnp.concatenate(
+        [
+            jnp.concatenate([out_weight, jnp.zeros((local_inner, 128), out_weight.dtype)], axis=1),
+            jnp.concatenate(
+                [jnp.zeros((128, width), out_weight.dtype), jnp.eye(128, dtype=out_weight.dtype)],
+                axis=1,
+            ),
+        ],
+        axis=0,
+    )
+    partials = jnp.dot(
+        jnp.concatenate([unscaled, square_columns], axis=1),
+        widened_weight,
+        preferred_element_type=jnp.float32,
+    ).astype(jnp.bfloat16)
+    received_partials = lax.all_to_all(partials, "tensor", 0, 0, tiled=True).reshape(
+        tensor_count, -1, width + 128
+    )
     totals = jnp.sum(
         received_partials[:, :, width].astype(jnp.float32)
         + received_partials[:, :, width + 1].astype(jnp.float32),

time: 161 us -> 145 us (0.901)
  other arithmetic: 27.1 us -> 14.4 us
  local copies, waits for them, and re-layouts: 21.8 us -> 17.1 us
    all_to_all x1, waiting for transfers between devices: 15.5 us -> 11.6 us  [per_device(): lax.all_to_all(partials, 'tensor', 0, 0, tiled=True)]
    all_to_all x1, waiting for transfers between devices: 4.78 us -> 7.26 us  [per_device(): lax.all_to_all(jnp.tile(packed[None], (seq_count, 1, 1, 1)), 'seq', 0, 0,...]
    ppermute x1, waiting for transfers between devices: 1.82 us -> 3.91 us  [passed_along(): return lax.ppermute(block, axis, route)]
    dot_general x2, matrix products: 1.96 us -> 3.76 us  [per_device(): jnp.einsum('rjhp,jn->rhpn', weight[..., None] * values[block][None], keys...]
    reduce_sum x1, other arithmetic: 3.03 us -> 1.25 us  [per_device(): jnp.sum(received_partials[:, :, :width].astype(jnp.float32) * scale[None]...]
    concatenate x1, other arithmetic: 1.75 us -> 0.05 us  [per_device(): jnp.concatenate([jnp.zeros((128, width), out_weight.dtype), jnp.eye(128,...]
    reshape x1, local copies, waits for them, and re-layouts: 1.82 us -> 0.17 us  [per_device(): active[:, local_inner:local_inner + state_size]]
    reshape x1, local copies, waits for them, and re-layouts: 1.8 us -> 0.17 us  [per_device(): active[:, local_inner + state_size:].reshape(block_count, BLOCK, state_size)]
where the time goes in v10:
time: 145 us; the launch traced here: 142 us
  waiting for transfers between devices  65.8 us (45%)
  starting transfers between devices  25.3 us (17%)
  matrix products  18.3 us (13%)
  local copies, waits for them, and re-layouts  17.1 us (12%)
  other arithmetic  14.4 us (10%)
  between operations  1.5 us (1%)
    all_to_all x1, waiting for transfers between devices, per_device(): lax.all_to_all(jnp.tile(tokens, (lax.axis_size('tensor'), 1)), 'tensor',...  30.6 us
    ppermute x7, waiting for transfers between devices, per_device(): lax.ppermute(jnp.take(chunks, target, axis=0), 'seq', route)  12.5 us
    all_to_all x1, waiting for transfers between devices, per_device(): lax.all_to_all(partials, 'tensor', 0, 0, tiled=True)  11.6 us
    all_to_all x1, starting transfers between devices, per_device(): lax.all_to_all(jnp.tile(tokens, (lax.axis_size('tensor'), 1)), 'tensor',...  8.18 us
    all_to_all x1, waiting for transfers between devices, per_device(): lax.all_to_all(jnp.tile(packed[None], (seq_count, 1, 1, 1)), 'seq', 0, 0,...  7.26 us
    ppermute x7, starting transfers between devices, per_device(): lax.ppermute(jnp.take(chunks, target, axis=0), 'seq', route)  6.68 us
    unnamed x60, local copies, waits for them, and re-layouts  6.44 us
    dot_general x1, matrix products, per_device(): jnp.dot(gathered, weight_all, preferred_element_type=jnp.float32)  4.91 us
  transfers between devices with their start and end apart: 11, of which 10 were waited for; matrix products, arithmetic and copies ran while one was open for 17% of the time, Pallas kernels for 0%

profile of v10, /device:TPU:6, one launch (start us, length us, event | category | flops | bytes accessed | tf_op | source)
XLA Modules:
  0.0 142.4 jit_solution(12388323995399469522)
XLA Ops:
  0.6 2.7 %tile.4 = bf16[16,32,2560]{2,1,0:T(8,128)(2,1)} broadcast(bf16[32,2560]{1,0:T(8,128)(2,1)} %param.21), dimensions={1,2} | broadcast | bytes 2785280 | tf_op jit(solution)/shard_map/tile | solution.py:51
  3.3 8.2 %all-to-all-start = ((bf16[16,32,2560]{2,1,0:T(8,128)(2,1)}), bf16[16,32,2560]{2,1,0:T(8,128)(2,1)S(1)}, u32[]{:S(2)}, u32[]{:S(2)}) async-start(bf16[16,32,2560]{2,1,0:T(8,128)(2,1)} %tile.4), calls=%async_computation | async-start | bytes 5242880 | tf_op jit(solution)/shard_map/all_to_all | solution.py:50
  11.6 0.6 iota_compare_fusion.6
  12.4 2.4 %copy.117 = bf16[2560,256]{0,1:T(8,128)(2,1)} copy(bf16[2560,256]{1,0:T(8,128)(2,1)} %param.25) | data formatting | bytes 2621440 | tf_op args[4]
  15.1 0.2 convert_reduce_fusion.1
  15.4 0.2 fusion.96
  15.6 0.2 slice_reduce_fusion.7
  16.0 0.6 fusion.110
  16.6 0.7 gather_fusion
  17.3 0.7 compare_and_fusion.4
  18.2 0.2 fusion.97
  18.5 1.2 compare_and_fusion.2
  20.0 0.8 compare_and_fusion
  20.8 30.6 %all-to-all-done = bf16[16,32,2560]{2,1,0:T(8,128)(2,1)S(1)} async-done(((bf16[16,32,2560]{2,1,0:T(8,128)(2,1)}), bf16[16,32,2560]{2,1,0:T(8,128)(2,1)S(1)}, u32[]{:S(2)}, u32[]{:S(2)}) %all-to-all-start) | async-done | bytes 2621472 | tf_op jit(solution)/shard_map/all_to_all | solution.py:50
  51.4 4.9 %fusion.31 = f32[512,901]{0,1:T(8,128)S(1)} fusion(bf16[512,2560]{1,0:T(8,128)(2,1)S(1)} %bitcast.103, bf16[2560,256]{0,1:T(8,128)(2,1)} %copy.117, bf16[2560,5]{0,1:T(8,128)(2,1)S(1)} %copy-done.26, bf16[2560,320]{0,1:T(8,128)(2,1)} %param.23, bf16[2560,320]{0,1:T(8,128)(2,1)} %param.22), kind=kOutput, calls=%fused_computation.35 | convolution fusion | flops 2380369920 | bytes 9079808 | tf_op jit(solution)/shard_map/dot_general | solution.py:53
  56.4 1.1 copy-done.1
  57.7 0.2 convolution_bitcast_fusion
  57.9 0.2 slice_reduce_fusion
  58.1 0.2 fusion.65
  58.3 1.9 %collective-permute-start = (f32[3,576]{0,1:T(8,128)S(1)}, f32[3,576]{0,1:T(8,128)S(1)}, u32[]{:S(2)}, u32[]{:S(2)}) collective-permute-start(f32[3,576]{0,1:T(8,128)S(1)} %fusion.65), channel_id=1, source_target_pairs={{0,16},{16,32},{32,48},{48,64},{64,80},{80,96},{96,112},{1,17},{17... | collective-permute-start | bytes 20744 | tf_op jit(solution)/shard_map/ppermute | solution.py:17
  60.4 0.6 gather_fusion.1
  61.2 0.6 slice_bitcast_fusion.8
  61.8 0.6 stack.8
  62.4 3.9 %collective-permute-done = f32[3,576]{0,1:T(8,128)S(1)} collective-permute-done((f32[3,576]{0,1:T(8,128)S(1)}, f32[3,576]{0,1:T(8,128)S(1)}, u32[]{:S(2)}, u32[]{:S(2)}) %collective-permute-start) | collective-permute-done | bytes 6944 | tf_op jit(solution)/shard_map/ppermute | solution.py:17
  66.3 0.4 maximum_maximum_fusion
  66.7 1.4 %divide_multiply_fusion = f32[512,576]{0,1:T(8,128)S(1)} fusion(f32[512,256]{0,1:T(8,128)S(1)} %slice.278, f32[512,320]{0,1:T(8,128)S(1)} %slice.277, f32[515,576]{0,1:T(8,128)S(1)} %maximum_maximum_fusion, f32[576]{0:T(1024)S(1)} %get-tuple-element.24, f32[512]{0:T(512)S(1)} %get-tuple-element.64, f32[576]{0:T(1024)S(1)} %get-tuple-element.25, ...), kind=kLoop, calls=%fused_computation.63 | loop fusion | flops 4718592 | bytes 5915904 | tf_op jit(solution)/shard_map/jit(silu)/mul | solution.py:80
  68.2 1.0 copy-done
  69.3 0.4 reshape.566
  69.7 0.2 reshape.568
  69.9 0.2 reshape.567
  70.0 0.4 fusion.54
  70.7 1.0 tile.5
  71.7 4.8 %all-to-all-start.1 = ((bf16[8,5,80,128]{3,2,1,0:T(8,128)(2,1)}), bf16[8,5,80,128]{3,2,1,0:T(8,128)(2,1)S(1)}, u32[]{:S(2)}, u32[]{:S(2)}) async-start(bf16[8,5,80,128]{3,2,1,0:T(8,128)(2,1)} %tile.5), calls=%async_computation.1 | async-start | bytes 1638400 | tf_op jit(solution)/shard_map/all_to_all | solution.py:135
  76.5 0.4 fusion.66
  77.0 3.6 %fusion.40 = f32[2,256,5,64]{1,3,2,0:T(8,128)} fusion(f32[2,256,5]{1,2,0:T(8,128)S(1)} %bitcast.115, f32[2,256,5]{1,2,0:T(8,128)S(1)} %convolution_bitcast_fusion, f32[2,256,256]{2,1,0:T(8,128)S(1)} %fusion.66, pred[2,256,256]{2,1,0:T(8,128)(4,1)} %compare_and_fusion, f32[2,256,5,64]{1,0,3,2:T(2,128)S(1)} %reshape.566), kind=kOutput, calls=%fused_computation.47 | convolution fusion | flops 254935040 | bytes 1986560 | tf_op jit(solution)/shard_map/cijh,cjhp->cihp/dot_general | solution.py:104
  80.6 7.3 %all-to-all-done.1 = bf16[8,5,80,128]{3,2,1,0:T(8,128)(2,1)S(1)} async-done(((bf16[8,5,80,128]{3,2,1,0:T(8,128)(2,1)}), bf16[8,5,80,128]{3,2,1,0:T(8,128)(2,1)S(1)}, u32[]{:S(2)}, u32[]{:S(2)}) %all-to-all-start.1) | async-done | bytes 819232 | tf_op jit(solution)/shard_map/all_to_all | solution.py:135
  88.0 0.2 select_bitcast_fusion.7
  88.3 1.7 %fusion.44 = f32[2,256,5,64]{1,3,2,0:T(8,128)S(1)} fusion(f32[2,256,5,64]{1,3,2,0:T(8,128)} %fusion.40, f32[2,256,5,64]{1,0,3,2:T(2,128)S(1)} %reshape.566, f32[5]{0:T(128)S(1)} %copy-done.24, f32[1,5,64,128]{3,2,1,0:T(8,128)S(1)} %slice_add_fusion, f32[2,256,5]{1,2,0:T(8,128)S(1)} %get-tuple-element.61, f32[2,256,128,1]{1,0,2,3:T(2,128)S(1)} %bitcast.112, ...), kind=kOutput, calls=%fused_computation.50 | convolution fusion | flops 126648320 | bytes 2566204 | tf_op jit(solution)/shard_map/cin,chpn->cihp/dot_general | solution.py:149
  90.0 0.5 copy.130
  90.6 1.4 multiply_convert_fusion
  92.2 3.2 %convolution_convert_fusion = bf16[512,2688]{1,0:T(8,128)(2,1)} fusion(bf16[320,2560]{1,0:T(8,128)(2,1)S(1)} %copy-done.25, bf16[128,2688]{1,0:T(8,128)(2,1)S(1)} %pad_convert_fusion, bf16[512,128]{0,1:T(8,128)(2,1)S(1)} %select_select_fusion, bf16[512,320]{0,1:T(8,128)(2,1)S(1)} %get-tuple-element.40), kind=kOutput, calls=%fused_computation.18 | convolution fusion | flops 1242644480 | bytes 5537792 | tf_op jit(solution)/shard_map/dot_general | solution.py:177
  95.5 3.7 %all-to-all-start.2 = ((bf16[16,32,2688]{2,1,0:T(8,128)(2,1)}), bf16[16,32,2688]{2,1,0:T(8,128)(2,1)S(1)}, u32[]{:S(2)}, u32[]{:S(2)}) async-start(bf16[16,32,2688]{2,1,0:T(8,128)(2,1)} %bitcast.102), calls=%async_computation.2 | async-start | bytes 5505024 | tf_op jit(solution)/shard_map/all_to_all | solution.py:182
  99.4 0.6 gather_fusion.2
  100.4 1.1 fusion.106
  101.5 1.7 %fusion = f32[16,5,64,128]{3,2,1,0:T(8,128)S(1)} fusion(f32[256,5,64]{0,2,1:T(8,128)S(1)} %bitcast.108, f32[16,256,5]{1,2,0:T(8,128)S(1)} %multiply_select_fusion, f32[512,576]{0,1:T(8,128)} %copy-done), kind=kOutput, calls=%fused_computation.3 | convolution fusion | flops 336855040 | bytes 3096576 | tf_op jit(solution)/shard_map/rjhp,jn->rhpn/dot_general | solution.py:221
  103.3 2.0 %add_convert_fusion = bf16[16,5,64,128]{3,2,1,0:T(8,128)(2,1)S(1)} fusion(f32[16,5,64,128]{3,2,1,0:T(8,128)S(1)} %fusion, f32[256,5,64]{0,2,1:T(8,128)S(1)} %bitcast.113, f32[16,256,5]{1,2,0:T(8,128)S(1)} %multiply_select_fusion.1, f32[5,64,128]{2,1,0:T(8,128)S(1)} %copy-done.4, f32[16,5]{1,0:T(8,128)S(1)} %get-tuple-element.28, ...), kind=kOutput, calls=%fused_computation.19 | convolution fusion | flops 341442560 | bytes 4735936 | tf_op jit(solution)/shard_map/rjhp,jn->rhpn/dot_general | solution.py:221
  105.3 1.1 copy-done.2
  106.4 0.8 select_bitcast_fusion.6
  107.2 1.2 collective-permute-start.6
  108.3 2.2 %collective-permute-start.5 = (bf16[2,5,64,128]{3,2,1,0:T(8,128)(2,1)}, bf16[2,5,64,128]{3,2,1,0:T(8,128)(2,1)}, u32[]{:S(2)}, u32[]{:S(2)}) collective-permute-start(bf16[2,5,64,128]{3,2,1,0:T(8,128)(2,1)} %get-tuple-element.49), channel_id=1, source_target_pairs={{0,80},{16,96},{32,112},{48,0},{64,16},{80,32},{96,48},{112,64},{1... | collective-permute-start | bytes 491528 | tf_op jit(solution)/shard_map/ppermute | solution.py:241
  110.5 0.5 collective-permute-start.4
  111.0 2.1 %collective-permute-start.3 = (bf16[2,5,64,128]{3,2,1,0:T(8,128)(2,1)S(1)}, bf16[2,5,64,128]{3,2,1,0:T(8,128)(2,1)}, u32[]{:S(2)}, u32[]{:S(2)}) collective-permute-start(bf16[2,5,64,128]{3,2,1,0:T(8,128)(2,1)S(1)} %get-tuple-element.51), channel_id=1, source_target_pairs={{0,48},{16,64},{32,80},{48,96},{64,112},{80,0},{96,16},{112,32},{1... | collective-permute-start | bytes 491528 | tf_op jit(solution)/shard_map/ppermute | solution.py:241
  113.1 0.8 collective-permute-start.2
  113.8 3.8 %collective-permute-done.6 = bf16[2,5,64,128]{3,2,1,0:T(8,128)(2,1)S(1)} collective-permute-done((bf16[2,5,64,128]{3,2,1,0:T(8,128)(2,1)S(1)}, bf16[2,5,64,128]{3,2,1,0:T(8,128)(2,1)S(1)}, u32[]{:S(2)}, u32[]{:S(2)}) %collective-permute-start.6) | collective-permute-done | bytes 163872 | tf_op jit(solution)/shard_map/ppermute | solution.py:241
  117.7 0.7 copy-done.6
  118.4 0.5 collective-permute-done.5
  118.9 6.2 %collective-permute-done.4 = bf16[2,5,64,128]{3,2,1,0:T(8,128)(2,1)} collective-permute-done((bf16[2,5,64,128]{3,2,1,0:T(8,128)(2,1)S(1)}, bf16[2,5,64,128]{3,2,1,0:T(8,128)(2,1)}, u32[]{:S(2)}, u32[]{:S(2)}) %collective-permute-start.4) | collective-permute-done | bytes 163872 | tf_op jit(solution)/shard_map/ppermute | solution.py:241
  125.1 0.4 collective-permute-done.3
  125.5 1.2 collective-permute-done.2
  126.8 0.3 collective-permute-done.1
  127.0 2.3 %convert_add_fusion = f32[2,5,64,128]{3,2,1,0:T(8,128)} fusion(bf16[2,5,64,128]{3,2,1,0:T(8,128)(2,1)} %copy-done.5, bf16[2,5,64,128]{3,2,1,0:T(8,128)(2,1)} %copy-done.6, bf16[2,5,64,128]{3,2,1,0:T(8,128)(2,1)} %collective-permute-done.5, bf16[2,5,64,128]{3,2,1,0:T(8,128)(2,1)} %collective-permute-done.4, ...), kind=kLoop, calls=%fused_computation.76 | loop fusion | flops 1310720 | bytes 1638405 | tf_op jit(solution)/shard_map/add | solution.py:243
  129.4 11.6 %all-to-all-done.2 = bf16[16,32,2688]{2,1,0:T(8,128)(2,1)S(1)} async-done(((bf16[16,32,2688]{2,1,0:T(8,128)(2,1)}), bf16[16,32,2688]{2,1,0:T(8,128)(2,1)S(1)}, u32[]{:S(2)}, u32[]{:S(2)}) %all-to-all-start.2) | async-done | bytes 2752544 | tf_op jit(solution)/shard_map/all_to_all | solution.py:182
  140.9 0.2 add_reduce_fusion
  141.1 1.3 multiply_reduce_fusion
  (117 shorter events, 3.2 us)
Async XLA Ops:
  3.3 9.0 %copy-start.27 = (f32[5]{0:T(128)S(1)}, f32[5]{0:T(128)}, u32[]{:S(2)}) copy-start(f32[5]{0:T(128)} %param.31) | copy-start | bytes 64
  3.3 48.1 %all-to-all-start = ((bf16[16,32,2560]{2,1,0:T(8,128)(2,1)}), bf16[16,32,2560]{2,1,0:T(8,128)(2,1)S(1)}, u32[]{:S(2)}, u32[]{:S(2)}) async-start(bf16[16,32,2560]{2,1,0:T(8,128)(2,1)} %tile.4), calls=%async_computation | async-start | bytes 5242880 | tf_op jit(solution)/shard_map/all_to_all | solution.py:50
  11.5 3.3 %copy-start.17 = (s32[16]{0:T(128)S(1)}, s32[16]{0:T(128)}, u32[]{:S(2)}) copy-start(s32[16]{0:T(128)} %param.35) | copy-start | bytes 196
  11.5 3.5 %copy-start.23 = (s32[16]{0:T(128)S(1)}, s32[16]{0:T(128)}, u32[]{:S(2)}) copy-start(s32[16]{0:T(128)} %param.36) | copy-start | bytes 196
  11.5 4.4 %copy-start.28 = (s32[16]{0:T(128)S(1)}, s32[16]{0:T(128)}, u32[]{:S(2)}) copy-start(s32[16]{0:T(128)} %param.37) | copy-start | bytes 196
  11.5 6.4 %copy-start.7 = (f32[4,320]{1,0:T(4,128)S(1)}, f32[4,320]{1,0:T(4,128)}, u32[]{:S(2)}) copy-start(f32[4,320]{1,0:T(4,128)} %param.26) | copy-start | bytes 15364
  11.6 6.4 %copy-start.13 = (f32[4,256]{1,0:T(4,128)S(1)}, f32[4,256]{1,0:T(4,128)}, u32[]{:S(2)}) copy-start(f32[4,256]{1,0:T(4,128)} %param.28) | copy-start | bytes 12292
  11.6 6.6 %copy-start.16 = (f32[320]{0:T(512)S(1)}, f32[320]{0:T(512)}, u32[]{:S(2)}) copy-start(f32[320]{0:T(512)} %param.27) | copy-start | bytes 3844
  11.6 6.6 %copy-start.19 = (f32[256]{0:T(256)S(1)}, f32[256]{0:T(256)}, u32[]{:S(2)}) copy-start(f32[256]{0:T(256)} %param.29) | copy-start | bytes 3076
  11.6 39.8 %copy-start.26 = (bf16[2560,5]{0,1:T(8,128)(2,1)S(1)}, bf16[2560,5]{0,1:T(8,128)(2,1)}, u32[]{:S(2)}) copy-start(bf16[2560,5]{0,1:T(8,128)(2,1)} %param.24) | copy-start | bytes 76804
  17.9 43.1 %copy-start.8 = (pred[16]{0:T(512)(128)(4,1)}, pred[16]{0:T(512)(128)(4,1)S(1)}, u32[]{:S(2)}) copy-start(pred[16]{0:T(512)(128)(4,1)S(1)} %get-tuple-element.31) | copy-start | bytes 52
  18.0 43.1 %copy-start.10 = (pred[16]{0:T(512)(128)(4,1)}, pred[16]{0:T(512)(128)(4,1)S(1)}, u32[]{:S(2)}) copy-start(pred[16]{0:T(512)(128)(4,1)S(1)} %get-tuple-element.38) | copy-start | bytes 52
  51.4 6.2 %copy-start.20 = (f32[5]{0:T(128)S(1)}, f32[5]{0:T(128)}, u32[]{:S(2)}) copy-start(f32[5]{0:T(128)} %param.30) | copy-start | bytes 64
  56.3 1.3 copy-start.1
  58.3 8.0 %collective-permute-start = (f32[3,576]{0,1:T(8,128)S(1)}, f32[3,576]{0,1:T(8,128)S(1)}, u32[]{:S(2)}, u32[]{:S(2)}) collective-permute-start(f32[3,576]{0,1:T(8,128)S(1)} %fusion.65), channel_id=1, source_target_pairs={{0,16},{16,32},{32,48},{48,64},{64,80},{80,96},{96,112},{1,17},{17... | collective-permute-start | bytes 20744 | tf_op jit(solution)/shard_map/ppermute | solution.py:17
  68.2 1.0 copy-start
  71.7 16.2 %all-to-all-start.1 = ((bf16[8,5,80,128]{3,2,1,0:T(8,128)(2,1)}), bf16[8,5,80,128]{3,2,1,0:T(8,128)(2,1)S(1)}, u32[]{:S(2)}, u32[]{:S(2)}) async-start(bf16[8,5,80,128]{3,2,1,0:T(8,128)(2,1)} %tile.5), calls=%async_computation.1 | async-start | bytes 1638400 | tf_op jit(solution)/shard_map/all_to_all | solution.py:135
  77.0 11.3 %copy-start.12 = (f32[2,5]{1,0:T(2,128)S(1)}, f32[2,5]{1,0:T(2,128)}, u32[]{:S(2)}) copy-start(f32[2,5]{1,0:T(2,128)} %stack.8) | copy-start | bytes 124
  77.0 11.3 %copy-start.24 = (f32[5]{0:T(128)S(1)}, f32[5]{0:T(128)}, u32[]{:S(2)}) copy-start(f32[5]{0:T(128)} %param.32) | copy-start | bytes 64
  88.3 2.3 %copy-start.3 = (f32[5,64,128]{2,1,0:T(8,128)}, f32[5,64,128]{2,1,0:T(8,128)S(1)}, u32[]{:S(2)}) copy-start(f32[5,64,128]{2,1,0:T(8,128)S(1)} %select_bitcast_fusion.7) | copy-start | bytes 491524
  88.3 2.3 %copy-start.18 = (f32[320]{0:T(512)S(1)}, f32[320]{0:T(512)}, u32[]{:S(2)}) copy-start(f32[320]{0:T(512)} %param.33) | copy-start | bytes 3844
  90.5 1.6 %copy-start.21 = (pred[128]{0:T(512)(128)(4,1)S(1)}, pred[128]{0:T(512)(128)(4,1)}, u32[]{:S(2)}) copy-start(pred[128]{0:T(512)(128)(4,1)} %get-tuple-element.85) | copy-start | bytes 388
  90.5 1.6 %copy-start.22 = (pred[128]{0:T(512)(128)(4,1)S(1)}, pred[128]{0:T(512)(128)(4,1)}, u32[]{:S(2)}) copy-start(pred[128]{0:T(512)(128)(4,1)} %get-tuple-element.86) | copy-start | bytes 388
  90.5 1.7 %copy-start.25 = (bf16[320,2560]{1,0:T(8,128)(2,1)S(1)}, bf16[320,2560]{1,0:T(8,128)(2,1)}, u32[]{:S(2)}) copy-start(bf16[320,2560]{1,0:T(8,128)(2,1)} %param.34) | copy-start | bytes 4915204
  95.5 4.5 %copy-start.9 = (pred[16]{0:T(512)(128)(4,1)S(1)}, pred[16]{0:T(512)(128)(4,1)}, u32[]{:S(2)}) copy-start(pred[16]{0:T(512)(128)(4,1)} %copy-done.8) | copy-start | bytes 52
  95.5 4.5 %copy-start.11 = (pred[16]{0:T(512)(128)(4,1)S(1)}, pred[16]{0:T(512)(128)(4,1)}, u32[]{:S(2)}) copy-start(pred[16]{0:T(512)(128)(4,1)} %copy-done.10) | copy-start | bytes 52
  95.5 4.5 %copy-start.14 = (f32[5]{0:T(128)S(1)}, f32[5]{0:T(128)}, u32[]{:S(2)}) copy-start(f32[5]{0:T(128)} %get-tuple-element.72) | copy-start | bytes 64
  95.5 4.5 %copy-start.15 = (pred[16]{0:T(512)(128)(4,1)S(1)}, pred[16]{0:T(512)(128)(4,1)}, u32[]{:S(2)}) copy-start(pred[16]{0:T(512)(128)(4,1)} %get-tuple-element.36) | copy-start | bytes 52
  95.5 45.4 %all-to-all-start.2 = ((bf16[16,32,2688]{2,1,0:T(8,128)(2,1)}), bf16[16,32,2688]{2,1,0:T(8,128)(2,1)S(1)}, u32[]{:S(2)}, u32[]{:S(2)}) async-start(bf16[16,32,2688]{2,1,0:T(8,128)(2,1)} %bitcast.102), calls=%async_computation.2 | async-start | bytes 5505024 | tf_op jit(solution)/shard_map/all_to_all | solution.py:182
  100.3 3.0 %copy-start.4 = (f32[5,64,128]{2,1,0:T(8,128)S(1)}, f32[5,64,128]{2,1,0:T(8,128)}, u32[]{:S(2)}) copy-start(f32[5,64,128]{2,1,0:T(8,128)} %copy-done.3) | copy-start | bytes 491524
  105.3 1.1 copy-start.2
  107.2 5.9 %collective-permute-start.7 = (bf16[2,5,64,128]{3,2,1,0:T(8,128)(2,1)S(1)}, bf16[2,5,64,128]{3,2,1,0:T(8,128)(2,1)S(1)}, u32[]{:S(2)}, u32[]{:S(2)}) collective-permute-start(bf16[2,5,64,128]{3,2,1,0:T(8,128)(2,1)S(1)} %get-tuple-element.47), channel_id=1, source_target_pairs={{0,112},{16,0},{32,16},{48,32},{64,48},{80,64},{96,80},{112,96},{1... | collective-permute-start | bytes 491528 | tf_op jit(solution)/shard_map/ppermute | solution.py:241
  107.2 10.5 %collective-permute-start.6 = (bf16[2,5,64,128]{3,2,1,0:T(8,128)(2,1)S(1)}, bf16[2,5,64,128]{3,2,1,0:T(8,128)(2,1)S(1)}, u32[]{:S(2)}, u32[]{:S(2)}) collective-permute-start(bf16[2,5,64,128]{3,2,1,0:T(8,128)(2,1)S(1)} %get-tuple-element.48), channel_id=1, source_target_pairs={{0,96},{16,112},{32,0},{48,16},{64,32},{80,48},{96,64},{112,80},{1... | collective-permute-start | bytes 491528 | tf_op jit(solution)/shard_map/ppermute | solution.py:241
  108.3 10.5 %collective-permute-start.5 = (bf16[2,5,64,128]{3,2,1,0:T(8,128)(2,1)}, bf16[2,5,64,128]{3,2,1,0:T(8,128)(2,1)}, u32[]{:S(2)}, u32[]{:S(2)}) collective-permute-start(bf16[2,5,64,128]{3,2,1,0:T(8,128)(2,1)} %get-tuple-element.49), channel_id=1, source_target_pairs={{0,80},{16,96},{32,112},{48,0},{64,16},{80,32},{96,48},{112,64},{1... | collective-permute-start | bytes 491528 | tf_op jit(solution)/shard_map/ppermute | solution.py:241
  110.5 14.6 %collective-permute-start.4 = (bf16[2,5,64,128]{3,2,1,0:T(8,128)(2,1)S(1)}, bf16[2,5,64,128]{3,2,1,0:T(8,128)(2,1)}, u32[]{:S(2)}, u32[]{:S(2)}) collective-permute-start(bf16[2,5,64,128]{3,2,1,0:T(8,128)(2,1)S(1)} %get-tuple-element.50), channel_id=1, source_target_pairs={{0,64},{16,80},{32,96},{48,112},{64,0},{80,16},{96,32},{112,48},{1... | collective-permute-start | bytes 491528 | tf_op jit(solution)/shard_map/ppermute | solution.py:241
  111.0 14.5 %collective-permute-start.3 = (bf16[2,5,64,128]{3,2,1,0:T(8,128)(2,1)S(1)}, bf16[2,5,64,128]{3,2,1,0:T(8,128)(2,1)}, u32[]{:S(2)}, u32[]{:S(2)}) collective-permute-start(bf16[2,5,64,128]{3,2,1,0:T(8,128)(2,1)S(1)} %get-tuple-element.51), channel_id=1, source_target_pairs={{0,48},{16,64},{32,80},{48,96},{64,112},{80,0},{96,16},{112,32},{1... | collective-permute-start | bytes 491528 | tf_op jit(solution)/shard_map/ppermute | solution.py:241
  113.1 4.6 %copy-start.5 = (bf16[2,5,64,128]{3,2,1,0:T(8,128)(2,1)}, bf16[2,5,64,128]{3,2,1,0:T(8,128)(2,1)S(1)}, u32[]{:S(2)}) copy-start(bf16[2,5,64,128]{3,2,1,0:T(8,128)(2,1)S(1)} %collective-permute-done.7) | copy-start | bytes 491524
  113.1 13.7 %collective-permute-start.2 = (bf16[2,5,64,128]{3,2,1,0:T(8,128)(2,1)S(1)}, bf16[2,5,64,128]{3,2,1,0:T(8,128)(2,1)}, u32[]{:S(2)}, u32[]{:S(2)}) collective-permute-start(bf16[2,5,64,128]{3,2,1,0:T(8,128)(2,1)S(1)} %get-tuple-element.52), channel_id=1, source_target_pairs={{0,32},{16,48},{32,64},{48,80},{64,96},{80,112},{96,0},{112,16},{1... | collective-permute-start | bytes 491528 | tf_op jit(solution)/shard_map/ppermute | solution.py:241
  117.7 0.7 copy-start.6
  118.3 8.7 %collective-permute-start.1 = (bf16[2,5,64,128]{3,2,1,0:T(8,128)(2,1)S(1)}, bf16[2,5,64,128]{3,2,1,0:T(8,128)(2,1)}, u32[]{:S(2)}, u32[]{:S(2)}) collective-permute-start(bf16[2,5,64,128]{3,2,1,0:T(8,128)(2,1)S(1)} %get-tuple-element.46), channel_id=1, source_target_pairs={{0,16},{16,32},{32,48},{48,64},{64,80},{80,96},{96,112},{112,0},{1... | collective-permute-start | bytes 491528 | tf_op jit(solution)/shard_map/ppermute | solution.py:241

commit v11 on v10

--- a/solution.py
+++ b/solution.py
@@ -132,18 +132,18 @@
     )
     factor_rows = jnp.broadcast_to(factor_rows, (local_heads, 16, state_size))
     packed = jnp.concatenate([zero_end.astype(jnp.bfloat16), factor_rows], axis=1)
-    sent = lax.all_to_all(jnp.tile(packed[None], (seq_count, 1, 1, 1)), "seq", 0, 0, tiled=True)
-    sent_states = sent[:, :, :head_size]
-    sent_factors = sent[:, :, head_size, 0].astype(jnp.float32) + sent[
-        :, :, head_size + 1, 0
-    ].astype(jnp.float32)
     seq_index = lax.axis_index("seq")
     incoming = empty
-    for earlier in range(seq_count - 1):
-        advanced = sent_factors[earlier][:, None, None] * incoming + sent_states[earlier].astype(
+    for distance in range(seq_count - 1, 0, -1):
+        route = [(i, i + distance) for i in range(seq_count - distance)]
+        message = lax.ppermute(packed, "seq", route)
+        message_factor = message[:, head_size, 0].astype(jnp.float32) + message[
+            :, head_size + 1, 0
+        ].astype(jnp.float32)
+        advanced = message_factor[:, None, None] * incoming + message[:, :head_size].astype(
             jnp.float32
         )
-        incoming = jnp.where(earlier < seq_index, advanced, incoming)
+        incoming = jnp.where(distance <= seq_index, advanced, incoming)
     block_states = zero_starts + factors[:, :, None, None] * incoming[None]
     keep = jnp.exp(decay_sum) * (segs == prior[:, None]).astype(jnp.float32)[..., None]
     outer = keep[..., None] * jnp.einsum(

time: 145 us -> 151 us (1.041); the launches traced: 142 us -> 151 us
  other arithmetic: 14.4 us -> 20.6 us
  starting transfers between devices: 25.3 us -> 30.4 us
  matrix products: 18.3 us -> 15.7 us
    ppermute x0 -> x7, waiting for transfers between devices: none -> 14.1 us  [per_device(): message = lax.ppermute(packed, 'seq', route)]
    ppermute x0 -> x7, starting transfers between devices: none -> 9.85 us  [per_device(): message = lax.ppermute(packed, 'seq', route)]
    all_to_all x1 -> x0, waiting for transfers between devices: 7.26 us -> none  [per_device(): lax.all_to_all(jnp.tile(packed[None], (seq_count, 1, 1, 1)), 'seq', 0, 0,...]
    all_to_all x1 -> x0, starting transfers between devices: 4.78 us -> none  [per_device(): lax.all_to_all(jnp.tile(packed[None], (seq_count, 1, 1, 1)), 'seq', 0, 0,...]
    all_to_all x1, waiting for transfers between devices: 11.6 us -> 7.37 us  [per_device(): lax.all_to_all(partials, 'tensor', 0, 0, tiled=True)]
    all_to_all x1, waiting for transfers between devices: 30.6 us -> 27.5 us  [per_device(): lax.all_to_all(jnp.tile(tokens, (lax.axis_size('tensor'), 1)), 'tensor',...]
    ppermute x7, waiting for transfers between devices: 12.5 us -> 14.1 us  [per_device(): lax.ppermute(jnp.take(chunks, target, axis=0), 'seq', route)]
    unnamed x60 -> x68, local copies, waits for them, and re-layouts: 6.44 us -> 6.39 us
  transfers between devices with their start and end apart: 11 -> 17, of which waited for: 10 -> 9; matrix products, arithmetic and copies ran while one was open for 17% -> 19% of each run, Pallas kernels for 0% -> 0%
where the time goes in v11:
time: 151 us
  waiting for transfers between devices  66.8 us (44%)
  starting transfers between devices  30.4 us (20%)
  other arithmetic  20.6 us (14%)
  local copies, waits for them, and re-layouts  15.7 us (10%)
  matrix products  15.7 us (10%)
    all_to_all x1, waiting for transfers between devices, per_device(): lax.all_to_all(jnp.tile(tokens, (lax.axis_size('tensor'), 1)), 'tensor',...  27.5 us
    ppermute x7, waiting for transfers between devices, per_device(): lax.ppermute(jnp.take(chunks, target, axis=0), 'seq', route)  14.1 us
    ppermute x7, waiting for transfers between devices, per_device(): message = lax.ppermute(packed, 'seq', route)  14.1 us
    ppermute x7, starting transfers between devices, per_device(): message = lax.ppermute(packed, 'seq', route)  9.85 us
    all_to_all x1, starting transfers between devices, per_device(): lax.all_to_all(jnp.tile(tokens, (lax.axis_size('tensor'), 1)), 'tensor',...  8.18 us
    all_to_all x1, waiting for transfers between devices, per_device(): lax.all_to_all(partials, 'tensor', 0, 0, tiled=True)  7.37 us
    ppermute x7, starting transfers between devices, per_device(): lax.ppermute(jnp.take(chunks, target, axis=0), 'seq', route)  6.68 us
    unnamed x68, local copies, waits for them, and re-layouts  6.39 us
  transfers between devices with their start and end apart: 17, of which 9 were waited for; matrix products, arithmetic and copies ran while one was open for 19% of the time, Pallas kernels for 0%

profile of v11, /device:TPU:6, one launch (start us, length us, event | category | flops | bytes accessed | tf_op | source)
XLA Modules:
  0.0 150.7 jit_solution(15832648722568904964)
XLA Ops:
  0.6 2.7 %tile.2 = bf16[16,32,2560]{2,1,0:T(8,128)(2,1)} broadcast(bf16[32,2560]{1,0:T(8,128)(2,1)} %param.21), dimensions={1,2} | broadcast | bytes 2785280 | tf_op jit(solution)/shard_map/tile | solution.py:51
  3.3 8.2 %all-to-all-start = ((bf16[16,32,2560]{2,1,0:T(8,128)(2,1)}), bf16[16,32,2560]{2,1,0:T(8,128)(2,1)S(1)}, u32[]{:S(2)}, u32[]{:S(2)}) async-start(bf16[16,32,2560]{2,1,0:T(8,128)(2,1)} %tile.2), calls=%async_computation | async-start | bytes 5242880 | tf_op jit(solution)/shard_map/all_to_all | solution.py:50
  11.6 0.6 iota_compare_fusion.6
  12.2 0.5 iota_compare_fusion.8
  12.7 2.4 %copy.72 = bf16[2560,256]{0,1:T(8,128)(2,1)} copy(bf16[2560,256]{1,0:T(8,128)(2,1)} %param.25) | data formatting | bytes 2621440 | tf_op args[4]
  16.4 0.6 fusion.123
  17.0 0.7 gather_fusion
  17.6 1.3 compare_and_fusion.4
  18.9 0.5 compare_and_fusion.1
  19.6 0.6 pad_clamp_fusion
  20.3 0.8 fusion.110
  21.1 1.2 compare_and_fusion.2
  22.3 0.6 compare_convert_fusion.1
  22.9 0.7 fusion.106
  23.9 27.5 %all-to-all-done = bf16[16,32,2560]{2,1,0:T(8,128)(2,1)S(1)} async-done(((bf16[16,32,2560]{2,1,0:T(8,128)(2,1)}), bf16[16,32,2560]{2,1,0:T(8,128)(2,1)S(1)}, u32[]{:S(2)}, u32[]{:S(2)}) %all-to-all-start) | async-done | bytes 2621472 | tf_op jit(solution)/shard_map/all_to_all | solution.py:50
  51.4 4.9 %fusion.29 = f32[512,901]{0,1:T(8,128)S(1)} fusion(bf16[512,2560]{1,0:T(8,128)(2,1)S(1)} %bitcast.103, bf16[2560,256]{0,1:T(8,128)(2,1)} %copy.72, bf16[2560,5]{0,1:T(8,128)(2,1)S(1)} %copy-done.30, bf16[2560,320]{0,1:T(8,128)(2,1)} %param.23, bf16[2560,320]{0,1:T(8,128)(2,1)} %param.22), kind=kOutput, calls=%fused_computation.35 | convolution fusion | flops 2380369920 | bytes 9079808 | tf_op jit(solution)/shard_map/dot_general | solution.py:53
  56.5 1.1 copy-done.1
  57.7 0.2 convolution_bitcast_fusion
  58.3 1.9 %collective-permute-start = (f32[3,576]{0,1:T(8,128)S(1)}, f32[3,576]{0,1:T(8,128)S(1)}, u32[]{:S(2)}, u32[]{:S(2)}) collective-permute-start(f32[3,576]{0,1:T(8,128)S(1)} %fusion.63), channel_id=1, source_target_pairs={{0,16},{16,32},{32,48},{48,64},{64,80},{80,96},{96,112},{1,17},{17... | collective-permute-start | bytes 20744 | tf_op jit(solution)/shard_map/ppermute | solution.py:17
  60.4 0.7 gather_fusion.1
  61.2 0.7 fusion.83
  62.0 0.5 slice_bitcast_fusion.10
  62.5 3.8 %collective-permute-done = f32[3,576]{0,1:T(8,128)S(1)} collective-permute-done((f32[3,576]{0,1:T(8,128)S(1)}, f32[3,576]{0,1:T(8,128)S(1)}, u32[]{:S(2)}, u32[]{:S(2)}) %collective-permute-start) | collective-permute-done | bytes 6944 | tf_op jit(solution)/shard_map/ppermute | solution.py:17
  66.3 0.4 maximum_maximum_fusion
  66.8 1.4 divide_multiply_fusion
  68.3 1.0 copy-done
  69.3 0.4 reshape.538
  69.9 0.4 fusion.52
  70.5 1.3 collective-permute-start.7
  71.8 0.4 fusion.64
  72.3 2.1 %fusion.38 = f32[2,256,5,64]{1,3,2,0:T(8,128)S(1)} fusion(f32[2,256,5]{1,2,0:T(8,128)S(1)} %bitcast.115, f32[2,256,5]{1,2,0:T(8,128)S(1)} %convolution_bitcast_fusion, f32[2,256,256]{2,1,0:T(8,128)S(1)} %fusion.64, pred[2,256,256]{2,1,0:T(8,128)(4,1)S(1)} %compare_and_fusion, f32[2,256,5,64]{1,0,3,2:T(2,128)S(1)} %reshape.538), kind=kOutput, calls=%fused_computation.47 | convolution fusion | flops 254935040 | bytes 1986560 | tf_op jit(solution)/shard_map/cijh,cjhp->cihp/dot_general | solution.py:104
  74.7 1.9 %collective-permute-start.1 = (bf16[5,80,128]{2,1,0:T(8,128)(2,1)S(1)}, bf16[5,80,128]{2,1,0:T(8,128)(2,1)S(1)}, u32[]{:S(2)}, u32[]{:S(2)}) collective-permute-start(bf16[5,80,128]{2,1,0:T(8,128)(2,1)S(1)} %pad_maximum_fusion.1), channel_id=1, source_target_pairs={{0,16},{16,32},{32,48},{48,64},{64,80},{80,96},{96,112},{1,17},{17... | collective-permute-start | bytes 307208 | tf_op jit(solution)/shard_map/ppermute | solution.py:139
  76.6 1.3 collective-permute-start.2
  77.9 1.3 collective-permute-start.3
  79.2 1.3 collective-permute-start.4
  80.5 1.3 collective-permute-start.6
  81.8 0.9 fusion.105
  82.7 8.3 %collective-permute-done.6 = bf16[5,80,128]{2,1,0:T(8,128)(2,1)S(1)} collective-permute-done((bf16[5,80,128]{2,1,0:T(8,128)(2,1)S(1)}, bf16[5,80,128]{2,1,0:T(8,128)(2,1)S(1)}, u32[]{:S(2)}, u32[]{:S(2)}) %collective-permute-start.6) | collective-permute-done | bytes 102432 | tf_op jit(solution)/shard_map/ppermute | solution.py:139
  91.0 1.5 collective-permute-start.5
  92.6 5.8 %collective-permute-done.5 = bf16[5,80,128]{2,1,0:T(8,128)(2,1)S(1)} collective-permute-done((bf16[5,80,128]{2,1,0:T(8,128)(2,1)S(1)}, bf16[5,80,128]{2,1,0:T(8,128)(2,1)S(1)}, u32[]{:S(2)}, u32[]{:S(2)}) %collective-permute-start.5) | collective-permute-done | bytes 102432 | tf_op jit(solution)/shard_map/ppermute | solution.py:139
  99.0 1.2 add_select_fusion
  100.2 0.5 fusion.42
  100.7 0.5 copy.85
  101.3 1.4 multiply_convert_fusion
  102.9 3.2 %convolution_convert_fusion = bf16[512,2688]{1,0:T(8,128)(2,1)} fusion(bf16[320,2560]{1,0:T(8,128)(2,1)S(1)} %copy-done.29, bf16[128,2688]{1,0:T(8,128)(2,1)S(1)} %pad_convert_fusion, bf16[512,128]{0,1:T(8,128)(2,1)S(1)} %select_select_fusion, bf16[512,320]{0,1:T(8,128)(2,1)S(1)} %get-tuple-element.33), kind=kOutput, calls=%fused_computation.18 | convolution fusion | flops 1242644480 | bytes 5537792 | tf_op jit(solution)/shard_map/dot_general | solution.py:177
  106.2 3.7 %all-to-all-start.1 = ((bf16[16,32,2688]{2,1,0:T(8,128)(2,1)}), bf16[16,32,2688]{2,1,0:T(8,128)(2,1)S(1)}, u32[]{:S(2)}, u32[]{:S(2)}) async-start(bf16[16,32,2688]{2,1,0:T(8,128)(2,1)} %bitcast.102), calls=%async_computation.1 | async-start | bytes 5505024 | tf_op jit(solution)/shard_map/all_to_all | solution.py:182
  110.1 0.7 gather_fusion.2
  111.2 1.1 fusion.119
  112.3 1.7 %fusion.2 = f32[16,5,64,128]{3,2,1,0:T(8,128)S(1)} fusion(f32[256,5,64]{0,2,1:T(8,128)S(1)} %bitcast.108, f32[16,256,5]{1,2,0:T(8,128)S(1)} %multiply_select_fusion.1, f32[512,576]{0,1:T(8,128)} %copy-done), kind=kOutput, calls=%fused_computation.5 | convolution fusion | flops 336855040 | bytes 3096576 | tf_op jit(solution)/shard_map/rjhp,jn->rhpn/dot_general | solution.py:221
  114.1 2.1 %add_convert_fusion = bf16[16,5,64,128]{3,2,1,0:T(8,128)(2,1)S(1)} fusion(f32[16,5,64,128]{3,2,1,0:T(8,128)S(1)} %fusion.2, f32[5,64,128]{2,1,0:T(8,128)S(1)} %add_select_fusion, f32[16,5]{1,0:T(8,128)S(1)} %get-tuple-element.21, f32[5,64,128]{2,1,0:T(8,128)S(1)} %fusion.126, f32[16,5]{1,0:T(8,128)S(1)} %get-tuple-element.22, f32[16,5]{1,0:T(8,128)S(1)} %copy-done.7, ...), kind=kOutput, calls=%fused_computation.19 | convolution fusion | flops 341442560 | bytes 4735936 | tf_op jit(solution)/shard_map/rjhp,jn->rhpn/dot_general | solution.py:221
  116.2 1.1 copy-done.2
  117.2 0.8 select_bitcast_fusion.6
  118.0 0.4 collective-permute-start.12
  118.5 3.2 %collective-permute-start.11 = (bf16[2,5,64,128]{3,2,1,0:T(8,128)(2,1)S(1)}, bf16[2,5,64,128]{3,2,1,0:T(8,128)(2,1)}, u32[]{:S(2)}, u32[]{:S(2)}) collective-permute-start(bf16[2,5,64,128]{3,2,1,0:T(8,128)(2,1)S(1)} %get-tuple-element.43), channel_id=1, source_target_pairs={{0,64},{16,80},{32,96},{48,112},{64,0},{80,16},{96,32},{112,48},{1... | collective-permute-start | bytes 491528 | tf_op jit(solution)/shard_map/ppermute | solution.py:241
  121.7 1.5 collective-permute-start.10
  123.1 1.6 %collective-permute-start.9 = (bf16[2,5,64,128]{3,2,1,0:T(8,128)(2,1)S(1)}, bf16[2,5,64,128]{3,2,1,0:T(8,128)(2,1)}, u32[]{:S(2)}, u32[]{:S(2)}) collective-permute-start(bf16[2,5,64,128]{3,2,1,0:T(8,128)(2,1)S(1)} %get-tuple-element.45), channel_id=1, source_target_pairs={{0,32},{16,48},{32,64},{48,80},{64,96},{80,112},{96,0},{112,16},{1... | collective-permute-start | bytes 491528 | tf_op jit(solution)/shard_map/ppermute | solution.py:241
  124.7 9.3 %collective-permute-done.13 = bf16[2,5,64,128]{3,2,1,0:T(8,128)(2,1)S(1)} collective-permute-done((bf16[2,5,64,128]{3,2,1,0:T(8,128)(2,1)S(1)}, bf16[2,5,64,128]{3,2,1,0:T(8,128)(2,1)S(1)}, u32[]{:S(2)}, u32[]{:S(2)}) %collective-permute-start.13) | collective-permute-done | bytes 163872 | tf_op jit(solution)/shard_map/ppermute | solution.py:241
  134.0 0.7 copy-done.4
  134.6 0.6 collective-permute-done.12
  135.3 0.6 collective-permute-done.9
  135.9 3.6 %collective-permute-done.8 = bf16[2,5,64,128]{3,2,1,0:T(8,128)(2,1)} collective-permute-done((bf16[2,5,64,128]{3,2,1,0:T(8,128)(2,1)S(1)}, bf16[2,5,64,128]{3,2,1,0:T(8,128)(2,1)}, u32[]{:S(2)}, u32[]{:S(2)}) %collective-permute-start.8) | collective-permute-done | bytes 163872 | tf_op jit(solution)/shard_map/ppermute | solution.py:241
  139.5 2.3 %convert_add_fusion = f32[2,5,64,128]{3,2,1,0:T(8,128)} fusion(bf16[2,5,64,128]{3,2,1,0:T(8,128)(2,1)} %copy-done.3, bf16[2,5,64,128]{3,2,1,0:T(8,128)(2,1)} %copy-done.4, bf16[2,5,64,128]{3,2,1,0:T(8,128)(2,1)} %collective-permute-done.12, bf16[2,5,64,128]{3,2,1,0:T(8,128)(2,1)} %collective-permute-done.11, ...), kind=kLoop, calls=%fused_computation.76 | loop fusion | flops 1310720 | bytes 1638405 | tf_op jit(solution)/shard_map/add | solution.py:243
  141.8 7.4 %all-to-all-done.1 = bf16[16,32,2688]{2,1,0:T(8,128)(2,1)S(1)} async-done(((bf16[16,32,2688]{2,1,0:T(8,128)(2,1)}), bf16[16,32,2688]{2,1,0:T(8,128)(2,1)S(1)}, u32[]{:S(2)}, u32[]{:S(2)}) %all-to-all-start.1) | async-done | bytes 2752544 | tf_op jit(solution)/shard_map/all_to_all | solution.py:182
  149.4 1.3 multiply_reduce_fusion
  (141 shorter events, 5.2 us)
Async XLA Ops:
  3.3 9.4 %copy-start.31 = (f32[5]{0:T(128)S(1)}, f32[5]{0:T(128)}, u32[]{:S(2)}) copy-start(f32[5]{0:T(128)} %param.31) | copy-start | bytes 64
  3.3 48.1 %all-to-all-start = ((bf16[16,32,2560]{2,1,0:T(8,128)(2,1)}), bf16[16,32,2560]{2,1,0:T(8,128)(2,1)S(1)}, u32[]{:S(2)}, u32[]{:S(2)}) async-start(bf16[16,32,2560]{2,1,0:T(8,128)(2,1)} %tile.2), calls=%async_computation | async-start | bytes 5242880 | tf_op jit(solution)/shard_map/all_to_all | solution.py:50
  11.5 3.7 %copy-start.18 = (s32[16]{0:T(128)S(1)}, s32[16]{0:T(128)}, u32[]{:S(2)}) copy-start(s32[16]{0:T(128)} %param.35) | copy-start | bytes 196
  11.5 3.9 %copy-start.26 = (s32[16]{0:T(128)S(1)}, s32[16]{0:T(128)}, u32[]{:S(2)}) copy-start(s32[16]{0:T(128)} %param.36) | copy-start | bytes 196
  11.5 4.7 %copy-start.32 = (s32[16]{0:T(128)S(1)}, s32[16]{0:T(128)}, u32[]{:S(2)}) copy-start(s32[16]{0:T(128)} %param.37) | copy-start | bytes 196
  11.5 7.9 %copy-start.9 = (f32[4,320]{1,0:T(4,128)S(1)}, f32[4,320]{1,0:T(4,128)}, u32[]{:S(2)}) copy-start(f32[4,320]{1,0:T(4,128)} %param.26) | copy-start | bytes 15364
  11.6 7.9 %copy-start.14 = (f32[4,256]{1,0:T(4,128)S(1)}, f32[4,256]{1,0:T(4,128)}, u32[]{:S(2)}) copy-start(f32[4,256]{1,0:T(4,128)} %param.28) | copy-start | bytes 12292
  11.6 8.6 %copy-start.17 = (f32[320]{0:T(512)S(1)}, f32[320]{0:T(512)}, u32[]{:S(2)}) copy-start(f32[320]{0:T(512)} %param.27) | copy-start | bytes 3844
  11.6 8.6 %copy-start.22 = (f32[256]{0:T(256)S(1)}, f32[256]{0:T(256)}, u32[]{:S(2)}) copy-start(f32[256]{0:T(256)} %param.29) | copy-start | bytes 3076
  11.6 39.8 %copy-start.30 = (bf16[2560,5]{0,1:T(8,128)(2,1)S(1)}, bf16[2560,5]{0,1:T(8,128)(2,1)}, u32[]{:S(2)}) copy-start(bf16[2560,5]{0,1:T(8,128)(2,1)} %param.24) | copy-start | bytes 76804
  51.4 6.2 %copy-start.23 = (f32[5]{0:T(128)S(1)}, f32[5]{0:T(128)}, u32[]{:S(2)}) copy-start(f32[5]{0:T(128)} %param.30) | copy-start | bytes 64
  56.3 1.3 copy-start.1
  56.4 3.9 %copy-start.19 = (f32[2]{0:T(128)S(1)}, f32[2]{0:T(128)}, u32[]{:S(2)}) copy-start(f32[2]{0:T(128)} %fusion.110) | copy-start | bytes 28
  56.4 4.8 %copy-start.8 = (f32[2,256]{1,0:T(2,128)S(1)}, f32[2,256]{1,0:T(2,128)}, u32[]{:S(2)}) copy-start(f32[2,256]{1,0:T(2,128)} %get-tuple-element.62) | copy-start | bytes 6148
  56.4 4.9 %copy-start.10 = (pred[16]{0:T(512)(128)(4,1)S(1)}, pred[16]{0:T(512)(128)(4,1)}, u32[]{:S(2)}) copy-start(pred[16]{0:T(512)(128)(4,1)} %get-tuple-element.24) | copy-start | bytes 52
  56.4 4.9 %copy-start.12 = (pred[16]{0:T(512)(128)(4,1)S(1)}, pred[16]{0:T(512)(128)(4,1)}, u32[]{:S(2)}) copy-start(pred[16]{0:T(512)(128)(4,1)} %get-tuple-element.31) | copy-start | bytes 52
  56.4 5.5 %copy-start.20 = (pred[16]{0:T(512)(128)(4,1)S(1)}, pred[16]{0:T(512)(128)(4,1)}, u32[]{:S(2)}) copy-start(pred[16]{0:T(512)(128)(4,1)} %get-tuple-element.77) | copy-start | bytes 52
  56.4 5.5 %copy-start.27 = (pred[16]{0:T(512)(128)(4,1)S(1)}, pred[16]{0:T(512)(128)(4,1)}, u32[]{:S(2)}) copy-start(pred[16]{0:T(512)(128)(4,1)} %iota_compare_fusion.8) | copy-start | bytes 52
  58.1 8.7 %copy-start.5 = (f32[512]{0:T(512)S(1)}, f32[512]{0:T(512)}, u32[]{:S(2)}) copy-start(f32[512]{0:T(512)} %get-tuple-element.57) | copy-start | bytes 6148
  58.1 8.7 %copy-start.6 = (f32[512]{0:T(512)S(1)}, f32[512]{0:T(512)}, u32[]{:S(2)}) copy-start(f32[512]{0:T(512)} %get-tuple-element.58) | copy-start | bytes 6148
  58.3 8.0 %collective-permute-start = (f32[3,576]{0,1:T(8,128)S(1)}, f32[3,576]{0,1:T(8,128)S(1)}, u32[]{:S(2)}, u32[]{:S(2)}) collective-permute-start(f32[3,576]{0,1:T(8,128)S(1)} %fusion.63), channel_id=1, source_target_pairs={{0,16},{16,32},{32,48},{48,64},{64,80},{80,96},{96,112},{1,17},{17... | collective-permute-start | bytes 20744 | tf_op jit(solution)/shard_map/ppermute | solution.py:17
  68.2 1.0 copy-start
  70.5 10.0 %collective-permute-start.7 = (bf16[5,80,128]{2,1,0:T(8,128)(2,1)S(1)}, bf16[5,80,128]{2,1,0:T(8,128)(2,1)}, u32[]{:S(2)}, u32[]{:S(2)}) collective-permute-start(bf16[5,80,128]{2,1,0:T(8,128)(2,1)S(1)} %pad_maximum_fusion.1), channel_id=1, source_target_pairs={{0,112},{1,113},{2,114},{3,115},{4,116},{5,117},{6,118},{7,119},{8... | collective-permute-start | bytes 307208 | tf_op jit(solution)/shard_map/ppermute | solution.py:139
  72.3 27.9 %copy-start.28 = (f32[5]{0:T(128)S(1)}, f32[5]{0:T(128)}, u32[]{:S(2)}) copy-start(f32[5]{0:T(128)} %param.32) | copy-start | bytes 64
  74.7 24.2 %collective-permute-start.1 = (bf16[5,80,128]{2,1,0:T(8,128)(2,1)S(1)}, bf16[5,80,128]{2,1,0:T(8,128)(2,1)S(1)}, u32[]{:S(2)}, u32[]{:S(2)}) collective-permute-start(bf16[5,80,128]{2,1,0:T(8,128)(2,1)S(1)} %pad_maximum_fusion.1), channel_id=1, source_target_pairs={{0,16},{16,32},{32,48},{48,64},{64,80},{80,96},{96,112},{1,17},{17... | collective-permute-start | bytes 307208 | tf_op jit(solution)/shard_map/ppermute | solution.py:139
  76.6 22.1 %collective-permute-start.2 = (bf16[5,80,128]{2,1,0:T(8,128)(2,1)S(1)}, bf16[5,80,128]{2,1,0:T(8,128)(2,1)S(1)}, u32[]{:S(2)}, u32[]{:S(2)}) collective-permute-start(bf16[5,80,128]{2,1,0:T(8,128)(2,1)S(1)} %pad_maximum_fusion.1), channel_id=1, source_target_pairs={{0,32},{16,48},{32,64},{48,80},{64,96},{80,112},{1,33},{17,49},{33... | collective-permute-start | bytes 307208 | tf_op jit(solution)/shard_map/ppermute | solution.py:139
  77.9 20.7 %collective-permute-start.3 = (bf16[5,80,128]{2,1,0:T(8,128)(2,1)S(1)}, bf16[5,80,128]{2,1,0:T(8,128)(2,1)S(1)}, u32[]{:S(2)}, u32[]{:S(2)}) collective-permute-start(bf16[5,80,128]{2,1,0:T(8,128)(2,1)S(1)} %pad_maximum_fusion.1), channel_id=1, source_target_pairs={{0,48},{16,64},{32,80},{48,96},{64,112},{1,49},{17,65},{33,81},{49... | collective-permute-start | bytes 307208 | tf_op jit(solution)/shard_map/ppermute | solution.py:139
  79.2 19.3 %collective-permute-start.4 = (bf16[5,80,128]{2,1,0:T(8,128)(2,1)S(1)}, bf16[5,80,128]{2,1,0:T(8,128)(2,1)S(1)}, u32[]{:S(2)}, u32[]{:S(2)}) collective-permute-start(bf16[5,80,128]{2,1,0:T(8,128)(2,1)S(1)} %pad_maximum_fusion.1), channel_id=1, source_target_pairs={{0,64},{16,80},{32,96},{48,112},{1,65},{17,81},{33,97},{49,113},{2... | collective-permute-start | bytes 307208 | tf_op jit(solution)/shard_map/ppermute | solution.py:139
  80.5 10.5 %collective-permute-start.6 = (bf16[5,80,128]{2,1,0:T(8,128)(2,1)S(1)}, bf16[5,80,128]{2,1,0:T(8,128)(2,1)S(1)}, u32[]{:S(2)}, u32[]{:S(2)}) collective-permute-start(bf16[5,80,128]{2,1,0:T(8,128)(2,1)S(1)} %pad_maximum_fusion.1), channel_id=1, source_target_pairs={{0,96},{16,112},{1,97},{17,113},{2,98},{18,114},{3,99},{19,115},{4... | collective-permute-start | bytes 307208 | tf_op jit(solution)/shard_map/ppermute | solution.py:139
  91.0 7.4 %collective-permute-start.5 = (bf16[5,80,128]{2,1,0:T(8,128)(2,1)S(1)}, bf16[5,80,128]{2,1,0:T(8,128)(2,1)S(1)}, u32[]{:S(2)}, u32[]{:S(2)}) collective-permute-start(bf16[5,80,128]{2,1,0:T(8,128)(2,1)S(1)} %pad_maximum_fusion.1), channel_id=1, source_target_pairs={{0,80},{16,96},{32,112},{1,81},{17,97},{33,113},{2,82},{18,98},{34... | collective-permute-start | bytes 307208 | tf_op jit(solution)/shard_map/ppermute | solution.py:139
  100.2 1.1 copy-start.21
  101.2 1.6 %copy-start.24 = (pred[128]{0:T(512)(128)(4,1)S(1)}, pred[128]{0:T(512)(128)(4,1)}, u32[]{:S(2)}) copy-start(pred[128]{0:T(512)(128)(4,1)} %get-tuple-element.78) | copy-start | bytes 388
  101.2 1.6 %copy-start.25 = (pred[128]{0:T(512)(128)(4,1)S(1)}, pred[128]{0:T(512)(128)(4,1)}, u32[]{:S(2)}) copy-start(pred[128]{0:T(512)(128)(4,1)} %get-tuple-element.79) | copy-start | bytes 388
  101.2 1.7 %copy-start.29 = (bf16[320,2560]{1,0:T(8,128)(2,1)S(1)}, bf16[320,2560]{1,0:T(8,128)(2,1)}, u32[]{:S(2)}) copy-start(bf16[320,2560]{1,0:T(8,128)(2,1)} %param.34) | copy-start | bytes 4915204
  106.2 4.6 %copy-start.11 = (pred[16]{0:T(512)(128)(4,1)S(1)}, pred[16]{0:T(512)(128)(4,1)}, u32[]{:S(2)}) copy-start(pred[16]{0:T(512)(128)(4,1)} %get-tuple-element.24) | copy-start | bytes 52
  106.2 4.6 %copy-start.13 = (pred[16]{0:T(512)(128)(4,1)S(1)}, pred[16]{0:T(512)(128)(4,1)}, u32[]{:S(2)}) copy-start(pred[16]{0:T(512)(128)(4,1)} %get-tuple-element.31) | copy-start | bytes 52
  106.2 4.6 %copy-start.15 = (f32[5]{0:T(128)S(1)}, f32[5]{0:T(128)}, u32[]{:S(2)}) copy-start(f32[5]{0:T(128)} %get-tuple-element.65) | copy-start | bytes 64
  106.2 4.6 %copy-start.16 = (pred[16]{0:T(512)(128)(4,1)S(1)}, pred[16]{0:T(512)(128)(4,1)}, u32[]{:S(2)}) copy-start(pred[16]{0:T(512)(128)(4,1)} %get-tuple-element.29) | copy-start | bytes 52
  106.2 43.0 %all-to-all-start.1 = ((bf16[16,32,2688]{2,1,0:T(8,128)(2,1)}), bf16[16,32,2688]{2,1,0:T(8,128)(2,1)S(1)}, u32[]{:S(2)}, u32[]{:S(2)}) async-start(bf16[16,32,2688]{2,1,0:T(8,128)(2,1)} %bitcast.102), calls=%async_computation.1 | async-start | bytes 5505024 | tf_op jit(solution)/shard_map/all_to_all | solution.py:182
  111.1 3.0 %copy-start.7 = (f32[16,5]{1,0:T(8,128)S(1)}, f32[16,5]{1,0:T(8,128)}, u32[]{:S(2)}) copy-start(f32[16,5]{1,0:T(8,128)} %get-tuple-element.19) | copy-start | bytes 964
  116.2 1.1 copy-start.2
  118.0 5.1 %collective-permute-start.14 = (bf16[2,5,64,128]{3,2,1,0:T(8,128)(2,1)S(1)}, bf16[2,5,64,128]{3,2,1,0:T(8,128)(2,1)S(1)}, u32[]{:S(2)}, u32[]{:S(2)}) collective-permute-start(bf16[2,5,64,128]{3,2,1,0:T(8,128)(2,1)S(1)} %get-tuple-element.40), channel_id=1, source_target_pairs={{0,112},{16,0},{32,16},{48,32},{64,48},{80,64},{96,80},{112,96},{1... | collective-permute-start | bytes 491528 | tf_op jit(solution)/shard_map/ppermute | solution.py:241
  118.0 16.0 %collective-permute-start.13 = (bf16[2,5,64,128]{3,2,1,0:T(8,128)(2,1)S(1)}, bf16[2,5,64,128]{3,2,1,0:T(8,128)(2,1)S(1)}, u32[]{:S(2)}, u32[]{:S(2)}) collective-permute-start(bf16[2,5,64,128]{3,2,1,0:T(8,128)(2,1)S(1)} %get-tuple-element.41), channel_id=1, source_target_pairs={{0,96},{16,112},{32,0},{48,16},{64,32},{80,48},{96,64},{112,80},{1... | collective-permute-start | bytes 491528 | tf_op jit(solution)/shard_map/ppermute | solution.py:241
  118.0 17.3 %collective-permute-start.12 = (bf16[2,5,64,128]{3,2,1,0:T(8,128)(2,1)}, bf16[2,5,64,128]{3,2,1,0:T(8,128)(2,1)}, u32[]{:S(2)}, u32[]{:S(2)}) collective-permute-start(bf16[2,5,64,128]{3,2,1,0:T(8,128)(2,1)} %get-tuple-element.42), channel_id=1, source_target_pairs={{0,80},{16,96},{32,112},{48,0},{64,16},{80,32},{96,48},{112,64},{1... | collective-permute-start | bytes 491528 | tf_op jit(solution)/shard_map/ppermute | solution.py:241
  118.5 16.8 %collective-permute-start.11 = (bf16[2,5,64,128]{3,2,1,0:T(8,128)(2,1)S(1)}, bf16[2,5,64,128]{3,2,1,0:T(8,128)(2,1)}, u32[]{:S(2)}, u32[]{:S(2)}) collective-permute-start(bf16[2,5,64,128]{3,2,1,0:T(8,128)(2,1)S(1)} %get-tuple-element.43), channel_id=1, source_target_pairs={{0,64},{16,80},{32,96},{48,112},{64,0},{80,16},{96,32},{112,48},{1... | collective-permute-start | bytes 491528 | tf_op jit(solution)/shard_map/ppermute | solution.py:241
  121.7 13.6 %collective-permute-start.10 = (bf16[2,5,64,128]{3,2,1,0:T(8,128)(2,1)S(1)}, bf16[2,5,64,128]{3,2,1,0:T(8,128)(2,1)}, u32[]{:S(2)}, u32[]{:S(2)}) collective-permute-start(bf16[2,5,64,128]{3,2,1,0:T(8,128)(2,1)S(1)} %get-tuple-element.44), channel_id=1, source_target_pairs={{0,48},{16,64},{32,80},{48,96},{64,112},{80,0},{96,16},{112,32},{1... | collective-permute-start | bytes 491528 | tf_op jit(solution)/shard_map/ppermute | solution.py:241
  123.1 10.8 %copy-start.3 = (bf16[2,5,64,128]{3,2,1,0:T(8,128)(2,1)}, bf16[2,5,64,128]{3,2,1,0:T(8,128)(2,1)S(1)}, u32[]{:S(2)}) copy-start(bf16[2,5,64,128]{3,2,1,0:T(8,128)(2,1)S(1)} %collective-permute-done.14) | copy-start | bytes 491524
  123.1 12.7 %collective-permute-start.9 = (bf16[2,5,64,128]{3,2,1,0:T(8,128)(2,1)S(1)}, bf16[2,5,64,128]{3,2,1,0:T(8,128)(2,1)}, u32[]{:S(2)}, u32[]{:S(2)}) collective-permute-start(bf16[2,5,64,128]{3,2,1,0:T(8,128)(2,1)S(1)} %get-tuple-element.45), channel_id=1, source_target_pairs={{0,32},{16,48},{32,64},{48,80},{64,96},{80,112},{96,0},{112,16},{1... | collective-permute-start | bytes 491528 | tf_op jit(solution)/shard_map/ppermute | solution.py:241
  134.0 0.7 copy-start.4
  134.6 4.8 %collective-permute-start.8 = (bf16[2,5,64,128]{3,2,1,0:T(8,128)(2,1)S(1)}, bf16[2,5,64,128]{3,2,1,0:T(8,128)(2,1)}, u32[]{:S(2)}, u32[]{:S(2)}) collective-permute-start(bf16[2,5,64,128]{3,2,1,0:T(8,128)(2,1)S(1)} %get-tuple-element.39), channel_id=1, source_target_pairs={{0,16},{16,32},{32,48},{48,64},{64,80},{80,96},{96,112},{112,0},{1... | collective-permute-start | bytes 491528 | tf_op jit(solution)/shard_map/ppermute | solution.py:241

commit v12 on v10

--- a/solution.py
+++ b/solution.py
@@ -132,7 +132,7 @@
     )
     factor_rows = jnp.broadcast_to(factor_rows, (local_heads, 16, state_size))
     packed = jnp.concatenate([zero_end.astype(jnp.bfloat16), factor_rows], axis=1)
-    sent = lax.all_to_all(jnp.tile(packed[None], (seq_count, 1, 1, 1)), "seq", 0, 0, tiled=True)
+    sent = lax.all_gather(packed, "seq", axis=0)
     sent_states = sent[:, :, :head_size]
     sent_factors = sent[:, :, head_size, 0].astype(jnp.float32) + sent[
         :, :, head_size + 1, 0

time: 145 us -> 146 us (level); the launches traced: 142 us -> 145 us
  blocking collectives: 0 us -> 13.6 us
  waiting for transfers between devices: 65.8 us -> 57.8 us
  starting transfers between devices: 25.3 us -> 21.6 us
  other arithmetic: 14.4 us -> 16.6 us
  matrix products: 18.3 us -> 16.5 us
    all_gather x0 -> x1, blocking collectives: none -> 13.6 us  [per_device(): sent = lax.all_gather(packed, 'seq', axis=0)]
    all_to_all x1 -> x0, waiting for transfers between devices: 7.26 us -> none  [per_device(): lax.all_to_all(jnp.tile(packed[None], (seq_count, 1, 1, 1)), 'seq', 0, 0,...]
    all_to_all x1 -> x0, starting transfers between devices: 4.78 us -> none  [per_device(): lax.all_to_all(jnp.tile(packed[None], (seq_count, 1, 1, 1)), 'seq', 0, 0,...]
    ppermute x7, waiting for transfers between devices: 12.5 us -> 15.4 us  [per_device(): lax.ppermute(jnp.take(chunks, target, axis=0), 'seq', route)]
    all_to_all x1, waiting for transfers between devices: 11.6 us -> 9.52 us  [per_device(): lax.all_to_all(partials, 'tensor', 0, 0, tiled=True)]
    unnamed x60 -> x74, local copies, waits for them, and re-layouts: 6.44 us -> 7.34 us
  transfers between devices with their start and end apart: 11 -> 10, of which waited for: 10 -> 5; matrix products, arithmetic and copies ran while one was open for 17% -> 15% of each run, Pallas kernels for 0% -> 0%
where the time goes in v12:
time: 146 us; the launch traced here: 145 us
  waiting for transfers between devices  57.8 us (40%)
  starting transfers between devices  21.6 us (15%)
  local copies, waits for them, and re-layouts  17.1 us (12%)
  other arithmetic  16.6 us (11%)
  matrix products  16.5 us (11%)
  blocking collectives  13.6 us (9%)
  between operations  1.61 us (1%)
    all_to_all x1, waiting for transfers between devices, per_device(): lax.all_to_all(jnp.tile(tokens, (lax.axis_size('tensor'), 1)), 'tensor',...  30 us
    ppermute x7, waiting for transfers between devices, per_device(): lax.ppermute(jnp.take(chunks, target, axis=0), 'seq', route)  15.4 us
    all_gather x1, blocking collectives, per_device(): sent = lax.all_gather(packed, 'seq', axis=0)  13.6 us
    all_to_all x1, waiting for transfers between devices, per_device(): lax.all_to_all(partials, 'tensor', 0, 0, tiled=True)  9.52 us
    all_to_all x1, starting transfers between devices, per_device(): lax.all_to_all(jnp.tile(tokens, (lax.axis_size('tensor'), 1)), 'tensor',...  8.18 us
    ppermute x7, starting transfers between devices, per_device(): lax.ppermute(jnp.take(chunks, target, axis=0), 'seq', route)  7.78 us
    unnamed x74, local copies, waits for them, and re-layouts  7.34 us
    dot_general x1, matrix products, per_device(): jnp.dot(gathered, weight_all, preferred_element_type=jnp.float32)  4.95 us
  transfers between devices with their start and end apart: 10, of which 5 were waited for; matrix products, arithmetic and copies ran while one was open for 15% of the time, Pallas kernels for 0%

profile of v12, /device:TPU:6, one launch (start us, length us, event | category | flops | bytes accessed | tf_op | source)
XLA Modules:
  0.0 144.9 jit_solution(10669648068259034432)
XLA Ops:
  0.6 2.7 %tile.2 = bf16[16,32,2560]{2,1,0:T(8,128)(2,1)} broadcast(bf16[32,2560]{1,0:T(8,128)(2,1)} %param.21), dimensions={1,2} | broadcast | bytes 2785280 | tf_op jit(solution)/shard_map/tile | solution.py:51
  3.3 8.2 %all-to-all-start = ((bf16[16,32,2560]{2,1,0:T(8,128)(2,1)}), bf16[16,32,2560]{2,1,0:T(8,128)(2,1)S(1)}, u32[]{:S(2)}, u32[]{:S(2)}) async-start(bf16[16,32,2560]{2,1,0:T(8,128)(2,1)} %tile.2), calls=%async_computation | async-start | bytes 5242880 | tf_op jit(solution)/shard_map/all_to_all | solution.py:50
  11.6 0.6 iota_compare_fusion.6
  12.4 2.4 %copy.98 = bf16[2560,256]{0,1:T(8,128)(2,1)} copy(bf16[2560,256]{1,0:T(8,128)(2,1)} %param.25) | data formatting | bytes 2621440 | tf_op args[4]
  15.2 0.2 convert_reduce_fusion.1
  15.4 0.2 fusion.94
  15.6 0.2 slice_reduce_fusion.1
  16.0 0.6 fusion.110
  16.6 0.7 gather_fusion
  17.3 0.7 compare_and_fusion.4
  18.3 0.2 fusion.95
  18.5 1.1 compare_and_fusion.2
  19.8 0.7 fusion.81
  20.5 0.8 compare_and_fusion
  21.3 30.0 %all-to-all-done = bf16[16,32,2560]{2,1,0:T(8,128)(2,1)S(1)} async-done(((bf16[16,32,2560]{2,1,0:T(8,128)(2,1)}), bf16[16,32,2560]{2,1,0:T(8,128)(2,1)S(1)}, u32[]{:S(2)}, u32[]{:S(2)}) %all-to-all-start) | async-done | bytes 2621472 | tf_op jit(solution)/shard_map/all_to_all | solution.py:50
  51.4 4.9 %fusion.31 = f32[512,901]{0,1:T(8,128)S(1)} fusion(bf16[512,2560]{1,0:T(8,128)(2,1)S(1)} %bitcast.118, bf16[2560,256]{0,1:T(8,128)(2,1)} %copy.98, bf16[2560,5]{0,1:T(8,128)(2,1)S(1)} %copy-done.32, bf16[2560,320]{0,1:T(8,128)(2,1)} %param.23, bf16[2560,320]{0,1:T(8,128)(2,1)} %param.22), kind=kOutput, calls=%fused_computation.35 | convolution fusion | flops 2380369920 | bytes 9079808 | tf_op jit(solution)/shard_map/dot_general | solution.py:53
  56.4 1.1 copy-done.1
  57.7 0.2 convolution_bitcast_fusion
  57.9 0.2 slice_reduce_fusion
  58.1 0.2 fusion.65
  58.3 1.9 %collective-permute-start = (f32[3,576]{0,1:T(8,128)S(1)}, f32[3,576]{0,1:T(8,128)S(1)}, u32[]{:S(2)}, u32[]{:S(2)}) collective-permute-start(f32[3,576]{0,1:T(8,128)S(1)} %fusion.65), channel_id=1, source_target_pairs={{0,16},{16,32},{32,48},{48,64},{64,80},{80,96},{96,112},{1,17},{17... | collective-permute-start | bytes 20744 | tf_op jit(solution)/shard_map/ppermute | solution.py:17
  60.3 0.5 multiply_convert_fusion.1
  60.9 0.6 gather_fusion.1
  61.6 0.7 fusion.83
  62.4 0.5 slice_bitcast_fusion.14
  62.9 0.6 stack.8
  63.5 2.8 %collective-permute-done = f32[3,576]{0,1:T(8,128)S(1)} collective-permute-done((f32[3,576]{0,1:T(8,128)S(1)}, f32[3,576]{0,1:T(8,128)S(1)}, u32[]{:S(2)}, u32[]{:S(2)}) %collective-permute-start) | collective-permute-done | bytes 6944 | tf_op jit(solution)/shard_map/ppermute | solution.py:17
  66.3 0.4 maximum_maximum_fusion
  66.7 1.4 divide_multiply_fusion
  68.2 1.0 copy-done
  69.3 0.4 reshape.563
  69.7 0.2 reshape.565
  69.9 0.2 reshape.564
  70.1 0.4 fusion.54
  70.8 13.6 %all-gather = bf16[40,80,128]{2,1,0:T(8,128)(2,1)S(1)} all-gather(bf16[5,80,128]{2,1,0:T(8,128)(2,1)S(1)} %pad_maximum_fusion.1), channel_id=2, replica_groups=mesh['seq'=8,'tensor'=16] {'seq'}, dimensions={0}, use_global_device_ids=true | all-gather | bytes 921600 | tf_op jit(solution)/shard_map/all_gather | solution.py:135
  84.5 0.7 copy.129
  85.2 0.1 copy.128
  85.3 0.7 convert_add_fusion.1
  86.0 0.4 fusion.66
  86.4 3.0 %fusion.40 = f32[2,256,5,64]{1,3,2,0:T(8,128)S(1)} fusion(f32[2,256,5]{1,2,0:T(8,128)S(1)} %bitcast.132, f32[2,256,5]{1,2,0:T(8,128)S(1)} %convolution_bitcast_fusion, f32[2,256,256]{2,1,0:T(8,128)S(1)} %fusion.66, pred[2,256,256]{2,1,0:T(8,128)(4,1)} %compare_and_fusion, f32[2,256,5,64]{1,0,3,2:T(2,128)S(1)} %reshape.563), kind=kOutput, calls=%fused_computation.47 | convolution fusion | flops 254935040 | bytes 1986560 | tf_op jit(solution)/shard_map/cijh,cjhp->cihp/dot_general | solution.py:104
  89.4 0.3 select_bitcast_fusion.7
  89.7 0.5 fusion.44
  90.3 0.5 copy.113
  90.9 1.4 multiply_convert_fusion
  92.5 3.2 %convolution_convert_fusion = bf16[512,2688]{1,0:T(8,128)(2,1)} fusion(bf16[320,2560]{1,0:T(8,128)(2,1)S(1)} %copy-done.31, bf16[128,2688]{1,0:T(8,128)(2,1)S(1)} %pad_convert_fusion, bf16[512,128]{0,1:T(8,128)(2,1)S(1)} %select_select_fusion, bf16[512,320]{0,1:T(8,128)(2,1)S(1)} %get-tuple-element.33), kind=kOutput, calls=%fused_computation.18 | convolution fusion | flops 1242644480 | bytes 5537792 | tf_op jit(solution)/shard_map/dot_general | solution.py:177
  95.8 3.7 %all-to-all-start.1 = ((bf16[16,32,2688]{2,1,0:T(8,128)(2,1)}), bf16[16,32,2688]{2,1,0:T(8,128)(2,1)S(1)}, u32[]{:S(2)}, u32[]{:S(2)}) async-start(bf16[16,32,2688]{2,1,0:T(8,128)(2,1)} %bitcast.117), calls=%async_computation.1 | async-start | bytes 5505024 | tf_op jit(solution)/shard_map/all_to_all | solution.py:182
  99.7 0.7 gather_fusion.2
  100.9 1.1 fusion.105
  102.0 1.7 %fusion = f32[16,5,64,128]{3,2,1,0:T(8,128)S(1)} fusion(f32[256,5,64]{0,2,1:T(8,128)S(1)} %bitcast.125, f32[16,256,5]{1,2,0:T(8,128)S(1)} %multiply_select_fusion, f32[512,576]{0,1:T(8,128)} %copy-done), kind=kOutput, calls=%fused_computation.3 | convolution fusion | flops 336855040 | bytes 3096576 | tf_op jit(solution)/shard_map/rjhp,jn->rhpn/dot_general | solution.py:221
  103.8 2.0 %add_convert_fusion = bf16[16,5,64,128]{3,2,1,0:T(8,128)(2,1)S(1)} fusion(f32[16,5,64,128]{3,2,1,0:T(8,128)S(1)} %fusion, f32[256,5,64]{0,2,1:T(8,128)S(1)} %bitcast.130, f32[16,256,5]{1,2,0:T(8,128)S(1)} %multiply_select_fusion.1, f32[5,64,128]{2,1,0:T(8,128)S(1)} %copy-done.4, f32[16,5]{1,0:T(8,128)S(1)} %get-tuple-element.21, ...), kind=kOutput, calls=%fused_computation.19 | convolution fusion | flops 341442560 | bytes 4735936 | tf_op jit(solution)/shard_map/rjhp,jn->rhpn/dot_general | solution.py:221
  105.8 1.1 copy-done.2
  106.9 0.8 select_bitcast_fusion.6
  107.7 1.4 collective-permute-start.6
  109.0 0.7 collective-permute-start.5
  109.8 2.5 %collective-permute-start.4 = (bf16[2,5,64,128]{3,2,1,0:T(8,128)(2,1)S(1)}, bf16[2,5,64,128]{3,2,1,0:T(8,128)(2,1)}, u32[]{:S(2)}, u32[]{:S(2)}) collective-permute-start(bf16[2,5,64,128]{3,2,1,0:T(8,128)(2,1)S(1)} %get-tuple-element.43), channel_id=1, source_target_pairs={{0,64},{16,80},{32,96},{48,112},{64,0},{80,16},{96,32},{112,48},{1... | collective-permute-start | bytes 491528 | tf_op jit(solution)/shard_map/ppermute | solution.py:241
  112.3 2.1 %collective-permute-start.3 = (bf16[2,5,64,128]{3,2,1,0:T(8,128)(2,1)S(1)}, bf16[2,5,64,128]{3,2,1,0:T(8,128)(2,1)}, u32[]{:S(2)}, u32[]{:S(2)}) collective-permute-start(bf16[2,5,64,128]{3,2,1,0:T(8,128)(2,1)S(1)} %get-tuple-element.44), channel_id=1, source_target_pairs={{0,48},{16,64},{32,80},{48,96},{64,112},{80,0},{96,16},{112,32},{1... | collective-permute-start | bytes 491528 | tf_op jit(solution)/shard_map/ppermute | solution.py:241
  114.4 1.1 collective-permute-start.2
  115.4 10.6 %collective-permute-done.6 = bf16[2,5,64,128]{3,2,1,0:T(8,128)(2,1)S(1)} collective-permute-done((bf16[2,5,64,128]{3,2,1,0:T(8,128)(2,1)S(1)}, bf16[2,5,64,128]{3,2,1,0:T(8,128)(2,1)S(1)}, u32[]{:S(2)}, u32[]{:S(2)}) %collective-permute-start.6) | collective-permute-done | bytes 163872 | tf_op jit(solution)/shard_map/ppermute | solution.py:241
  126.0 0.7 copy-done.6
  126.7 4.8 %collective-permute-done.1 = bf16[2,5,64,128]{3,2,1,0:T(8,128)(2,1)} collective-permute-done((bf16[2,5,64,128]{3,2,1,0:T(8,128)(2,1)S(1)}, bf16[2,5,64,128]{3,2,1,0:T(8,128)(2,1)}, u32[]{:S(2)}, u32[]{:S(2)}) %collective-permute-start.1) | collective-permute-done | bytes 163872 | tf_op jit(solution)/shard_map/ppermute | solution.py:241
  131.5 2.3 %convert_add_fusion = f32[2,5,64,128]{3,2,1,0:T(8,128)} fusion(bf16[2,5,64,128]{3,2,1,0:T(8,128)(2,1)} %copy-done.5, bf16[2,5,64,128]{3,2,1,0:T(8,128)(2,1)} %copy-done.6, bf16[2,5,64,128]{3,2,1,0:T(8,128)(2,1)} %collective-permute-done.5, bf16[2,5,64,128]{3,2,1,0:T(8,128)(2,1)} %collective-permute-done.4, ...), kind=kLoop, calls=%fused_computation.76 | loop fusion | flops 1310720 | bytes 1638405 | tf_op jit(solution)/shard_map/add | solution.py:243
  133.9 9.5 %all-to-all-done.1 = bf16[16,32,2688]{2,1,0:T(8,128)(2,1)S(1)} async-done(((bf16[16,32,2688]{2,1,0:T(8,128)(2,1)}), bf16[16,32,2688]{2,1,0:T(8,128)(2,1)S(1)}, u32[]{:S(2)}, u32[]{:S(2)}) %all-to-all-start.1) | async-done | bytes 2752544 | tf_op jit(solution)/shard_map/all_to_all | solution.py:182
  143.4 0.2 add_reduce_fusion
  143.6 1.3 multiply_reduce_fusion
  (130 shorter events, 2.9 us)
Async XLA Ops:
  3.3 9.1 %copy-start.33 = (f32[5]{0:T(128)S(1)}, f32[5]{0:T(128)}, u32[]{:S(2)}) copy-start(f32[5]{0:T(128)} %param.31) | copy-start | bytes 64
  3.3 48.1 %all-to-all-start = ((bf16[16,32,2560]{2,1,0:T(8,128)(2,1)}), bf16[16,32,2560]{2,1,0:T(8,128)(2,1)S(1)}, u32[]{:S(2)}, u32[]{:S(2)}) async-start(bf16[16,32,2560]{2,1,0:T(8,128)(2,1)} %tile.2), calls=%async_computation | async-start | bytes 5242880 | tf_op jit(solution)/shard_map/all_to_all | solution.py:50
  11.5 3.3 %copy-start.23 = (s32[16]{0:T(128)S(1)}, s32[16]{0:T(128)}, u32[]{:S(2)}) copy-start(s32[16]{0:T(128)} %param.35) | copy-start | bytes 196
  11.5 3.5 %copy-start.29 = (s32[16]{0:T(128)S(1)}, s32[16]{0:T(128)}, u32[]{:S(2)}) copy-start(s32[16]{0:T(128)} %param.36) | copy-start | bytes 196
  11.5 4.4 %copy-start.34 = (s32[16]{0:T(128)S(1)}, s32[16]{0:T(128)}, u32[]{:S(2)}) copy-start(s32[16]{0:T(128)} %param.37) | copy-start | bytes 196
  11.5 6.5 %copy-start.13 = (f32[4,320]{1,0:T(4,128)S(1)}, f32[4,320]{1,0:T(4,128)}, u32[]{:S(2)}) copy-start(f32[4,320]{1,0:T(4,128)} %param.26) | copy-start | bytes 15364
  11.5 6.5 %copy-start.19 = (f32[4,256]{1,0:T(4,128)S(1)}, f32[4,256]{1,0:T(4,128)}, u32[]{:S(2)}) copy-start(f32[4,256]{1,0:T(4,128)} %param.28) | copy-start | bytes 12292
  11.5 6.6 %copy-start.22 = (f32[320]{0:T(512)S(1)}, f32[320]{0:T(512)}, u32[]{:S(2)}) copy-start(f32[320]{0:T(512)} %param.27) | copy-start | bytes 3844
  11.6 6.6 %copy-start.25 = (f32[256]{0:T(256)S(1)}, f32[256]{0:T(256)}, u32[]{:S(2)}) copy-start(f32[256]{0:T(256)} %param.29) | copy-start | bytes 3076
  11.6 39.8 %copy-start.32 = (bf16[2560,5]{0,1:T(8,128)(2,1)S(1)}, bf16[2560,5]{0,1:T(8,128)(2,1)}, u32[]{:S(2)}) copy-start(bf16[2560,5]{0,1:T(8,128)(2,1)} %param.24) | copy-start | bytes 76804
  18.0 43.6 %copy-start.14 = (pred[16]{0:T(512)(128)(4,1)}, pred[16]{0:T(512)(128)(4,1)S(1)}, u32[]{:S(2)}) copy-start(pred[16]{0:T(512)(128)(4,1)S(1)} %get-tuple-element.24) | copy-start | bytes 52
  18.0 43.6 %copy-start.16 = (pred[16]{0:T(512)(128)(4,1)}, pred[16]{0:T(512)(128)(4,1)S(1)}, u32[]{:S(2)}) copy-start(pred[16]{0:T(512)(128)(4,1)S(1)} %get-tuple-element.31) | copy-start | bytes 52
  18.2 42.7 %copy-start.12 = (s32[1024]{0:T(1024)}, s32[1024]{0:T(1024)S(1)}, u32[]{:S(2)}) copy-start(s32[1024]{0:T(1024)S(1)} %pad_clamp_fusion) | copy-start | bytes 12292
  51.4 6.2 %copy-start.26 = (f32[5]{0:T(128)S(1)}, f32[5]{0:T(128)}, u32[]{:S(2)}) copy-start(f32[5]{0:T(128)} %param.30) | copy-start | bytes 64
  56.3 1.3 copy-start.1
  58.3 8.0 %collective-permute-start = (f32[3,576]{0,1:T(8,128)S(1)}, f32[3,576]{0,1:T(8,128)S(1)}, u32[]{:S(2)}, u32[]{:S(2)}) collective-permute-start(f32[3,576]{0,1:T(8,128)S(1)} %fusion.65), channel_id=1, source_target_pairs={{0,16},{16,32},{32,48},{48,64},{64,80},{80,96},{96,112},{1,17},{17... | collective-permute-start | bytes 20744 | tf_op jit(solution)/shard_map/ppermute | solution.py:17
  68.2 1.0 copy-start
  69.2 1.3 copy-start.9
  86.4 3.3 %copy-start.18 = (f32[2,5]{1,0:T(2,128)S(1)}, f32[2,5]{1,0:T(2,128)}, u32[]{:S(2)}) copy-start(f32[2,5]{1,0:T(2,128)} %stack.8) | copy-start | bytes 124
  86.4 3.3 %copy-start.30 = (f32[5]{0:T(128)S(1)}, f32[5]{0:T(128)}, u32[]{:S(2)}) copy-start(f32[5]{0:T(128)} %param.32) | copy-start | bytes 64
  89.7 1.2 copy-start.3
  89.7 1.2 copy-start.24
  90.8 1.6 %copy-start.27 = (pred[128]{0:T(512)(128)(4,1)S(1)}, pred[128]{0:T(512)(128)(4,1)}, u32[]{:S(2)}) copy-start(pred[128]{0:T(512)(128)(4,1)} %get-tuple-element.87) | copy-start | bytes 388
  90.8 1.6 %copy-start.28 = (pred[128]{0:T(512)(128)(4,1)S(1)}, pred[128]{0:T(512)(128)(4,1)}, u32[]{:S(2)}) copy-start(pred[128]{0:T(512)(128)(4,1)} %get-tuple-element.88) | copy-start | bytes 388
  90.8 1.7 %copy-start.31 = (bf16[320,2560]{1,0:T(8,128)(2,1)S(1)}, bf16[320,2560]{1,0:T(8,128)(2,1)}, u32[]{:S(2)}) copy-start(bf16[320,2560]{1,0:T(8,128)(2,1)} %param.34) | copy-start | bytes 4915204
  95.8 4.6 %copy-start.15 = (pred[16]{0:T(512)(128)(4,1)S(1)}, pred[16]{0:T(512)(128)(4,1)}, u32[]{:S(2)}) copy-start(pred[16]{0:T(512)(128)(4,1)} %copy-done.14) | copy-start | bytes 52
  95.8 4.6 %copy-start.17 = (pred[16]{0:T(512)(128)(4,1)S(1)}, pred[16]{0:T(512)(128)(4,1)}, u32[]{:S(2)}) copy-start(pred[16]{0:T(512)(128)(4,1)} %copy-done.16) | copy-start | bytes 52
  95.8 4.7 %copy-start.20 = (f32[5]{0:T(128)S(1)}, f32[5]{0:T(128)}, u32[]{:S(2)}) copy-start(f32[5]{0:T(128)} %get-tuple-element.74) | copy-start | bytes 64
  95.8 4.7 %copy-start.21 = (pred[16]{0:T(512)(128)(4,1)S(1)}, pred[16]{0:T(512)(128)(4,1)}, u32[]{:S(2)}) copy-start(pred[16]{0:T(512)(128)(4,1)} %get-tuple-element.29) | copy-start | bytes 52
  95.8 4.8 %copy-start.8 = (pred[16,256]{1,0:T(8,128)(4,1)S(1)}, pred[16,256]{1,0:T(8,128)(4,1)}, u32[]{:S(2)}) copy-start(pred[16,256]{1,0:T(8,128)(4,1)} %get-tuple-element.72) | copy-start | bytes 12292
  95.8 4.9 %copy-start.7 = (pred[16,256]{1,0:T(8,128)(4,1)S(1)}, pred[16,256]{1,0:T(8,128)(4,1)}, u32[]{:S(2)}) copy-start(pred[16,256]{1,0:T(8,128)(4,1)} %get-tuple-element.73) | copy-start | bytes 12292
  95.8 5.0 %copy-start.10 = (f32[5]{0:T(128)S(1)}, f32[5]{0:T(128)}, u32[]{:S(2)}) copy-start(f32[5]{0:T(128)} %get-tuple-element.78) | copy-start | bytes 64
  95.8 47.6 %all-to-all-start.1 = ((bf16[16,32,2688]{2,1,0:T(8,128)(2,1)}), bf16[16,32,2688]{2,1,0:T(8,128)(2,1)S(1)}, u32[]{:S(2)}, u32[]{:S(2)}) async-start(bf16[16,32,2688]{2,1,0:T(8,128)(2,1)} %bitcast.117), calls=%async_computation.1 | async-start | bytes 5505024 | tf_op jit(solution)/shard_map/all_to_all | solution.py:182
  100.8 3.0 %copy-start.4 = (f32[5,64,128]{2,1,0:T(8,128)S(1)}, f32[5,64,128]{2,1,0:T(8,128)}, u32[]{:S(2)}) copy-start(f32[5,64,128]{2,1,0:T(8,128)} %copy-done.3) | copy-start | bytes 491524
  100.8 3.0 %copy-start.11 = (f32[16,5]{1,0:T(8,128)S(1)}, f32[16,5]{1,0:T(8,128)}, u32[]{:S(2)}) copy-start(f32[16,5]{1,0:T(8,128)} %get-tuple-element.19) | copy-start | bytes 964
  105.8 1.1 copy-start.2
  107.7 6.7 %collective-permute-start.7 = (bf16[2,5,64,128]{3,2,1,0:T(8,128)(2,1)S(1)}, bf16[2,5,64,128]{3,2,1,0:T(8,128)(2,1)S(1)}, u32[]{:S(2)}, u32[]{:S(2)}) collective-permute-start(bf16[2,5,64,128]{3,2,1,0:T(8,128)(2,1)S(1)} %get-tuple-element.40), channel_id=1, source_target_pairs={{0,112},{16,0},{32,16},{48,32},{64,48},{80,64},{96,80},{112,96},{1... | collective-permute-start | bytes 491528 | tf_op jit(solution)/shard_map/ppermute | solution.py:241
  107.7 18.4 %collective-permute-start.6 = (bf16[2,5,64,128]{3,2,1,0:T(8,128)(2,1)S(1)}, bf16[2,5,64,128]{3,2,1,0:T(8,128)(2,1)S(1)}, u32[]{:S(2)}, u32[]{:S(2)}) collective-permute-start(bf16[2,5,64,128]{3,2,1,0:T(8,128)(2,1)S(1)} %get-tuple-element.41), channel_id=1, source_target_pairs={{0,96},{16,112},{32,0},{48,16},{64,32},{80,48},{96,64},{112,80},{1... | collective-permute-start | bytes 491528 | tf_op jit(solution)/shard_map/ppermute | solution.py:241
  109.0 17.7 %collective-permute-start.5 = (bf16[2,5,64,128]{3,2,1,0:T(8,128)(2,1)}, bf16[2,5,64,128]{3,2,1,0:T(8,128)(2,1)}, u32[]{:S(2)}, u32[]{:S(2)}) collective-permute-start(bf16[2,5,64,128]{3,2,1,0:T(8,128)(2,1)} %get-tuple-element.42), channel_id=1, source_target_pairs={{0,80},{16,96},{32,112},{48,0},{64,16},{80,32},{96,48},{112,64},{1... | collective-permute-start | bytes 491528 | tf_op jit(solution)/shard_map/ppermute | solution.py:241
  109.8 16.9 %collective-permute-start.4 = (bf16[2,5,64,128]{3,2,1,0:T(8,128)(2,1)S(1)}, bf16[2,5,64,128]{3,2,1,0:T(8,128)(2,1)}, u32[]{:S(2)}, u32[]{:S(2)}) collective-permute-start(bf16[2,5,64,128]{3,2,1,0:T(8,128)(2,1)S(1)} %get-tuple-element.43), channel_id=1, source_target_pairs={{0,64},{16,80},{32,96},{48,112},{64,0},{80,16},{96,32},{112,48},{1... | collective-permute-start | bytes 491528 | tf_op jit(solution)/shard_map/ppermute | solution.py:241
  112.3 14.4 %collective-permute-start.3 = (bf16[2,5,64,128]{3,2,1,0:T(8,128)(2,1)S(1)}, bf16[2,5,64,128]{3,2,1,0:T(8,128)(2,1)}, u32[]{:S(2)}, u32[]{:S(2)}) collective-permute-start(bf16[2,5,64,128]{3,2,1,0:T(8,128)(2,1)S(1)} %get-tuple-element.44), channel_id=1, source_target_pairs={{0,48},{16,64},{32,80},{48,96},{64,112},{80,0},{96,16},{112,32},{1... | collective-permute-start | bytes 491528 | tf_op jit(solution)/shard_map/ppermute | solution.py:241
  114.4 11.6 %copy-start.5 = (bf16[2,5,64,128]{3,2,1,0:T(8,128)(2,1)}, bf16[2,5,64,128]{3,2,1,0:T(8,128)(2,1)S(1)}, u32[]{:S(2)}) copy-start(bf16[2,5,64,128]{3,2,1,0:T(8,128)(2,1)S(1)} %collective-permute-done.7) | copy-start | bytes 491524
  114.4 12.3 %collective-permute-start.2 = (bf16[2,5,64,128]{3,2,1,0:T(8,128)(2,1)S(1)}, bf16[2,5,64,128]{3,2,1,0:T(8,128)(2,1)}, u32[]{:S(2)}, u32[]{:S(2)}) collective-permute-start(bf16[2,5,64,128]{3,2,1,0:T(8,128)(2,1)S(1)} %get-tuple-element.45), channel_id=1, source_target_pairs={{0,32},{16,48},{32,64},{48,80},{64,96},{80,112},{96,0},{112,16},{1... | collective-permute-start | bytes 491528 | tf_op jit(solution)/shard_map/ppermute | solution.py:241
  126.0 0.7 copy-start.6
  126.7 4.8 %collective-permute-start.1 = (bf16[2,5,64,128]{3,2,1,0:T(8,128)(2,1)S(1)}, bf16[2,5,64,128]{3,2,1,0:T(8,128)(2,1)}, u32[]{:S(2)}, u32[]{:S(2)}) collective-permute-start(bf16[2,5,64,128]{3,2,1,0:T(8,128)(2,1)S(1)} %get-tuple-element.39), channel_id=1, source_target_pairs={{0,16},{16,32},{32,48},{48,64},{64,80},{80,96},{96,112},{112,0},{1... | collective-permute-start | bytes 491528 | tf_op jit(solution)/shard_map/ppermute | solution.py:241

commit v13 on v10

--- a/solution.py
+++ b/solution.py
@@ -105,7 +105,7 @@
     last_match = (segs == segs[:, -1:]).astype(jnp.float32)
     weight_last = jnp.exp(decay_sum[:, -1:, :] - decay_sum) * steps * last_match[..., None]
     local = jnp.einsum(
-        "cjhp,cjn->chpn", weight_last[..., None] * values, keys, precision=HIGH_PRECISION
+        "cjhp,cjn->chpn", weight_last[..., None] * values, keys, preferred_element_type=jnp.float32
     )
     passes = jnp.exp(decay_sum[:, -1, :]) * (segs[:, -1] == prior).astype(jnp.float32)[:, None]
 
@@ -147,7 +147,7 @@
     block_states = zero_starts + factors[:, :, None, None] * incoming[None]
     keep = jnp.exp(decay_sum) * (segs == prior[:, None]).astype(jnp.float32)[..., None]
     outer = keep[..., None] * jnp.einsum(
-        "cin,chpn->cihp", queries, block_states, precision=HIGH_PRECISION
+        "cin,chpn->cihp", queries, block_states, preferred_element_type=jnp.float32
     )
     output = (inner + outer + skip_gain[None, None, :, None] * values).reshape(
         row_count, local_inner

time: 145 us -> 144 us (level)
  other arithmetic: 14.4 us -> 18.2 us
  waiting for transfers between devices: 65.8 us -> 62.9 us
    all_to_all x1, waiting for transfers between devices: 30.6 us -> 27.5 us  [per_device(): lax.all_to_all(jnp.tile(tokens, (lax.axis_size('tensor'), 1)), 'tensor',...]
    unnamed x60 -> x80, local copies, waits for them, and re-layouts: 6.44 us -> 6.46 us
  transfers between devices with their start and end apart: 11 -> 11, of which waited for: 10 -> 10; matrix products, arithmetic and copies ran while one was open for 17% -> 19% of each run, Pallas kernels for 0% -> 0%
where the time goes in v13:
time: 144 us; the launch traced here: 142 us
  waiting for transfers between devices  62.9 us (44%)
  starting transfers between devices  25.5 us (18%)
  other arithmetic  18.2 us (13%)
  local copies, waits for them, and re-layouts  17 us (12%)
  matrix products  16.9 us (12%)
    all_to_all x1, waiting for transfers between devices, per_device(): lax.all_to_all(jnp.tile(tokens, (lax.axis_size('tensor'), 1)), 'tensor',...  27.5 us
    ppermute x7, waiting for transfers between devices, per_device(): lax.ppermute(jnp.take(chunks, target, axis=0), 'seq', route)  12.5 us
    all_to_all x1, waiting for transfers between devices, per_device(): lax.all_to_all(partials, 'tensor', 0, 0, tiled=True)  11.4 us
    all_to_all x1, starting transfers between devices, per_device(): lax.all_to_all(jnp.tile(tokens, (lax.axis_size('tensor'), 1)), 'tensor',...  8.18 us
    all_to_all x1, waiting for transfers between devices, per_device(): lax.all_to_all(jnp.tile(packed[None], (seq_count, 1, 1, 1)), 'seq', 0, 0,...  8.17 us
    ppermute x7, starting transfers between devices, per_device(): lax.ppermute(jnp.take(chunks, target, axis=0), 'seq', route)  6.68 us
    unnamed x80, local copies, waits for them, and re-layouts  6.46 us
    dot_general x1, matrix products, per_device(): jnp.dot(gathered, weight_all, preferred_element_type=jnp.float32)  4.91 us
  transfers between devices with their start and end apart: 11, of which 10 were waited for; matrix products, arithmetic and copies ran while one was open for 19% of the time, Pallas kernels for 0%

profile of v13, /device:TPU:6, one launch (start us, length us, event | category | flops | bytes accessed | tf_op | source)
XLA Modules:
  0.0 141.9 jit_solution(6722864287608977177)
XLA Ops:
  0.6 2.7 %tile.4 = bf16[16,32,2560]{2,1,0:T(8,128)(2,1)} broadcast(bf16[32,2560]{1,0:T(8,128)(2,1)} %param.21), dimensions={1,2} | broadcast | bytes 2785280 | tf_op jit(solution)/shard_map/tile | solution.py:51
  3.3 8.2 %all-to-all-start = ((bf16[16,32,2560]{2,1,0:T(8,128)(2,1)}), bf16[16,32,2560]{2,1,0:T(8,128)(2,1)S(1)}, u32[]{:S(2)}, u32[]{:S(2)}) async-start(bf16[16,32,2560]{2,1,0:T(8,128)(2,1)} %tile.4), calls=%async_computation | async-start | bytes 5242880 | tf_op jit(solution)/shard_map/all_to_all | solution.py:50
  11.6 0.6 iota_compare_fusion.6
  12.2 0.5 iota_compare_fusion.8
  12.7 2.4 %copy.117 = bf16[2560,256]{0,1:T(8,128)(2,1)} copy(bf16[2560,256]{1,0:T(8,128)(2,1)} %param.25) | data formatting | bytes 2621440 | tf_op args[4]
  15.5 0.2 convert_reduce_fusion.1
  16.0 0.2 slice_reduce_fusion.7
  16.4 0.6 fusion.110
  17.0 0.7 gather_fusion
  17.7 1.2 compare_and_fusion.4
  18.9 0.6 compare_and_fusion.1
  19.4 0.7 fusion.90
  20.2 0.7 fusion.97
  21.0 1.2 compare_and_fusion.2
  22.2 0.6 compare_convert_fusion.1
  22.9 0.7 fusion.93
  23.9 27.5 %all-to-all-done = bf16[16,32,2560]{2,1,0:T(8,128)(2,1)S(1)} async-done(((bf16[16,32,2560]{2,1,0:T(8,128)(2,1)}), bf16[16,32,2560]{2,1,0:T(8,128)(2,1)S(1)}, u32[]{:S(2)}, u32[]{:S(2)}) %all-to-all-start) | async-done | bytes 2621472 | tf_op jit(solution)/shard_map/all_to_all | solution.py:50
  51.4 4.9 %fusion.31 = f32[512,901]{0,1:T(8,128)S(1)} fusion(bf16[512,2560]{1,0:T(8,128)(2,1)S(1)} %bitcast.103, bf16[2560,256]{0,1:T(8,128)(2,1)} %copy.117, bf16[2560,5]{0,1:T(8,128)(2,1)S(1)} %copy-done.36, bf16[2560,320]{0,1:T(8,128)(2,1)} %param.23, bf16[2560,320]{0,1:T(8,128)(2,1)} %param.22), kind=kOutput, calls=%fused_computation.35 | convolution fusion | flops 2380369920 | bytes 9079808 | tf_op jit(solution)/shard_map/dot_general | solution.py:53
  56.5 1.1 copy-done.1
  57.7 0.2 convolution_bitcast_fusion
  58.3 1.9 %collective-permute-start = (f32[3,576]{0,1:T(8,128)S(1)}, f32[3,576]{0,1:T(8,128)S(1)}, u32[]{:S(2)}, u32[]{:S(2)}) collective-permute-start(f32[3,576]{0,1:T(8,128)S(1)} %fusion.65), channel_id=1, source_target_pairs={{0,16},{16,32},{32,48},{48,64},{64,80},{80,96},{96,112},{1,17},{17... | collective-permute-start | bytes 20744 | tf_op jit(solution)/shard_map/ppermute | solution.py:17
  60.5 0.6 gather_fusion.1
  61.1 0.7 fusion.84
  61.9 0.6 slice_bitcast_fusion.8
  62.5 0.5 stack.8
  63.0 3.3 %collective-permute-done = f32[3,576]{0,1:T(8,128)S(1)} collective-permute-done((f32[3,576]{0,1:T(8,128)S(1)}, f32[3,576]{0,1:T(8,128)S(1)}, u32[]{:S(2)}, u32[]{:S(2)}) %collective-permute-start) | collective-permute-done | bytes 6944 | tf_op jit(solution)/shard_map/ppermute | solution.py:17
  66.3 0.4 maximum_maximum_fusion
  66.8 1.4 %divide_multiply_fusion = f32[512,576]{0,1:T(8,128)S(1)} fusion(f32[512,256]{0,1:T(8,128)S(1)} %slice.278, f32[512,320]{0,1:T(8,128)S(1)} %slice.277, f32[515,576]{0,1:T(8,128)S(1)} %maximum_maximum_fusion, f32[576]{0:T(1024)S(1)} %get-tuple-element.24, f32[512]{0:T(512)S(1)} %copy-done.9, f32[576]{0:T(1024)S(1)} %copy-done.5, f32[512]{0:T(512)S(1)} %copy-done.10, ...), kind=kLoop, calls=%fused_computation.63 | loop fusion | flops 4718592 | bytes 5915904 | tf_op jit(solution)/shard_map/jit(silu)/mul | solution.py:80
  68.3 1.0 copy-done
  69.3 0.4 reshape.566
  69.8 0.2 fusion.54
  70.3 1.0 tile.5
  71.3 4.8 %all-to-all-start.1 = ((bf16[8,5,80,128]{3,2,1,0:T(8,128)(2,1)}), bf16[8,5,80,128]{3,2,1,0:T(8,128)(2,1)S(1)}, u32[]{:S(2)}, u32[]{:S(2)}) async-start(bf16[8,5,80,128]{3,2,1,0:T(8,128)(2,1)} %tile.5), calls=%async_computation.1 | async-start | bytes 1638400 | tf_op jit(solution)/shard_map/all_to_all | solution.py:135
  76.2 0.4 fusion.66
  76.6 2.7 %fusion.40 = f32[2,256,5,64]{1,3,2,0:T(8,128)} fusion(f32[2,256,5]{1,2,0:T(8,128)S(1)} %bitcast.115, f32[2,256,5]{1,2,0:T(8,128)S(1)} %convolution_bitcast_fusion, f32[2,256,256]{2,1,0:T(8,128)S(1)} %fusion.66, pred[2,256,256]{2,1,0:T(8,128)(4,1)S(1)} %compare_and_fusion, f32[2,256,5,64]{1,0,3,2:T(2,128)S(1)} %reshape.566), kind=kOutput, calls=%fused_computation.47 | convolution fusion | flops 254935040 | bytes 1986560 | tf_op jit(solution)/shard_map/cijh,cjhp->cihp/dot_general | solution.py:104
  79.3 8.2 %all-to-all-done.1 = bf16[8,5,80,128]{3,2,1,0:T(8,128)(2,1)S(1)} async-done(((bf16[8,5,80,128]{3,2,1,0:T(8,128)(2,1)}), bf16[8,5,80,128]{3,2,1,0:T(8,128)(2,1)S(1)}, u32[]{:S(2)}, u32[]{:S(2)}) %all-to-all-start.1) | async-done | bytes 819232 | tf_op jit(solution)/shard_map/all_to_all | solution.py:135
  87.7 0.3 select_bitcast_fusion.7
  88.0 1.4 fusion.44
  89.4 0.5 copy.130
  90.0 1.4 multiply_convert_fusion
  91.6 3.2 %convolution_convert_fusion = bf16[512,2688]{1,0:T(8,128)(2,1)} fusion(bf16[320,2560]{1,0:T(8,128)(2,1)S(1)} %copy-done.35, bf16[128,2688]{1,0:T(8,128)(2,1)S(1)} %pad_convert_fusion, bf16[512,128]{0,1:T(8,128)(2,1)S(1)} %select_select_fusion, bf16[512,320]{0,1:T(8,128)(2,1)S(1)} %get-tuple-element.40), kind=kOutput, calls=%fused_computation.18 | convolution fusion | flops 1242644480 | bytes 5537792 | tf_op jit(solution)/shard_map/dot_general | solution.py:177
  94.8 3.9 %all-to-all-start.2 = ((bf16[16,32,2688]{2,1,0:T(8,128)(2,1)}), bf16[16,32,2688]{2,1,0:T(8,128)(2,1)S(1)}, u32[]{:S(2)}, u32[]{:S(2)}) async-start(bf16[16,32,2688]{2,1,0:T(8,128)(2,1)} %bitcast.102), calls=%async_computation.2 | async-start | bytes 5505024 | tf_op jit(solution)/shard_map/all_to_all | solution.py:182
  98.9 0.7 gather_fusion.2
  100.1 1.1 fusion.106
  101.2 1.7 %fusion = f32[16,5,64,128]{3,2,1,0:T(8,128)S(1)} fusion(f32[256,5,64]{0,2,1:T(8,128)S(1)} %bitcast.108, f32[16,256,5]{1,2,0:T(8,128)S(1)} %multiply_select_fusion, f32[512,576]{0,1:T(8,128)} %copy-done), kind=kOutput, calls=%fused_computation.3 | convolution fusion | flops 336855040 | bytes 3096576 | tf_op jit(solution)/shard_map/rjhp,jn->rhpn/dot_general | solution.py:221
  102.9 2.0 %add_convert_fusion = bf16[16,5,64,128]{3,2,1,0:T(8,128)(2,1)S(1)} fusion(f32[16,5,64,128]{3,2,1,0:T(8,128)S(1)} %fusion, f32[256,5,64]{0,2,1:T(8,128)S(1)} %bitcast.113, f32[16,256,5]{1,2,0:T(8,128)S(1)} %multiply_select_fusion.1, f32[5,64,128]{2,1,0:T(8,128)S(1)} %select_bitcast_fusion.7, f32[16,5]{1,0:T(8,128)S(1)} %get-tuple-element.28, ...), kind=kOutput, calls=%fused_computation.19 | convolution fusion | flops 341442560 | bytes 4735936 | tf_op jit(solution)/shard_map/rjhp,jn->rhpn/dot_general | solution.py:221
  105.0 1.1 copy-done.2
  106.0 0.8 select_bitcast_fusion.6
  106.8 1.2 collective-permute-start.6
  108.0 2.2 %collective-permute-start.5 = (bf16[2,5,64,128]{3,2,1,0:T(8,128)(2,1)}, bf16[2,5,64,128]{3,2,1,0:T(8,128)(2,1)}, u32[]{:S(2)}, u32[]{:S(2)}) collective-permute-start(bf16[2,5,64,128]{3,2,1,0:T(8,128)(2,1)} %get-tuple-element.49), channel_id=1, source_target_pairs={{0,80},{16,96},{32,112},{48,0},{64,16},{80,32},{96,48},{112,64},{1... | collective-permute-start | bytes 491528 | tf_op jit(solution)/shard_map/ppermute | solution.py:241
  110.2 0.5 collective-permute-start.4
  110.7 2.1 %collective-permute-start.3 = (bf16[2,5,64,128]{3,2,1,0:T(8,128)(2,1)S(1)}, bf16[2,5,64,128]{3,2,1,0:T(8,128)(2,1)}, u32[]{:S(2)}, u32[]{:S(2)}) collective-permute-start(bf16[2,5,64,128]{3,2,1,0:T(8,128)(2,1)S(1)} %get-tuple-element.51), channel_id=1, source_target_pairs={{0,48},{16,64},{32,80},{48,96},{64,112},{80,0},{96,16},{112,32},{1... | collective-permute-start | bytes 491528 | tf_op jit(solution)/shard_map/ppermute | solution.py:241
  112.8 0.7 collective-permute-start.2
  113.5 3.9 %collective-permute-done.6 = bf16[2,5,64,128]{3,2,1,0:T(8,128)(2,1)S(1)} collective-permute-done((bf16[2,5,64,128]{3,2,1,0:T(8,128)(2,1)S(1)}, bf16[2,5,64,128]{3,2,1,0:T(8,128)(2,1)S(1)}, u32[]{:S(2)}, u32[]{:S(2)}) %collective-permute-start.6) | collective-permute-done | bytes 163872 | tf_op jit(solution)/shard_map/ppermute | solution.py:241
  117.4 0.7 copy-done.4
  118.1 0.5 collective-permute-done.5
  118.5 6.3 %collective-permute-done.4 = bf16[2,5,64,128]{3,2,1,0:T(8,128)(2,1)} collective-permute-done((bf16[2,5,64,128]{3,2,1,0:T(8,128)(2,1)S(1)}, bf16[2,5,64,128]{3,2,1,0:T(8,128)(2,1)}, u32[]{:S(2)}, u32[]{:S(2)}) %collective-permute-start.4) | collective-permute-done | bytes 163872 | tf_op jit(solution)/shard_map/ppermute | solution.py:241
  124.8 0.4 collective-permute-done.3
  125.2 1.2 collective-permute-done.2
  126.4 0.3 collective-permute-done.1
  126.7 2.3 %convert_add_fusion = f32[2,5,64,128]{3,2,1,0:T(8,128)} fusion(bf16[2,5,64,128]{3,2,1,0:T(8,128)(2,1)} %copy-done.3, bf16[2,5,64,128]{3,2,1,0:T(8,128)(2,1)} %copy-done.4, bf16[2,5,64,128]{3,2,1,0:T(8,128)(2,1)} %collective-permute-done.5, bf16[2,5,64,128]{3,2,1,0:T(8,128)(2,1)} %collective-permute-done.4, ...), kind=kLoop, calls=%fused_computation.76 | loop fusion | flops 1310720 | bytes 1638405 | tf_op jit(solution)/shard_map/add | solution.py:243
  129.0 11.4 %all-to-all-done.2 = bf16[16,32,2688]{2,1,0:T(8,128)(2,1)S(1)} async-done(((bf16[16,32,2688]{2,1,0:T(8,128)(2,1)}), bf16[16,32,2688]{2,1,0:T(8,128)(2,1)S(1)}, u32[]{:S(2)}, u32[]{:S(2)}) %all-to-all-start.2) | async-done | bytes 2752544 | tf_op jit(solution)/shard_map/all_to_all | solution.py:182
  140.4 0.2 add_reduce_fusion
  140.6 1.3 multiply_reduce_fusion
  (137 shorter events, 3.7 us)
Async XLA Ops:
  3.3 9.4 %copy-start.37 = (f32[5]{0:T(128)S(1)}, f32[5]{0:T(128)}, u32[]{:S(2)}) copy-start(f32[5]{0:T(128)} %param.31) | copy-start | bytes 64
  3.3 48.1 %all-to-all-start = ((bf16[16,32,2560]{2,1,0:T(8,128)(2,1)}), bf16[16,32,2560]{2,1,0:T(8,128)(2,1)S(1)}, u32[]{:S(2)}, u32[]{:S(2)}) async-start(bf16[16,32,2560]{2,1,0:T(8,128)(2,1)} %tile.4), calls=%async_computation | async-start | bytes 5242880 | tf_op jit(solution)/shard_map/all_to_all | solution.py:50
  11.5 3.7 %copy-start.24 = (s32[16]{0:T(128)S(1)}, s32[16]{0:T(128)}, u32[]{:S(2)}) copy-start(s32[16]{0:T(128)} %param.35) | copy-start | bytes 196
  11.5 3.9 %copy-start.33 = (s32[16]{0:T(128)S(1)}, s32[16]{0:T(128)}, u32[]{:S(2)}) copy-start(s32[16]{0:T(128)} %param.36) | copy-start | bytes 196
  11.5 4.7 %copy-start.38 = (s32[16]{0:T(128)S(1)}, s32[16]{0:T(128)}, u32[]{:S(2)}) copy-start(s32[16]{0:T(128)} %param.37) | copy-start | bytes 196
  11.5 7.9 %copy-start.14 = (f32[4,320]{1,0:T(4,128)S(1)}, f32[4,320]{1,0:T(4,128)}, u32[]{:S(2)}) copy-start(f32[4,320]{1,0:T(4,128)} %param.26) | copy-start | bytes 15364
  11.6 7.9 %copy-start.20 = (f32[4,256]{1,0:T(4,128)S(1)}, f32[4,256]{1,0:T(4,128)}, u32[]{:S(2)}) copy-start(f32[4,256]{1,0:T(4,128)} %param.28) | copy-start | bytes 12292
  11.6 8.6 %copy-start.23 = (f32[320]{0:T(512)S(1)}, f32[320]{0:T(512)}, u32[]{:S(2)}) copy-start(f32[320]{0:T(512)} %param.27) | copy-start | bytes 3844
  11.6 8.6 %copy-start.28 = (f32[256]{0:T(256)S(1)}, f32[256]{0:T(256)}, u32[]{:S(2)}) copy-start(f32[256]{0:T(256)} %param.29) | copy-start | bytes 3076
  11.6 39.8 %copy-start.36 = (bf16[2560,5]{0,1:T(8,128)(2,1)S(1)}, bf16[2560,5]{0,1:T(8,128)(2,1)}, u32[]{:S(2)}) copy-start(bf16[2560,5]{0,1:T(8,128)(2,1)} %param.24) | copy-start | bytes 76804
  20.2 40.3 %copy-start.13 = (s32[1024]{0:T(1024)}, s32[1024]{0:T(1024)S(1)}, u32[]{:S(2)}) copy-start(s32[1024]{0:T(1024)S(1)} %pad_clamp_fusion) | copy-start | bytes 12292
  51.4 6.2 %copy-start.29 = (f32[5]{0:T(128)S(1)}, f32[5]{0:T(128)}, u32[]{:S(2)}) copy-start(f32[5]{0:T(128)} %param.30) | copy-start | bytes 64
  56.3 1.3 copy-start.1
  56.3 3.9 %copy-start.25 = (f32[2]{0:T(128)S(1)}, f32[2]{0:T(128)}, u32[]{:S(2)}) copy-start(f32[2]{0:T(128)} %fusion.97) | copy-start | bytes 28
  56.3 4.7 %copy-start.12 = (f32[2,256]{1,0:T(2,128)S(1)}, f32[2,256]{1,0:T(2,128)}, u32[]{:S(2)}) copy-start(f32[2,256]{1,0:T(2,128)} %get-tuple-element.69) | copy-start | bytes 6148
  56.3 4.8 %copy-start.15 = (pred[16]{0:T(512)(128)(4,1)S(1)}, pred[16]{0:T(512)(128)(4,1)}, u32[]{:S(2)}) copy-start(pred[16]{0:T(512)(128)(4,1)} %get-tuple-element.31) | copy-start | bytes 52
  56.4 4.8 %copy-start.17 = (pred[16]{0:T(512)(128)(4,1)S(1)}, pred[16]{0:T(512)(128)(4,1)}, u32[]{:S(2)}) copy-start(pred[16]{0:T(512)(128)(4,1)} %get-tuple-element.38) | copy-start | bytes 52
  56.4 5.4 %copy-start.26 = (pred[16]{0:T(512)(128)(4,1)S(1)}, pred[16]{0:T(512)(128)(4,1)}, u32[]{:S(2)}) copy-start(pred[16]{0:T(512)(128)(4,1)} %get-tuple-element.84) | copy-start | bytes 52
  56.4 5.4 %copy-start.34 = (pred[16]{0:T(512)(128)(4,1)S(1)}, pred[16]{0:T(512)(128)(4,1)}, u32[]{:S(2)}) copy-start(pred[16]{0:T(512)(128)(4,1)} %iota_compare_fusion.8) | copy-start | bytes 52
  58.1 8.7 %copy-start.5 = (f32[576]{0:T(1024)S(1)}, f32[576]{0:T(1024)}, u32[]{:S(2)}) copy-start(f32[576]{0:T(1024)} %get-tuple-element.25) | copy-start | bytes 6916
  58.1 8.7 %copy-start.8 = (f32[512]{0:T(512)S(1)}, f32[512]{0:T(512)}, u32[]{:S(2)}) copy-start(f32[512]{0:T(512)} %get-tuple-element.63) | copy-start | bytes 6148
  58.1 8.7 %copy-start.9 = (f32[512]{0:T(512)S(1)}, f32[512]{0:T(512)}, u32[]{:S(2)}) copy-start(f32[512]{0:T(512)} %get-tuple-element.64) | copy-start | bytes 6148
  58.1 8.7 %copy-start.10 = (f32[512]{0:T(512)S(1)}, f32[512]{0:T(512)}, u32[]{:S(2)}) copy-start(f32[512]{0:T(512)} %get-tuple-element.65) | copy-start | bytes 6148
  58.3 8.0 %collective-permute-start = (f32[3,576]{0,1:T(8,128)S(1)}, f32[3,576]{0,1:T(8,128)S(1)}, u32[]{:S(2)}, u32[]{:S(2)}) collective-permute-start(f32[3,576]{0,1:T(8,128)S(1)} %fusion.65), channel_id=1, source_target_pairs={{0,16},{16,32},{32,48},{48,64},{64,80},{80,96},{96,112},{1,17},{17... | collective-permute-start | bytes 20744 | tf_op jit(solution)/shard_map/ppermute | solution.py:17
  60.3 9.8 %copy-start.6 = (f32[5]{0:T(128)}, f32[5]{0:T(128)S(1)}, u32[]{:S(2)}) copy-start(f32[5]{0:T(128)S(1)} %get-tuple-element.76) | copy-start | bytes 64
  68.2 1.0 copy-start
  70.2 5.9 %copy-start.7 = (f32[5]{0:T(128)S(1)}, f32[5]{0:T(128)}, u32[]{:S(2)}) copy-start(f32[5]{0:T(128)} %copy-done.6) | copy-start | bytes 64
  71.3 16.2 %all-to-all-start.1 = ((bf16[8,5,80,128]{3,2,1,0:T(8,128)(2,1)}), bf16[8,5,80,128]{3,2,1,0:T(8,128)(2,1)S(1)}, u32[]{:S(2)}, u32[]{:S(2)}) async-start(bf16[8,5,80,128]{3,2,1,0:T(8,128)(2,1)} %tile.5), calls=%async_computation.1 | async-start | bytes 1638400 | tf_op jit(solution)/shard_map/all_to_all | solution.py:135
  76.6 11.3 %copy-start.19 = (f32[2,5]{1,0:T(2,128)S(1)}, f32[2,5]{1,0:T(2,128)}, u32[]{:S(2)}) copy-start(f32[2,5]{1,0:T(2,128)} %stack.8) | copy-start | bytes 124
  76.6 11.3 %copy-start.30 = (f32[5]{0:T(128)S(1)}, f32[5]{0:T(128)}, u32[]{:S(2)}) copy-start(f32[5]{0:T(128)} %param.32) | copy-start | bytes 64
  87.9 2.0 %copy-start.27 = (f32[320]{0:T(512)S(1)}, f32[320]{0:T(512)}, u32[]{:S(2)}) copy-start(f32[320]{0:T(512)} %param.33) | copy-start | bytes 3844
  89.9 1.6 %copy-start.31 = (pred[128]{0:T(512)(128)(4,1)S(1)}, pred[128]{0:T(512)(128)(4,1)}, u32[]{:S(2)}) copy-start(pred[128]{0:T(512)(128)(4,1)} %get-tuple-element.85) | copy-start | bytes 388
  89.9 1.6 %copy-start.32 = (pred[128]{0:T(512)(128)(4,1)S(1)}, pred[128]{0:T(512)(128)(4,1)}, u32[]{:S(2)}) copy-start(pred[128]{0:T(512)(128)(4,1)} %get-tuple-element.86) | copy-start | bytes 388
  89.9 1.7 %copy-start.35 = (bf16[320,2560]{1,0:T(8,128)(2,1)S(1)}, bf16[320,2560]{1,0:T(8,128)(2,1)}, u32[]{:S(2)}) copy-start(bf16[320,2560]{1,0:T(8,128)(2,1)} %param.34) | copy-start | bytes 4915204
  94.8 4.8 %copy-start.16 = (pred[16]{0:T(512)(128)(4,1)S(1)}, pred[16]{0:T(512)(128)(4,1)}, u32[]{:S(2)}) copy-start(pred[16]{0:T(512)(128)(4,1)} %get-tuple-element.31) | copy-start | bytes 52
  94.8 4.8 %copy-start.18 = (pred[16]{0:T(512)(128)(4,1)S(1)}, pred[16]{0:T(512)(128)(4,1)}, u32[]{:S(2)}) copy-start(pred[16]{0:T(512)(128)(4,1)} %get-tuple-element.38) | copy-start | bytes 52
  94.8 4.8 %copy-start.21 = (f32[5]{0:T(128)S(1)}, f32[5]{0:T(128)}, u32[]{:S(2)}) copy-start(f32[5]{0:T(128)} %get-tuple-element.72) | copy-start | bytes 64
  94.8 4.8 %copy-start.22 = (pred[16]{0:T(512)(128)(4,1)S(1)}, pred[16]{0:T(512)(128)(4,1)}, u32[]{:S(2)}) copy-start(pred[16]{0:T(512)(128)(4,1)} %get-tuple-element.36) | copy-start | bytes 52
  94.8 45.6 %all-to-all-start.2 = ((bf16[16,32,2688]{2,1,0:T(8,128)(2,1)}), bf16[16,32,2688]{2,1,0:T(8,128)(2,1)S(1)}, u32[]{:S(2)}, u32[]{:S(2)}) async-start(bf16[16,32,2688]{2,1,0:T(8,128)(2,1)} %bitcast.102), calls=%async_computation.2 | async-start | bytes 5505024 | tf_op jit(solution)/shard_map/all_to_all | solution.py:182
  100.0 3.0 %copy-start.11 = (f32[16,5]{1,0:T(8,128)S(1)}, f32[16,5]{1,0:T(8,128)}, u32[]{:S(2)}) copy-start(f32[16,5]{1,0:T(8,128)} %get-tuple-element.26) | copy-start | bytes 964
  105.0 1.1 copy-start.2
  106.8 5.9 %collective-permute-start.7 = (bf16[2,5,64,128]{3,2,1,0:T(8,128)(2,1)S(1)}, bf16[2,5,64,128]{3,2,1,0:T(8,128)(2,1)S(1)}, u32[]{:S(2)}, u32[]{:S(2)}) collective-permute-start(bf16[2,5,64,128]{3,2,1,0:T(8,128)(2,1)S(1)} %get-tuple-element.47), channel_id=1, source_target_pairs={{0,112},{16,0},{32,16},{48,32},{64,48},{80,64},{96,80},{112,96},{1... | collective-permute-start | bytes 491528 | tf_op jit(solution)/shard_map/ppermute | solution.py:241
  106.8 10.6 %collective-permute-start.6 = (bf16[2,5,64,128]{3,2,1,0:T(8,128)(2,1)S(1)}, bf16[2,5,64,128]{3,2,1,0:T(8,128)(2,1)S(1)}, u32[]{:S(2)}, u32[]{:S(2)}) collective-permute-start(bf16[2,5,64,128]{3,2,1,0:T(8,128)(2,1)S(1)} %get-tuple-element.48), channel_id=1, source_target_pairs={{0,96},{16,112},{32,0},{48,16},{64,32},{80,48},{96,64},{112,80},{1... | collective-permute-start | bytes 491528 | tf_op jit(solution)/shard_map/ppermute | solution.py:241
  108.0 10.5 %collective-permute-start.5 = (bf16[2,5,64,128]{3,2,1,0:T(8,128)(2,1)}, bf16[2,5,64,128]{3,2,1,0:T(8,128)(2,1)}, u32[]{:S(2)}, u32[]{:S(2)}) collective-permute-start(bf16[2,5,64,128]{3,2,1,0:T(8,128)(2,1)} %get-tuple-element.49), channel_id=1, source_target_pairs={{0,80},{16,96},{32,112},{48,0},{64,16},{80,32},{96,48},{112,64},{1... | collective-permute-start | bytes 491528 | tf_op jit(solution)/shard_map/ppermute | solution.py:241
  110.2 14.6 %collective-permute-start.4 = (bf16[2,5,64,128]{3,2,1,0:T(8,128)(2,1)S(1)}, bf16[2,5,64,128]{3,2,1,0:T(8,128)(2,1)}, u32[]{:S(2)}, u32[]{:S(2)}) collective-permute-start(bf16[2,5,64,128]{3,2,1,0:T(8,128)(2,1)S(1)} %get-tuple-element.50), channel_id=1, source_target_pairs={{0,64},{16,80},{32,96},{48,112},{64,0},{80,16},{96,32},{112,48},{1... | collective-permute-start | bytes 491528 | tf_op jit(solution)/shard_map/ppermute | solution.py:241
  110.7 14.5 %collective-permute-start.3 = (bf16[2,5,64,128]{3,2,1,0:T(8,128)(2,1)S(1)}, bf16[2,5,64,128]{3,2,1,0:T(8,128)(2,1)}, u32[]{:S(2)}, u32[]{:S(2)}) collective-permute-start(bf16[2,5,64,128]{3,2,1,0:T(8,128)(2,1)S(1)} %get-tuple-element.51), channel_id=1, source_target_pairs={{0,48},{16,64},{32,80},{48,96},{64,112},{80,0},{96,16},{112,32},{1... | collective-permute-start | bytes 491528 | tf_op jit(solution)/shard_map/ppermute | solution.py:241
  112.8 4.6 %copy-start.3 = (bf16[2,5,64,128]{3,2,1,0:T(8,128)(2,1)}, bf16[2,5,64,128]{3,2,1,0:T(8,128)(2,1)S(1)}, u32[]{:S(2)}) copy-start(bf16[2,5,64,128]{3,2,1,0:T(8,128)(2,1)S(1)} %collective-permute-done.7) | copy-start | bytes 491524
  112.8 13.7 %collective-permute-start.2 = (bf16[2,5,64,128]{3,2,1,0:T(8,128)(2,1)S(1)}, bf16[2,5,64,128]{3,2,1,0:T(8,128)(2,1)}, u32[]{:S(2)}, u32[]{:S(2)}) collective-permute-start(bf16[2,5,64,128]{3,2,1,0:T(8,128)(2,1)S(1)} %get-tuple-element.52), channel_id=1, source_target_pairs={{0,32},{16,48},{32,64},{48,80},{64,96},{80,112},{96,0},{112,16},{1... | collective-permute-start | bytes 491528 | tf_op jit(solution)/shard_map/ppermute | solution.py:241
  117.4 0.7 copy-start.4
  118.1 8.6 %collective-permute-start.1 = (bf16[2,5,64,128]{3,2,1,0:T(8,128)(2,1)S(1)}, bf16[2,5,64,128]{3,2,1,0:T(8,128)(2,1)}, u32[]{:S(2)}, u32[]{:S(2)}) collective-permute-start(bf16[2,5,64,128]{3,2,1,0:T(8,128)(2,1)S(1)} %get-tuple-element.46), channel_id=1, source_target_pairs={{0,16},{16,32},{32,48},{48,64},{64,80},{80,96},{96,112},{112,0},{1... | collective-permute-start | bytes 491528 | tf_op jit(solution)/shard_map/ppermute | solution.py:241
